TPU v7x, 32 devices: a whole 2x2x4 slice. The times are simulated.
32 devices in a mesh: group: 2 (over x), row: 8 (over z, y), col: 2 (over core).
Axes of the slice: x: 2, y: 2, z: 4, core: 2. Of those that a mesh axis runs over, the one named last changes fastest.
Arguments:
- observed: float32 [32, 65536], P('group', ('row', 'col')), parts along dimension 0, may hold values from -50 to 50
- blocks: float32 [32, 160, 128, 128], P(('group', 'row', 'col')), parts along dimension 0, may hold values from -0.25 to 0.25
- block_rows: int32 [32, 160], P(('group', 'row', 'col')), parts along dimension 0, may hold values from 0 to 31
- block_cols: int32 [32, 160], P(('group', 'row', 'col')), parts along dimension 0, may hold values from 0 to 191, as said below
- counts: int32 [32], P(('group', 'row', 'col')), parts along dimension 0, may hold values from 32 to 160, as said below
Outputs:
- solution: float32 [32, 131072], P('group', ('row', 'col')), parts along dimension 0
- search_direction: float32 [32, 131072], P('group', ('row', 'col')), parts along dimension 0
There are 2 independent parts, one for each index of `group`. A program takes and returns all parts, laid end to end along the dimension named above; each array names one. Nothing has to cross between parts.
Inputs may be any that keep to these rules, and one draw needn't show every extreme that they name: block_cols of band 0 are 64 or more, those of the last band under 2 * 64. `counts`: some band has exactly 160 live slots.
All inputs are finite; a program needn't handle non-finite values.
Results may differ from a plain program's by a relative error of at most 0.0003.
Values sent between devices are 32-bit elements; how exact they have to be, the bound alone decides.
No kernel may reach another device: no remote copies, remote signals or barrier semaphores. Data moves between devices by JAX's collectives and lax.ppermute only.
A program may use at most 64 MiB of HBM per device.

v0:
```python
import jax
import jax.numpy as jnp
from jax import lax
from jax.sharding import PartitionSpec as P

ROW_BLOCKS = 32
COL_BLOCKS = 64
ITERATIONS = 2


PRECISE = lax.Precision.HIGHEST


def with_halo(shard, sides, width):
    for axis, dim in sides:
        peers, length = (lax.axis_size(axis), shard.shape[dim])
        up = [(i, (i + 1) % peers) for i in range(peers - 1)]
        down = [(j, i) for i, j in up]
        last = lax.slice_in_dim(shard, length - width, length, axis=dim)
        leading = lax.slice_in_dim(shard, 0, width, axis=dim)
        before = lax.ppermute(last, axis, up)
        after = lax.ppermute(leading, axis, down)
        shard = jnp.concatenate([before, shard, after], axis=dim)
    return shard


def from_behind(shard, axis, by):
    peers = lax.axis_size(axis)
    pairs = [(i, i + by) for i in range(peers) if 0 <= i + by < peers]
    return lax.ppermute(shard, axis, pairs)


def forward_local(window, tile_stack, rows_idx, cols_idx, live_slot):
    scenario_rows = window.shape[0]
    tile_edge = tile_stack.shape[1]
    pieces = window.reshape(scenario_rows, 3 * COL_BLOCKS, tile_edge)[:, cols_idx, :]
    products = (
        jnp.einsum("skj,kij->ksi", pieces, tile_stack, precision=PRECISE) * live_slot[:, None, None]
    )
    onehot = (rows_idx[:, None] == jnp.arange(ROW_BLOCKS)[None, :]).astype(jnp.float32)
    summed = jnp.einsum("kr,ksi->sri", onehot, products, precision=PRECISE)
    return summed.reshape(scenario_rows, ROW_BLOCKS * tile_edge)


def transpose_local(field, tile_stack, rows_idx, cols_idx, live_slot):
    scenario_rows = field.shape[0]
    tile_edge = tile_stack.shape[1]
    pieces = field.reshape(scenario_rows, ROW_BLOCKS, tile_edge)[:, rows_idx, :]
    products = (
        jnp.einsum("ski,kij->ksj", pieces, tile_stack, precision=PRECISE) * live_slot[:, None, None]
    )
    onehot = (cols_idx[:, None] == jnp.arange(3 * COL_BLOCKS)[None, :]).astype(jnp.float32)
    summed = jnp.einsum("kc,ksj->scj", onehot, products, precision=PRECISE)
    return summed.reshape(scenario_rows, 3 * COL_BLOCKS * tile_edge)


def forward_apply(vector, tile_stack, rows_idx, cols_idx, live_slot):
    window = with_halo(vector, ((("row", "col"), 1),), vector.shape[1])
    return forward_local(window, tile_stack, rows_idx, cols_idx, live_slot)


def transpose_apply(field, tile_stack, rows_idx, cols_idx, live_slot):
    partial_sums = transpose_local(field, tile_stack, rows_idx, cols_idx, live_slot)
    band_width = partial_sums.shape[1] // 3
    lower = partial_sums[:, :band_width]
    middle = partial_sums[:, band_width : 2 * band_width]
    upper = partial_sums[:, 2 * band_width :]
    from_below = from_behind(upper, ("row", "col"), 1)
    from_above = from_behind(lower, ("row", "col"), -1)
    result = middle + from_below + from_above
    return result


def all_sum(values, axes):
    peers = 1
    for axis in axes:
        peers *= lax.axis_size(axis)
    if peers & (peers - 1):
        return lax.psum(values, axes)
    shift = 1
    while shift < peers:
        width = 4 if shift * 4 <= peers else 2
        parts = [values]
        for k in range(1, width):
            pairs = [(i, i ^ (k * shift)) for i in range(peers)]
            parts.append(lax.ppermute(values, axes, pairs))
        if width == 4:
            values = (parts[0] + parts[1]) + (parts[2] + parts[3])
        else:
            values = parts[0] + parts[1]
        shift *= width
    return values


def squares(field):
    return jnp.sum(field * field, axis=1)


def per_device(observed, blocks, block_rows, block_cols, counts):
    tile_stack = blocks[0]
    rows_idx = block_rows[0]
    cols_idx = block_cols[0]
    slot_ids = jnp.arange(tile_stack.shape[0])
    live_slot = (slot_ids < counts[0]).astype(jnp.float32)
    axes = ("row", "col")

    def backward(field):
        return transpose_apply(field, tile_stack, rows_idx, cols_idx, live_slot)

    def forward(vector):
        return forward_apply(vector, tile_stack, rows_idx, cols_idx, live_slot)

    start_raw = backward(observed)
    totals = all_sum(jnp.stack([squares(observed), squares(start_raw)]), axes)
    row_norm = jnp.sqrt(totals[0] + 1e-06)
    col_norm = jnp.sqrt(totals[1] / (row_norm * row_norm) + 1e-06)
    scale = row_norm * col_norm
    left_vec = observed / row_norm[:, None]
    right_vec = start_raw / scale[:, None]
    left_prod = forward(start_raw)
    left_raw = left_prod / scale[:, None] - col_norm[:, None] * left_vec
    dir_now = right_vec
    solution = jnp.zeros_like(dir_now)
    phi_bar = row_norm
    diag_bar = col_norm
    for iteration in range(ITERATIONS):
        right_prod = backward(left_raw)
        row_norm = jnp.sqrt(all_sum(squares(left_raw), axes) + 1e-06)
        left_vec = left_raw / row_norm[:, None]
        right_raw = right_prod / row_norm[:, None] - row_norm[:, None] * right_vec
        if iteration + 1 < ITERATIONS:
            left_prod = forward(right_raw)
        col_norm = jnp.sqrt(all_sum(squares(right_raw), axes) + 1e-06)
        right_vec = right_raw / col_norm[:, None]
        if iteration + 1 < ITERATIONS:
            left_raw = left_prod / col_norm[:, None] - col_norm[:, None] * left_vec
        diag_new = jnp.sqrt(diag_bar * diag_bar + row_norm * row_norm)
        rot_cosine = diag_bar / diag_new
        rot_sine = row_norm / diag_new
        off_diag = rot_sine * col_norm
        diag_bar = -rot_cosine * col_norm
        phi_now = rot_cosine * phi_bar
        phi_bar = rot_sine * phi_bar
        solution = solution + (phi_now / diag_new)[:, None] * dir_now
        dir_now = right_vec - (off_diag / diag_new)[:, None] * dir_now
    return (solution, dir_now)


def solution(mesh):
    in_specs = (
        P("group", ("row", "col")),
        P(("group", "row", "col"), None, None, None),
        P(("group", "row", "col"), None),
        P(("group", "row", "col"), None),
        P(("group", "row", "col")),
    )
    out_specs = (P("group", ("row", "col")), P("group", ("row", "col")))
    return jax.shard_map(
        per_device, mesh=mesh, in_specs=in_specs, out_specs=out_specs, check_vma=False
    )
```

profile of v0, /device:TPU:0, one launch (start us, length us, event | category | flops | bytes accessed | tf_op | source)
XLA Modules:
  0.0 221.6 jit_solution(18083759820366063870)
XLA Ops:
  2.0 1.0 copy_bitcast_fusion.7
  3.8 11.5 %fusion.10 = f32[160,16,128]{2,1,0:T(8,128)S(1)} fusion(f32[1,160,128,128]{3,2,1,0:T(8,128)} %param.6, f32[160,16,128]{2,1,0:T(8,128)S(1)} %gather_fusion, f32[160]{0:T(256)S(1)} %compare_convert_fusion), kind=kOutput, calls=%fused_computation.22 | convolution fusion | flops 503644160 | bytes 13107840 | tf_op jit(solution)/shard_map/ski,kij->ksj/dot_general | solution.py:50
  15.3 1.3 fusion.38
  16.6 0.9 copy.51
  17.7 2.4 %collective-permute-start = (f32[16,8192]{1,0:T(8,128)S(1)}, f32[16,8192]{1,0:T(8,128)S(1)}, u32[]{:S(2)}, u32[]{:S(2)}) collective-permute-start(f32[16,8192]{1,0:T(8,128)S(1)} %get-tuple-element.23), channel_id=1, source_target_pairs={{0,1},{1,2},{2,3},{3,4},{4,5},{5,6},{6,7},{7,8},{8,9},{9,10},{10,1... | collective-permute-start | bytes 1572872 | tf_op jit(solution)/shard_map/ppermute | solution.py:30
  20.0 1.3 collective-permute-start.1
  21.5 4.4 %collective-permute-done.1 = f32[16,8192]{1,0:T(8,128)S(1)} collective-permute-done((f32[16,8192]{1,0:T(8,128)S(1)}, f32[16,8192]{1,0:T(8,128)S(1)}, u32[]{:S(2)}, u32[]{:S(2)}) %collective-permute-start.1) | collective-permute-done | bytes 524320 | tf_op jit(solution)/shard_map/ppermute | solution.py:30
  26.2 10.8 %collective-permute-start.3 = (f32[2,16]{1,0:T(2,128)S(1)}, f32[2,16]{1,0:T(2,128)S(1)}, u32[]{:S(2)}, u32[]{:S(2)}) collective-permute-start(f32[2,16]{1,0:T(2,128)S(1)} %pad_maximum_fusion), channel_id=1, source_target_pairs={{0,2},{1,3},{2,0},{3,1},{4,6},{5,7},{6,4},{7,5},{8,10},{9,11},{10,... | collective-permute-start | bytes 392 | tf_op jit(solution)/shard_map/ppermute | solution.py:86
  37.2 1.3 collective-permute-start.9
  38.5 3.1 %collective-permute-start.8 = (f32[16,8192]{1,0:T(8,128)S(1)}, f32[16,8192]{1,0:T(8,128)S(1)}, u32[]{:S(2)}, u32[]{:S(2)}) collective-permute-start(f32[16,8192]{1,0:T(8,128)S(1)} %get-tuple-element.18), channel_id=1, source_target_pairs={{0,1},{1,2},{2,3},{3,4},{4,5},{5,6},{6,7},{7,8},{8,9},{9,10},{10,1... | collective-permute-start | bytes 1572872 | tf_op jit(solution)/shard_map/ppermute | solution.py:21
  41.6 4.6 %collective-permute-start.7 = (f32[2,16]{1,0:T(2,128)S(1)}, f32[2,16]{1,0:T(2,128)S(1)}, u32[]{:S(2)}, u32[]{:S(2)}) collective-permute-start(f32[2,16]{1,0:T(2,128)S(1)} %add_add_fusion.1), channel_id=1, source_target_pairs={{0,12},{1,13},{2,14},{3,15},{4,8},{5,9},{6,10},{7,11},{8,4},{9,5},... | collective-permute-start | bytes 392 | tf_op jit(solution)/shard_map/ppermute | solution.py:86
  46.9 4.5 %collective-permute-done.7 = f32[2,16]{1,0:T(2,128)S(1)} collective-permute-done((f32[2,16]{1,0:T(2,128)S(1)}, f32[2,16]{1,0:T(2,128)S(1)}, u32[]{:S(2)}, u32[]{:S(2)}) %collective-permute-start.7) | collective-permute-done | bytes 160 | tf_op jit(solution)/shard_map/ppermute | solution.py:86
  52.4 19.2 %fusion.13 = f32[160,16,128]{2,1,0:T(8,128)S(1)} fusion(f32[1,160,128,128]{3,2,1,0:T(8,128)} %param.6, f32[160,16,128]{2,1,0:T(8,128)S(1)} %gather_fusion.1, f32[160]{0:T(256)S(1)} %compare_convert_fusion), kind=kOutput, calls=%fused_computation.23 | convolution fusion | flops 503644160 | bytes 13107840 | tf_op jit(solution)/shard_map/skj,kij->ksi/dot_general | solution.py:38
  73.7 22.9 %fusion.16 = f32[160,16,128]{2,1,0:T(8,128)S(1)} fusion(f32[1,160,128,128]{3,2,1,0:T(8,128)} %param.6, f32[160,16,128]{2,1,0:T(8,128)S(1)} %gather_fusion.2, f32[160]{0:T(256)S(1)} %compare_convert_fusion), kind=kOutput, calls=%fused_computation.24 | convolution fusion | flops 503644160 | bytes 13107840 | tf_op jit(solution)/shard_map/ski,kij->ksj/dot_general | solution.py:50
  96.6 1.3 fusion.34
  98.9 4.5 %collective-permute-start.16 = (f32[16,8192]{1,0:T(8,128)S(1)}, f32[16,8192]{1,0:T(8,128)S(1)}, u32[]{:S(2)}, u32[]{:S(2)}) collective-permute-start(f32[16,8192]{1,0:T(8,128)S(1)} %get-tuple-element.21), channel_id=1, source_target_pairs={{0,1},{1,2},{2,3},{3,4},{4,5},{5,6},{6,7},{7,8},{8,9},{9,10},{10,1... | collective-permute-start | bytes 1572872 | tf_op jit(solution)/shard_map/ppermute | solution.py:30
  103.4 1.3 collective-permute-start.17
  104.7 3.1 %collective-permute-start.12 = (f32[16]{0:T(128)S(1)}, f32[16]{0:T(128)S(1)}, u32[]{:S(2)}, u32[]{:S(2)}) collective-permute-start(f32[16]{0:T(128)S(1)} %get-tuple-element.13), channel_id=1, source_target_pairs={{0,3},{1,2},{2,1},{3,0},{4,7},{5,6},{6,5},{7,4},{8,11},{9,10},{10,... | collective-permute-start | bytes 200 | tf_op jit(solution)/shard_map/ppermute | solution.py:86
  107.8 1.7 collective-permute-start.11
  109.6 6.9 %collective-permute-done.11 = f32[16]{0:T(128)S(1)} collective-permute-done((f32[16]{0:T(128)S(1)}, f32[16]{0:T(128)S(1)}, u32[]{:S(2)}, u32[]{:S(2)}) %collective-permute-start.11) | collective-permute-done | bytes 96 | tf_op jit(solution)/shard_map/ppermute | solution.py:86
  116.5 3.7 %collective-permute-start.15 = (f32[16]{0:T(128)S(1)}, f32[16]{0:T(128)S(1)}, u32[]{:S(2)}, u32[]{:S(2)}) collective-permute-start(f32[16]{0:T(128)S(1)} %add_add_fusion.5), channel_id=1, source_target_pairs={{0,12},{1,13},{2,14},{3,15},{4,8},{5,9},{6,10},{7,11},{8,4},{9,5},... | collective-permute-start | bytes 200 | tf_op jit(solution)/shard_map/ppermute | solution.py:86
  121.0 0.9 collective-permute-done.15
  121.9 2.8 %collective-permute-done.14 = f32[16]{0:T(128)S(1)} collective-permute-done((f32[16]{0:T(128)S(1)}, f32[16]{0:T(128)S(1)}, u32[]{:S(2)}, u32[]{:S(2)}) %collective-permute-start.14) | collective-permute-done | bytes 96 | tf_op jit(solution)/shard_map/ppermute | solution.py:86
  125.0 1.3 collective-permute-start.25
  126.3 3.1 %collective-permute-start.24 = (f32[16,8192]{1,0:T(8,128)S(1)}, f32[16,8192]{1,0:T(8,128)S(1)}, u32[]{:S(2)}, u32[]{:S(2)}) collective-permute-start(f32[16,8192]{1,0:T(8,128)S(1)} %get-tuple-element.12), channel_id=1, source_target_pairs={{0,1},{1,2},{2,3},{3,4},{4,5},{5,6},{6,7},{7,8},{8,9},{9,10},{10,1... | collective-permute-start | bytes 1572872 | tf_op jit(solution)/shard_map/ppermute | solution.py:21
  129.4 2.1 collective-permute-start.20
  131.5 1.2 collective-permute-start.19
  132.8 3.3 %collective-permute-done.19 = f32[16]{0:T(128)S(1)} collective-permute-done((f32[16]{0:T(128)S(1)}, f32[16]{0:T(128)S(1)}, u32[]{:S(2)}, u32[]{:S(2)}) %collective-permute-start.19) | collective-permute-done | bytes 96 | tf_op jit(solution)/shard_map/ppermute | solution.py:86
  136.1 8.2 %collective-permute-start.23 = (f32[16]{0:T(128)S(1)}, f32[16]{0:T(128)S(1)}, u32[]{:S(2)}, u32[]{:S(2)}) collective-permute-start(f32[16]{0:T(128)S(1)} %add_add_fusion.4), channel_id=1, source_target_pairs={{0,12},{1,13},{2,14},{3,15},{4,8},{5,9},{6,10},{7,11},{8,4},{9,5},... | collective-permute-start | bytes 200 | tf_op jit(solution)/shard_map/ppermute | solution.py:86
  145.7 2.9 %collective-permute-done.22 = f32[16]{0:T(128)S(1)} collective-permute-done((f32[16]{0:T(128)S(1)}, f32[16]{0:T(128)S(1)}, u32[]{:S(2)}, u32[]{:S(2)}) %collective-permute-start.22) | collective-permute-done | bytes 96 | tf_op jit(solution)/shard_map/ppermute | solution.py:86
  148.8 1.9 gather_fusion.3
  150.7 19.1 %fusion.19 = f32[160,16,128]{2,1,0:T(8,128)S(1)} fusion(f32[1,160,128,128]{3,2,1,0:T(8,128)} %param.6, f32[160,16,128]{2,1,0:T(8,128)} %gather_fusion.3, f32[160]{0:T(256)S(1)} %compare_convert_fusion), kind=kOutput, calls=%fused_computation.25 | convolution fusion | flops 503644160 | bytes 13107840 | tf_op jit(solution)/shard_map/skj,kij->ksi/dot_general | solution.py:38
  171.9 11.7 %fusion.22 = f32[160,16,128]{2,1,0:T(8,128)S(1)} fusion(f32[1,160,128,128]{3,2,1,0:T(8,128)} %param.6, f32[160,16,128]{2,1,0:T(8,128)S(1)} %gather_fusion.4, f32[160]{0:T(256)S(1)} %compare_convert_fusion), kind=kOutput, calls=%fused_computation.26 | convolution fusion | flops 503644160 | bytes 13107840 | tf_op jit(solution)/shard_map/ski,kij->ksj/dot_general | solution.py:50
  183.7 1.3 fusion.30
  185.9 1.3 collective-permute-start.32
  187.3 1.3 collective-permute-start.33
  188.6 2.2 collective-permute-start.28
  190.8 1.3 collective-permute-start.27
  192.1 6.9 %collective-permute-done.27 = f32[16]{0:T(128)S(1)} collective-permute-done((f32[16]{0:T(128)S(1)}, f32[16]{0:T(128)S(1)}, u32[]{:S(2)}, u32[]{:S(2)}) %collective-permute-start.27) | collective-permute-done | bytes 96 | tf_op jit(solution)/shard_map/ppermute | solution.py:86
  199.0 5.5 %collective-permute-start.31 = (f32[16]{0:T(128)S(1)}, f32[16]{0:T(128)S(1)}, u32[]{:S(2)}, u32[]{:S(2)}) collective-permute-start(f32[16]{0:T(128)S(1)} %add_add_fusion.3), channel_id=1, source_target_pairs={{0,12},{1,13},{2,14},{3,15},{4,8},{5,9},{6,10},{7,11},{8,4},{9,5},... | collective-permute-start | bytes 200 | tf_op jit(solution)/shard_map/ppermute | solution.py:86
  206.0 2.9 %collective-permute-done.30 = f32[16]{0:T(128)S(1)} collective-permute-done((f32[16]{0:T(128)S(1)}, f32[16]{0:T(128)S(1)}, u32[]{:S(2)}, u32[]{:S(2)}) %collective-permute-start.30) | collective-permute-done | bytes 96 | tf_op jit(solution)/shard_map/ppermute | solution.py:86
  209.6 1.6 collective-permute-start.34
  211.2 1.1 collective-permute-done.36
  213.0 2.6 %collective-permute-start.39 = (f32[16]{0:T(128)S(1)}, f32[16]{0:T(128)S(1)}, u32[]{:S(2)}, u32[]{:S(2)}) collective-permute-start(f32[16]{0:T(128)S(1)} %add_add_fusion.2), channel_id=1, source_target_pairs={{0,12},{1,13},{2,14},{3,15},{4,8},{5,9},{6,10},{7,11},{8,4},{9,5},... | collective-permute-start | bytes 200 | tf_op jit(solution)/shard_map/ppermute | solution.py:86
  215.6 1.8 collective-permute-start.37
  217.4 0.9 collective-permute-done.39
  218.4 1.7 collective-permute-done.38
  220.1 1.2 multiply_subtract_fusion
  (93 shorter events, 15.8 us)
Async XLA Ops:
  3.8 11.5 %copy-start.2 = (s32[1,160]{1,0:T(1,128)S(1)}, s32[1,160]{1,0:T(1,128)}, u32[]{:S(2)}) copy-start(s32[1,160]{1,0:T(1,128)} %param.8) | copy-start | bytes 1924
  17.6 3.8 %copy-start = (f32[16,4096]{1,0:T(8,128)S(1)}, f32[16,4096]{1,0:T(8,128)}, u32[]{:S(2)}) copy-start(f32[16,4096]{1,0:T(8,128)} %param.5) | copy-start | bytes 786436
  17.7 3.9 %collective-permute-start = (f32[16,8192]{1,0:T(8,128)S(1)}, f32[16,8192]{1,0:T(8,128)S(1)}, u32[]{:S(2)}, u32[]{:S(2)}) collective-permute-start(f32[16,8192]{1,0:T(8,128)S(1)} %get-tuple-element.23), channel_id=1, source_target_pairs={{0,1},{1,2},{2,3},{3,4},{4,5},{5,6},{6,7},{7,8},{8,9},{9,10},{10,1... | collective-permute-start | bytes 1572872 | tf_op jit(solution)/shard_map/ppermute | solution.py:30
  20.0 5.9 %collective-permute-start.1 = (f32[16,8192]{1,0:T(8,128)S(1)}, f32[16,8192]{1,0:T(8,128)S(1)}, u32[]{:S(2)}, u32[]{:S(2)}) collective-permute-start(f32[16,8192]{1,0:T(8,128)S(1)} %get-tuple-element.24), channel_id=1, source_target_pairs={{1,0},{2,1},{3,2},{4,3},{5,4},{6,5},{7,6},{8,7},{9,8},{10,9},{11,1... | collective-permute-start | bytes 1572872 | tf_op jit(solution)/shard_map/ppermute | solution.py:30
  26.2 15.4 %collective-permute-start.3 = (f32[2,16]{1,0:T(2,128)S(1)}, f32[2,16]{1,0:T(2,128)S(1)}, u32[]{:S(2)}, u32[]{:S(2)}) collective-permute-start(f32[2,16]{1,0:T(2,128)S(1)} %pad_maximum_fusion), channel_id=1, source_target_pairs={{0,2},{1,3},{2,0},{3,1},{4,6},{5,7},{6,4},{7,5},{8,10},{9,11},{10,... | collective-permute-start | bytes 392 | tf_op jit(solution)/shard_map/ppermute | solution.py:86
  37.0 4.6 %collective-permute-start.4 = (f32[2,16]{1,0:T(2,128)S(1)}, f32[2,16]{1,0:T(2,128)S(1)}, u32[]{:S(2)}, u32[]{:S(2)}) collective-permute-start(f32[2,16]{1,0:T(2,128)S(1)} %pad_maximum_fusion), channel_id=1, source_target_pairs={{0,3},{1,2},{2,1},{3,0},{4,7},{5,6},{6,5},{7,4},{8,11},{9,10},{10,... | collective-permute-start | bytes 392 | tf_op jit(solution)/shard_map/ppermute | solution.py:86
  37.0 4.6 %collective-permute-start.2 = (f32[2,16]{1,0:T(2,128)S(1)}, f32[2,16]{1,0:T(2,128)S(1)}, u32[]{:S(2)}, u32[]{:S(2)}) collective-permute-start(f32[2,16]{1,0:T(2,128)S(1)} %pad_maximum_fusion), channel_id=1, source_target_pairs={{0,1},{1,0},{2,3},{3,2},{4,5},{5,4},{6,7},{7,6},{8,9},{9,8},{10,11... | collective-permute-start | bytes 392 | tf_op jit(solution)/shard_map/ppermute | solution.py:86
  37.2 14.2 %collective-permute-start.9 = (f32[16,8192]{1,0:T(8,128)S(1)}, f32[16,8192]{1,0:T(8,128)S(1)}, u32[]{:S(2)}, u32[]{:S(2)}) collective-permute-start(f32[16,8192]{1,0:T(8,128)S(1)} %get-tuple-element.18), channel_id=1, source_target_pairs={{1,0},{2,1},{3,2},{4,3},{5,4},{6,5},{7,6},{8,7},{9,8},{10,9},{11,1... | collective-permute-start | bytes 1572872 | tf_op jit(solution)/shard_map/ppermute | solution.py:22
  38.5 12.9 %collective-permute-start.8 = (f32[16,8192]{1,0:T(8,128)S(1)}, f32[16,8192]{1,0:T(8,128)S(1)}, u32[]{:S(2)}, u32[]{:S(2)}) collective-permute-start(f32[16,8192]{1,0:T(8,128)S(1)} %get-tuple-element.18), channel_id=1, source_target_pairs={{0,1},{1,2},{2,3},{3,4},{4,5},{5,6},{6,7},{7,8},{8,9},{9,10},{10,1... | collective-permute-start | bytes 1572872 | tf_op jit(solution)/shard_map/ppermute | solution.py:21
  41.6 9.7 %collective-permute-start.7 = (f32[2,16]{1,0:T(2,128)S(1)}, f32[2,16]{1,0:T(2,128)S(1)}, u32[]{:S(2)}, u32[]{:S(2)}) collective-permute-start(f32[2,16]{1,0:T(2,128)S(1)} %add_add_fusion.1), channel_id=1, source_target_pairs={{0,12},{1,13},{2,14},{3,15},{4,8},{5,9},{6,10},{7,11},{8,4},{9,5},... | collective-permute-start | bytes 392 | tf_op jit(solution)/shard_map/ppermute | solution.py:86
  46.2 5.2 %collective-permute-start.6 = (f32[2,16]{1,0:T(2,128)S(1)}, f32[2,16]{1,0:T(2,128)S(1)}, u32[]{:S(2)}, u32[]{:S(2)}) collective-permute-start(f32[2,16]{1,0:T(2,128)S(1)} %add_add_fusion.1), channel_id=1, source_target_pairs={{0,8},{1,9},{2,10},{3,11},{4,12},{5,13},{6,14},{7,15},{8,0},{9,1},... | collective-permute-start | bytes 392 | tf_op jit(solution)/shard_map/ppermute | solution.py:86
  46.2 5.2 %collective-permute-start.5 = (f32[2,16]{1,0:T(2,128)S(1)}, f32[2,16]{1,0:T(2,128)S(1)}, u32[]{:S(2)}, u32[]{:S(2)}) collective-permute-start(f32[2,16]{1,0:T(2,128)S(1)} %add_add_fusion.1), channel_id=1, source_target_pairs={{0,4},{1,5},{2,6},{3,7},{4,0},{5,1},{6,2},{7,3},{8,12},{9,13},{10,... | collective-permute-start | bytes 392 | tf_op jit(solution)/shard_map/ppermute | solution.py:86
  52.4 19.2 %copy-start.3 = (s32[1,160]{1,0:T(1,128)S(1)}, s32[1,160]{1,0:T(1,128)}, u32[]{:S(2)}) copy-start(s32[1,160]{1,0:T(1,128)} %param.7) | copy-start | bytes 1924
  71.6 1.0 copy-start.1
  98.9 25.8 %collective-permute-start.16 = (f32[16,8192]{1,0:T(8,128)S(1)}, f32[16,8192]{1,0:T(8,128)S(1)}, u32[]{:S(2)}, u32[]{:S(2)}) collective-permute-start(f32[16,8192]{1,0:T(8,128)S(1)} %get-tuple-element.21), channel_id=1, source_target_pairs={{0,1},{1,2},{2,3},{3,4},{4,5},{5,6},{6,7},{7,8},{8,9},{9,10},{10,1... | collective-permute-start | bytes 1572872 | tf_op jit(solution)/shard_map/ppermute | solution.py:30
  103.4 21.3 %collective-permute-start.17 = (f32[16,8192]{1,0:T(8,128)S(1)}, f32[16,8192]{1,0:T(8,128)S(1)}, u32[]{:S(2)}, u32[]{:S(2)}) collective-permute-start(f32[16,8192]{1,0:T(8,128)S(1)} %get-tuple-element.22), channel_id=1, source_target_pairs={{1,0},{2,1},{3,2},{4,3},{5,4},{6,5},{7,6},{8,7},{9,8},{10,9},{11,1... | collective-permute-start | bytes 1572872 | tf_op jit(solution)/shard_map/ppermute | solution.py:30
  104.7 4.9 %collective-permute-start.12 = (f32[16]{0:T(128)S(1)}, f32[16]{0:T(128)S(1)}, u32[]{:S(2)}, u32[]{:S(2)}) collective-permute-start(f32[16]{0:T(128)S(1)} %get-tuple-element.13), channel_id=1, source_target_pairs={{0,3},{1,2},{2,1},{3,0},{4,7},{5,6},{6,5},{7,4},{8,11},{9,10},{10,... | collective-permute-start | bytes 200 | tf_op jit(solution)/shard_map/ppermute | solution.py:86
  107.8 8.7 %collective-permute-start.11 = (f32[16]{0:T(128)S(1)}, f32[16]{0:T(128)S(1)}, u32[]{:S(2)}, u32[]{:S(2)}) collective-permute-start(f32[16]{0:T(128)S(1)} %get-tuple-element.13), channel_id=1, source_target_pairs={{0,2},{1,3},{2,0},{3,1},{4,6},{5,7},{6,4},{7,5},{8,10},{9,11},{10,... | collective-permute-start | bytes 200 | tf_op jit(solution)/shard_map/ppermute | solution.py:86
  109.5 7.0 %collective-permute-start.10 = (f32[16]{0:T(128)S(1)}, f32[16]{0:T(128)S(1)}, u32[]{:S(2)}, u32[]{:S(2)}) collective-permute-start(f32[16]{0:T(128)S(1)} %get-tuple-element.13), channel_id=1, source_target_pairs={{0,1},{1,0},{2,3},{3,2},{4,5},{5,4},{6,7},{7,6},{8,9},{9,8},{10,11... | collective-permute-start | bytes 200 | tf_op jit(solution)/shard_map/ppermute | solution.py:86
  116.5 5.4 %collective-permute-start.15 = (f32[16]{0:T(128)S(1)}, f32[16]{0:T(128)S(1)}, u32[]{:S(2)}, u32[]{:S(2)}) collective-permute-start(f32[16]{0:T(128)S(1)} %add_add_fusion.5), channel_id=1, source_target_pairs={{0,12},{1,13},{2,14},{3,15},{4,8},{5,9},{6,10},{7,11},{8,4},{9,5},... | collective-permute-start | bytes 200 | tf_op jit(solution)/shard_map/ppermute | solution.py:86
  120.3 4.4 %collective-permute-start.14 = (f32[16]{0:T(128)S(1)}, f32[16]{0:T(128)S(1)}, u32[]{:S(2)}, u32[]{:S(2)}) collective-permute-start(f32[16]{0:T(128)S(1)} %add_add_fusion.5), channel_id=1, source_target_pairs={{0,8},{1,9},{2,10},{3,11},{4,12},{5,13},{6,14},{7,15},{8,0},{9,1},... | collective-permute-start | bytes 200 | tf_op jit(solution)/shard_map/ppermute | solution.py:86
  120.3 4.4 %collective-permute-start.13 = (f32[16]{0:T(128)S(1)}, f32[16]{0:T(128)S(1)}, u32[]{:S(2)}, u32[]{:S(2)}) collective-permute-start(f32[16]{0:T(128)S(1)} %add_add_fusion.5), channel_id=1, source_target_pairs={{0,4},{1,5},{2,6},{3,7},{4,0},{5,1},{6,2},{7,3},{8,12},{9,13},{10,... | collective-permute-start | bytes 200 | tf_op jit(solution)/shard_map/ppermute | solution.py:86
  125.0 23.6 %collective-permute-start.25 = (f32[16,8192]{1,0:T(8,128)S(1)}, f32[16,8192]{1,0:T(8,128)S(1)}, u32[]{:S(2)}, u32[]{:S(2)}) collective-permute-start(f32[16,8192]{1,0:T(8,128)S(1)} %get-tuple-element.12), channel_id=1, source_target_pairs={{1,0},{2,1},{3,2},{4,3},{5,4},{6,5},{7,6},{8,7},{9,8},{10,9},{11,1... | collective-permute-start | bytes 1572872 | tf_op jit(solution)/shard_map/ppermute | solution.py:22
  126.3 22.4 %collective-permute-start.24 = (f32[16,8192]{1,0:T(8,128)S(1)}, f32[16,8192]{1,0:T(8,128)S(1)}, u32[]{:S(2)}, u32[]{:S(2)}) collective-permute-start(f32[16,8192]{1,0:T(8,128)S(1)} %get-tuple-element.12), channel_id=1, source_target_pairs={{0,1},{1,2},{2,3},{3,4},{4,5},{5,6},{6,7},{7,8},{8,9},{9,10},{10,1... | collective-permute-start | bytes 1572872 | tf_op jit(solution)/shard_map/ppermute | solution.py:21
  129.4 3.4 %collective-permute-start.20 = (f32[16]{0:T(128)S(1)}, f32[16]{0:T(128)S(1)}, u32[]{:S(2)}, u32[]{:S(2)}) collective-permute-start(f32[16]{0:T(128)S(1)} %get-tuple-element.11), channel_id=1, source_target_pairs={{0,3},{1,2},{2,1},{3,0},{4,7},{5,6},{6,5},{7,4},{8,11},{9,10},{10,... | collective-permute-start | bytes 200 | tf_op jit(solution)/shard_map/ppermute | solution.py:86
  131.5 4.6 %collective-permute-start.19 = (f32[16]{0:T(128)S(1)}, f32[16]{0:T(128)S(1)}, u32[]{:S(2)}, u32[]{:S(2)}) collective-permute-start(f32[16]{0:T(128)S(1)} %get-tuple-element.11), channel_id=1, source_target_pairs={{0,2},{1,3},{2,0},{3,1},{4,6},{5,7},{6,4},{7,5},{8,10},{9,11},{10,... | collective-permute-start | bytes 200 | tf_op jit(solution)/shard_map/ppermute | solution.py:86
  132.7 3.4 %collective-permute-start.18 = (f32[16]{0:T(128)S(1)}, f32[16]{0:T(128)S(1)}, u32[]{:S(2)}, u32[]{:S(2)}) collective-permute-start(f32[16]{0:T(128)S(1)} %get-tuple-element.11), channel_id=1, source_target_pairs={{0,1},{1,0},{2,3},{3,2},{4,5},{5,4},{6,7},{7,6},{8,9},{9,8},{10,11... | collective-permute-start | bytes 200 | tf_op jit(solution)/shard_map/ppermute | solution.py:86
  136.1 9.7 %collective-permute-start.23 = (f32[16]{0:T(128)S(1)}, f32[16]{0:T(128)S(1)}, u32[]{:S(2)}, u32[]{:S(2)}) collective-permute-start(f32[16]{0:T(128)S(1)} %add_add_fusion.4), channel_id=1, source_target_pairs={{0,12},{1,13},{2,14},{3,15},{4,8},{5,9},{6,10},{7,11},{8,4},{9,5},... | collective-permute-start | bytes 200 | tf_op jit(solution)/shard_map/ppermute | solution.py:86
  144.2 4.4 %collective-permute-start.22 = (f32[16]{0:T(128)S(1)}, f32[16]{0:T(128)S(1)}, u32[]{:S(2)}, u32[]{:S(2)}) collective-permute-start(f32[16]{0:T(128)S(1)} %add_add_fusion.4), channel_id=1, source_target_pairs={{0,8},{1,9},{2,10},{3,11},{4,12},{5,13},{6,14},{7,15},{8,0},{9,1},... | collective-permute-start | bytes 200 | tf_op jit(solution)/shard_map/ppermute | solution.py:86
  144.6 4.1 %collective-permute-start.21 = (f32[16]{0:T(128)S(1)}, f32[16]{0:T(128)S(1)}, u32[]{:S(2)}, u32[]{:S(2)}) collective-permute-start(f32[16]{0:T(128)S(1)} %add_add_fusion.4), channel_id=1, source_target_pairs={{0,4},{1,5},{2,6},{3,7},{4,0},{5,1},{6,2},{7,3},{8,12},{9,13},{10,... | collective-permute-start | bytes 200 | tf_op jit(solution)/shard_map/ppermute | solution.py:86
  185.9 23.0 %collective-permute-start.32 = (f32[16,8192]{1,0:T(8,128)S(1)}, f32[16,8192]{1,0:T(8,128)S(1)}, u32[]{:S(2)}, u32[]{:S(2)}) collective-permute-start(f32[16,8192]{1,0:T(8,128)S(1)} %get-tuple-element.19), channel_id=1, source_target_pairs={{0,1},{1,2},{2,3},{3,4},{4,5},{5,6},{6,7},{7,8},{8,9},{9,10},{10,1... | collective-permute-start | bytes 1572872 | tf_op jit(solution)/shard_map/ppermute | solution.py:30
  187.3 21.7 %collective-permute-start.33 = (f32[16,8192]{1,0:T(8,128)S(1)}, f32[16,8192]{1,0:T(8,128)S(1)}, u32[]{:S(2)}, u32[]{:S(2)}) collective-permute-start(f32[16,8192]{1,0:T(8,128)S(1)} %get-tuple-element.20), channel_id=1, source_target_pairs={{1,0},{2,1},{3,2},{4,3},{5,4},{6,5},{7,6},{8,7},{9,8},{10,9},{11,1... | collective-permute-start | bytes 1572872 | tf_op jit(solution)/shard_map/ppermute | solution.py:30
  188.6 3.5 %collective-permute-start.28 = (f32[16]{0:T(128)S(1)}, f32[16]{0:T(128)S(1)}, u32[]{:S(2)}, u32[]{:S(2)}) collective-permute-start(f32[16]{0:T(128)S(1)} %get-tuple-element.9), channel_id=1, source_target_pairs={{0,3},{1,2},{2,1},{3,0},{4,7},{5,6},{6,5},{7,4},{8,11},{9,10},{10,... | collective-permute-start | bytes 200 | tf_op jit(solution)/shard_map/ppermute | solution.py:86
  190.8 8.2 %collective-permute-start.27 = (f32[16]{0:T(128)S(1)}, f32[16]{0:T(128)S(1)}, u32[]{:S(2)}, u32[]{:S(2)}) collective-permute-start(f32[16]{0:T(128)S(1)} %get-tuple-element.9), channel_id=1, source_target_pairs={{0,2},{1,3},{2,0},{3,1},{4,6},{5,7},{6,4},{7,5},{8,10},{9,11},{10,... | collective-permute-start | bytes 200 | tf_op jit(solution)/shard_map/ppermute | solution.py:86
  192.0 7.0 %collective-permute-start.26 = (f32[16]{0:T(128)S(1)}, f32[16]{0:T(128)S(1)}, u32[]{:S(2)}, u32[]{:S(2)}) collective-permute-start(f32[16]{0:T(128)S(1)} %get-tuple-element.9), channel_id=1, source_target_pairs={{0,1},{1,0},{2,3},{3,2},{4,5},{5,4},{6,7},{7,6},{8,9},{9,8},{10,11... | collective-permute-start | bytes 200 | tf_op jit(solution)/shard_map/ppermute | solution.py:86
  199.0 7.0 %collective-permute-start.31 = (f32[16]{0:T(128)S(1)}, f32[16]{0:T(128)S(1)}, u32[]{:S(2)}, u32[]{:S(2)}) collective-permute-start(f32[16]{0:T(128)S(1)} %add_add_fusion.3), channel_id=1, source_target_pairs={{0,12},{1,13},{2,14},{3,15},{4,8},{5,9},{6,10},{7,11},{8,4},{9,5},... | collective-permute-start | bytes 200 | tf_op jit(solution)/shard_map/ppermute | solution.py:86
  204.5 4.4 %collective-permute-start.30 = (f32[16]{0:T(128)S(1)}, f32[16]{0:T(128)S(1)}, u32[]{:S(2)}, u32[]{:S(2)}) collective-permute-start(f32[16]{0:T(128)S(1)} %add_add_fusion.3), channel_id=1, source_target_pairs={{0,8},{1,9},{2,10},{3,11},{4,12},{5,13},{6,14},{7,15},{8,0},{9,1},... | collective-permute-start | bytes 200 | tf_op jit(solution)/shard_map/ppermute | solution.py:86
  205.1 3.8 %collective-permute-start.29 = (f32[16]{0:T(128)S(1)}, f32[16]{0:T(128)S(1)}, u32[]{:S(2)}, u32[]{:S(2)}) collective-permute-start(f32[16]{0:T(128)S(1)} %add_add_fusion.3), channel_id=1, source_target_pairs={{0,4},{1,5},{2,6},{3,7},{4,0},{5,1},{6,2},{7,3},{8,12},{9,13},{10,... | collective-permute-start | bytes 200 | tf_op jit(solution)/shard_map/ppermute | solution.py:86
  209.3 3.0 %collective-permute-start.36 = (f32[16]{0:T(128)S(1)}, f32[16]{0:T(128)S(1)}, u32[]{:S(2)}, u32[]{:S(2)}) collective-permute-start(f32[16]{0:T(128)S(1)} %get-tuple-element.5), channel_id=1, source_target_pairs={{0,3},{1,2},{2,1},{3,0},{4,7},{5,6},{6,5},{7,4},{8,11},{9,10},{10,... | collective-permute-start | bytes 200 | tf_op jit(solution)/shard_map/ppermute | solution.py:86
  209.4 3.6 %collective-permute-start.35 = (f32[16]{0:T(128)S(1)}, f32[16]{0:T(128)S(1)}, u32[]{:S(2)}, u32[]{:S(2)}) collective-permute-start(f32[16]{0:T(128)S(1)} %get-tuple-element.5), channel_id=1, source_target_pairs={{0,2},{1,3},{2,0},{3,1},{4,6},{5,7},{6,4},{7,5},{8,10},{9,11},{10,... | collective-permute-start | bytes 200 | tf_op jit(solution)/shard_map/ppermute | solution.py:86
  209.6 3.3 %collective-permute-start.34 = (f32[16]{0:T(128)S(1)}, f32[16]{0:T(128)S(1)}, u32[]{:S(2)}, u32[]{:S(2)}) collective-permute-start(f32[16]{0:T(128)S(1)} %get-tuple-element.5), channel_id=1, source_target_pairs={{0,1},{1,0},{2,3},{3,2},{4,5},{5,4},{6,7},{7,6},{8,9},{9,8},{10,11... | collective-permute-start | bytes 200 | tf_op jit(solution)/shard_map/ppermute | solution.py:86
  213.0 5.4 %collective-permute-start.39 = (f32[16]{0:T(128)S(1)}, f32[16]{0:T(128)S(1)}, u32[]{:S(2)}, u32[]{:S(2)}) collective-permute-start(f32[16]{0:T(128)S(1)} %add_add_fusion.2), channel_id=1, source_target_pairs={{0,12},{1,13},{2,14},{3,15},{4,8},{5,9},{6,10},{7,11},{8,4},{9,5},... | collective-permute-start | bytes 200 | tf_op jit(solution)/shard_map/ppermute | solution.py:86
  215.6 4.4 %collective-permute-start.38 = (f32[16]{0:T(128)S(1)}, f32[16]{0:T(128)S(1)}, u32[]{:S(2)}, u32[]{:S(2)}) collective-permute-start(f32[16]{0:T(128)S(1)} %add_add_fusion.2), channel_id=1, source_target_pairs={{0,8},{1,9},{2,10},{3,11},{4,12},{5,13},{6,14},{7,15},{8,0},{9,1},... | collective-permute-start | bytes 200 | tf_op jit(solution)/shard_map/ppermute | solution.py:86
  215.6 4.4 %collective-permute-start.37 = (f32[16]{0:T(128)S(1)}, f32[16]{0:T(128)S(1)}, u32[]{:S(2)}, u32[]{:S(2)}) collective-permute-start(f32[16]{0:T(128)S(1)} %add_add_fusion.2), channel_id=1, source_target_pairs={{0,4},{1,5},{2,6},{3,7},{4,0},{5,1},{6,2},{7,3},{8,12},{9,13},{10,... | collective-permute-start | bytes 200 | tf_op jit(solution)/shard_map/ppermute | solution.py:86
where the time goes:
time: 223 us; the launch traced here: 222 us
  matrix products  90.1 us (40%)
  starting transfers between devices  74.9 us (34%)
  waiting for transfers between devices  41.5 us (19%)
  local copies, waits for them, and re-layouts  9.24 us (4%)
  other arithmetic  3.91 us (2%)
    ppermute x30, starting transfers between devices, all_sum(): parts.append(lax.ppermute(values, axes, pairs))  54.1 us
    dot_general x3, matrix products, transpose_local(): jnp.einsum('ski,kij->ksj', pieces, tile_stack, precision=PRECISE)  46.2 us
    dot_general x2, matrix products, forward_local(): jnp.einsum('skj,kij->ksi', pieces, tile_stack, precision=PRECISE)  38.3 us
    ppermute x30, waiting for transfers between devices, all_sum(): parts.append(lax.ppermute(values, axes, pairs))  37 us
    ppermute x6, starting transfers between devices, from_behind(): return lax.ppermute(shard, axis, pairs)  12.1 us
    ppermute x2, starting transfers between devices, with_halo(): before = lax.ppermute(last, axis, up)  6.13 us
  transfers between devices with their start and end apart: 40, of which 16 were waited for; matrix products, arithmetic and copies ran while one was open for 0% of the time, Pallas kernels for 0%

commit v1 on v0

--- a/solution.py
+++ b/solution.py
@@ -9,6 +9,7 @@
 
 
 PRECISE = lax.Precision.HIGHEST
+PRODUCT_PRECISION = lax.Precision.HIGH
 
 
 def with_halo(shard, sides, width):
@@ -35,7 +36,7 @@
     tile_edge = tile_stack.shape[1]
     pieces = window.reshape(scenario_rows, 3 * COL_BLOCKS, tile_edge)[:, cols_idx, :]
     products = (
-        jnp.einsum("skj,kij->ksi", pieces, tile_stack, precision=PRECISE) * live_slot[:, None, None]
+        jnp.einsum("skj,kij->ksi", pieces, tile_stack, precision=PRODUCT_PRECISION) * live_slot[:, None, None]
     )
     onehot = (rows_idx[:, None] == jnp.arange(ROW_BLOCKS)[None, :]).astype(jnp.float32)
     summed = jnp.einsum("kr,ksi->sri", onehot, products, precision=PRECISE)
@@ -47,7 +48,7 @@
     tile_edge = tile_stack.shape[1]
     pieces = field.reshape(scenario_rows, ROW_BLOCKS, tile_edge)[:, rows_idx, :]
     products = (
-        jnp.einsum("ski,kij->ksj", pieces, tile_stack, precision=PRECISE) * live_slot[:, None, None]
+        jnp.einsum("ski,kij->ksj", pieces, tile_stack, precision=PRODUCT_PRECISION) * live_slot[:, None, None]
     )
     onehot = (cols_idx[:, None] == jnp.arange(3 * COL_BLOCKS)[None, :]).astype(jnp.float32)
     summed = jnp.einsum("kc,ksj->scj", onehot, products, precision=PRECISE)

time: 223 us -> 180 us (0.81)
  matrix products: 90.1 us -> 47.9 us
    dot_general x5, matrix products: 84.4 us -> 42.2 us  [the longest x2 21.9 us: forward_local(): jnp.einsum('skj,kij->ksi', pieces, tile_stack, precision=PRODUCT_PRECISION)]
where the time goes in v1:
time: 180 us; the launch traced here: 179 us
  starting transfers between devices  75.3 us (42%)
  matrix products  47.9 us (27%)
  waiting for transfers between devices  41.1 us (23%)
  local copies, waits for them, and re-layouts  9.24 us (5%)
  other arithmetic  3.91 us (2%)
    ppermute x30, starting transfers between devices, all_sum(): parts.append(lax.ppermute(values, axes, pairs))  54.1 us
    ppermute x30, waiting for transfers between devices, all_sum(): parts.append(lax.ppermute(values, axes, pairs))  36.6 us
    dot_general x2, matrix products, forward_local(): jnp.einsum('skj,kij->ksi', pieces, tile_stack, precision=PRODUCT_PRECISION)  21.9 us
    dot_general x3, matrix products, transpose_local(): jnp.einsum('ski,kij->ksj', pieces, tile_stack, precision=PRODUCT_PRECISION)  20.3 us
    ppermute x6, starting transfers between devices, from_behind(): return lax.ppermute(shard, axis, pairs)  12.1 us
    ppermute x2, starting transfers between devices, with_halo(): before = lax.ppermute(last, axis, up)  6.53 us
    ppermute x6, waiting for transfers between devices, from_behind(): return lax.ppermute(shard, axis, pairs)  4.44 us
    dot_general x3, matrix products, transpose_local(): summed = jnp.einsum('kc,ksj->scj', onehot, products, precision=PRECISE)  3.87 us
  transfers between devices with their start and end apart: 40, of which 16 were waited for; matrix products, arithmetic and copies ran while one was open for 0% of the time, Pallas kernels for 0%

profile of v1, /device:TPU:0, one launch (start us, length us, event | category | flops | bytes accessed | tf_op | source)
XLA Modules:
  0.0 179.1 jit_solution(6681942751336719938)
XLA Ops:
  2.0 1.0 copy_bitcast_fusion.7
  3.8 6.8 %fusion.10 = f32[160,16,128]{2,1,0:T(8,128)S(1)} fusion(f32[1,160,128,128]{3,2,1,0:T(8,128)} %param.6, f32[160,16,128]{2,1,0:T(8,128)S(1)} %gather_fusion, f32[160]{0:T(256)S(1)} %compare_convert_fusion), kind=kOutput, calls=%fused_computation.22 | convolution fusion | flops 251985920 | bytes 13107840 | tf_op jit(solution)/shard_map/ski,kij->ksj/dot_general | solution.py:51
  10.6 1.3 fusion.38
  11.9 0.9 copy.51
  12.9 2.4 %collective-permute-start = (f32[16,8192]{1,0:T(8,128)S(1)}, f32[16,8192]{1,0:T(8,128)S(1)}, u32[]{:S(2)}, u32[]{:S(2)}) collective-permute-start(f32[16,8192]{1,0:T(8,128)S(1)} %get-tuple-element.23), channel_id=1, source_target_pairs={{0,1},{1,2},{2,3},{3,4},{4,5},{5,6},{6,7},{7,8},{8,9},{9,10},{10,1... | collective-permute-start | bytes 1572872 | tf_op jit(solution)/shard_map/ppermute | solution.py:31
  15.3 1.3 collective-permute-start.1
  16.8 4.4 %collective-permute-done.1 = f32[16,8192]{1,0:T(8,128)S(1)} collective-permute-done((f32[16,8192]{1,0:T(8,128)S(1)}, f32[16,8192]{1,0:T(8,128)S(1)}, u32[]{:S(2)}, u32[]{:S(2)}) %collective-permute-start.1) | collective-permute-done | bytes 524320 | tf_op jit(solution)/shard_map/ppermute | solution.py:31
  21.4 10.8 %collective-permute-start.3 = (f32[2,16]{1,0:T(2,128)S(1)}, f32[2,16]{1,0:T(2,128)S(1)}, u32[]{:S(2)}, u32[]{:S(2)}) collective-permute-start(f32[2,16]{1,0:T(2,128)S(1)} %pad_maximum_fusion), channel_id=1, source_target_pairs={{0,2},{1,3},{2,0},{3,1},{4,6},{5,7},{6,4},{7,5},{8,10},{9,11},{10,... | collective-permute-start | bytes 392 | tf_op jit(solution)/shard_map/ppermute | solution.py:87
  32.5 1.3 collective-permute-start.9
  33.8 3.2 %collective-permute-start.8 = (f32[16,8192]{1,0:T(8,128)S(1)}, f32[16,8192]{1,0:T(8,128)S(1)}, u32[]{:S(2)}, u32[]{:S(2)}) collective-permute-start(f32[16,8192]{1,0:T(8,128)S(1)} %get-tuple-element.18), channel_id=1, source_target_pairs={{0,1},{1,2},{2,3},{3,4},{4,5},{5,6},{6,7},{7,8},{8,9},{9,10},{10,1... | collective-permute-start | bytes 1572872 | tf_op jit(solution)/shard_map/ppermute | solution.py:22
  37.1 4.6 %collective-permute-start.7 = (f32[2,16]{1,0:T(2,128)S(1)}, f32[2,16]{1,0:T(2,128)S(1)}, u32[]{:S(2)}, u32[]{:S(2)}) collective-permute-start(f32[2,16]{1,0:T(2,128)S(1)} %add_add_fusion.1), channel_id=1, source_target_pairs={{0,12},{1,13},{2,14},{3,15},{4,8},{5,9},{6,10},{7,11},{8,4},{9,5},... | collective-permute-start | bytes 392 | tf_op jit(solution)/shard_map/ppermute | solution.py:87
  42.3 4.3 %collective-permute-done.7 = f32[2,16]{1,0:T(2,128)S(1)} collective-permute-done((f32[2,16]{1,0:T(2,128)S(1)}, f32[2,16]{1,0:T(2,128)S(1)}, u32[]{:S(2)}, u32[]{:S(2)}) %collective-permute-start.7) | collective-permute-done | bytes 160 | tf_op jit(solution)/shard_map/ppermute | solution.py:87
  47.7 10.8 %fusion.13 = f32[160,16,128]{2,1,0:T(8,128)S(1)} fusion(f32[1,160,128,128]{3,2,1,0:T(8,128)} %param.6, f32[160,16,128]{2,1,0:T(8,128)S(1)} %gather_fusion.1, f32[160]{0:T(256)S(1)} %compare_convert_fusion), kind=kOutput, calls=%fused_computation.23 | convolution fusion | flops 251985920 | bytes 13107840 | tf_op jit(solution)/shard_map/skj,kij->ksi/dot_general | solution.py:39
  60.6 6.8 %fusion.16 = f32[160,16,128]{2,1,0:T(8,128)S(1)} fusion(f32[1,160,128,128]{3,2,1,0:T(8,128)} %param.6, f32[160,16,128]{2,1,0:T(8,128)S(1)} %gather_fusion.2, f32[160]{0:T(256)S(1)} %compare_convert_fusion), kind=kOutput, calls=%fused_computation.24 | convolution fusion | flops 251985920 | bytes 13107840 | tf_op jit(solution)/shard_map/ski,kij->ksj/dot_general | solution.py:51
  67.4 1.3 fusion.34
  69.7 4.5 %collective-permute-start.16 = (f32[16,8192]{1,0:T(8,128)S(1)}, f32[16,8192]{1,0:T(8,128)S(1)}, u32[]{:S(2)}, u32[]{:S(2)}) collective-permute-start(f32[16,8192]{1,0:T(8,128)S(1)} %get-tuple-element.21), channel_id=1, source_target_pairs={{0,1},{1,2},{2,3},{3,4},{4,5},{5,6},{6,7},{7,8},{8,9},{9,10},{10,1... | collective-permute-start | bytes 1572872 | tf_op jit(solution)/shard_map/ppermute | solution.py:31
  74.2 1.3 collective-permute-start.17
  75.5 3.1 %collective-permute-start.12 = (f32[16]{0:T(128)S(1)}, f32[16]{0:T(128)S(1)}, u32[]{:S(2)}, u32[]{:S(2)}) collective-permute-start(f32[16]{0:T(128)S(1)} %get-tuple-element.13), channel_id=1, source_target_pairs={{0,3},{1,2},{2,1},{3,0},{4,7},{5,6},{6,5},{7,4},{8,11},{9,10},{10,... | collective-permute-start | bytes 200 | tf_op jit(solution)/shard_map/ppermute | solution.py:87
  78.6 1.7 collective-permute-start.11
  80.4 6.9 %collective-permute-done.11 = f32[16]{0:T(128)S(1)} collective-permute-done((f32[16]{0:T(128)S(1)}, f32[16]{0:T(128)S(1)}, u32[]{:S(2)}, u32[]{:S(2)}) %collective-permute-start.11) | collective-permute-done | bytes 96 | tf_op jit(solution)/shard_map/ppermute | solution.py:87
  87.3 3.7 %collective-permute-start.15 = (f32[16]{0:T(128)S(1)}, f32[16]{0:T(128)S(1)}, u32[]{:S(2)}, u32[]{:S(2)}) collective-permute-start(f32[16]{0:T(128)S(1)} %add_add_fusion.5), channel_id=1, source_target_pairs={{0,12},{1,13},{2,14},{3,15},{4,8},{5,9},{6,10},{7,11},{8,4},{9,5},... | collective-permute-start | bytes 200 | tf_op jit(solution)/shard_map/ppermute | solution.py:87
  91.8 0.9 collective-permute-done.15
  92.7 2.8 %collective-permute-done.14 = f32[16]{0:T(128)S(1)} collective-permute-done((f32[16]{0:T(128)S(1)}, f32[16]{0:T(128)S(1)}, u32[]{:S(2)}, u32[]{:S(2)}) %collective-permute-start.14) | collective-permute-done | bytes 96 | tf_op jit(solution)/shard_map/ppermute | solution.py:87
  95.8 1.3 collective-permute-start.25
  97.1 3.3 %collective-permute-start.24 = (f32[16,8192]{1,0:T(8,128)S(1)}, f32[16,8192]{1,0:T(8,128)S(1)}, u32[]{:S(2)}, u32[]{:S(2)}) collective-permute-start(f32[16,8192]{1,0:T(8,128)S(1)} %get-tuple-element.12), channel_id=1, source_target_pairs={{0,1},{1,2},{2,3},{3,4},{4,5},{5,6},{6,7},{7,8},{8,9},{9,10},{10,1... | collective-permute-start | bytes 1572872 | tf_op jit(solution)/shard_map/ppermute | solution.py:22
  100.4 2.1 %collective-permute-start.20 = (f32[16]{0:T(128)S(1)}, f32[16]{0:T(128)S(1)}, u32[]{:S(2)}, u32[]{:S(2)}) collective-permute-start(f32[16]{0:T(128)S(1)} %get-tuple-element.11), channel_id=1, source_target_pairs={{0,3},{1,2},{2,1},{3,0},{4,7},{5,6},{6,5},{7,4},{8,11},{9,10},{10,... | collective-permute-start | bytes 200 | tf_op jit(solution)/shard_map/ppermute | solution.py:87
  102.5 1.2 collective-permute-start.19
  103.8 3.1 %collective-permute-done.19 = f32[16]{0:T(128)S(1)} collective-permute-done((f32[16]{0:T(128)S(1)}, f32[16]{0:T(128)S(1)}, u32[]{:S(2)}, u32[]{:S(2)}) %collective-permute-start.19) | collective-permute-done | bytes 96 | tf_op jit(solution)/shard_map/ppermute | solution.py:87
  106.9 8.2 %collective-permute-start.23 = (f32[16]{0:T(128)S(1)}, f32[16]{0:T(128)S(1)}, u32[]{:S(2)}, u32[]{:S(2)}) collective-permute-start(f32[16]{0:T(128)S(1)} %add_add_fusion.4), channel_id=1, source_target_pairs={{0,12},{1,13},{2,14},{3,15},{4,8},{5,9},{6,10},{7,11},{8,4},{9,5},... | collective-permute-start | bytes 200 | tf_op jit(solution)/shard_map/ppermute | solution.py:87
  116.5 2.9 %collective-permute-done.22 = f32[16]{0:T(128)S(1)} collective-permute-done((f32[16]{0:T(128)S(1)}, f32[16]{0:T(128)S(1)}, u32[]{:S(2)}, u32[]{:S(2)}) %collective-permute-start.22) | collective-permute-done | bytes 96 | tf_op jit(solution)/shard_map/ppermute | solution.py:87
  119.6 1.9 %gather_fusion.3 = f32[160,16,128]{2,1,0:T(8,128)} fusion(f32[16,192,128]{2,0,1:T(8,128)S(1)} %copy_bitcast_fusion.3, s32[1024]{0:T(1024)S(1)} %pad_clamp_fusion), kind=kCustom, calls=%fused_computation.3 | custom fusion | bytes 2622080 | tf_op jit(solution)/shard_map/gather | solution.py:37
  121.5 11.0 %fusion.19 = f32[160,16,128]{2,1,0:T(8,128)S(1)} fusion(f32[1,160,128,128]{3,2,1,0:T(8,128)} %param.6, f32[160,16,128]{2,1,0:T(8,128)} %gather_fusion.3, f32[160]{0:T(256)S(1)} %compare_convert_fusion), kind=kOutput, calls=%fused_computation.25 | convolution fusion | flops 251985920 | bytes 13107840 | tf_op jit(solution)/shard_map/skj,kij->ksi/dot_general | solution.py:39
  134.6 6.8 %fusion.22 = f32[160,16,128]{2,1,0:T(8,128)S(1)} fusion(f32[1,160,128,128]{3,2,1,0:T(8,128)} %param.6, f32[160,16,128]{2,1,0:T(8,128)S(1)} %gather_fusion.4, f32[160]{0:T(256)S(1)} %compare_convert_fusion), kind=kOutput, calls=%fused_computation.26 | convolution fusion | flops 251985920 | bytes 13107840 | tf_op jit(solution)/shard_map/ski,kij->ksj/dot_general | solution.py:51
  141.4 1.3 fusion.30
  143.7 1.3 collective-permute-start.32
  145.0 1.3 collective-permute-start.33
  146.3 2.2 %collective-permute-start.28 = (f32[16]{0:T(128)S(1)}, f32[16]{0:T(128)S(1)}, u32[]{:S(2)}, u32[]{:S(2)}) collective-permute-start(f32[16]{0:T(128)S(1)} %get-tuple-element.9), channel_id=1, source_target_pairs={{0,3},{1,2},{2,1},{3,0},{4,7},{5,6},{6,5},{7,4},{8,11},{9,10},{10,... | collective-permute-start | bytes 200 | tf_op jit(solution)/shard_map/ppermute | solution.py:87
  148.5 1.2 collective-permute-start.27
  149.8 6.9 %collective-permute-done.27 = f32[16]{0:T(128)S(1)} collective-permute-done((f32[16]{0:T(128)S(1)}, f32[16]{0:T(128)S(1)}, u32[]{:S(2)}, u32[]{:S(2)}) %collective-permute-start.27) | collective-permute-done | bytes 96 | tf_op jit(solution)/shard_map/ppermute | solution.py:87
  156.8 5.5 %collective-permute-start.31 = (f32[16]{0:T(128)S(1)}, f32[16]{0:T(128)S(1)}, u32[]{:S(2)}, u32[]{:S(2)}) collective-permute-start(f32[16]{0:T(128)S(1)} %add_add_fusion.3), channel_id=1, source_target_pairs={{0,12},{1,13},{2,14},{3,15},{4,8},{5,9},{6,10},{7,11},{8,4},{9,5},... | collective-permute-start | bytes 200 | tf_op jit(solution)/shard_map/ppermute | solution.py:87
  163.8 2.9 %collective-permute-done.30 = f32[16]{0:T(128)S(1)} collective-permute-done((f32[16]{0:T(128)S(1)}, f32[16]{0:T(128)S(1)}, u32[]{:S(2)}, u32[]{:S(2)}) %collective-permute-start.30) | collective-permute-done | bytes 96 | tf_op jit(solution)/shard_map/ppermute | solution.py:87
  167.4 1.6 collective-permute-start.34
  169.0 1.1 collective-permute-done.36
  170.7 2.6 %collective-permute-start.39 = (f32[16]{0:T(128)S(1)}, f32[16]{0:T(128)S(1)}, u32[]{:S(2)}, u32[]{:S(2)}) collective-permute-start(f32[16]{0:T(128)S(1)} %add_add_fusion.2), channel_id=1, source_target_pairs={{0,12},{1,13},{2,14},{3,15},{4,8},{5,9},{6,10},{7,11},{8,4},{9,5},... | collective-permute-start | bytes 200 | tf_op jit(solution)/shard_map/ppermute | solution.py:87
  173.4 1.8 %collective-permute-start.37 = (f32[16]{0:T(128)S(1)}, f32[16]{0:T(128)S(1)}, u32[]{:S(2)}, u32[]{:S(2)}) collective-permute-start(f32[16]{0:T(128)S(1)} %add_add_fusion.2), channel_id=1, source_target_pairs={{0,4},{1,5},{2,6},{3,7},{4,0},{5,1},{6,2},{7,3},{8,12},{9,13},{10,... | collective-permute-start | bytes 200 | tf_op jit(solution)/shard_map/ppermute | solution.py:87
  175.2 0.9 collective-permute-done.39
  176.1 1.7 collective-permute-done.38
  177.9 1.2 multiply_subtract_fusion
  (93 shorter events, 15.8 us)
Async XLA Ops:
  3.8 6.8 %copy-start.2 = (s32[1,160]{1,0:T(1,128)S(1)}, s32[1,160]{1,0:T(1,128)}, u32[]{:S(2)}) copy-start(s32[1,160]{1,0:T(1,128)} %param.8) | copy-start | bytes 1924
  12.8 3.8 %copy-start = (f32[16,4096]{1,0:T(8,128)S(1)}, f32[16,4096]{1,0:T(8,128)}, u32[]{:S(2)}) copy-start(f32[16,4096]{1,0:T(8,128)} %param.5) | copy-start | bytes 786436
  12.9 3.9 %collective-permute-start = (f32[16,8192]{1,0:T(8,128)S(1)}, f32[16,8192]{1,0:T(8,128)S(1)}, u32[]{:S(2)}, u32[]{:S(2)}) collective-permute-start(f32[16,8192]{1,0:T(8,128)S(1)} %get-tuple-element.23), channel_id=1, source_target_pairs={{0,1},{1,2},{2,3},{3,4},{4,5},{5,6},{6,7},{7,8},{8,9},{9,10},{10,1... | collective-permute-start | bytes 1572872 | tf_op jit(solution)/shard_map/ppermute | solution.py:31
  15.3 5.9 %collective-permute-start.1 = (f32[16,8192]{1,0:T(8,128)S(1)}, f32[16,8192]{1,0:T(8,128)S(1)}, u32[]{:S(2)}, u32[]{:S(2)}) collective-permute-start(f32[16,8192]{1,0:T(8,128)S(1)} %get-tuple-element.24), channel_id=1, source_target_pairs={{1,0},{2,1},{3,2},{4,3},{5,4},{6,5},{7,6},{8,7},{9,8},{10,9},{11,1... | collective-permute-start | bytes 1572872 | tf_op jit(solution)/shard_map/ppermute | solution.py:31
  21.4 15.6 %collective-permute-start.3 = (f32[2,16]{1,0:T(2,128)S(1)}, f32[2,16]{1,0:T(2,128)S(1)}, u32[]{:S(2)}, u32[]{:S(2)}) collective-permute-start(f32[2,16]{1,0:T(2,128)S(1)} %pad_maximum_fusion), channel_id=1, source_target_pairs={{0,2},{1,3},{2,0},{3,1},{4,6},{5,7},{6,4},{7,5},{8,10},{9,11},{10,... | collective-permute-start | bytes 392 | tf_op jit(solution)/shard_map/ppermute | solution.py:87
  32.3 4.7 %collective-permute-start.4 = (f32[2,16]{1,0:T(2,128)S(1)}, f32[2,16]{1,0:T(2,128)S(1)}, u32[]{:S(2)}, u32[]{:S(2)}) collective-permute-start(f32[2,16]{1,0:T(2,128)S(1)} %pad_maximum_fusion), channel_id=1, source_target_pairs={{0,3},{1,2},{2,1},{3,0},{4,7},{5,6},{6,5},{7,4},{8,11},{9,10},{10,... | collective-permute-start | bytes 392 | tf_op jit(solution)/shard_map/ppermute | solution.py:87
  32.3 4.8 %collective-permute-start.2 = (f32[2,16]{1,0:T(2,128)S(1)}, f32[2,16]{1,0:T(2,128)S(1)}, u32[]{:S(2)}, u32[]{:S(2)}) collective-permute-start(f32[2,16]{1,0:T(2,128)S(1)} %pad_maximum_fusion), channel_id=1, source_target_pairs={{0,1},{1,0},{2,3},{3,2},{4,5},{5,4},{6,7},{7,6},{8,9},{9,8},{10,11... | collective-permute-start | bytes 392 | tf_op jit(solution)/shard_map/ppermute | solution.py:87
  32.5 14.2 %collective-permute-start.9 = (f32[16,8192]{1,0:T(8,128)S(1)}, f32[16,8192]{1,0:T(8,128)S(1)}, u32[]{:S(2)}, u32[]{:S(2)}) collective-permute-start(f32[16,8192]{1,0:T(8,128)S(1)} %get-tuple-element.18), channel_id=1, source_target_pairs={{1,0},{2,1},{3,2},{4,3},{5,4},{6,5},{7,6},{8,7},{9,8},{10,9},{11,1... | collective-permute-start | bytes 1572872 | tf_op jit(solution)/shard_map/ppermute | solution.py:23
  33.8 12.9 %collective-permute-start.8 = (f32[16,8192]{1,0:T(8,128)S(1)}, f32[16,8192]{1,0:T(8,128)S(1)}, u32[]{:S(2)}, u32[]{:S(2)}) collective-permute-start(f32[16,8192]{1,0:T(8,128)S(1)} %get-tuple-element.18), channel_id=1, source_target_pairs={{0,1},{1,2},{2,3},{3,4},{4,5},{5,6},{6,7},{7,8},{8,9},{9,10},{10,1... | collective-permute-start | bytes 1572872 | tf_op jit(solution)/shard_map/ppermute | solution.py:22
  37.1 9.6 %collective-permute-start.7 = (f32[2,16]{1,0:T(2,128)S(1)}, f32[2,16]{1,0:T(2,128)S(1)}, u32[]{:S(2)}, u32[]{:S(2)}) collective-permute-start(f32[2,16]{1,0:T(2,128)S(1)} %add_add_fusion.1), channel_id=1, source_target_pairs={{0,12},{1,13},{2,14},{3,15},{4,8},{5,9},{6,10},{7,11},{8,4},{9,5},... | collective-permute-start | bytes 392 | tf_op jit(solution)/shard_map/ppermute | solution.py:87
  41.6 5.0 %collective-permute-start.6 = (f32[2,16]{1,0:T(2,128)S(1)}, f32[2,16]{1,0:T(2,128)S(1)}, u32[]{:S(2)}, u32[]{:S(2)}) collective-permute-start(f32[2,16]{1,0:T(2,128)S(1)} %add_add_fusion.1), channel_id=1, source_target_pairs={{0,8},{1,9},{2,10},{3,11},{4,12},{5,13},{6,14},{7,15},{8,0},{9,1},... | collective-permute-start | bytes 392 | tf_op jit(solution)/shard_map/ppermute | solution.py:87
  41.7 5.0 %collective-permute-start.5 = (f32[2,16]{1,0:T(2,128)S(1)}, f32[2,16]{1,0:T(2,128)S(1)}, u32[]{:S(2)}, u32[]{:S(2)}) collective-permute-start(f32[2,16]{1,0:T(2,128)S(1)} %add_add_fusion.1), channel_id=1, source_target_pairs={{0,4},{1,5},{2,6},{3,7},{4,0},{5,1},{6,2},{7,3},{8,12},{9,13},{10,... | collective-permute-start | bytes 392 | tf_op jit(solution)/shard_map/ppermute | solution.py:87
  47.6 10.9 %copy-start.3 = (s32[1,160]{1,0:T(1,128)S(1)}, s32[1,160]{1,0:T(1,128)}, u32[]{:S(2)}) copy-start(s32[1,160]{1,0:T(1,128)} %param.7) | copy-start | bytes 1924
  58.5 1.0 copy-start.1
  69.7 25.8 %collective-permute-start.16 = (f32[16,8192]{1,0:T(8,128)S(1)}, f32[16,8192]{1,0:T(8,128)S(1)}, u32[]{:S(2)}, u32[]{:S(2)}) collective-permute-start(f32[16,8192]{1,0:T(8,128)S(1)} %get-tuple-element.21), channel_id=1, source_target_pairs={{0,1},{1,2},{2,3},{3,4},{4,5},{5,6},{6,7},{7,8},{8,9},{9,10},{10,1... | collective-permute-start | bytes 1572872 | tf_op jit(solution)/shard_map/ppermute | solution.py:31
  74.2 21.3 %collective-permute-start.17 = (f32[16,8192]{1,0:T(8,128)S(1)}, f32[16,8192]{1,0:T(8,128)S(1)}, u32[]{:S(2)}, u32[]{:S(2)}) collective-permute-start(f32[16,8192]{1,0:T(8,128)S(1)} %get-tuple-element.22), channel_id=1, source_target_pairs={{1,0},{2,1},{3,2},{4,3},{5,4},{6,5},{7,6},{8,7},{9,8},{10,9},{11,1... | collective-permute-start | bytes 1572872 | tf_op jit(solution)/shard_map/ppermute | solution.py:31
  75.5 4.9 %collective-permute-start.12 = (f32[16]{0:T(128)S(1)}, f32[16]{0:T(128)S(1)}, u32[]{:S(2)}, u32[]{:S(2)}) collective-permute-start(f32[16]{0:T(128)S(1)} %get-tuple-element.13), channel_id=1, source_target_pairs={{0,3},{1,2},{2,1},{3,0},{4,7},{5,6},{6,5},{7,4},{8,11},{9,10},{10,... | collective-permute-start | bytes 200 | tf_op jit(solution)/shard_map/ppermute | solution.py:87
  78.6 8.7 %collective-permute-start.11 = (f32[16]{0:T(128)S(1)}, f32[16]{0:T(128)S(1)}, u32[]{:S(2)}, u32[]{:S(2)}) collective-permute-start(f32[16]{0:T(128)S(1)} %get-tuple-element.13), channel_id=1, source_target_pairs={{0,2},{1,3},{2,0},{3,1},{4,6},{5,7},{6,4},{7,5},{8,10},{9,11},{10,... | collective-permute-start | bytes 200 | tf_op jit(solution)/shard_map/ppermute | solution.py:87
  80.3 7.0 %collective-permute-start.10 = (f32[16]{0:T(128)S(1)}, f32[16]{0:T(128)S(1)}, u32[]{:S(2)}, u32[]{:S(2)}) collective-permute-start(f32[16]{0:T(128)S(1)} %get-tuple-element.13), channel_id=1, source_target_pairs={{0,1},{1,0},{2,3},{3,2},{4,5},{5,4},{6,7},{7,6},{8,9},{9,8},{10,11... | collective-permute-start | bytes 200 | tf_op jit(solution)/shard_map/ppermute | solution.py:87
  87.3 5.4 %collective-permute-start.15 = (f32[16]{0:T(128)S(1)}, f32[16]{0:T(128)S(1)}, u32[]{:S(2)}, u32[]{:S(2)}) collective-permute-start(f32[16]{0:T(128)S(1)} %add_add_fusion.5), channel_id=1, source_target_pairs={{0,12},{1,13},{2,14},{3,15},{4,8},{5,9},{6,10},{7,11},{8,4},{9,5},... | collective-permute-start | bytes 200 | tf_op jit(solution)/shard_map/ppermute | solution.py:87
  91.1 4.4 %collective-permute-start.14 = (f32[16]{0:T(128)S(1)}, f32[16]{0:T(128)S(1)}, u32[]{:S(2)}, u32[]{:S(2)}) collective-permute-start(f32[16]{0:T(128)S(1)} %add_add_fusion.5), channel_id=1, source_target_pairs={{0,8},{1,9},{2,10},{3,11},{4,12},{5,13},{6,14},{7,15},{8,0},{9,1},... | collective-permute-start | bytes 200 | tf_op jit(solution)/shard_map/ppermute | solution.py:87
  91.1 4.4 %collective-permute-start.13 = (f32[16]{0:T(128)S(1)}, f32[16]{0:T(128)S(1)}, u32[]{:S(2)}, u32[]{:S(2)}) collective-permute-start(f32[16]{0:T(128)S(1)} %add_add_fusion.5), channel_id=1, source_target_pairs={{0,4},{1,5},{2,6},{3,7},{4,0},{5,1},{6,2},{7,3},{8,12},{9,13},{10,... | collective-permute-start | bytes 200 | tf_op jit(solution)/shard_map/ppermute | solution.py:87
  95.8 23.6 %collective-permute-start.25 = (f32[16,8192]{1,0:T(8,128)S(1)}, f32[16,8192]{1,0:T(8,128)S(1)}, u32[]{:S(2)}, u32[]{:S(2)}) collective-permute-start(f32[16,8192]{1,0:T(8,128)S(1)} %get-tuple-element.12), channel_id=1, source_target_pairs={{1,0},{2,1},{3,2},{4,3},{5,4},{6,5},{7,6},{8,7},{9,8},{10,9},{11,1... | collective-permute-start | bytes 1572872 | tf_op jit(solution)/shard_map/ppermute | solution.py:23
  97.1 22.3 %collective-permute-start.24 = (f32[16,8192]{1,0:T(8,128)S(1)}, f32[16,8192]{1,0:T(8,128)S(1)}, u32[]{:S(2)}, u32[]{:S(2)}) collective-permute-start(f32[16,8192]{1,0:T(8,128)S(1)} %get-tuple-element.12), channel_id=1, source_target_pairs={{0,1},{1,2},{2,3},{3,4},{4,5},{5,6},{6,7},{7,8},{8,9},{9,10},{10,1... | collective-permute-start | bytes 1572872 | tf_op jit(solution)/shard_map/ppermute | solution.py:22
  100.4 3.4 %collective-permute-start.20 = (f32[16]{0:T(128)S(1)}, f32[16]{0:T(128)S(1)}, u32[]{:S(2)}, u32[]{:S(2)}) collective-permute-start(f32[16]{0:T(128)S(1)} %get-tuple-element.11), channel_id=1, source_target_pairs={{0,3},{1,2},{2,1},{3,0},{4,7},{5,6},{6,5},{7,4},{8,11},{9,10},{10,... | collective-permute-start | bytes 200 | tf_op jit(solution)/shard_map/ppermute | solution.py:87
  102.5 4.4 %collective-permute-start.19 = (f32[16]{0:T(128)S(1)}, f32[16]{0:T(128)S(1)}, u32[]{:S(2)}, u32[]{:S(2)}) collective-permute-start(f32[16]{0:T(128)S(1)} %get-tuple-element.11), channel_id=1, source_target_pairs={{0,2},{1,3},{2,0},{3,1},{4,6},{5,7},{6,4},{7,5},{8,10},{9,11},{10,... | collective-permute-start | bytes 200 | tf_op jit(solution)/shard_map/ppermute | solution.py:87
  103.7 3.2 %collective-permute-start.18 = (f32[16]{0:T(128)S(1)}, f32[16]{0:T(128)S(1)}, u32[]{:S(2)}, u32[]{:S(2)}) collective-permute-start(f32[16]{0:T(128)S(1)} %get-tuple-element.11), channel_id=1, source_target_pairs={{0,1},{1,0},{2,3},{3,2},{4,5},{5,4},{6,7},{7,6},{8,9},{9,8},{10,11... | collective-permute-start | bytes 200 | tf_op jit(solution)/shard_map/ppermute | solution.py:87
  106.9 9.7 %collective-permute-start.23 = (f32[16]{0:T(128)S(1)}, f32[16]{0:T(128)S(1)}, u32[]{:S(2)}, u32[]{:S(2)}) collective-permute-start(f32[16]{0:T(128)S(1)} %add_add_fusion.4), channel_id=1, source_target_pairs={{0,12},{1,13},{2,14},{3,15},{4,8},{5,9},{6,10},{7,11},{8,4},{9,5},... | collective-permute-start | bytes 200 | tf_op jit(solution)/shard_map/ppermute | solution.py:87
  115.0 4.4 %collective-permute-start.22 = (f32[16]{0:T(128)S(1)}, f32[16]{0:T(128)S(1)}, u32[]{:S(2)}, u32[]{:S(2)}) collective-permute-start(f32[16]{0:T(128)S(1)} %add_add_fusion.4), channel_id=1, source_target_pairs={{0,8},{1,9},{2,10},{3,11},{4,12},{5,13},{6,14},{7,15},{8,0},{9,1},... | collective-permute-start | bytes 200 | tf_op jit(solution)/shard_map/ppermute | solution.py:87
  115.4 4.1 %collective-permute-start.21 = (f32[16]{0:T(128)S(1)}, f32[16]{0:T(128)S(1)}, u32[]{:S(2)}, u32[]{:S(2)}) collective-permute-start(f32[16]{0:T(128)S(1)} %add_add_fusion.4), channel_id=1, source_target_pairs={{0,4},{1,5},{2,6},{3,7},{4,0},{5,1},{6,2},{7,3},{8,12},{9,13},{10,... | collective-permute-start | bytes 200 | tf_op jit(solution)/shard_map/ppermute | solution.py:87
  143.7 23.0 %collective-permute-start.32 = (f32[16,8192]{1,0:T(8,128)S(1)}, f32[16,8192]{1,0:T(8,128)S(1)}, u32[]{:S(2)}, u32[]{:S(2)}) collective-permute-start(f32[16,8192]{1,0:T(8,128)S(1)} %get-tuple-element.19), channel_id=1, source_target_pairs={{0,1},{1,2},{2,3},{3,4},{4,5},{5,6},{6,7},{7,8},{8,9},{9,10},{10,1... | collective-permute-start | bytes 1572872 | tf_op jit(solution)/shard_map/ppermute | solution.py:31
  145.0 21.7 %collective-permute-start.33 = (f32[16,8192]{1,0:T(8,128)S(1)}, f32[16,8192]{1,0:T(8,128)S(1)}, u32[]{:S(2)}, u32[]{:S(2)}) collective-permute-start(f32[16,8192]{1,0:T(8,128)S(1)} %get-tuple-element.20), channel_id=1, source_target_pairs={{1,0},{2,1},{3,2},{4,3},{5,4},{6,5},{7,6},{8,7},{9,8},{10,9},{11,1... | collective-permute-start | bytes 1572872 | tf_op jit(solution)/shard_map/ppermute | solution.py:31
  146.3 3.5 %collective-permute-start.28 = (f32[16]{0:T(128)S(1)}, f32[16]{0:T(128)S(1)}, u32[]{:S(2)}, u32[]{:S(2)}) collective-permute-start(f32[16]{0:T(128)S(1)} %get-tuple-element.9), channel_id=1, source_target_pairs={{0,3},{1,2},{2,1},{3,0},{4,7},{5,6},{6,5},{7,4},{8,11},{9,10},{10,... | collective-permute-start | bytes 200 | tf_op jit(solution)/shard_map/ppermute | solution.py:87
  148.5 8.2 %collective-permute-start.27 = (f32[16]{0:T(128)S(1)}, f32[16]{0:T(128)S(1)}, u32[]{:S(2)}, u32[]{:S(2)}) collective-permute-start(f32[16]{0:T(128)S(1)} %get-tuple-element.9), channel_id=1, source_target_pairs={{0,2},{1,3},{2,0},{3,1},{4,6},{5,7},{6,4},{7,5},{8,10},{9,11},{10,... | collective-permute-start | bytes 200 | tf_op jit(solution)/shard_map/ppermute | solution.py:87
  149.8 7.0 %collective-permute-start.26 = (f32[16]{0:T(128)S(1)}, f32[16]{0:T(128)S(1)}, u32[]{:S(2)}, u32[]{:S(2)}) collective-permute-start(f32[16]{0:T(128)S(1)} %get-tuple-element.9), channel_id=1, source_target_pairs={{0,1},{1,0},{2,3},{3,2},{4,5},{5,4},{6,7},{7,6},{8,9},{9,8},{10,11... | collective-permute-start | bytes 200 | tf_op jit(solution)/shard_map/ppermute | solution.py:87
  156.8 7.0 %collective-permute-start.31 = (f32[16]{0:T(128)S(1)}, f32[16]{0:T(128)S(1)}, u32[]{:S(2)}, u32[]{:S(2)}) collective-permute-start(f32[16]{0:T(128)S(1)} %add_add_fusion.3), channel_id=1, source_target_pairs={{0,12},{1,13},{2,14},{3,15},{4,8},{5,9},{6,10},{7,11},{8,4},{9,5},... | collective-permute-start | bytes 200 | tf_op jit(solution)/shard_map/ppermute | solution.py:87
  162.3 4.4 %collective-permute-start.30 = (f32[16]{0:T(128)S(1)}, f32[16]{0:T(128)S(1)}, u32[]{:S(2)}, u32[]{:S(2)}) collective-permute-start(f32[16]{0:T(128)S(1)} %add_add_fusion.3), channel_id=1, source_target_pairs={{0,8},{1,9},{2,10},{3,11},{4,12},{5,13},{6,14},{7,15},{8,0},{9,1},... | collective-permute-start | bytes 200 | tf_op jit(solution)/shard_map/ppermute | solution.py:87
  162.9 3.8 %collective-permute-start.29 = (f32[16]{0:T(128)S(1)}, f32[16]{0:T(128)S(1)}, u32[]{:S(2)}, u32[]{:S(2)}) collective-permute-start(f32[16]{0:T(128)S(1)} %add_add_fusion.3), channel_id=1, source_target_pairs={{0,4},{1,5},{2,6},{3,7},{4,0},{5,1},{6,2},{7,3},{8,12},{9,13},{10,... | collective-permute-start | bytes 200 | tf_op jit(solution)/shard_map/ppermute | solution.py:87
  167.0 3.0 %collective-permute-start.36 = (f32[16]{0:T(128)S(1)}, f32[16]{0:T(128)S(1)}, u32[]{:S(2)}, u32[]{:S(2)}) collective-permute-start(f32[16]{0:T(128)S(1)} %get-tuple-element.5), channel_id=1, source_target_pairs={{0,3},{1,2},{2,1},{3,0},{4,7},{5,6},{6,5},{7,4},{8,11},{9,10},{10,... | collective-permute-start | bytes 200 | tf_op jit(solution)/shard_map/ppermute | solution.py:87
  167.1 3.6 %collective-permute-start.35 = (f32[16]{0:T(128)S(1)}, f32[16]{0:T(128)S(1)}, u32[]{:S(2)}, u32[]{:S(2)}) collective-permute-start(f32[16]{0:T(128)S(1)} %get-tuple-element.5), channel_id=1, source_target_pairs={{0,2},{1,3},{2,0},{3,1},{4,6},{5,7},{6,4},{7,5},{8,10},{9,11},{10,... | collective-permute-start | bytes 200 | tf_op jit(solution)/shard_map/ppermute | solution.py:87
  167.4 3.3 %collective-permute-start.34 = (f32[16]{0:T(128)S(1)}, f32[16]{0:T(128)S(1)}, u32[]{:S(2)}, u32[]{:S(2)}) collective-permute-start(f32[16]{0:T(128)S(1)} %get-tuple-element.5), channel_id=1, source_target_pairs={{0,1},{1,0},{2,3},{3,2},{4,5},{5,4},{6,7},{7,6},{8,9},{9,8},{10,11... | collective-permute-start | bytes 200 | tf_op jit(solution)/shard_map/ppermute | solution.py:87
  170.7 5.4 %collective-permute-start.39 = (f32[16]{0:T(128)S(1)}, f32[16]{0:T(128)S(1)}, u32[]{:S(2)}, u32[]{:S(2)}) collective-permute-start(f32[16]{0:T(128)S(1)} %add_add_fusion.2), channel_id=1, source_target_pairs={{0,12},{1,13},{2,14},{3,15},{4,8},{5,9},{6,10},{7,11},{8,4},{9,5},... | collective-permute-start | bytes 200 | tf_op jit(solution)/shard_map/ppermute | solution.py:87
  173.4 4.4 %collective-permute-start.38 = (f32[16]{0:T(128)S(1)}, f32[16]{0:T(128)S(1)}, u32[]{:S(2)}, u32[]{:S(2)}) collective-permute-start(f32[16]{0:T(128)S(1)} %add_add_fusion.2), channel_id=1, source_target_pairs={{0,8},{1,9},{2,10},{3,11},{4,12},{5,13},{6,14},{7,15},{8,0},{9,1},... | collective-permute-start | bytes 200 | tf_op jit(solution)/shard_map/ppermute | solution.py:87
  173.4 4.4 %collective-permute-start.37 = (f32[16]{0:T(128)S(1)}, f32[16]{0:T(128)S(1)}, u32[]{:S(2)}, u32[]{:S(2)}) collective-permute-start(f32[16]{0:T(128)S(1)} %add_add_fusion.2), channel_id=1, source_target_pairs={{0,4},{1,5},{2,6},{3,7},{4,0},{5,1},{6,2},{7,3},{8,12},{9,13},{10,... | collective-permute-start | bytes 200 | tf_op jit(solution)/shard_map/ppermute | solution.py:87

commit v2 on v1

--- a/solution.py
+++ b/solution.py
@@ -76,21 +76,9 @@
     peers = 1
     for axis in axes:
         peers *= lax.axis_size(axis)
-    if peers & (peers - 1):
-        return lax.psum(values, axes)
-    shift = 1
-    while shift < peers:
-        width = 4 if shift * 4 <= peers else 2
-        parts = [values]
-        for k in range(1, width):
-            pairs = [(i, i ^ (k * shift)) for i in range(peers)]
-            parts.append(lax.ppermute(values, axes, pairs))
-        if width == 4:
-            values = (parts[0] + parts[1]) + (parts[2] + parts[3])
-        else:
-            values = parts[0] + parts[1]
-        shift *= width
-    return values
+    spread = jnp.broadcast_to(values[None], (peers,) + values.shape)
+    gathered = lax.all_to_all(spread, axes, 0, 0, tiled=True)
+    return jnp.sum(gathered, axis=0)
 
 
 def squares(field):

time: 180 us -> 164 us (0.911)
  blocking collectives: 0 us -> 50 us
  starting transfers between devices: 75.3 us -> 33.3 us
  waiting for transfers between devices: 41.1 us -> 10.9 us
  other arithmetic: 3.91 us -> 7.25 us
  local copies, waits for them, and re-layouts: 9.24 us -> 11.5 us
    ppermute x30 -> x0, starting transfers between devices: 54.1 us -> none  [all_sum(): parts.append(lax.ppermute(values, axes, pairs))]
    all_to_all x0 -> x4, blocking collectives: none -> 50 us  [all_sum(): gathered = lax.all_to_all(spread, axes, 0, 0, tiled=True)]
    ppermute x30 -> x0, waiting for transfers between devices: 36.6 us -> none  [all_sum(): parts.append(lax.ppermute(values, axes, pairs))]
    all_to_all x0 -> x1, starting transfers between devices: none -> 8.22 us  [all_sum(): gathered = lax.all_to_all(spread, axes, 0, 0, tiled=True)]
    all_to_all x0 -> x1, waiting for transfers between devices: none -> 6.48 us  [all_sum(): gathered = lax.all_to_all(spread, axes, 0, 0, tiled=True)]
    ppermute x2, starting transfers between devices: 6.53 us -> 12.1 us  [with_halo(): before = lax.ppermute(last, axis, up)]
    reduce_sum x6, other arithmetic: 1.56 us -> 3.77 us  [squares(): return jnp.sum(field * field, axis=1)]
  transfers between devices with their start and end apart: 40 -> 11, of which waited for: 16 -> 2; matrix products, arithmetic and copies ran while one was open for 0% -> 1% of each run, Pallas kernels for 0% -> 0%
where the time goes in v2:
time: 164 us; the launch traced here: 163 us
  blocking collectives  50 us (30%)
  matrix products  48.1 us (29%)
  starting transfers between devices  33.3 us (20%)
  local copies, waits for them, and re-layouts  11.5 us (7%)
  waiting for transfers between devices  10.9 us (7%)
  other arithmetic  7.25 us (4%)
  between operations  1.7 us (1%)
    all_to_all x4, blocking collectives, all_sum(): gathered = lax.all_to_all(spread, axes, 0, 0, tiled=True)  50 us
    dot_general x2, matrix products, forward_local(): jnp.einsum('skj,kij->ksi', pieces, tile_stack, precision=PRODUCT_PRECISION)  21.9 us
    dot_general x3, matrix products, transpose_local(): jnp.einsum('ski,kij->ksj', pieces, tile_stack, precision=PRODUCT_PRECISION)  20.5 us
    ppermute x2, starting transfers between devices, with_halo(): before = lax.ppermute(last, axis, up)  12.1 us
    ppermute x6, starting transfers between devices, from_behind(): return lax.ppermute(shard, axis, pairs)  10.4 us
    all_to_all x1, starting transfers between devices, all_sum(): gathered = lax.all_to_all(spread, axes, 0, 0, tiled=True)  8.22 us
    all_to_all x1, waiting for transfers between devices, all_sum(): gathered = lax.all_to_all(spread, axes, 0, 0, tiled=True)  6.48 us
    ppermute x6, waiting for transfers between devices, from_behind(): return lax.ppermute(shard, axis, pairs)  4.46 us
  transfers between devices with their start and end apart: 11, of which 2 were waited for; matrix products, arithmetic and copies ran while one was open for 1% of the time, Pallas kernels for 0%

profile of v2, /device:TPU:0, one launch (start us, length us, event | category | flops | bytes accessed | tf_op | source)
XLA Modules:
  0.0 162.8 jit_solution(6962273421662552629)
XLA Ops:
  1.3 0.7 compare_select_fusion.1
  2.0 1.0 copy_bitcast_fusion.7
  3.0 0.8 gather_fusion
  3.8 6.8 %fusion.10 = f32[160,16,128]{2,1,0:T(8,128)S(1)} fusion(f32[1,160,128,128]{3,2,1,0:T(8,128)} %param.6, f32[160,16,128]{2,1,0:T(8,128)S(1)} %gather_fusion, f32[160]{0:T(256)S(1)} %compare_convert_fusion), kind=kOutput, calls=%fused_computation.22 | convolution fusion | flops 251985920 | bytes 13107840 | tf_op jit(solution)/shard_map/ski,kij->ksj/dot_general | solution.py:51
  10.7 1.3 fusion.38
  12.0 0.9 copy.79
  13.0 2.4 %collective-permute-start = (f32[16,8192]{1,0:T(8,128)S(1)}, f32[16,8192]{1,0:T(8,128)S(1)}, u32[]{:S(2)}, u32[]{:S(2)}) collective-permute-start(f32[16,8192]{1,0:T(8,128)S(1)} %get-tuple-element.24), channel_id=1, source_target_pairs={{0,1},{1,2},{2,3},{3,4},{4,5},{5,6},{6,7},{7,8},{8,9},{9,10},{10,1... | collective-permute-start | bytes 1572872 | tf_op jit(solution)/shard_map/ppermute | solution.py:31
  15.4 1.3 collective-permute-start.1
  16.7 0.1 multiply_reduce_fusion.5
  16.9 4.4 %collective-permute-done.1 = f32[16,8192]{1,0:T(8,128)S(1)} collective-permute-done((f32[16,8192]{1,0:T(8,128)S(1)}, f32[16,8192]{1,0:T(8,128)S(1)}, u32[]{:S(2)}, u32[]{:S(2)}) %collective-permute-start.1) | collective-permute-done | bytes 524320 | tf_op jit(solution)/shard_map/ppermute | solution.py:31
  21.3 0.2 multiply_reduce_fusion.2
  21.5 10.3 %collective-permute-start.2 = (f32[16,8192]{1,0:T(8,128)S(1)}, f32[16,8192]{1,0:T(8,128)S(1)}, u32[]{:S(2)}, u32[]{:S(2)}) collective-permute-start(f32[16,8192]{1,0:T(8,128)S(1)} %get-tuple-element.19), channel_id=1, source_target_pairs={{0,1},{1,2},{2,3},{3,4},{4,5},{5,6},{6,7},{7,8},{8,9},{9,10},{10,1... | collective-permute-start | bytes 1572872 | tf_op jit(solution)/shard_map/ppermute | solution.py:22
  31.8 1.3 collective-permute-start.3
  33.2 0.6 broadcast_in_dim.10
  33.8 8.2 %all-to-all-start = ((f32[16,2,16]{2,1,0:T(2,128)}), f32[16,2,16]{2,1,0:T(2,128)S(1)}, u32[]{:S(2)}, u32[]{:S(2)}) async-start(f32[16,2,16]{2,1,0:T(2,128)} %broadcast_in_dim.10), calls=%async_computation | async-start | bytes 32768 | tf_op jit(solution)/shard_map/all_to_all | solution.py:80
  42.0 6.5 %all-to-all-done = f32[16,2,16]{2,1,0:T(2,128)S(1)} async-done(((f32[16,2,16]{2,1,0:T(2,128)}), f32[16,2,16]{2,1,0:T(2,128)S(1)}, u32[]{:S(2)}, u32[]{:S(2)}) %all-to-all-start) | async-done | bytes 2080 | tf_op jit(solution)/shard_map/all_to_all | solution.py:80
  48.7 0.8 gather_fusion.1
  49.5 10.9 %fusion.13 = f32[160,16,128]{2,1,0:T(8,128)S(1)} fusion(f32[1,160,128,128]{3,2,1,0:T(8,128)} %param.6, f32[160,16,128]{2,1,0:T(8,128)S(1)} %gather_fusion.1, f32[160]{0:T(256)S(1)} %compare_convert_fusion), kind=kOutput, calls=%fused_computation.23 | convolution fusion | flops 251985920 | bytes 13107840 | tf_op jit(solution)/shard_map/skj,kij->ksi/dot_general | solution.py:39
  60.4 0.9 fusion.36
  61.4 0.3 multiply_reduce_fusion.4
  61.7 0.8 gather_fusion.2
  62.5 6.8 %fusion.16 = f32[160,16,128]{2,1,0:T(8,128)S(1)} fusion(f32[1,160,128,128]{3,2,1,0:T(8,128)} %param.6, f32[160,16,128]{2,1,0:T(8,128)S(1)} %gather_fusion.2, f32[160]{0:T(256)S(1)} %compare_convert_fusion), kind=kOutput, calls=%fused_computation.24 | convolution fusion | flops 251985920 | bytes 13107840 | tf_op jit(solution)/shard_map/ski,kij->ksj/dot_general | solution.py:51
  69.4 1.3 fusion.34
  70.7 0.9 copy.78
  71.6 0.9 fusion.68
  72.4 1.7 %collective-permute-start.4 = (f32[16,8192]{1,0:T(8,128)}, f32[16,8192]{1,0:T(8,128)S(1)}, u32[]{:S(2)}, u32[]{:S(2)}) collective-permute-start(f32[16,8192]{1,0:T(8,128)} %get-tuple-element.22), channel_id=1, source_target_pairs={{0,1},{1,2},{2,3},{3,4},{4,5},{5,6},{6,7},{7,8},{8,9},{9,10},{10,1... | collective-permute-start | bytes 1572872 | tf_op jit(solution)/shard_map/ppermute | solution.py:31
  74.1 1.3 collective-permute-start.5
  75.4 12.3 %all_to_all.29 = f32[16,1,16]{2,1,0:T(1,128)S(1)} all-to-all(f32[16,1,16]{2,1,0:T(1,128)S(1)} %broadcast_in_dim.11), channel_id=1, replica_groups=mesh['group'=2,'row'=8,'col'=2] {'row','col'}, dimensions={0} | all-to-all | bytes 2048 | tf_op jit(solution)/shard_map/all_to_all | solution.py:80
  87.8 1.3 multiply_reduce_fusion.1
  89.1 1.7 %collective-permute-start.6 = (f32[16,8192]{1,0:T(8,128)S(1)}, f32[16,8192]{1,0:T(8,128)S(1)}, u32[]{:S(2)}, u32[]{:S(2)}) collective-permute-start(f32[16,8192]{1,0:T(8,128)S(1)} %get-tuple-element.13), channel_id=1, source_target_pairs={{0,1},{1,2},{2,3},{3,4},{4,5},{5,6},{6,7},{7,8},{8,9},{9,10},{10,1... | collective-permute-start | bytes 1572872 | tf_op jit(solution)/shard_map/ppermute | solution.py:22
  90.8 1.3 collective-permute-start.7
  92.2 13.6 %all_to_all.30 = f32[16,1,16]{2,1,0:T(1,128)S(1)} all-to-all(f32[16,1,16]{2,1,0:T(1,128)S(1)} %broadcast_in_dim.12), channel_id=1, replica_groups=mesh['group'=2,'row'=8,'col'=2] {'row','col'}, dimensions={0} | all-to-all | bytes 2048 | tf_op jit(solution)/shard_map/all_to_all | solution.py:80
  105.9 1.2 copy_bitcast_fusion.3
  107.0 1.9 %gather_fusion.3 = f32[160,16,128]{2,1,0:T(8,128)} fusion(f32[16,192,128]{2,0,1:T(8,128)S(1)} %copy_bitcast_fusion.3, s32[1024]{0:T(1024)S(1)} %pad_clamp_fusion), kind=kCustom, calls=%fused_computation.3 | custom fusion | bytes 2622080 | tf_op jit(solution)/shard_map/gather | solution.py:37
  108.9 11.1 %fusion.19 = f32[160,16,128]{2,1,0:T(8,128)S(1)} fusion(f32[1,160,128,128]{3,2,1,0:T(8,128)} %param.6, f32[160,16,128]{2,1,0:T(8,128)} %gather_fusion.3, f32[160]{0:T(256)S(1)} %compare_convert_fusion), kind=kOutput, calls=%fused_computation.25 | convolution fusion | flops 251985920 | bytes 13107840 | tf_op jit(solution)/shard_map/skj,kij->ksi/dot_general | solution.py:39
  120.0 0.9 fusion.32
  120.9 0.3 multiply_reduce_fusion.3
  121.2 0.8 gather_fusion.4
  122.0 6.8 %fusion.22 = f32[160,16,128]{2,1,0:T(8,128)S(1)} fusion(f32[1,160,128,128]{3,2,1,0:T(8,128)} %param.6, f32[160,16,128]{2,1,0:T(8,128)S(1)} %gather_fusion.4, f32[160]{0:T(256)S(1)} %compare_convert_fusion), kind=kOutput, calls=%fused_computation.26 | convolution fusion | flops 251985920 | bytes 13107840 | tf_op jit(solution)/shard_map/ski,kij->ksj/dot_general | solution.py:51
  128.9 1.3 fusion.30
  130.2 0.9 copy.77
  131.1 0.9 fusion.67
  132.0 2.5 %collective-permute-start.8 = (f32[16,8192]{1,0:T(8,128)}, f32[16,8192]{1,0:T(8,128)}, u32[]{:S(2)}, u32[]{:S(2)}) collective-permute-start(f32[16,8192]{1,0:T(8,128)} %get-tuple-element.20), channel_id=1, source_target_pairs={{0,1},{1,2},{2,3},{3,4},{4,5},{5,6},{6,7},{7,8},{8,9},{9,10},{10,1... | collective-permute-start | bytes 1572872 | tf_op jit(solution)/shard_map/ppermute | solution.py:31
  134.5 1.3 collective-permute-start.9
  135.8 13.3 %all_to_all.31 = f32[16,1,16]{2,1,0:T(1,128)S(1)} all-to-all(f32[16,1,16]{2,1,0:T(1,128)S(1)} %broadcast_in_dim.13), channel_id=1, replica_groups=mesh['group'=2,'row'=8,'col'=2] {'row','col'}, dimensions={0} | all-to-all | bytes 2048 | tf_op jit(solution)/shard_map/all_to_all | solution.py:80
  149.1 1.5 multiply_reduce_fusion
  150.6 10.8 %all_to_all.32 = f32[16,1,16]{2,1,0:T(1,128)S(1)} all-to-all(f32[16,1,16]{2,1,0:T(1,128)S(1)} %broadcast_in_dim.14), channel_id=1, replica_groups=mesh['group'=2,'row'=8,'col'=2] {'row','col'}, dimensions={0} | all-to-all | bytes 2048 | tf_op jit(solution)/shard_map/all_to_all | solution.py:80
  161.5 1.2 multiply_subtract_fusion
  (44 shorter events, 0.6 us)
Async XLA Ops:
  3.8 6.9 %copy-start.2 = (s32[1,160]{1,0:T(1,128)S(1)}, s32[1,160]{1,0:T(1,128)}, u32[]{:S(2)}) copy-start(s32[1,160]{1,0:T(1,128)} %param.8) | copy-start | bytes 1924
  12.9 3.8 %copy-start = (f32[16,4096]{1,0:T(8,128)S(1)}, f32[16,4096]{1,0:T(8,128)}, u32[]{:S(2)}) copy-start(f32[16,4096]{1,0:T(8,128)} %param.5) | copy-start | bytes 786436
  13.0 3.9 %collective-permute-start = (f32[16,8192]{1,0:T(8,128)S(1)}, f32[16,8192]{1,0:T(8,128)S(1)}, u32[]{:S(2)}, u32[]{:S(2)}) collective-permute-start(f32[16,8192]{1,0:T(8,128)S(1)} %get-tuple-element.24), channel_id=1, source_target_pairs={{0,1},{1,2},{2,3},{3,4},{4,5},{5,6},{6,7},{7,8},{8,9},{9,10},{10,1... | collective-permute-start | bytes 1572872 | tf_op jit(solution)/shard_map/ppermute | solution.py:31
  15.4 5.9 %collective-permute-start.1 = (f32[16,8192]{1,0:T(8,128)S(1)}, f32[16,8192]{1,0:T(8,128)S(1)}, u32[]{:S(2)}, u32[]{:S(2)}) collective-permute-start(f32[16,8192]{1,0:T(8,128)S(1)} %get-tuple-element.25), channel_id=1, source_target_pairs={{1,0},{2,1},{3,2},{4,3},{5,4},{6,5},{7,6},{8,7},{9,8},{10,9},{11,1... | collective-permute-start | bytes 1572872 | tf_op jit(solution)/shard_map/ppermute | solution.py:31
  21.5 27.1 %collective-permute-start.2 = (f32[16,8192]{1,0:T(8,128)S(1)}, f32[16,8192]{1,0:T(8,128)S(1)}, u32[]{:S(2)}, u32[]{:S(2)}) collective-permute-start(f32[16,8192]{1,0:T(8,128)S(1)} %get-tuple-element.19), channel_id=1, source_target_pairs={{0,1},{1,2},{2,3},{3,4},{4,5},{5,6},{6,7},{7,8},{8,9},{9,10},{10,1... | collective-permute-start | bytes 1572872 | tf_op jit(solution)/shard_map/ppermute | solution.py:22
  31.8 16.7 %collective-permute-start.3 = (f32[16,8192]{1,0:T(8,128)S(1)}, f32[16,8192]{1,0:T(8,128)S(1)}, u32[]{:S(2)}, u32[]{:S(2)}) collective-permute-start(f32[16,8192]{1,0:T(8,128)S(1)} %get-tuple-element.19), channel_id=1, source_target_pairs={{1,0},{2,1},{3,2},{4,3},{5,4},{6,5},{7,6},{8,7},{9,8},{10,9},{11,1... | collective-permute-start | bytes 1572872 | tf_op jit(solution)/shard_map/ppermute | solution.py:23
  33.8 14.7 %all-to-all-start = ((f32[16,2,16]{2,1,0:T(2,128)}), f32[16,2,16]{2,1,0:T(2,128)S(1)}, u32[]{:S(2)}, u32[]{:S(2)}) async-start(f32[16,2,16]{2,1,0:T(2,128)} %broadcast_in_dim.10), calls=%async_computation | async-start | bytes 32768 | tf_op jit(solution)/shard_map/all_to_all | solution.py:80
  49.5 10.9 %copy-start.3 = (s32[1,160]{1,0:T(1,128)S(1)}, s32[1,160]{1,0:T(1,128)}, u32[]{:S(2)}) copy-start(s32[1,160]{1,0:T(1,128)} %param.7) | copy-start | bytes 1924
  60.4 1.0 copy-start.1
  72.4 15.3 %collective-permute-start.4 = (f32[16,8192]{1,0:T(8,128)}, f32[16,8192]{1,0:T(8,128)S(1)}, u32[]{:S(2)}, u32[]{:S(2)}) collective-permute-start(f32[16,8192]{1,0:T(8,128)} %get-tuple-element.22), channel_id=1, source_target_pairs={{0,1},{1,2},{2,3},{3,4},{4,5},{5,6},{6,7},{7,8},{8,9},{9,10},{10,1... | collective-permute-start | bytes 1572872 | tf_op jit(solution)/shard_map/ppermute | solution.py:31
  74.1 13.6 %collective-permute-start.5 = (f32[16,8192]{1,0:T(8,128)S(1)}, f32[16,8192]{1,0:T(8,128)}, u32[]{:S(2)}, u32[]{:S(2)}) collective-permute-start(f32[16,8192]{1,0:T(8,128)S(1)} %get-tuple-element.23), channel_id=1, source_target_pairs={{1,0},{2,1},{3,2},{4,3},{5,4},{6,5},{7,6},{8,7},{9,8},{10,9},{11,1... | collective-permute-start | bytes 1572872 | tf_op jit(solution)/shard_map/ppermute | solution.py:31
  89.1 16.7 %collective-permute-start.6 = (f32[16,8192]{1,0:T(8,128)S(1)}, f32[16,8192]{1,0:T(8,128)S(1)}, u32[]{:S(2)}, u32[]{:S(2)}) collective-permute-start(f32[16,8192]{1,0:T(8,128)S(1)} %get-tuple-element.13), channel_id=1, source_target_pairs={{0,1},{1,2},{2,3},{3,4},{4,5},{5,6},{6,7},{7,8},{8,9},{9,10},{10,1... | collective-permute-start | bytes 1572872 | tf_op jit(solution)/shard_map/ppermute | solution.py:22
  90.8 15.0 %collective-permute-start.7 = (f32[16,8192]{1,0:T(8,128)S(1)}, f32[16,8192]{1,0:T(8,128)}, u32[]{:S(2)}, u32[]{:S(2)}) collective-permute-start(f32[16,8192]{1,0:T(8,128)S(1)} %get-tuple-element.13), channel_id=1, source_target_pairs={{1,0},{2,1},{3,2},{4,3},{5,4},{6,5},{7,6},{8,7},{9,8},{10,9},{11,1... | collective-permute-start | bytes 1572872 | tf_op jit(solution)/shard_map/ppermute | solution.py:23
  132.0 17.1 %collective-permute-start.8 = (f32[16,8192]{1,0:T(8,128)}, f32[16,8192]{1,0:T(8,128)}, u32[]{:S(2)}, u32[]{:S(2)}) collective-permute-start(f32[16,8192]{1,0:T(8,128)} %get-tuple-element.20), channel_id=1, source_target_pairs={{0,1},{1,2},{2,3},{3,4},{4,5},{5,6},{6,7},{7,8},{8,9},{9,10},{10,1... | collective-permute-start | bytes 1572872 | tf_op jit(solution)/shard_map/ppermute | solution.py:31
  134.5 14.6 %collective-permute-start.9 = (f32[16,8192]{1,0:T(8,128)S(1)}, f32[16,8192]{1,0:T(8,128)}, u32[]{:S(2)}, u32[]{:S(2)}) collective-permute-start(f32[16,8192]{1,0:T(8,128)S(1)} %get-tuple-element.21), channel_id=1, source_target_pairs={{1,0},{2,1},{3,2},{4,3},{5,4},{6,5},{7,6},{8,7},{9,8},{10,9},{11,1... | collective-permute-start | bytes 1572872 | tf_op jit(solution)/shard_map/ppermute | solution.py:31

commit v3 on v2

--- a/solution.py
+++ b/solution.py
@@ -36,7 +36,7 @@
     tile_edge = tile_stack.shape[1]
     pieces = window.reshape(scenario_rows, 3 * COL_BLOCKS, tile_edge)[:, cols_idx, :]
     products = (
-        jnp.einsum("skj,kij->ksi", pieces, tile_stack, precision=PRODUCT_PRECISION) * live_slot[:, None, None]
+        jnp.einsum("skj,kji->ksi", pieces, tile_stack, precision=PRODUCT_PRECISION) * live_slot[:, None, None]
     )
     onehot = (rows_idx[:, None] == jnp.arange(ROW_BLOCKS)[None, :]).astype(jnp.float32)
     summed = jnp.einsum("kr,ksi->sri", onehot, products, precision=PRECISE)
@@ -96,8 +96,10 @@
     def backward(field):
         return transpose_apply(field, tile_stack, rows_idx, cols_idx, live_slot)
 
+    tile_stack_t = lax.optimization_barrier(jnp.swapaxes(tile_stack, 1, 2))
+
     def forward(vector):
-        return forward_apply(vector, tile_stack, rows_idx, cols_idx, live_slot)
+        return forward_apply(vector, tile_stack_t, rows_idx, cols_idx, live_slot)
 
     start_raw = backward(observed)
     totals = all_sum(jnp.stack([squares(observed), squares(start_raw)]), axes)

time: 164 us -> 167 us (1.018)
  local copies, waits for them, and re-layouts: 11.5 us -> 13.4 us
where the time goes in v3:
time: 167 us; the launch traced here: 166 us
  blocking collectives  50.7 us (30%)
  matrix products  48.4 us (29%)
  starting transfers between devices  32.5 us (19%)
  local copies, waits for them, and re-layouts  13.4 us (8%)
  waiting for transfers between devices  11 us (7%)
  other arithmetic  8.29 us (5%)
  between operations  1.69 us (1%)
    all_to_all x4, blocking collectives, all_sum(): gathered = lax.all_to_all(spread, axes, 0, 0, tiled=True)  50.7 us
    dot_general x2, matrix products, forward_local(): jnp.einsum('skj,kji->ksi', pieces, tile_stack, precision=PRODUCT_PRECISION)  22.1 us
    dot_general x3, matrix products, transpose_local(): jnp.einsum('ski,kij->ksj', pieces, tile_stack, precision=PRODUCT_PRECISION)  20.5 us
    ppermute x2, starting transfers between devices, with_halo(): before = lax.ppermute(last, axis, up)  12.1 us
    ppermute x6, starting transfers between devices, from_behind(): return lax.ppermute(shard, axis, pairs)  9.64 us
    all_to_all x1, starting transfers between devices, all_sum(): gathered = lax.all_to_all(spread, axes, 0, 0, tiled=True)  8.21 us
    all_to_all x1, waiting for transfers between devices, all_sum(): gathered = lax.all_to_all(spread, axes, 0, 0, tiled=True)  6.48 us
    ppermute x6, waiting for transfers between devices, from_behind(): return lax.ppermute(shard, axis, pairs)  4.46 us
  transfers between devices with their start and end apart: 11, of which 2 were waited for; matrix products, arithmetic and copies ran while one was open for 1% of the time, Pallas kernels for 0%

profile of v3, /device:TPU:0, one launch (start us, length us, event | category | flops | bytes accessed | tf_op | source)
XLA Modules:
  0.0 166.0 jit_solution(17159085486251240290)
XLA Ops:
  1.3 0.7 compare_select_fusion.1
  2.0 1.0 copy_bitcast_fusion.7
  3.0 0.8 gather_fusion
  3.8 6.8 %fusion.6 = f32[160,16,128]{2,1,0:T(8,128)S(1)} fusion(f32[1,160,128,128]{3,2,1,0:T(8,128)} %param.6, f32[160,16,128]{2,1,0:T(8,128)S(1)} %gather_fusion, f32[160]{0:T(256)S(1)} %compare_convert_fusion), kind=kOutput, calls=%fused_computation.18 | convolution fusion | flops 251985920 | bytes 13107840 | tf_op jit(solution)/shard_map/ski,kij->ksj/dot_general | solution.py:51
  10.7 1.3 fusion.28
  12.0 0.9 copy.87
  13.0 2.4 %collective-permute-start = (f32[16,8192]{1,0:T(8,128)S(1)}, f32[16,8192]{1,0:T(8,128)S(1)}, u32[]{:S(2)}, u32[]{:S(2)}) collective-permute-start(f32[16,8192]{1,0:T(8,128)S(1)} %get-tuple-element.24), channel_id=1, source_target_pairs={{0,1},{1,2},{2,3},{3,4},{4,5},{5,6},{6,7},{7,8},{8,9},{9,10},{10,1... | collective-permute-start | bytes 1572872 | tf_op jit(solution)/shard_map/ppermute | solution.py:31
  15.4 1.3 collective-permute-start.1
  16.9 4.4 %collective-permute-done.1 = f32[16,8192]{1,0:T(8,128)S(1)} collective-permute-done((f32[16,8192]{1,0:T(8,128)S(1)}, f32[16,8192]{1,0:T(8,128)S(1)}, u32[]{:S(2)}, u32[]{:S(2)}) %collective-permute-start.1) | collective-permute-done | bytes 524320 | tf_op jit(solution)/shard_map/ppermute | solution.py:31
  21.5 10.3 %collective-permute-start.2 = (f32[16,8192]{1,0:T(8,128)S(1)}, f32[16,8192]{1,0:T(8,128)S(1)}, u32[]{:S(2)}, u32[]{:S(2)}) collective-permute-start(f32[16,8192]{1,0:T(8,128)S(1)} %get-tuple-element.19), channel_id=1, source_target_pairs={{0,1},{1,2},{2,3},{3,4},{4,5},{5,6},{6,7},{7,8},{8,9},{9,10},{10,1... | collective-permute-start | bytes 1572872 | tf_op jit(solution)/shard_map/ppermute | solution.py:22
  31.9 1.3 collective-permute-start.3
  33.2 0.6 broadcast_in_dim.10
  33.8 8.2 %all-to-all-start = ((f32[16,2,16]{2,1,0:T(2,128)}), f32[16,2,16]{2,1,0:T(2,128)S(1)}, u32[]{:S(2)}, u32[]{:S(2)}) async-start(f32[16,2,16]{2,1,0:T(2,128)} %broadcast_in_dim.10), calls=%async_computation | async-start | bytes 32768 | tf_op jit(solution)/shard_map/all_to_all | solution.py:80
  42.0 6.5 %all-to-all-done = f32[16,2,16]{2,1,0:T(2,128)S(1)} async-done(((f32[16,2,16]{2,1,0:T(2,128)}), f32[16,2,16]{2,1,0:T(2,128)S(1)}, u32[]{:S(2)}, u32[]{:S(2)}) %all-to-all-start) | async-done | bytes 2080 | tf_op jit(solution)/shard_map/all_to_all | solution.py:80
  48.6 1.2 copy_bitcast_fusion.4
  49.7 1.9 %gather_fusion.1 = f32[160,16,128]{2,1,0:T(8,128)} fusion(f32[16,192,128]{2,0,1:T(8,128)S(1)} %copy_bitcast_fusion.4, s32[1024]{0:T(1024)S(1)} %pad_clamp_fusion), kind=kCustom, calls=%fused_computation.1 | custom fusion | bytes 2622080 | tf_op jit(solution)/shard_map/gather | solution.py:37
  51.6 11.1 %convolution_multiply_fusion.1 = f32[160,16,128]{2,1,0:T(8,128)S(1)} fusion(f32[160,128,128]{1,2,0:T(8,128)} %bitcast.127, f32[160,16,128]{2,1,0:T(8,128)} %gather_fusion.1, f32[160]{0:T(256)S(1)} %compare_convert_fusion), kind=kOutput, calls=%fused_computation.22 | convolution fusion | flops 251985920 | bytes 13107840 | tf_op jit(solution)/shard_map/skj,kji->ksi/dot_general | solution.py:39
  62.7 0.9 fusion.26
  63.6 0.3 multiply_reduce_fusion.4
  63.9 0.8 gather_fusion.2
  64.8 6.8 %fusion.12 = f32[160,16,128]{2,1,0:T(8,128)S(1)} fusion(f32[1,160,128,128]{3,2,1,0:T(8,128)} %param.6, f32[160,16,128]{2,1,0:T(8,128)S(1)} %gather_fusion.2, f32[160]{0:T(256)S(1)} %compare_convert_fusion), kind=kOutput, calls=%fused_computation.20 | convolution fusion | flops 251985920 | bytes 13107840 | tf_op jit(solution)/shard_map/ski,kij->ksj/dot_general | solution.py:51
  71.6 1.3 fusion.24
  72.9 0.9 copy.86
  73.8 0.9 fusion.58
  74.7 1.7 %collective-permute-start.4 = (f32[16,8192]{1,0:T(8,128)}, f32[16,8192]{1,0:T(8,128)S(1)}, u32[]{:S(2)}, u32[]{:S(2)}) collective-permute-start(f32[16,8192]{1,0:T(8,128)} %get-tuple-element.22), channel_id=1, source_target_pairs={{0,1},{1,2},{2,3},{3,4},{4,5},{5,6},{6,7},{7,8},{8,9},{9,10},{10,1... | collective-permute-start | bytes 1572872 | tf_op jit(solution)/shard_map/ppermute | solution.py:31
  76.4 1.3 collective-permute-start.5
  77.7 12.3 %all_to_all.29 = f32[16,1,16]{2,1,0:T(1,128)S(1)} all-to-all(f32[16,1,16]{2,1,0:T(1,128)S(1)} %broadcast_in_dim.11), channel_id=1, replica_groups=mesh['group'=2,'row'=8,'col'=2] {'row','col'}, dimensions={0} | all-to-all | bytes 2048 | tf_op jit(solution)/shard_map/all_to_all | solution.py:80
  90.0 1.3 multiply_reduce_fusion.1
  91.4 1.7 %collective-permute-start.6 = (f32[16,8192]{1,0:T(8,128)S(1)}, f32[16,8192]{1,0:T(8,128)S(1)}, u32[]{:S(2)}, u32[]{:S(2)}) collective-permute-start(f32[16,8192]{1,0:T(8,128)S(1)} %get-tuple-element.13), channel_id=1, source_target_pairs={{0,1},{1,2},{2,3},{3,4},{4,5},{5,6},{6,7},{7,8},{8,9},{9,10},{10,1... | collective-permute-start | bytes 1572872 | tf_op jit(solution)/shard_map/ppermute | solution.py:22
  93.1 1.3 collective-permute-start.7
  94.4 13.6 %all_to_all.30 = f32[16,1,16]{2,1,0:T(1,128)S(1)} all-to-all(f32[16,1,16]{2,1,0:T(1,128)S(1)} %broadcast_in_dim.12), channel_id=1, replica_groups=mesh['group'=2,'row'=8,'col'=2] {'row','col'}, dimensions={0} | all-to-all | bytes 2048 | tf_op jit(solution)/shard_map/all_to_all | solution.py:80
  108.1 1.2 copy_bitcast_fusion.3
  109.3 1.9 %gather_fusion.3 = f32[160,16,128]{2,1,0:T(8,128)} fusion(f32[16,192,128]{2,0,1:T(8,128)S(1)} %copy_bitcast_fusion.3, s32[1024]{0:T(1024)S(1)} %pad_clamp_fusion), kind=kCustom, calls=%fused_computation.3 | custom fusion | bytes 2622080 | tf_op jit(solution)/shard_map/gather | solution.py:37
  111.2 11.1 %convolution_multiply_fusion = f32[160,16,128]{2,1,0:T(8,128)S(1)} fusion(f32[160,128,128]{1,2,0:T(8,128)} %bitcast.128, f32[160,16,128]{2,1,0:T(8,128)} %gather_fusion.3, f32[160]{0:T(256)S(1)} %compare_convert_fusion), kind=kOutput, calls=%fused_computation.21 | convolution fusion | flops 251985920 | bytes 13107840 | tf_op jit(solution)/shard_map/skj,kji->ksi/dot_general | solution.py:39
  122.2 0.9 fusion.22
  123.2 0.3 multiply_reduce_fusion.3
  123.5 0.8 gather_fusion.4
  124.3 6.8 %fusion.9 = f32[160,16,128]{2,1,0:T(8,128)S(1)} fusion(f32[1,160,128,128]{3,2,1,0:T(8,128)} %param.6, f32[160,16,128]{2,1,0:T(8,128)S(1)} %gather_fusion.4, f32[160]{0:T(256)S(1)} %compare_convert_fusion), kind=kOutput, calls=%fused_computation.19 | convolution fusion | flops 251985920 | bytes 13107840 | tf_op jit(solution)/shard_map/ski,kij->ksj/dot_general | solution.py:51
  131.2 1.3 fusion.20
  132.5 0.9 copy.85
  133.4 1.0 fusion.57
  134.4 1.7 %collective-permute-start.8 = (f32[16,8192]{1,0:T(8,128)}, f32[16,8192]{1,0:T(8,128)S(1)}, u32[]{:S(2)}, u32[]{:S(2)}) collective-permute-start(f32[16,8192]{1,0:T(8,128)} %get-tuple-element.20), channel_id=1, source_target_pairs={{0,1},{1,2},{2,3},{3,4},{4,5},{5,6},{6,7},{7,8},{8,9},{9,10},{10,1... | collective-permute-start | bytes 1572872 | tf_op jit(solution)/shard_map/ppermute | solution.py:31
  136.1 1.3 collective-permute-start.9
  137.5 14.0 %all_to_all.31 = f32[16,1,16]{2,1,0:T(1,128)S(1)} all-to-all(f32[16,1,16]{2,1,0:T(1,128)S(1)} %broadcast_in_dim.13), channel_id=1, replica_groups=mesh['group'=2,'row'=8,'col'=2] {'row','col'}, dimensions={0} | all-to-all | bytes 2048 | tf_op jit(solution)/shard_map/all_to_all | solution.py:80
  151.5 0.8 copy-done.1
  152.3 1.5 multiply_reduce_fusion
  153.8 10.8 %all_to_all.32 = f32[16,1,16]{2,1,0:T(1,128)S(1)} all-to-all(f32[16,1,16]{2,1,0:T(1,128)S(1)} %broadcast_in_dim.14), channel_id=1, replica_groups=mesh['group'=2,'row'=8,'col'=2] {'row','col'}, dimensions={0} | all-to-all | bytes 2048 | tf_op jit(solution)/shard_map/all_to_all | solution.py:80
  164.7 1.2 multiply_subtract_fusion
  (44 shorter events, 0.8 us)
Async XLA Ops:
  3.8 6.9 %copy-start.2 = (s32[1,160]{1,0:T(1,128)S(1)}, s32[1,160]{1,0:T(1,128)}, u32[]{:S(2)}) copy-start(s32[1,160]{1,0:T(1,128)} %param.8) | copy-start | bytes 1924
  12.9 3.8 %copy-start = (f32[16,4096]{1,0:T(8,128)S(1)}, f32[16,4096]{1,0:T(8,128)}, u32[]{:S(2)}) copy-start(f32[16,4096]{1,0:T(8,128)} %param.5) | copy-start | bytes 786436
  13.0 3.9 %collective-permute-start = (f32[16,8192]{1,0:T(8,128)S(1)}, f32[16,8192]{1,0:T(8,128)S(1)}, u32[]{:S(2)}, u32[]{:S(2)}) collective-permute-start(f32[16,8192]{1,0:T(8,128)S(1)} %get-tuple-element.24), channel_id=1, source_target_pairs={{0,1},{1,2},{2,3},{3,4},{4,5},{5,6},{6,7},{7,8},{8,9},{9,10},{10,1... | collective-permute-start | bytes 1572872 | tf_op jit(solution)/shard_map/ppermute | solution.py:31
  15.4 5.9 %collective-permute-start.1 = (f32[16,8192]{1,0:T(8,128)S(1)}, f32[16,8192]{1,0:T(8,128)S(1)}, u32[]{:S(2)}, u32[]{:S(2)}) collective-permute-start(f32[16,8192]{1,0:T(8,128)S(1)} %get-tuple-element.25), channel_id=1, source_target_pairs={{1,0},{2,1},{3,2},{4,3},{5,4},{6,5},{7,6},{8,7},{9,8},{10,9},{11,1... | collective-permute-start | bytes 1572872 | tf_op jit(solution)/shard_map/ppermute | solution.py:31
  21.5 27.1 %collective-permute-start.2 = (f32[16,8192]{1,0:T(8,128)S(1)}, f32[16,8192]{1,0:T(8,128)S(1)}, u32[]{:S(2)}, u32[]{:S(2)}) collective-permute-start(f32[16,8192]{1,0:T(8,128)S(1)} %get-tuple-element.19), channel_id=1, source_target_pairs={{0,1},{1,2},{2,3},{3,4},{4,5},{5,6},{6,7},{7,8},{8,9},{9,10},{10,1... | collective-permute-start | bytes 1572872 | tf_op jit(solution)/shard_map/ppermute | solution.py:22
  31.9 16.7 %collective-permute-start.3 = (f32[16,8192]{1,0:T(8,128)S(1)}, f32[16,8192]{1,0:T(8,128)}, u32[]{:S(2)}, u32[]{:S(2)}) collective-permute-start(f32[16,8192]{1,0:T(8,128)S(1)} %get-tuple-element.19), channel_id=1, source_target_pairs={{1,0},{2,1},{3,2},{4,3},{5,4},{6,5},{7,6},{8,7},{9,8},{10,9},{11,1... | collective-permute-start | bytes 1572872 | tf_op jit(solution)/shard_map/ppermute | solution.py:23
  33.8 14.7 %all-to-all-start = ((f32[16,2,16]{2,1,0:T(2,128)}), f32[16,2,16]{2,1,0:T(2,128)S(1)}, u32[]{:S(2)}, u32[]{:S(2)}) async-start(f32[16,2,16]{2,1,0:T(2,128)} %broadcast_in_dim.10), calls=%async_computation | async-start | bytes 32768 | tf_op jit(solution)/shard_map/all_to_all | solution.py:80
  51.6 11.1 %copy-start.3 = (s32[1,160]{1,0:T(1,128)S(1)}, s32[1,160]{1,0:T(1,128)}, u32[]{:S(2)}) copy-start(s32[1,160]{1,0:T(1,128)} %param.7) | copy-start | bytes 1924
  74.7 15.3 %collective-permute-start.4 = (f32[16,8192]{1,0:T(8,128)}, f32[16,8192]{1,0:T(8,128)S(1)}, u32[]{:S(2)}, u32[]{:S(2)}) collective-permute-start(f32[16,8192]{1,0:T(8,128)} %get-tuple-element.22), channel_id=1, source_target_pairs={{0,1},{1,2},{2,3},{3,4},{4,5},{5,6},{6,7},{7,8},{8,9},{9,10},{10,1... | collective-permute-start | bytes 1572872 | tf_op jit(solution)/shard_map/ppermute | solution.py:31
  76.4 13.6 %collective-permute-start.5 = (f32[16,8192]{1,0:T(8,128)S(1)}, f32[16,8192]{1,0:T(8,128)}, u32[]{:S(2)}, u32[]{:S(2)}) collective-permute-start(f32[16,8192]{1,0:T(8,128)S(1)} %get-tuple-element.23), channel_id=1, source_target_pairs={{1,0},{2,1},{3,2},{4,3},{5,4},{6,5},{7,6},{8,7},{9,8},{10,9},{11,1... | collective-permute-start | bytes 1572872 | tf_op jit(solution)/shard_map/ppermute | solution.py:31
  91.4 16.7 %collective-permute-start.6 = (f32[16,8192]{1,0:T(8,128)S(1)}, f32[16,8192]{1,0:T(8,128)S(1)}, u32[]{:S(2)}, u32[]{:S(2)}) collective-permute-start(f32[16,8192]{1,0:T(8,128)S(1)} %get-tuple-element.13), channel_id=1, source_target_pairs={{0,1},{1,2},{2,3},{3,4},{4,5},{5,6},{6,7},{7,8},{8,9},{9,10},{10,1... | collective-permute-start | bytes 1572872 | tf_op jit(solution)/shard_map/ppermute | solution.py:22
  93.1 15.0 %collective-permute-start.7 = (f32[16,8192]{1,0:T(8,128)S(1)}, f32[16,8192]{1,0:T(8,128)}, u32[]{:S(2)}, u32[]{:S(2)}) collective-permute-start(f32[16,8192]{1,0:T(8,128)S(1)} %get-tuple-element.13), channel_id=1, source_target_pairs={{1,0},{2,1},{3,2},{4,3},{5,4},{6,5},{7,6},{8,7},{9,8},{10,9},{11,1... | collective-permute-start | bytes 1572872 | tf_op jit(solution)/shard_map/ppermute | solution.py:23
  134.4 17.1 %collective-permute-start.8 = (f32[16,8192]{1,0:T(8,128)}, f32[16,8192]{1,0:T(8,128)S(1)}, u32[]{:S(2)}, u32[]{:S(2)}) collective-permute-start(f32[16,8192]{1,0:T(8,128)} %get-tuple-element.20), channel_id=1, source_target_pairs={{0,1},{1,2},{2,3},{3,4},{4,5},{5,6},{6,7},{7,8},{8,9},{9,10},{10,1... | collective-permute-start | bytes 1572872 | tf_op jit(solution)/shard_map/ppermute | solution.py:31
  136.1 16.2 %collective-permute-start.9 = (f32[16,8192]{1,0:T(8,128)}, f32[16,8192]{1,0:T(8,128)}, u32[]{:S(2)}, u32[]{:S(2)}) collective-permute-start(f32[16,8192]{1,0:T(8,128)} %get-tuple-element.21), channel_id=1, source_target_pairs={{1,0},{2,1},{3,2},{4,3},{5,4},{6,5},{7,6},{8,7},{9,8},{10,9},{11,1... | collective-permute-start | bytes 1572872 | tf_op jit(solution)/shard_map/ppermute | solution.py:31
  151.5 0.8 copy-start.1

commit v4 on v3

--- a/solution.py
+++ b/solution.py
@@ -2,6 +2,8 @@
 import jax.numpy as jnp
 from jax import lax
 from jax.sharding import PartitionSpec as P
+from jax.experimental import pallas as pl
+from jax.experimental.pallas import tpu as pltpu
 
 ROW_BLOCKS = 32
 COL_BLOCKS = 64
@@ -29,6 +31,25 @@
     peers = lax.axis_size(axis)
     pairs = [(i, i + by) for i in range(peers) if 0 <= i + by < peers]
     return lax.ppermute(shard, axis, pairs)
+
+
+def transpose_blocks(tile_stack):
+    slots, edge, _ = tile_stack.shape
+    step = 16 if slots % 16 == 0 else 1
+
+    def body(x_ref, o_ref):
+        for i in range(step):
+            o_ref[i] = x_ref[i].T
+
+    nbytes = 2 * tile_stack.size * tile_stack.dtype.itemsize
+    return pl.pallas_call(
+        body,
+        grid=(slots // step,),
+        in_specs=[pl.BlockSpec((step, edge, edge), lambda k: (k, 0, 0))],
+        out_specs=pl.BlockSpec((step, edge, edge), lambda k: (k, 0, 0)),
+        out_shape=jax.ShapeDtypeStruct(tile_stack.shape, tile_stack.dtype),
+        cost_estimate=pl.CostEstimate(flops=0, transcendentals=0, bytes_accessed=nbytes),
+    )(tile_stack)
 
 
 def forward_local(window, tile_stack, rows_idx, cols_idx, live_slot):
@@ -96,7 +117,7 @@
     def backward(field):
         return transpose_apply(field, tile_stack, rows_idx, cols_idx, live_slot)
 
-    tile_stack_t = lax.optimization_barrier(jnp.swapaxes(tile_stack, 1, 2))
+    tile_stack_t = transpose_blocks(tile_stack)
 
     def forward(vector):
         return forward_apply(vector, tile_stack_t, rows_idx, cols_idx, live_slot)

time: 167 us -> 168 us (level)
  Pallas kernels: 0 us -> 12.3 us
  matrix products: 48.4 us -> 40.3 us
  waiting for transfers between devices: 11 us -> 4.47 us
  blocking collectives: 50.7 us -> 53.2 us
    pallas_call x0 -> x1, Pallas kernels: none -> 12.3 us  [transpose_blocks(): pl.pallas_call(body, grid=(slots // step,), in_specs=[pl.BlockSpec((step,...]
    dot_general x2, matrix products: 22.1 us -> 14.1 us  [forward_local(): jnp.einsum('skj,kji->ksi', pieces, tile_stack, precision=PRODUCT_PRECISION)]
    all_to_all x1, waiting for transfers between devices: 6.48 us -> 0.01 us  [all_sum(): gathered = lax.all_to_all(spread, axes, 0, 0, tiled=True)]
    all_to_all x4, blocking collectives: 50.7 us -> 53.2 us  [all_sum(): gathered = lax.all_to_all(spread, axes, 0, 0, tiled=True)]
  transfers between devices with their start and end apart: 11 -> 11, of which waited for: 2 -> 1; matrix products, arithmetic and copies ran while one was open for 1% -> 1% of each run, Pallas kernels for 0% -> 7%
where the time goes in v4:
time: 168 us; the launch traced here: 167 us
  blocking collectives  53.2 us (32%)
  matrix products  40.3 us (24%)
  starting transfers between devices  33.2 us (20%)
  local copies, waits for them, and re-layouts  13.5 us (8%)
  Pallas kernels  12.3 us (7%)
  other arithmetic  8.29 us (5%)
  waiting for transfers between devices  4.47 us (3%)
  between operations  1.71 us (1%)
    all_to_all x4, blocking collectives, all_sum(): gathered = lax.all_to_all(spread, axes, 0, 0, tiled=True)  53.2 us
    dot_general x3, matrix products, transpose_local(): jnp.einsum('ski,kij->ksj', pieces, tile_stack, precision=PRODUCT_PRECISION)  20.5 us
    dot_general x2, matrix products, forward_local(): jnp.einsum('skj,kji->ksi', pieces, tile_stack, precision=PRODUCT_PRECISION)  14.1 us
    pallas_call x1, Pallas kernels, transpose_blocks(): pl.pallas_call(body, grid=(slots // step,), in_specs=[pl.BlockSpec((step,...  12.3 us
    ppermute x2, starting transfers between devices, with_halo(): before = lax.ppermute(last, axis, up)  12.1 us
    ppermute x6, starting transfers between devices, from_behind(): return lax.ppermute(shard, axis, pairs)  10.3 us
    all_to_all x1, starting transfers between devices, all_sum(): gathered = lax.all_to_all(spread, axes, 0, 0, tiled=True)  8.22 us
    ppermute x6, waiting for transfers between devices, from_behind(): return lax.ppermute(shard, axis, pairs)  4.46 us
  transfers between devices with their start and end apart: 11, of which 1 were waited for; matrix products, arithmetic and copies ran while one was open for 1% of the time, Pallas kernels for 7%

profile of v4, /device:TPU:0, one launch (start us, length us, event | category | flops | bytes accessed | tf_op | source)
XLA Modules:
  0.0 166.9 jit_solution(13923837025343969810)
XLA Ops:
  1.3 0.7 compare_select_fusion.1
  2.0 1.0 copy_bitcast_fusion.7
  3.0 0.8 gather_fusion
  3.8 6.8 %convolution_multiply_fusion.4 = f32[160,16,128]{2,1,0:T(8,128)S(1)} fusion(f32[160,16,128]{2,1,0:T(8,128)S(1)} %gather_fusion, f32[160]{0:T(256)S(1)} %compare_convert_fusion, f32[1,160,128,128]{3,2,1,0:T(8,128)} %param.6), kind=kOutput, calls=%fused_computation.16 | convolution fusion | flops 251985920 | bytes 13107840 | tf_op jit(solution)/shard_map/ski,kij->ksj/dot_general | solution.py:72
  10.7 1.3 fusion.13
  12.0 0.9 copy.79
  13.0 2.4 %collective-permute-start = (f32[16,8192]{1,0:T(8,128)S(1)}, f32[16,8192]{1,0:T(8,128)S(1)}, u32[]{:S(2)}, u32[]{:S(2)}) collective-permute-start(f32[16,8192]{1,0:T(8,128)S(1)} %get-tuple-element.24), channel_id=1, source_target_pairs={{0,1},{1,2},{2,3},{3,4},{4,5},{5,6},{6,7},{7,8},{8,9},{9,10},{10,1... | collective-permute-start | bytes 1572872 | tf_op jit(solution)/shard_map/ppermute | solution.py:33
  15.4 1.3 collective-permute-start.1
  16.9 4.4 %collective-permute-done.1 = f32[16,8192]{1,0:T(8,128)S(1)} collective-permute-done((f32[16,8192]{1,0:T(8,128)S(1)}, f32[16,8192]{1,0:T(8,128)S(1)}, u32[]{:S(2)}, u32[]{:S(2)}) %collective-permute-start.1) | collective-permute-done | bytes 524320 | tf_op jit(solution)/shard_map/ppermute | solution.py:33
  21.5 10.3 %collective-permute-start.2 = (f32[16,8192]{1,0:T(8,128)S(1)}, f32[16,8192]{1,0:T(8,128)S(1)}, u32[]{:S(2)}, u32[]{:S(2)}) collective-permute-start(f32[16,8192]{1,0:T(8,128)S(1)} %get-tuple-element.19), channel_id=1, source_target_pairs={{0,1},{1,2},{2,3},{3,4},{4,5},{5,6},{6,7},{7,8},{8,9},{9,10},{10,1... | collective-permute-start | bytes 1572872 | tf_op jit(solution)/shard_map/ppermute | solution.py:24
  31.8 1.3 collective-permute-start.3
  33.2 0.6 broadcast_in_dim.10
  33.8 8.2 %all-to-all-start = ((f32[16,2,16]{2,1,0:T(2,128)}), f32[16,2,16]{2,1,0:T(2,128)S(1)}, u32[]{:S(2)}, u32[]{:S(2)}) async-start(f32[16,2,16]{2,1,0:T(2,128)} %broadcast_in_dim.10), calls=%async_computation | async-start | bytes 32768 | tf_op jit(solution)/shard_map/all_to_all | solution.py:101
  42.0 12.3 %shard_map.68 = f32[160,128,128]{2,1,0:T(8,128)} custom-call(f32[160,128,128]{2,1,0:T(8,128)} %bitcast.119), custom_call_target="tpu_custom_call" | custom-call | bytes 20971520 | tf_op jit(solution)/shard_map/pallas_call | solution.py:45
  54.4 1.2 copy_bitcast_fusion.4
  55.5 1.9 %gather_fusion.1 = f32[160,16,128]{2,1,0:T(8,128)} fusion(f32[16,192,128]{2,0,1:T(8,128)S(1)} %copy_bitcast_fusion.4, s32[1024]{0:T(1024)S(1)} %pad_clamp_fusion), kind=kCustom, calls=%fused_computation.1 | custom fusion | bytes 2622080 | tf_op jit(solution)/shard_map/gather | solution.py:58
  57.4 7.1 %convolution_multiply_fusion.3 = f32[160,16,128]{2,1,0:T(8,128)S(1)} fusion(f32[160,128,128]{2,1,0:T(8,128)} %shard_map.68, f32[160,16,128]{2,1,0:T(8,128)} %gather_fusion.1, f32[160]{0:T(256)S(1)} %compare_convert_fusion), kind=kOutput, calls=%fused_computation.15 | convolution fusion | flops 251985920 | bytes 13107840 | tf_op jit(solution)/shard_map/skj,kji->ksi/dot_general | solution.py:60
  64.5 0.9 fusion.11
  65.4 0.3 multiply_reduce_fusion.4
  65.7 0.8 gather_fusion.2
  66.6 6.8 %convolution_multiply_fusion.2 = f32[160,16,128]{2,1,0:T(8,128)S(1)} fusion(f32[160,16,128]{2,1,0:T(8,128)S(1)} %gather_fusion.2, f32[160]{0:T(256)S(1)} %compare_convert_fusion, f32[1,160,128,128]{3,2,1,0:T(8,128)} %param.6), kind=kOutput, calls=%fused_computation.14 | convolution fusion | flops 251985920 | bytes 13107840 | tf_op jit(solution)/shard_map/ski,kij->ksj/dot_general | solution.py:72
  73.4 1.3 fusion.9
  74.7 0.9 copy.78
  75.7 0.9 fusion.46
  76.5 2.3 %collective-permute-start.4 = (f32[16,8192]{1,0:T(8,128)}, f32[16,8192]{1,0:T(8,128)S(1)}, u32[]{:S(2)}, u32[]{:S(2)}) collective-permute-start(f32[16,8192]{1,0:T(8,128)} %get-tuple-element.22), channel_id=1, source_target_pairs={{0,1},{1,2},{2,3},{3,4},{4,5},{5,6},{6,7},{7,8},{8,9},{9,10},{10,1... | collective-permute-start | bytes 1572872 | tf_op jit(solution)/shard_map/ppermute | solution.py:33
  78.8 1.3 collective-permute-start.5
  80.2 14.1 %all_to_all.29 = f32[16,1,16]{2,1,0:T(1,128)S(1)} all-to-all(f32[16,1,16]{2,1,0:T(1,128)S(1)} %broadcast_in_dim.11), channel_id=1, replica_groups=mesh['group'=2,'row'=8,'col'=2] {'row','col'}, dimensions={0} | all-to-all | bytes 2048 | tf_op jit(solution)/shard_map/all_to_all | solution.py:101
  94.4 1.3 multiply_reduce_fusion.1
  95.7 1.7 %collective-permute-start.6 = (f32[16,8192]{1,0:T(8,128)S(1)}, f32[16,8192]{1,0:T(8,128)S(1)}, u32[]{:S(2)}, u32[]{:S(2)}) collective-permute-start(f32[16,8192]{1,0:T(8,128)S(1)} %get-tuple-element.13), channel_id=1, source_target_pairs={{0,1},{1,2},{2,3},{3,4},{4,5},{5,6},{6,7},{7,8},{8,9},{9,10},{10,1... | collective-permute-start | bytes 1572872 | tf_op jit(solution)/shard_map/ppermute | solution.py:24
  97.4 1.3 collective-permute-start.7
  98.7 14.2 %all_to_all.30 = f32[16,1,16]{2,1,0:T(1,128)S(1)} all-to-all(f32[16,1,16]{2,1,0:T(1,128)S(1)} %broadcast_in_dim.12), channel_id=1, replica_groups=mesh['group'=2,'row'=8,'col'=2] {'row','col'}, dimensions={0} | all-to-all | bytes 2048 | tf_op jit(solution)/shard_map/all_to_all | solution.py:101
  113.0 1.2 copy_bitcast_fusion.3
  114.2 1.9 %gather_fusion.3 = f32[160,16,128]{2,1,0:T(8,128)} fusion(f32[16,192,128]{2,0,1:T(8,128)S(1)} %copy_bitcast_fusion.3, s32[1024]{0:T(1024)S(1)} %pad_clamp_fusion), kind=kCustom, calls=%fused_computation.3 | custom fusion | bytes 2622080 | tf_op jit(solution)/shard_map/gather | solution.py:58
  116.1 7.1 %convolution_multiply_fusion.1 = f32[160,16,128]{2,1,0:T(8,128)S(1)} fusion(f32[160,128,128]{2,1,0:T(8,128)} %shard_map.68, f32[160,16,128]{2,1,0:T(8,128)} %gather_fusion.3, f32[160]{0:T(256)S(1)} %compare_convert_fusion), kind=kOutput, calls=%fused_computation.13 | convolution fusion | flops 251985920 | bytes 13107840 | tf_op jit(solution)/shard_map/skj,kji->ksi/dot_general | solution.py:60
  123.2 0.9 fusion.7
  124.1 0.3 multiply_reduce_fusion.3
  124.4 0.8 gather_fusion.4
  125.2 6.8 %convolution_multiply_fusion = f32[160,16,128]{2,1,0:T(8,128)S(1)} fusion(f32[160,16,128]{2,1,0:T(8,128)S(1)} %gather_fusion.4, f32[160]{0:T(256)S(1)} %compare_convert_fusion, f32[1,160,128,128]{3,2,1,0:T(8,128)} %param.6), kind=kOutput, calls=%fused_computation.12 | convolution fusion | flops 251985920 | bytes 13107840 | tf_op jit(solution)/shard_map/ski,kij->ksj/dot_general | solution.py:72
  132.1 1.3 fusion.5
  133.4 0.9 copy.77
  134.3 1.0 fusion.45
  135.3 1.7 %collective-permute-start.8 = (f32[16,8192]{1,0:T(8,128)}, f32[16,8192]{1,0:T(8,128)S(1)}, u32[]{:S(2)}, u32[]{:S(2)}) collective-permute-start(f32[16,8192]{1,0:T(8,128)} %get-tuple-element.20), channel_id=1, source_target_pairs={{0,1},{1,2},{2,3},{3,4},{4,5},{5,6},{6,7},{7,8},{8,9},{9,10},{10,1... | collective-permute-start | bytes 1572872 | tf_op jit(solution)/shard_map/ppermute | solution.py:33
  137.1 1.3 collective-permute-start.9
  138.4 14.0 %all_to_all.31 = f32[16,1,16]{2,1,0:T(1,128)S(1)} all-to-all(f32[16,1,16]{2,1,0:T(1,128)S(1)} %broadcast_in_dim.13), channel_id=1, replica_groups=mesh['group'=2,'row'=8,'col'=2] {'row','col'}, dimensions={0} | all-to-all | bytes 2048 | tf_op jit(solution)/shard_map/all_to_all | solution.py:101
  152.4 0.8 copy-done.1
  153.2 1.5 multiply_reduce_fusion
  154.7 10.8 %all_to_all.32 = f32[16,1,16]{2,1,0:T(1,128)S(1)} all-to-all(f32[16,1,16]{2,1,0:T(1,128)S(1)} %broadcast_in_dim.14), channel_id=1, replica_groups=mesh['group'=2,'row'=8,'col'=2] {'row','col'}, dimensions={0} | all-to-all | bytes 2048 | tf_op jit(solution)/shard_map/all_to_all | solution.py:101
  165.7 1.2 multiply_subtract_fusion
  (45 shorter events, 0.8 us)
Async XLA Ops:
  3.8 6.9 %copy-start.2 = (s32[1,160]{1,0:T(1,128)S(1)}, s32[1,160]{1,0:T(1,128)}, u32[]{:S(2)}) copy-start(s32[1,160]{1,0:T(1,128)} %param.8) | copy-start | bytes 1924
  12.9 3.8 %copy-start = (f32[16,4096]{1,0:T(8,128)S(1)}, f32[16,4096]{1,0:T(8,128)}, u32[]{:S(2)}) copy-start(f32[16,4096]{1,0:T(8,128)} %param.5) | copy-start | bytes 786436
  13.0 3.9 %collective-permute-start = (f32[16,8192]{1,0:T(8,128)S(1)}, f32[16,8192]{1,0:T(8,128)S(1)}, u32[]{:S(2)}, u32[]{:S(2)}) collective-permute-start(f32[16,8192]{1,0:T(8,128)S(1)} %get-tuple-element.24), channel_id=1, source_target_pairs={{0,1},{1,2},{2,3},{3,4},{4,5},{5,6},{6,7},{7,8},{8,9},{9,10},{10,1... | collective-permute-start | bytes 1572872 | tf_op jit(solution)/shard_map/ppermute | solution.py:33
  15.4 5.9 %collective-permute-start.1 = (f32[16,8192]{1,0:T(8,128)S(1)}, f32[16,8192]{1,0:T(8,128)S(1)}, u32[]{:S(2)}, u32[]{:S(2)}) collective-permute-start(f32[16,8192]{1,0:T(8,128)S(1)} %get-tuple-element.25), channel_id=1, source_target_pairs={{1,0},{2,1},{3,2},{4,3},{5,4},{6,5},{7,6},{8,7},{9,8},{10,9},{11,1... | collective-permute-start | bytes 1572872 | tf_op jit(solution)/shard_map/ppermute | solution.py:33
  21.5 32.9 %collective-permute-start.2 = (f32[16,8192]{1,0:T(8,128)S(1)}, f32[16,8192]{1,0:T(8,128)S(1)}, u32[]{:S(2)}, u32[]{:S(2)}) collective-permute-start(f32[16,8192]{1,0:T(8,128)S(1)} %get-tuple-element.19), channel_id=1, source_target_pairs={{0,1},{1,2},{2,3},{3,4},{4,5},{5,6},{6,7},{7,8},{8,9},{9,10},{10,1... | collective-permute-start | bytes 1572872 | tf_op jit(solution)/shard_map/ppermute | solution.py:24
  31.8 22.5 %collective-permute-start.3 = (f32[16,8192]{1,0:T(8,128)S(1)}, f32[16,8192]{1,0:T(8,128)}, u32[]{:S(2)}, u32[]{:S(2)}) collective-permute-start(f32[16,8192]{1,0:T(8,128)S(1)} %get-tuple-element.19), channel_id=1, source_target_pairs={{1,0},{2,1},{3,2},{4,3},{5,4},{6,5},{7,6},{8,7},{9,8},{10,9},{11,1... | collective-permute-start | bytes 1572872 | tf_op jit(solution)/shard_map/ppermute | solution.py:25
  33.8 20.5 %all-to-all-start = ((f32[16,2,16]{2,1,0:T(2,128)}), f32[16,2,16]{2,1,0:T(2,128)S(1)}, u32[]{:S(2)}, u32[]{:S(2)}) async-start(f32[16,2,16]{2,1,0:T(2,128)} %broadcast_in_dim.10), calls=%async_computation | async-start | bytes 32768 | tf_op jit(solution)/shard_map/all_to_all | solution.py:101
  57.4 7.1 %copy-start.3 = (s32[1,160]{1,0:T(1,128)S(1)}, s32[1,160]{1,0:T(1,128)}, u32[]{:S(2)}) copy-start(s32[1,160]{1,0:T(1,128)} %param.7) | copy-start | bytes 1924
  76.5 17.8 %collective-permute-start.4 = (f32[16,8192]{1,0:T(8,128)}, f32[16,8192]{1,0:T(8,128)S(1)}, u32[]{:S(2)}, u32[]{:S(2)}) collective-permute-start(f32[16,8192]{1,0:T(8,128)} %get-tuple-element.22), channel_id=1, source_target_pairs={{0,1},{1,2},{2,3},{3,4},{4,5},{5,6},{6,7},{7,8},{8,9},{9,10},{10,1... | collective-permute-start | bytes 1572872 | tf_op jit(solution)/shard_map/ppermute | solution.py:33
  78.8 15.5 %collective-permute-start.5 = (f32[16,8192]{1,0:T(8,128)S(1)}, f32[16,8192]{1,0:T(8,128)}, u32[]{:S(2)}, u32[]{:S(2)}) collective-permute-start(f32[16,8192]{1,0:T(8,128)S(1)} %get-tuple-element.23), channel_id=1, source_target_pairs={{1,0},{2,1},{3,2},{4,3},{5,4},{6,5},{7,6},{8,7},{9,8},{10,9},{11,1... | collective-permute-start | bytes 1572872 | tf_op jit(solution)/shard_map/ppermute | solution.py:33
  95.7 17.3 %collective-permute-start.6 = (f32[16,8192]{1,0:T(8,128)S(1)}, f32[16,8192]{1,0:T(8,128)S(1)}, u32[]{:S(2)}, u32[]{:S(2)}) collective-permute-start(f32[16,8192]{1,0:T(8,128)S(1)} %get-tuple-element.13), channel_id=1, source_target_pairs={{0,1},{1,2},{2,3},{3,4},{4,5},{5,6},{6,7},{7,8},{8,9},{9,10},{10,1... | collective-permute-start | bytes 1572872 | tf_op jit(solution)/shard_map/ppermute | solution.py:24
  97.4 15.6 %collective-permute-start.7 = (f32[16,8192]{1,0:T(8,128)S(1)}, f32[16,8192]{1,0:T(8,128)}, u32[]{:S(2)}, u32[]{:S(2)}) collective-permute-start(f32[16,8192]{1,0:T(8,128)S(1)} %get-tuple-element.13), channel_id=1, source_target_pairs={{1,0},{2,1},{3,2},{4,3},{5,4},{6,5},{7,6},{8,7},{9,8},{10,9},{11,1... | collective-permute-start | bytes 1572872 | tf_op jit(solution)/shard_map/ppermute | solution.py:25
  135.3 17.1 %collective-permute-start.8 = (f32[16,8192]{1,0:T(8,128)}, f32[16,8192]{1,0:T(8,128)S(1)}, u32[]{:S(2)}, u32[]{:S(2)}) collective-permute-start(f32[16,8192]{1,0:T(8,128)} %get-tuple-element.20), channel_id=1, source_target_pairs={{0,1},{1,2},{2,3},{3,4},{4,5},{5,6},{6,7},{7,8},{8,9},{9,10},{10,1... | collective-permute-start | bytes 1572872 | tf_op jit(solution)/shard_map/ppermute | solution.py:33
  137.1 16.2 %collective-permute-start.9 = (f32[16,8192]{1,0:T(8,128)}, f32[16,8192]{1,0:T(8,128)}, u32[]{:S(2)}, u32[]{:S(2)}) collective-permute-start(f32[16,8192]{1,0:T(8,128)} %get-tuple-element.21), channel_id=1, source_target_pairs={{1,0},{2,1},{3,2},{4,3},{5,4},{6,5},{7,6},{8,7},{9,8},{10,9},{11,1... | collective-permute-start | bytes 1572872 | tf_op jit(solution)/shard_map/ppermute | solution.py:33
  152.4 0.8 copy-start.1

commit v5 on v2

--- a/solution.py
+++ b/solution.py
@@ -114,12 +114,25 @@
     diag_bar = col_norm
     for iteration in range(ITERATIONS):
         right_prod = backward(left_raw)
-        row_norm = jnp.sqrt(all_sum(squares(left_raw), axes) + 1e-06)
+        sums = all_sum(
+            jnp.stack(
+                [
+                    squares(left_raw),
+                    squares(right_prod),
+                    jnp.sum(right_prod * right_vec, axis=1),
+                    squares(right_vec),
+                ]
+            ),
+            axes,
+        )
+        row_square = sums[0] + 1e-06
+        row_norm = jnp.sqrt(row_square)
         left_vec = left_raw / row_norm[:, None]
         right_raw = right_prod / row_norm[:, None] - row_norm[:, None] * right_vec
         if iteration + 1 < ITERATIONS:
             left_prod = forward(right_raw)
-        col_norm = jnp.sqrt(all_sum(squares(right_raw), axes) + 1e-06)
+        col_square = sums[1] / row_square - 2.0 * sums[2] + row_square * sums[3]
+        col_norm = jnp.sqrt(jnp.maximum(col_square, 0.0) + 1e-06)
         right_vec = right_raw / col_norm[:, None]
         if iteration + 1 < ITERATIONS:
             left_raw = left_prod / col_norm[:, None] - col_norm[:, None] * left_vec

time: 164 us -> 168 us (1.024)
  starting transfers between devices: 33.3 us -> 44 us
  blocking collectives: 50 us -> 39.9 us
  waiting for transfers between devices: 10.9 us -> 19.4 us
  other arithmetic: 7.25 us -> 4.36 us
    all_to_all x4 -> x2, blocking collectives: 50 us -> 39.9 us  [all_sum(): gathered = lax.all_to_all(spread, axes, 0, 0, tiled=True)]
    ppermute x6, starting transfers between devices: 10.4 us -> 19.3 us  [from_behind(): return lax.ppermute(shard, axis, pairs)]
    ppermute x6, waiting for transfers between devices: 4.46 us -> 11.7 us  [from_behind(): return lax.ppermute(shard, axis, pairs)]
    reduce_sum x6 -> x4, other arithmetic: 3.77 us -> 0.93 us  [squares(): return jnp.sum(field * field, axis=1)]
    ppermute x2, starting transfers between devices: 12.1 us -> 14.3 us  [with_halo(): before = lax.ppermute(last, axis, up)]
  transfers between devices with their start and end apart: 11 -> 11, of which waited for: 2 -> 7; matrix products, arithmetic and copies ran while one was open for 1% -> 0% of each run, Pallas kernels for 0% -> 0%
where the time goes in v5:
time: 168 us; the launch traced here: 167 us
  matrix products  47.9 us (29%)
  starting transfers between devices  44 us (26%)
  blocking collectives  39.9 us (24%)
  waiting for transfers between devices  19.4 us (12%)
  local copies, waits for them, and re-layouts  9.86 us (6%)
  other arithmetic  4.36 us (3%)
  between operations  1.7 us (1%)
    all_to_all x2, blocking collectives, all_sum(): gathered = lax.all_to_all(spread, axes, 0, 0, tiled=True)  39.9 us
    dot_general x2, matrix products, forward_local(): jnp.einsum('skj,kij->ksi', pieces, tile_stack, precision=PRODUCT_PRECISION)  21.9 us
    dot_general x3, matrix products, transpose_local(): jnp.einsum('ski,kij->ksj', pieces, tile_stack, precision=PRODUCT_PRECISION)  20.3 us
    ppermute x6, starting transfers between devices, from_behind(): return lax.ppermute(shard, axis, pairs)  19.3 us
    ppermute x2, starting transfers between devices, with_halo(): before = lax.ppermute(last, axis, up)  14.3 us
    ppermute x6, waiting for transfers between devices, from_behind(): return lax.ppermute(shard, axis, pairs)  11.7 us
    all_to_all x1, starting transfers between devices, all_sum(): gathered = lax.all_to_all(spread, axes, 0, 0, tiled=True)  7.86 us
    all_to_all x1, waiting for transfers between devices, all_sum(): gathered = lax.all_to_all(spread, axes, 0, 0, tiled=True)  6.48 us
  transfers between devices with their start and end apart: 11, of which 7 were waited for; matrix products, arithmetic and copies ran while one was open for 0% of the time, Pallas kernels for 0%

profile of v5, /device:TPU:0, one launch (start us, length us, event | category | flops | bytes accessed | tf_op | source)
XLA Modules:
  0.0 167.2 jit_solution(6938671207950595134)
XLA Ops:
  1.3 0.7 compare_select_fusion.1
  2.0 1.0 copy_bitcast_fusion.7
  3.0 0.8 gather_fusion
  3.8 6.8 %fusion.10 = f32[160,16,128]{2,1,0:T(8,128)S(1)} fusion(f32[1,160,128,128]{3,2,1,0:T(8,128)} %param.6, f32[160,16,128]{2,1,0:T(8,128)S(1)} %gather_fusion, f32[160]{0:T(256)S(1)} %compare_convert_fusion), kind=kOutput, calls=%fused_computation.22 | convolution fusion | flops 251985920 | bytes 13107840 | tf_op jit(solution)/shard_map/ski,kij->ksj/dot_general | solution.py:51
  10.6 1.3 fusion.38
  11.9 0.9 copy.87
  12.9 2.4 %collective-permute-start = (f32[16,8192]{1,0:T(8,128)S(1)}, f32[16,8192]{1,0:T(8,128)S(1)}, u32[]{:S(2)}, u32[]{:S(2)}) collective-permute-start(f32[16,8192]{1,0:T(8,128)S(1)} %get-tuple-element.29), channel_id=1, source_target_pairs={{0,1},{1,2},{2,3},{3,4},{4,5},{5,6},{6,7},{7,8},{8,9},{9,10},{10,1... | collective-permute-start | bytes 1572872 | tf_op jit(solution)/shard_map/ppermute | solution.py:31
  15.3 1.3 collective-permute-start.1
  16.8 4.4 %collective-permute-done.1 = f32[16,8192]{1,0:T(8,128)S(1)} collective-permute-done((f32[16,8192]{1,0:T(8,128)S(1)}, f32[16,8192]{1,0:T(8,128)S(1)}, u32[]{:S(2)}, u32[]{:S(2)}) %collective-permute-start.1) | collective-permute-done | bytes 524320 | tf_op jit(solution)/shard_map/ppermute | solution.py:31
  21.2 0.2 multiply_reduce_fusion.6
  21.4 1.3 collective-permute-start.3
  22.7 11.0 %collective-permute-start.2 = (f32[16,8192]{1,0:T(8,128)S(1)}, f32[16,8192]{1,0:T(8,128)S(1)}, u32[]{:S(2)}, u32[]{:S(2)}) collective-permute-start(f32[16,8192]{1,0:T(8,128)S(1)} %get-tuple-element.24), channel_id=1, source_target_pairs={{0,1},{1,2},{2,3},{3,4},{4,5},{5,6},{6,7},{7,8},{8,9},{9,10},{10,1... | collective-permute-start | bytes 1572872 | tf_op jit(solution)/shard_map/ppermute | solution.py:22
  33.7 0.6 broadcast_in_dim.6
  34.3 7.9 %all-to-all-start = ((f32[16,2,16]{2,1,0:T(2,128)}), f32[16,2,16]{2,1,0:T(2,128)S(1)}, u32[]{:S(2)}, u32[]{:S(2)}) async-start(f32[16,2,16]{2,1,0:T(2,128)} %broadcast_in_dim.6), calls=%async_computation | async-start | bytes 32768 | tf_op jit(solution)/shard_map/all_to_all | solution.py:80
  42.2 6.5 %all-to-all-done = f32[16,2,16]{2,1,0:T(2,128)S(1)} async-done(((f32[16,2,16]{2,1,0:T(2,128)}), f32[16,2,16]{2,1,0:T(2,128)S(1)}, u32[]{:S(2)}, u32[]{:S(2)}) %all-to-all-start) | async-done | bytes 2080 | tf_op jit(solution)/shard_map/all_to_all | solution.py:80
  48.9 0.8 gather_fusion.1
  49.7 10.8 %fusion.13 = f32[160,16,128]{2,1,0:T(8,128)S(1)} fusion(f32[1,160,128,128]{3,2,1,0:T(8,128)} %param.6, f32[160,16,128]{2,1,0:T(8,128)S(1)} %gather_fusion.1, f32[160]{0:T(256)S(1)} %compare_convert_fusion), kind=kOutput, calls=%fused_computation.23 | convolution fusion | flops 251985920 | bytes 13107840 | tf_op jit(solution)/shard_map/skj,kij->ksi/dot_general | solution.py:39
  60.6 0.9 fusion.36
  61.5 0.3 multiply_reduce_fusion.8
  61.8 0.8 gather_fusion.2
  62.7 6.8 %fusion.16 = f32[160,16,128]{2,1,0:T(8,128)S(1)} fusion(f32[1,160,128,128]{3,2,1,0:T(8,128)} %param.6, f32[160,16,128]{2,1,0:T(8,128)S(1)} %gather_fusion.2, f32[160]{0:T(256)S(1)} %compare_convert_fusion), kind=kOutput, calls=%fused_computation.24 | convolution fusion | flops 251985920 | bytes 13107840 | tf_op jit(solution)/shard_map/ski,kij->ksj/dot_general | solution.py:51
  69.5 1.3 fusion.34
  70.8 0.9 copy.86
  71.8 1.7 %collective-permute-start.4 = (f32[16,8192]{1,0:T(8,128)S(1)}, f32[16,8192]{1,0:T(8,128)S(1)}, u32[]{:S(2)}, u32[]{:S(2)}) collective-permute-start(f32[16,8192]{1,0:T(8,128)S(1)} %get-tuple-element.27), channel_id=1, source_target_pairs={{0,1},{1,2},{2,3},{3,4},{4,5},{5,6},{6,7},{7,8},{8,9},{9,10},{10,1... | collective-permute-start | bytes 1572872 | tf_op jit(solution)/shard_map/ppermute | solution.py:31
  73.5 1.3 collective-permute-start.5
  74.8 0.2 collective-permute-done.4
  75.0 2.6 %collective-permute-done.5 = f32[16,8192]{1,0:T(8,128)S(1)} collective-permute-done((f32[16,8192]{1,0:T(8,128)S(1)}, f32[16,8192]{1,0:T(8,128)S(1)}, u32[]{:S(2)}, u32[]{:S(2)}) %collective-permute-start.5) | collective-permute-done | bytes 524320 | tf_op jit(solution)/shard_map/ppermute | solution.py:31
  77.6 0.4 multiply_reduce_fusion.4
  78.0 21.2 %all_to_all.15 = f32[16,4,16]{2,1,0:T(4,128)S(1)} all-to-all(f32[16,4,16]{2,1,0:T(4,128)S(1)} %broadcast_in_dim.7), channel_id=1, replica_groups=mesh['group'=2,'row'=8,'col'=2] {'row','col'}, dimensions={0} | all-to-all | bytes 8192 | tf_op jit(solution)/shard_map/all_to_all | solution.py:80
  99.3 0.1 multiply_subtract_fusion.2
  99.4 1.3 collective-permute-start.7
  100.7 3.3 %collective-permute-start.6 = (f32[16,8192]{1,0:T(8,128)S(1)}, f32[16,8192]{1,0:T(8,128)S(1)}, u32[]{:S(2)}, u32[]{:S(2)}) collective-permute-start(f32[16,8192]{1,0:T(8,128)S(1)} %multiply_subtract_fusion.2), channel_id=1, source_target_pairs={{0,1},{1,2},{2,3},{3,4},{4,5},{5,6},{6,7},{7,8},{8,9},{9,10},{10,1... | collective-permute-start | bytes 1572872 | tf_op jit(solution)/shard_map/ppermute | solution.py:22
  104.0 1.3 collective-permute-done.6
  105.4 1.9 %gather_fusion.3 = f32[160,16,128]{2,1,0:T(8,128)} fusion(f32[16,192,128]{2,0,1:T(8,128)S(1)} %copy_bitcast_fusion.3, s32[1024]{0:T(1024)S(1)} %pad_clamp_fusion), kind=kCustom, calls=%fused_computation.3 | custom fusion | bytes 2622080 | tf_op jit(solution)/shard_map/gather | solution.py:37
  107.3 11.0 %fusion.19 = f32[160,16,128]{2,1,0:T(8,128)S(1)} fusion(f32[1,160,128,128]{3,2,1,0:T(8,128)} %param.6, f32[160,16,128]{2,1,0:T(8,128)} %gather_fusion.3, f32[160]{0:T(256)S(1)} %compare_convert_fusion), kind=kOutput, calls=%fused_computation.25 | convolution fusion | flops 251985920 | bytes 13107840 | tf_op jit(solution)/shard_map/skj,kij->ksi/dot_general | solution.py:39
  118.3 0.9 fusion.32
  119.2 0.3 multiply_reduce_fusion.7
  119.6 0.8 gather_fusion.4
  120.4 6.8 %fusion.22 = f32[160,16,128]{2,1,0:T(8,128)S(1)} fusion(f32[1,160,128,128]{3,2,1,0:T(8,128)} %param.6, f32[160,16,128]{2,1,0:T(8,128)S(1)} %gather_fusion.4, f32[160]{0:T(256)S(1)} %compare_convert_fusion), kind=kOutput, calls=%fused_computation.26 | convolution fusion | flops 251985920 | bytes 13107840 | tf_op jit(solution)/shard_map/ski,kij->ksj/dot_general | solution.py:51
  127.2 1.3 fusion.30
  128.5 0.9 copy.85
  129.5 11.4 %collective-permute-start.8 = (f32[16,8192]{1,0:T(8,128)S(1)}, f32[16,8192]{1,0:T(8,128)S(1)}, u32[]{:S(2)}, u32[]{:S(2)}) collective-permute-start(f32[16,8192]{1,0:T(8,128)S(1)} %get-tuple-element.25), channel_id=1, source_target_pairs={{0,1},{1,2},{2,3},{3,4},{4,5},{5,6},{6,7},{7,8},{8,9},{9,10},{10,1... | collective-permute-start | bytes 1572872 | tf_op jit(solution)/shard_map/ppermute | solution.py:31
  140.9 1.3 collective-permute-start.9
  142.2 0.2 collective-permute-done.8
  142.3 4.3 %collective-permute-done.9 = f32[16,8192]{1,0:T(8,128)S(1)} collective-permute-done((f32[16,8192]{1,0:T(8,128)S(1)}, f32[16,8192]{1,0:T(8,128)S(1)}, u32[]{:S(2)}, u32[]{:S(2)}) %collective-permute-start.9) | collective-permute-done | bytes 524320 | tf_op jit(solution)/shard_map/ppermute | solution.py:31
  146.6 0.4 multiply_reduce_fusion.1
  147.0 18.7 %all_to_all.16 = f32[16,4,16]{2,1,0:T(4,128)S(1)} all-to-all(f32[16,4,16]{2,1,0:T(4,128)S(1)} %broadcast_in_dim.8), channel_id=1, replica_groups=mesh['group'=2,'row'=8,'col'=2] {'row','col'}, dimensions={0} | all-to-all | bytes 8192 | tf_op jit(solution)/shard_map/all_to_all | solution.py:80
  165.9 1.3 multiply_subtract_fusion
  (40 shorter events, 1.0 us)
Async XLA Ops:
  3.8 6.8 %copy-start.2 = (s32[1,160]{1,0:T(1,128)S(1)}, s32[1,160]{1,0:T(1,128)}, u32[]{:S(2)}) copy-start(s32[1,160]{1,0:T(1,128)} %param.8) | copy-start | bytes 1924
  12.8 3.8 %copy-start = (f32[16,4096]{1,0:T(8,128)S(1)}, f32[16,4096]{1,0:T(8,128)}, u32[]{:S(2)}) copy-start(f32[16,4096]{1,0:T(8,128)} %param.5) | copy-start | bytes 786436
  12.9 3.9 %collective-permute-start = (f32[16,8192]{1,0:T(8,128)S(1)}, f32[16,8192]{1,0:T(8,128)S(1)}, u32[]{:S(2)}, u32[]{:S(2)}) collective-permute-start(f32[16,8192]{1,0:T(8,128)S(1)} %get-tuple-element.29), channel_id=1, source_target_pairs={{0,1},{1,2},{2,3},{3,4},{4,5},{5,6},{6,7},{7,8},{8,9},{9,10},{10,1... | collective-permute-start | bytes 1572872 | tf_op jit(solution)/shard_map/ppermute | solution.py:31
  15.3 5.9 %collective-permute-start.1 = (f32[16,8192]{1,0:T(8,128)S(1)}, f32[16,8192]{1,0:T(8,128)S(1)}, u32[]{:S(2)}, u32[]{:S(2)}) collective-permute-start(f32[16,8192]{1,0:T(8,128)S(1)} %get-tuple-element.30), channel_id=1, source_target_pairs={{1,0},{2,1},{3,2},{4,3},{5,4},{6,5},{7,6},{8,7},{9,8},{10,9},{11,1... | collective-permute-start | bytes 1572872 | tf_op jit(solution)/shard_map/ppermute | solution.py:31
  21.4 27.3 %collective-permute-start.3 = (f32[16,8192]{1,0:T(8,128)S(1)}, f32[16,8192]{1,0:T(8,128)S(1)}, u32[]{:S(2)}, u32[]{:S(2)}) collective-permute-start(f32[16,8192]{1,0:T(8,128)S(1)} %get-tuple-element.24), channel_id=1, source_target_pairs={{1,0},{2,1},{3,2},{4,3},{5,4},{6,5},{7,6},{8,7},{9,8},{10,9},{11,1... | collective-permute-start | bytes 1572872 | tf_op jit(solution)/shard_map/ppermute | solution.py:23
  22.7 26.0 %collective-permute-start.2 = (f32[16,8192]{1,0:T(8,128)S(1)}, f32[16,8192]{1,0:T(8,128)S(1)}, u32[]{:S(2)}, u32[]{:S(2)}) collective-permute-start(f32[16,8192]{1,0:T(8,128)S(1)} %get-tuple-element.24), channel_id=1, source_target_pairs={{0,1},{1,2},{2,3},{3,4},{4,5},{5,6},{6,7},{7,8},{8,9},{9,10},{10,1... | collective-permute-start | bytes 1572872 | tf_op jit(solution)/shard_map/ppermute | solution.py:22
  34.3 14.4 %all-to-all-start = ((f32[16,2,16]{2,1,0:T(2,128)}), f32[16,2,16]{2,1,0:T(2,128)S(1)}, u32[]{:S(2)}, u32[]{:S(2)}) async-start(f32[16,2,16]{2,1,0:T(2,128)} %broadcast_in_dim.6), calls=%async_computation | async-start | bytes 32768 | tf_op jit(solution)/shard_map/all_to_all | solution.py:80
  49.7 10.9 %copy-start.3 = (s32[1,160]{1,0:T(1,128)S(1)}, s32[1,160]{1,0:T(1,128)}, u32[]{:S(2)}) copy-start(s32[1,160]{1,0:T(1,128)} %param.7) | copy-start | bytes 1924
  60.6 1.0 copy-start.1
  71.8 3.2 %collective-permute-start.4 = (f32[16,8192]{1,0:T(8,128)S(1)}, f32[16,8192]{1,0:T(8,128)S(1)}, u32[]{:S(2)}, u32[]{:S(2)}) collective-permute-start(f32[16,8192]{1,0:T(8,128)S(1)} %get-tuple-element.27), channel_id=1, source_target_pairs={{0,1},{1,2},{2,3},{3,4},{4,5},{5,6},{6,7},{7,8},{8,9},{9,10},{10,1... | collective-permute-start | bytes 1572872 | tf_op jit(solution)/shard_map/ppermute | solution.py:31
  73.5 4.1 %collective-permute-start.5 = (f32[16,8192]{1,0:T(8,128)S(1)}, f32[16,8192]{1,0:T(8,128)S(1)}, u32[]{:S(2)}, u32[]{:S(2)}) collective-permute-start(f32[16,8192]{1,0:T(8,128)S(1)} %get-tuple-element.28), channel_id=1, source_target_pairs={{1,0},{2,1},{3,2},{4,3},{5,4},{6,5},{7,6},{8,7},{9,8},{10,9},{11,1... | collective-permute-start | bytes 1572872 | tf_op jit(solution)/shard_map/ppermute | solution.py:31
  99.4 4.6 %collective-permute-start.7 = (f32[16,8192]{1,0:T(8,128)S(1)}, f32[16,8192]{1,0:T(8,128)S(1)}, u32[]{:S(2)}, u32[]{:S(2)}) collective-permute-start(f32[16,8192]{1,0:T(8,128)S(1)} %multiply_subtract_fusion.2), channel_id=1, source_target_pairs={{1,0},{2,1},{3,2},{4,3},{5,4},{6,5},{7,6},{8,7},{9,8},{10,9},{11,1... | collective-permute-start | bytes 1572872 | tf_op jit(solution)/shard_map/ppermute | solution.py:23
  100.7 4.6 %collective-permute-start.6 = (f32[16,8192]{1,0:T(8,128)S(1)}, f32[16,8192]{1,0:T(8,128)S(1)}, u32[]{:S(2)}, u32[]{:S(2)}) collective-permute-start(f32[16,8192]{1,0:T(8,128)S(1)} %multiply_subtract_fusion.2), channel_id=1, source_target_pairs={{0,1},{1,2},{2,3},{3,4},{4,5},{5,6},{6,7},{7,8},{8,9},{9,10},{10,1... | collective-permute-start | bytes 1572872 | tf_op jit(solution)/shard_map/ppermute | solution.py:22
  129.5 12.9 %collective-permute-start.8 = (f32[16,8192]{1,0:T(8,128)S(1)}, f32[16,8192]{1,0:T(8,128)S(1)}, u32[]{:S(2)}, u32[]{:S(2)}) collective-permute-start(f32[16,8192]{1,0:T(8,128)S(1)} %get-tuple-element.25), channel_id=1, source_target_pairs={{0,1},{1,2},{2,3},{3,4},{4,5},{5,6},{6,7},{7,8},{8,9},{9,10},{10,1... | collective-permute-start | bytes 1572872 | tf_op jit(solution)/shard_map/ppermute | solution.py:31
  140.9 5.8 %collective-permute-start.9 = (f32[16,8192]{1,0:T(8,128)S(1)}, f32[16,8192]{1,0:T(8,128)S(1)}, u32[]{:S(2)}, u32[]{:S(2)}) collective-permute-start(f32[16,8192]{1,0:T(8,128)S(1)} %get-tuple-element.26), channel_id=1, source_target_pairs={{1,0},{2,1},{3,2},{4,3},{5,4},{6,5},{7,6},{8,7},{9,8},{10,9},{11,1... | collective-permute-start | bytes 1572872 | tf_op jit(solution)/shard_map/ppermute | solution.py:31

commit v6 on v2

--- a/solution.py
+++ b/solution.py
@@ -39,7 +39,7 @@
         jnp.einsum("skj,kij->ksi", pieces, tile_stack, precision=PRODUCT_PRECISION) * live_slot[:, None, None]
     )
     onehot = (rows_idx[:, None] == jnp.arange(ROW_BLOCKS)[None, :]).astype(jnp.float32)
-    summed = jnp.einsum("kr,ksi->sri", onehot, products, precision=PRECISE)
+    summed = jnp.einsum("kr,ksi->sri", onehot, products, precision=PRODUCT_PRECISION)
     return summed.reshape(scenario_rows, ROW_BLOCKS * tile_edge)
 
 
@@ -51,7 +51,7 @@
         jnp.einsum("ski,kij->ksj", pieces, tile_stack, precision=PRODUCT_PRECISION) * live_slot[:, None, None]
     )
     onehot = (cols_idx[:, None] == jnp.arange(3 * COL_BLOCKS)[None, :]).astype(jnp.float32)
-    summed = jnp.einsum("kc,ksj->scj", onehot, products, precision=PRECISE)
+    summed = jnp.einsum("kc,ksj->scj", onehot, products, precision=PRODUCT_PRECISION)
     return summed.reshape(scenario_rows, 3 * COL_BLOCKS * tile_edge)
 
 

time: 164 us -> 162 us (0.988)
  no operation moved by 1% of the time
where the time goes in v6:
time: 162 us
  blocking collectives  50 us (31%)
  matrix products  46.8 us (29%)
  starting transfers between devices  33.3 us (21%)
  local copies, waits for them, and re-layouts  11.7 us (7%)
  waiting for transfers between devices  10.9 us (7%)
  other arithmetic  7.25 us (4%)
  between operations  1.7 us (1%)
    all_to_all x4, blocking collectives, all_sum(): gathered = lax.all_to_all(spread, axes, 0, 0, tiled=True)  50 us
    dot_general x2, matrix products, forward_local(): jnp.einsum('skj,kij->ksi', pieces, tile_stack, precision=PRODUCT_PRECISION)  21.9 us
    dot_general x3, matrix products, transpose_local(): jnp.einsum('ski,kij->ksj', pieces, tile_stack, precision=PRODUCT_PRECISION)  20.5 us
    ppermute x2, starting transfers between devices, with_halo(): before = lax.ppermute(last, axis, up)  12.1 us
    ppermute x6, starting transfers between devices, from_behind(): return lax.ppermute(shard, axis, pairs)  10.4 us
    all_to_all x1, starting transfers between devices, all_sum(): gathered = lax.all_to_all(spread, axes, 0, 0, tiled=True)  8.21 us
    all_to_all x1, waiting for transfers between devices, all_sum(): gathered = lax.all_to_all(spread, axes, 0, 0, tiled=True)  6.48 us
    ppermute x6, waiting for transfers between devices, from_behind(): return lax.ppermute(shard, axis, pairs)  4.46 us
  transfers between devices with their start and end apart: 11, of which 2 were waited for; matrix products, arithmetic and copies ran while one was open for 1% of the time, Pallas kernels for 0%

profile of v6, /device:TPU:0, one launch (start us, length us, event | category | flops | bytes accessed | tf_op | source)
XLA Modules:
  0.0 161.6 jit_solution(14061273005688778336)
XLA Ops:
  1.3 0.7 compare_select_fusion.1
  2.0 1.0 copy_bitcast_fusion.7
  3.0 0.8 gather_fusion
  3.8 6.8 %fusion.10 = f32[160,16,128]{2,1,0:T(8,128)S(1)} fusion(f32[1,160,128,128]{3,2,1,0:T(8,128)} %param.6, f32[160,16,128]{2,1,0:T(8,128)S(1)} %gather_fusion, f32[160]{0:T(256)S(1)} %compare_convert_fusion), kind=kOutput, calls=%fused_computation.22 | convolution fusion | flops 251985920 | bytes 13107840 | tf_op jit(solution)/shard_map/ski,kij->ksj/dot_general | solution.py:51
  10.7 1.0 fusion.38
  11.7 0.9 copy.79
  12.7 2.4 %collective-permute-start = (f32[16,8192]{1,0:T(8,128)S(1)}, f32[16,8192]{1,0:T(8,128)S(1)}, u32[]{:S(2)}, u32[]{:S(2)}) collective-permute-start(f32[16,8192]{1,0:T(8,128)S(1)} %get-tuple-element.24), channel_id=1, source_target_pairs={{0,1},{1,2},{2,3},{3,4},{4,5},{5,6},{6,7},{7,8},{8,9},{9,10},{10,1... | collective-permute-start | bytes 1572872 | tf_op jit(solution)/shard_map/ppermute | solution.py:31
  15.1 1.3 collective-permute-start.1
  16.6 4.4 %collective-permute-done.1 = f32[16,8192]{1,0:T(8,128)S(1)} collective-permute-done((f32[16,8192]{1,0:T(8,128)S(1)}, f32[16,8192]{1,0:T(8,128)S(1)}, u32[]{:S(2)}, u32[]{:S(2)}) %collective-permute-start.1) | collective-permute-done | bytes 524320 | tf_op jit(solution)/shard_map/ppermute | solution.py:31
  21.0 0.2 multiply_reduce_fusion.2
  21.2 10.3 %collective-permute-start.2 = (f32[16,8192]{1,0:T(8,128)S(1)}, f32[16,8192]{1,0:T(8,128)S(1)}, u32[]{:S(2)}, u32[]{:S(2)}) collective-permute-start(f32[16,8192]{1,0:T(8,128)S(1)} %get-tuple-element.19), channel_id=1, source_target_pairs={{0,1},{1,2},{2,3},{3,4},{4,5},{5,6},{6,7},{7,8},{8,9},{9,10},{10,1... | collective-permute-start | bytes 1572872 | tf_op jit(solution)/shard_map/ppermute | solution.py:22
  31.6 1.3 collective-permute-start.3
  32.9 0.6 broadcast_in_dim.10
  33.5 8.2 %all-to-all-start = ((f32[16,2,16]{2,1,0:T(2,128)}), f32[16,2,16]{2,1,0:T(2,128)S(1)}, u32[]{:S(2)}, u32[]{:S(2)}) async-start(f32[16,2,16]{2,1,0:T(2,128)} %broadcast_in_dim.10), calls=%async_computation | async-start | bytes 32768 | tf_op jit(solution)/shard_map/all_to_all | solution.py:80
  41.7 6.5 %all-to-all-done = f32[16,2,16]{2,1,0:T(2,128)S(1)} async-done(((f32[16,2,16]{2,1,0:T(2,128)}), f32[16,2,16]{2,1,0:T(2,128)S(1)}, u32[]{:S(2)}, u32[]{:S(2)}) %all-to-all-start) | async-done | bytes 2080 | tf_op jit(solution)/shard_map/all_to_all | solution.py:80
  48.4 0.8 gather_fusion.1
  49.2 10.9 %fusion.13 = f32[160,16,128]{2,1,0:T(8,128)S(1)} fusion(f32[1,160,128,128]{3,2,1,0:T(8,128)} %param.6, f32[160,16,128]{2,1,0:T(8,128)S(1)} %gather_fusion.1, f32[160]{0:T(256)S(1)} %compare_convert_fusion), kind=kOutput, calls=%fused_computation.23 | convolution fusion | flops 251985920 | bytes 13107840 | tf_op jit(solution)/shard_map/skj,kij->ksi/dot_general | solution.py:39
  60.1 0.7 fusion.36
  60.8 0.3 copy-done.1
  61.1 0.3 multiply_reduce_fusion.4
  61.4 0.8 gather_fusion.2
  62.2 6.8 %fusion.16 = f32[160,16,128]{2,1,0:T(8,128)S(1)} fusion(f32[1,160,128,128]{3,2,1,0:T(8,128)} %param.6, f32[160,16,128]{2,1,0:T(8,128)S(1)} %gather_fusion.2, f32[160]{0:T(256)S(1)} %compare_convert_fusion), kind=kOutput, calls=%fused_computation.24 | convolution fusion | flops 251985920 | bytes 13107840 | tf_op jit(solution)/shard_map/ski,kij->ksj/dot_general | solution.py:51
  69.1 1.0 fusion.34
  70.1 0.9 copy.78
  71.0 0.9 fusion.68
  71.8 1.7 %collective-permute-start.4 = (f32[16,8192]{1,0:T(8,128)}, f32[16,8192]{1,0:T(8,128)S(1)}, u32[]{:S(2)}, u32[]{:S(2)}) collective-permute-start(f32[16,8192]{1,0:T(8,128)} %get-tuple-element.22), channel_id=1, source_target_pairs={{0,1},{1,2},{2,3},{3,4},{4,5},{5,6},{6,7},{7,8},{8,9},{9,10},{10,1... | collective-permute-start | bytes 1572872 | tf_op jit(solution)/shard_map/ppermute | solution.py:31
  73.5 1.3 collective-permute-start.5
  74.8 12.3 %all_to_all.29 = f32[16,1,16]{2,1,0:T(1,128)S(1)} all-to-all(f32[16,1,16]{2,1,0:T(1,128)S(1)} %broadcast_in_dim.11), channel_id=1, replica_groups=mesh['group'=2,'row'=8,'col'=2] {'row','col'}, dimensions={0} | all-to-all | bytes 2048 | tf_op jit(solution)/shard_map/all_to_all | solution.py:80
  87.2 1.3 multiply_reduce_fusion.1
  88.5 1.7 %collective-permute-start.6 = (f32[16,8192]{1,0:T(8,128)S(1)}, f32[16,8192]{1,0:T(8,128)S(1)}, u32[]{:S(2)}, u32[]{:S(2)}) collective-permute-start(f32[16,8192]{1,0:T(8,128)S(1)} %get-tuple-element.13), channel_id=1, source_target_pairs={{0,1},{1,2},{2,3},{3,4},{4,5},{5,6},{6,7},{7,8},{8,9},{9,10},{10,1... | collective-permute-start | bytes 1572872 | tf_op jit(solution)/shard_map/ppermute | solution.py:22
  90.3 1.3 collective-permute-start.7
  91.6 13.6 %all_to_all.30 = f32[16,1,16]{2,1,0:T(1,128)S(1)} all-to-all(f32[16,1,16]{2,1,0:T(1,128)S(1)} %broadcast_in_dim.12), channel_id=1, replica_groups=mesh['group'=2,'row'=8,'col'=2] {'row','col'}, dimensions={0} | all-to-all | bytes 2048 | tf_op jit(solution)/shard_map/all_to_all | solution.py:80
  105.3 1.2 copy_bitcast_fusion.3
  106.4 1.9 %gather_fusion.3 = f32[160,16,128]{2,1,0:T(8,128)} fusion(f32[16,192,128]{2,0,1:T(8,128)S(1)} %copy_bitcast_fusion.3, s32[1024]{0:T(1024)S(1)} %pad_clamp_fusion), kind=kCustom, calls=%fused_computation.3 | custom fusion | bytes 2622080 | tf_op jit(solution)/shard_map/gather | solution.py:37
  108.3 11.1 %fusion.19 = f32[160,16,128]{2,1,0:T(8,128)S(1)} fusion(f32[1,160,128,128]{3,2,1,0:T(8,128)} %param.6, f32[160,16,128]{2,1,0:T(8,128)} %gather_fusion.3, f32[160]{0:T(256)S(1)} %compare_convert_fusion), kind=kOutput, calls=%fused_computation.25 | convolution fusion | flops 251985920 | bytes 13107840 | tf_op jit(solution)/shard_map/skj,kij->ksi/dot_general | solution.py:39
  119.4 0.7 fusion.32
  120.1 0.3 multiply_reduce_fusion.3
  120.4 0.8 gather_fusion.4
  121.2 6.8 %fusion.22 = f32[160,16,128]{2,1,0:T(8,128)S(1)} fusion(f32[1,160,128,128]{3,2,1,0:T(8,128)} %param.6, f32[160,16,128]{2,1,0:T(8,128)S(1)} %gather_fusion.4, f32[160]{0:T(256)S(1)} %compare_convert_fusion), kind=kOutput, calls=%fused_computation.26 | convolution fusion | flops 251985920 | bytes 13107840 | tf_op jit(solution)/shard_map/ski,kij->ksj/dot_general | solution.py:51
  128.1 1.0 fusion.30
  129.1 0.9 copy.77
  130.0 0.9 fusion.67
  130.9 2.5 %collective-permute-start.8 = (f32[16,8192]{1,0:T(8,128)}, f32[16,8192]{1,0:T(8,128)}, u32[]{:S(2)}, u32[]{:S(2)}) collective-permute-start(f32[16,8192]{1,0:T(8,128)} %get-tuple-element.20), channel_id=1, source_target_pairs={{0,1},{1,2},{2,3},{3,4},{4,5},{5,6},{6,7},{7,8},{8,9},{9,10},{10,1... | collective-permute-start | bytes 1572872 | tf_op jit(solution)/shard_map/ppermute | solution.py:31
  133.4 1.3 collective-permute-start.9
  134.7 13.3 %all_to_all.31 = f32[16,1,16]{2,1,0:T(1,128)S(1)} all-to-all(f32[16,1,16]{2,1,0:T(1,128)S(1)} %broadcast_in_dim.13), channel_id=1, replica_groups=mesh['group'=2,'row'=8,'col'=2] {'row','col'}, dimensions={0} | all-to-all | bytes 2048 | tf_op jit(solution)/shard_map/all_to_all | solution.py:80
  148.0 1.5 multiply_reduce_fusion
  149.5 10.8 %all_to_all.32 = f32[16,1,16]{2,1,0:T(1,128)S(1)} all-to-all(f32[16,1,16]{2,1,0:T(1,128)S(1)} %broadcast_in_dim.14), channel_id=1, replica_groups=mesh['group'=2,'row'=8,'col'=2] {'row','col'}, dimensions={0} | all-to-all | bytes 2048 | tf_op jit(solution)/shard_map/all_to_all | solution.py:80
  160.4 1.2 multiply_subtract_fusion
  (44 shorter events, 0.8 us)
Async XLA Ops:
  3.8 6.9 %copy-start.2 = (s32[1,160]{1,0:T(1,128)S(1)}, s32[1,160]{1,0:T(1,128)}, u32[]{:S(2)}) copy-start(s32[1,160]{1,0:T(1,128)} %param.8) | copy-start | bytes 1924
  12.6 3.8 %copy-start = (f32[16,4096]{1,0:T(8,128)S(1)}, f32[16,4096]{1,0:T(8,128)}, u32[]{:S(2)}) copy-start(f32[16,4096]{1,0:T(8,128)} %param.5) | copy-start | bytes 786436
  12.7 3.9 %collective-permute-start = (f32[16,8192]{1,0:T(8,128)S(1)}, f32[16,8192]{1,0:T(8,128)S(1)}, u32[]{:S(2)}, u32[]{:S(2)}) collective-permute-start(f32[16,8192]{1,0:T(8,128)S(1)} %get-tuple-element.24), channel_id=1, source_target_pairs={{0,1},{1,2},{2,3},{3,4},{4,5},{5,6},{6,7},{7,8},{8,9},{9,10},{10,1... | collective-permute-start | bytes 1572872 | tf_op jit(solution)/shard_map/ppermute | solution.py:31
  15.1 5.9 %collective-permute-start.1 = (f32[16,8192]{1,0:T(8,128)S(1)}, f32[16,8192]{1,0:T(8,128)S(1)}, u32[]{:S(2)}, u32[]{:S(2)}) collective-permute-start(f32[16,8192]{1,0:T(8,128)S(1)} %get-tuple-element.25), channel_id=1, source_target_pairs={{1,0},{2,1},{3,2},{4,3},{5,4},{6,5},{7,6},{8,7},{9,8},{10,9},{11,1... | collective-permute-start | bytes 1572872 | tf_op jit(solution)/shard_map/ppermute | solution.py:31
  21.2 27.1 %collective-permute-start.2 = (f32[16,8192]{1,0:T(8,128)S(1)}, f32[16,8192]{1,0:T(8,128)S(1)}, u32[]{:S(2)}, u32[]{:S(2)}) collective-permute-start(f32[16,8192]{1,0:T(8,128)S(1)} %get-tuple-element.19), channel_id=1, source_target_pairs={{0,1},{1,2},{2,3},{3,4},{4,5},{5,6},{6,7},{7,8},{8,9},{9,10},{10,1... | collective-permute-start | bytes 1572872 | tf_op jit(solution)/shard_map/ppermute | solution.py:22
  31.6 16.7 %collective-permute-start.3 = (f32[16,8192]{1,0:T(8,128)S(1)}, f32[16,8192]{1,0:T(8,128)S(1)}, u32[]{:S(2)}, u32[]{:S(2)}) collective-permute-start(f32[16,8192]{1,0:T(8,128)S(1)} %get-tuple-element.19), channel_id=1, source_target_pairs={{1,0},{2,1},{3,2},{4,3},{5,4},{6,5},{7,6},{8,7},{9,8},{10,9},{11,1... | collective-permute-start | bytes 1572872 | tf_op jit(solution)/shard_map/ppermute | solution.py:23
  33.5 14.7 %all-to-all-start = ((f32[16,2,16]{2,1,0:T(2,128)}), f32[16,2,16]{2,1,0:T(2,128)S(1)}, u32[]{:S(2)}, u32[]{:S(2)}) async-start(f32[16,2,16]{2,1,0:T(2,128)} %broadcast_in_dim.10), calls=%async_computation | async-start | bytes 32768 | tf_op jit(solution)/shard_map/all_to_all | solution.py:80
  49.2 10.9 %copy-start.3 = (s32[1,160]{1,0:T(1,128)S(1)}, s32[1,160]{1,0:T(1,128)}, u32[]{:S(2)}) copy-start(s32[1,160]{1,0:T(1,128)} %param.7) | copy-start | bytes 1924
  60.1 1.0 copy-start.1
  71.8 15.3 %collective-permute-start.4 = (f32[16,8192]{1,0:T(8,128)}, f32[16,8192]{1,0:T(8,128)S(1)}, u32[]{:S(2)}, u32[]{:S(2)}) collective-permute-start(f32[16,8192]{1,0:T(8,128)} %get-tuple-element.22), channel_id=1, source_target_pairs={{0,1},{1,2},{2,3},{3,4},{4,5},{5,6},{6,7},{7,8},{8,9},{9,10},{10,1... | collective-permute-start | bytes 1572872 | tf_op jit(solution)/shard_map/ppermute | solution.py:31
  73.5 13.6 %collective-permute-start.5 = (f32[16,8192]{1,0:T(8,128)S(1)}, f32[16,8192]{1,0:T(8,128)}, u32[]{:S(2)}, u32[]{:S(2)}) collective-permute-start(f32[16,8192]{1,0:T(8,128)S(1)} %get-tuple-element.23), channel_id=1, source_target_pairs={{1,0},{2,1},{3,2},{4,3},{5,4},{6,5},{7,6},{8,7},{9,8},{10,9},{11,1... | collective-permute-start | bytes 1572872 | tf_op jit(solution)/shard_map/ppermute | solution.py:31
  88.5 16.7 %collective-permute-start.6 = (f32[16,8192]{1,0:T(8,128)S(1)}, f32[16,8192]{1,0:T(8,128)S(1)}, u32[]{:S(2)}, u32[]{:S(2)}) collective-permute-start(f32[16,8192]{1,0:T(8,128)S(1)} %get-tuple-element.13), channel_id=1, source_target_pairs={{0,1},{1,2},{2,3},{3,4},{4,5},{5,6},{6,7},{7,8},{8,9},{9,10},{10,1... | collective-permute-start | bytes 1572872 | tf_op jit(solution)/shard_map/ppermute | solution.py:22
  90.3 15.0 %collective-permute-start.7 = (f32[16,8192]{1,0:T(8,128)S(1)}, f32[16,8192]{1,0:T(8,128)}, u32[]{:S(2)}, u32[]{:S(2)}) collective-permute-start(f32[16,8192]{1,0:T(8,128)S(1)} %get-tuple-element.13), channel_id=1, source_target_pairs={{1,0},{2,1},{3,2},{4,3},{5,4},{6,5},{7,6},{8,7},{9,8},{10,9},{11,1... | collective-permute-start | bytes 1572872 | tf_op jit(solution)/shard_map/ppermute | solution.py:23
  130.9 17.1 %collective-permute-start.8 = (f32[16,8192]{1,0:T(8,128)}, f32[16,8192]{1,0:T(8,128)}, u32[]{:S(2)}, u32[]{:S(2)}) collective-permute-start(f32[16,8192]{1,0:T(8,128)} %get-tuple-element.20), channel_id=1, source_target_pairs={{0,1},{1,2},{2,3},{3,4},{4,5},{5,6},{6,7},{7,8},{8,9},{9,10},{10,1... | collective-permute-start | bytes 1572872 | tf_op jit(solution)/shard_map/ppermute | solution.py:31
  133.4 14.6 %collective-permute-start.9 = (f32[16,8192]{1,0:T(8,128)S(1)}, f32[16,8192]{1,0:T(8,128)}, u32[]{:S(2)}, u32[]{:S(2)}) collective-permute-start(f32[16,8192]{1,0:T(8,128)S(1)} %get-tuple-element.21), channel_id=1, source_target_pairs={{1,0},{2,1},{3,2},{4,3},{5,4},{6,5},{7,6},{8,7},{9,8},{10,9},{11,1... | collective-permute-start | bytes 1572872 | tf_op jit(solution)/shard_map/ppermute | solution.py:31

commit v7 on v4

--- a/solution.py
+++ b/solution.py
@@ -33,11 +33,11 @@
     return lax.ppermute(shard, axis, pairs)
 
 
-def transpose_blocks(tile_stack):
+def transpose_blocks(tile_stack, anchor):
     slots, edge, _ = tile_stack.shape
-    step = 16 if slots % 16 == 0 else 1
+    step = 32 if slots % 32 == 0 else 1
 
-    def body(x_ref, o_ref):
+    def body(anchor_ref, x_ref, o_ref):
         for i in range(step):
             o_ref[i] = x_ref[i].T
 
@@ -45,11 +45,14 @@
     return pl.pallas_call(
         body,
         grid=(slots // step,),
-        in_specs=[pl.BlockSpec((step, edge, edge), lambda k: (k, 0, 0))],
+        in_specs=[
+            pl.BlockSpec(memory_space=pltpu.SMEM),
+            pl.BlockSpec((step, edge, edge), lambda k: (k, 0, 0)),
+        ],
         out_specs=pl.BlockSpec((step, edge, edge), lambda k: (k, 0, 0)),
         out_shape=jax.ShapeDtypeStruct(tile_stack.shape, tile_stack.dtype),
         cost_estimate=pl.CostEstimate(flops=0, transcendentals=0, bytes_accessed=nbytes),
-    )(tile_stack)
+    )(anchor, tile_stack)
 
 
 def forward_local(window, tile_stack, rows_idx, cols_idx, live_slot):
@@ -60,7 +63,7 @@
         jnp.einsum("skj,kji->ksi", pieces, tile_stack, precision=PRODUCT_PRECISION) * live_slot[:, None, None]
     )
     onehot = (rows_idx[:, None] == jnp.arange(ROW_BLOCKS)[None, :]).astype(jnp.float32)
-    summed = jnp.einsum("kr,ksi->sri", onehot, products, precision=PRECISE)
+    summed = jnp.einsum("kr,ksi->sri", onehot, products, precision=PRODUCT_PRECISION)
     return summed.reshape(scenario_rows, ROW_BLOCKS * tile_edge)
 
 
@@ -72,7 +75,7 @@
         jnp.einsum("ski,kij->ksj", pieces, tile_stack, precision=PRODUCT_PRECISION) * live_slot[:, None, None]
     )
     onehot = (cols_idx[:, None] == jnp.arange(3 * COL_BLOCKS)[None, :]).astype(jnp.float32)
-    summed = jnp.einsum("kc,ksj->scj", onehot, products, precision=PRECISE)
+    summed = jnp.einsum("kc,ksj->scj", onehot, products, precision=PRODUCT_PRECISION)
     return summed.reshape(scenario_rows, 3 * COL_BLOCKS * tile_edge)
 
 
@@ -81,7 +84,7 @@
     return forward_local(window, tile_stack, rows_idx, cols_idx, live_slot)
 
 
-def transpose_apply(field, tile_stack, rows_idx, cols_idx, live_slot):
+def transpose_apply(field, tile_stack, rows_idx, cols_idx, live_slot, beside=None):
     partial_sums = transpose_local(field, tile_stack, rows_idx, cols_idx, live_slot)
     band_width = partial_sums.shape[1] // 3
     lower = partial_sums[:, :band_width]
@@ -89,8 +92,12 @@
     upper = partial_sums[:, 2 * band_width :]
     from_below = from_behind(upper, ("row", "col"), 1)
     from_above = from_behind(lower, ("row", "col"), -1)
+    extra = None
+    if beside is not None:
+        extra = beside(middle[:1, :1])
+        middle, extra = lax.optimization_barrier((middle, extra))
     result = middle + from_below + from_above
-    return result
+    return result, extra
 
 
 def all_sum(values, axes):
@@ -115,14 +122,16 @@
     axes = ("row", "col")
 
     def backward(field):
-        return transpose_apply(field, tile_stack, rows_idx, cols_idx, live_slot)
+        return transpose_apply(field, tile_stack, rows_idx, cols_idx, live_slot)[0]
 
-    tile_stack_t = transpose_blocks(tile_stack)
+    start_raw, tile_stack_t = transpose_apply(
+        observed, tile_stack, rows_idx, cols_idx, live_slot,
+        beside=lambda anchor: transpose_blocks(tile_stack, anchor),
+    )
 
     def forward(vector):
         return forward_apply(vector, tile_stack_t, rows_idx, cols_idx, live_slot)
 
-    start_raw = backward(observed)
     totals = all_sum(jnp.stack([squares(observed), squares(start_raw)]), axes)
     row_norm = jnp.sqrt(totals[0] + 1e-06)
     col_norm = jnp.sqrt(totals[1] / (row_norm * row_norm) + 1e-06)

time: 168 us -> 160 us (0.952)
  starting transfers between devices: 33.2 us -> 29.1 us
  waiting for transfers between devices: 4.47 us -> 6.5 us
  blocking collectives: 53.2 us -> 51.5 us
    all_to_all x1, waiting for transfers between devices: 0.01 us -> 6.48 us  [all_sum(): gathered = lax.all_to_all(spread, axes, 0, 0, tiled=True)]
    ppermute x2, starting transfers between devices: 12.1 us -> 6.88 us  [with_halo(): before = lax.ppermute(last, axis, up)]
    ppermute x6, waiting for transfers between devices: 4.46 us -> 0.02 us  [from_behind(): return lax.ppermute(shard, axis, pairs)]
where the time goes in v7:
time: 160 us; the launch traced here: 159 us
  blocking collectives  51.5 us (32%)
  matrix products  38.7 us (24%)
  starting transfers between devices  29.1 us (18%)
  local copies, waits for them, and re-layouts  12.2 us (8%)
  Pallas kernels  11.7 us (7%)
  other arithmetic  7.25 us (5%)
  waiting for transfers between devices  6.5 us (4%)
  between operations  1.72 us (1%)
    all_to_all x4, blocking collectives, all_sum(): gathered = lax.all_to_all(spread, axes, 0, 0, tiled=True)  51.5 us
    dot_general x3, matrix products, transpose_local(): jnp.einsum('ski,kij->ksj', pieces, tile_stack, precision=PRODUCT_PRECISION)  20.5 us
    dot_general x2, matrix products, forward_local(): jnp.einsum('skj,kji->ksi', pieces, tile_stack, precision=PRODUCT_PRECISION)  13.9 us
    pallas_call x1, Pallas kernels, transpose_blocks(): pl.pallas_call(body, grid=(slots // step,), in_specs=[pl.BlockSpec(memory...  11.7 us
    ppermute x6, starting transfers between devices, from_behind(): return lax.ppermute(shard, axis, pairs)  10.4 us
    all_to_all x1, starting transfers between devices, all_sum(): gathered = lax.all_to_all(spread, axes, 0, 0, tiled=True)  9.21 us
    ppermute x2, starting transfers between devices, with_halo(): before = lax.ppermute(last, axis, up)  6.88 us
    all_to_all x1, waiting for transfers between devices, all_sum(): gathered = lax.all_to_all(spread, axes, 0, 0, tiled=True)  6.48 us
  transfers between devices with their start and end apart: 11, of which 1 were waited for; matrix products, arithmetic and copies ran while one was open for 1% of the time, Pallas kernels for 7%

profile of v7, /device:TPU:0, one launch (start us, length us, event | category | flops | bytes accessed | tf_op | source)
XLA Modules:
  0.0 158.8 jit_solution(13696991694949717062)
XLA Ops:
  1.3 0.7 compare_select_fusion.1
  2.0 1.0 copy_bitcast_fusion.7
  3.0 0.8 gather_fusion
  3.8 6.8 %convolution_multiply_fusion.4 = f32[160,16,128]{2,1,0:T(8,128)S(1)} fusion(f32[160,16,128]{2,1,0:T(8,128)S(1)} %gather_fusion, f32[160]{0:T(256)S(1)} %compare_convert_fusion, f32[1,160,128,128]{3,2,1,0:T(8,128)} %param.6), kind=kOutput, calls=%fused_computation.16 | convolution fusion | flops 251985920 | bytes 13107840 | tf_op jit(solution)/shard_map/ski,kij->ksj/dot_general | solution.py:75
  10.7 1.0 fusion.13
  11.7 0.9 copy.81
  12.7 2.4 %collective-permute-start = (f32[16,8192]{1,0:T(8,128)S(1)}, f32[16,8192]{1,0:T(8,128)S(1)}, u32[]{:S(2)}, u32[]{:S(2)}) collective-permute-start(f32[16,8192]{1,0:T(8,128)S(1)} %get-tuple-element.28), channel_id=1, source_target_pairs={{0,1},{1,2},{2,3},{3,4},{4,5},{5,6},{6,7},{7,8},{8,9},{9,10},{10,1... | collective-permute-start | bytes 1572872 | tf_op jit(solution)/shard_map/ppermute | solution.py:33
  15.1 1.3 collective-permute-start.1
  16.4 0.5 slice.60.anchor_ref
  16.9 11.7 %shard_map.68 = f32[160,128,128]{2,1,0:T(8,128)} custom-call(f32[1,1]{1,0:T(1,128)} %slice.60.anchor_ref, f32[160,128,128]{2,1,0:T(8,128)} %bitcast.119), custom_call_target="tpu_custom_call" | custom-call | bytes 20971520 | tf_op jit(solution)/shard_map/pallas_call | solution.py:45
  29.0 5.2 %collective-permute-start.2 = (f32[16,8192]{1,0:T(8,128)S(1)}, f32[16,8192]{1,0:T(8,128)S(1)}, u32[]{:S(2)}, u32[]{:S(2)}) collective-permute-start(f32[16,8192]{1,0:T(8,128)S(1)} %get-tuple-element.23), channel_id=1, source_target_pairs={{0,1},{1,2},{2,3},{3,4},{4,5},{5,6},{6,7},{7,8},{8,9},{9,10},{10,1... | collective-permute-start | bytes 1572872 | tf_op jit(solution)/shard_map/ppermute | solution.py:24
  34.2 1.3 collective-permute-start.3
  35.5 0.6 broadcast_in_dim.10
  36.1 9.2 %all-to-all-start = ((f32[16,2,16]{2,1,0:T(2,128)}), f32[16,2,16]{2,1,0:T(2,128)S(1)}, u32[]{:S(2)}, u32[]{:S(2)}) async-start(f32[16,2,16]{2,1,0:T(2,128)} %broadcast_in_dim.10), calls=%async_computation | async-start | bytes 32768 | tf_op jit(solution)/shard_map/all_to_all | solution.py:108
  45.4 6.5 %all-to-all-done = f32[16,2,16]{2,1,0:T(2,128)S(1)} async-done(((f32[16,2,16]{2,1,0:T(2,128)}), f32[16,2,16]{2,1,0:T(2,128)S(1)}, u32[]{:S(2)}, u32[]{:S(2)}) %all-to-all-start) | async-done | bytes 2080 | tf_op jit(solution)/shard_map/all_to_all | solution.py:108
  52.0 0.8 gather_fusion.1
  52.9 6.8 %convolution_multiply_fusion.3 = f32[160,16,128]{2,1,0:T(8,128)S(1)} fusion(f32[160,128,128]{2,1,0:T(8,128)} %shard_map.68, f32[160,16,128]{2,1,0:T(8,128)S(1)} %gather_fusion.1, f32[160]{0:T(256)S(1)} %compare_convert_fusion), kind=kOutput, calls=%fused_computation.15 | convolution fusion | flops 251985920 | bytes 13107840 | tf_op jit(solution)/shard_map/skj,kji->ksi/dot_general | solution.py:63
  59.8 0.7 fusion.11
  60.4 0.3 copy-done.1
  60.7 0.3 multiply_reduce_fusion.4
  61.0 0.8 gather_fusion.2
  61.8 6.8 %convolution_multiply_fusion.2 = f32[160,16,128]{2,1,0:T(8,128)S(1)} fusion(f32[160,16,128]{2,1,0:T(8,128)S(1)} %gather_fusion.2, f32[160]{0:T(256)S(1)} %compare_convert_fusion, f32[1,160,128,128]{3,2,1,0:T(8,128)} %param.6), kind=kOutput, calls=%fused_computation.14 | convolution fusion | flops 251985920 | bytes 13107840 | tf_op jit(solution)/shard_map/ski,kij->ksj/dot_general | solution.py:75
  68.7 1.0 fusion.9
  69.7 0.9 copy.80
  70.6 0.9 fusion.44
  71.5 1.7 %collective-permute-start.4 = (f32[16,8192]{1,0:T(8,128)}, f32[16,8192]{1,0:T(8,128)S(1)}, u32[]{:S(2)}, u32[]{:S(2)}) collective-permute-start(f32[16,8192]{1,0:T(8,128)} %get-tuple-element.26), channel_id=1, source_target_pairs={{0,1},{1,2},{2,3},{3,4},{4,5},{5,6},{6,7},{7,8},{8,9},{9,10},{10,1... | collective-permute-start | bytes 1572872 | tf_op jit(solution)/shard_map/ppermute | solution.py:33
  73.2 1.3 collective-permute-start.5
  74.5 13.3 %all_to_all.29 = f32[16,1,16]{2,1,0:T(1,128)S(1)} all-to-all(f32[16,1,16]{2,1,0:T(1,128)S(1)} %broadcast_in_dim.11), channel_id=1, replica_groups=mesh['group'=2,'row'=8,'col'=2] {'row','col'}, dimensions={0} | all-to-all | bytes 2048 | tf_op jit(solution)/shard_map/all_to_all | solution.py:108
  87.8 1.3 multiply_reduce_fusion.1
  89.1 1.7 %collective-permute-start.6 = (f32[16,8192]{1,0:T(8,128)S(1)}, f32[16,8192]{1,0:T(8,128)S(1)}, u32[]{:S(2)}, u32[]{:S(2)}) collective-permute-start(f32[16,8192]{1,0:T(8,128)S(1)} %get-tuple-element.17), channel_id=1, source_target_pairs={{0,1},{1,2},{2,3},{3,4},{4,5},{5,6},{6,7},{7,8},{8,9},{9,10},{10,1... | collective-permute-start | bytes 1572872 | tf_op jit(solution)/shard_map/ppermute | solution.py:24
  90.9 1.3 collective-permute-start.7
  92.2 14.2 %all_to_all.30 = f32[16,1,16]{2,1,0:T(1,128)S(1)} all-to-all(f32[16,1,16]{2,1,0:T(1,128)S(1)} %broadcast_in_dim.12), channel_id=1, replica_groups=mesh['group'=2,'row'=8,'col'=2] {'row','col'}, dimensions={0} | all-to-all | bytes 2048 | tf_op jit(solution)/shard_map/all_to_all | solution.py:108
  106.5 1.2 copy_bitcast_fusion.3
  107.6 1.9 %gather_fusion.3 = f32[160,16,128]{2,1,0:T(8,128)} fusion(f32[16,192,128]{2,0,1:T(8,128)S(1)} %copy_bitcast_fusion.3, s32[1024]{0:T(1024)S(1)} %pad_clamp_fusion), kind=kCustom, calls=%fused_computation.3 | custom fusion | bytes 2622080 | tf_op jit(solution)/shard_map/gather | solution.py:61
  109.5 7.1 %convolution_multiply_fusion.1 = f32[160,16,128]{2,1,0:T(8,128)S(1)} fusion(f32[160,128,128]{2,1,0:T(8,128)} %shard_map.68, f32[160,16,128]{2,1,0:T(8,128)} %gather_fusion.3, f32[160]{0:T(256)S(1)} %compare_convert_fusion), kind=kOutput, calls=%fused_computation.13 | convolution fusion | flops 251985920 | bytes 13107840 | tf_op jit(solution)/shard_map/skj,kji->ksi/dot_general | solution.py:63
  116.6 0.7 fusion.7
  117.3 0.3 multiply_reduce_fusion.3
  117.6 0.8 gather_fusion.4
  118.4 6.8 %convolution_multiply_fusion = f32[160,16,128]{2,1,0:T(8,128)S(1)} fusion(f32[160,16,128]{2,1,0:T(8,128)S(1)} %gather_fusion.4, f32[160]{0:T(256)S(1)} %compare_convert_fusion, f32[1,160,128,128]{3,2,1,0:T(8,128)} %param.6), kind=kOutput, calls=%fused_computation.12 | convolution fusion | flops 251985920 | bytes 13107840 | tf_op jit(solution)/shard_map/ski,kij->ksj/dot_general | solution.py:75
  125.3 1.0 fusion.5
  126.3 0.9 copy.79
  127.2 0.9 fusion.43
  128.0 2.5 %collective-permute-start.8 = (f32[16,8192]{1,0:T(8,128)}, f32[16,8192]{1,0:T(8,128)}, u32[]{:S(2)}, u32[]{:S(2)}) collective-permute-start(f32[16,8192]{1,0:T(8,128)} %get-tuple-element.24), channel_id=1, source_target_pairs={{0,1},{1,2},{2,3},{3,4},{4,5},{5,6},{6,7},{7,8},{8,9},{9,10},{10,1... | collective-permute-start | bytes 1572872 | tf_op jit(solution)/shard_map/ppermute | solution.py:33
  130.5 1.3 collective-permute-start.9
  131.9 13.3 %all_to_all.31 = f32[16,1,16]{2,1,0:T(1,128)S(1)} all-to-all(f32[16,1,16]{2,1,0:T(1,128)S(1)} %broadcast_in_dim.13), channel_id=1, replica_groups=mesh['group'=2,'row'=8,'col'=2] {'row','col'}, dimensions={0} | all-to-all | bytes 2048 | tf_op jit(solution)/shard_map/all_to_all | solution.py:108
  145.2 1.5 multiply_reduce_fusion
  146.7 10.8 %all_to_all.32 = f32[16,1,16]{2,1,0:T(1,128)S(1)} all-to-all(f32[16,1,16]{2,1,0:T(1,128)S(1)} %broadcast_in_dim.14), channel_id=1, replica_groups=mesh['group'=2,'row'=8,'col'=2] {'row','col'}, dimensions={0} | all-to-all | bytes 2048 | tf_op jit(solution)/shard_map/all_to_all | solution.py:108
  157.6 1.2 multiply_subtract_fusion
  (46 shorter events, 1.0 us)
Async XLA Ops:
  3.8 6.9 %copy-start.2 = (s32[1,160]{1,0:T(1,128)S(1)}, s32[1,160]{1,0:T(1,128)}, u32[]{:S(2)}) copy-start(s32[1,160]{1,0:T(1,128)} %param.8) | copy-start | bytes 1924
  12.7 16.1 %collective-permute-start = (f32[16,8192]{1,0:T(8,128)S(1)}, f32[16,8192]{1,0:T(8,128)S(1)}, u32[]{:S(2)}, u32[]{:S(2)}) collective-permute-start(f32[16,8192]{1,0:T(8,128)S(1)} %get-tuple-element.28), channel_id=1, source_target_pairs={{0,1},{1,2},{2,3},{3,4},{4,5},{5,6},{6,7},{7,8},{8,9},{9,10},{10,1... | collective-permute-start | bytes 1572872 | tf_op jit(solution)/shard_map/ppermute | solution.py:33
  15.1 13.7 %collective-permute-start.1 = (f32[16,8192]{1,0:T(8,128)S(1)}, f32[16,8192]{1,0:T(8,128)S(1)}, u32[]{:S(2)}, u32[]{:S(2)}) collective-permute-start(f32[16,8192]{1,0:T(8,128)S(1)} %get-tuple-element.29), channel_id=1, source_target_pairs={{1,0},{2,1},{3,2},{4,3},{5,4},{6,5},{7,6},{8,7},{9,8},{10,9},{11,1... | collective-permute-start | bytes 1572872 | tf_op jit(solution)/shard_map/ppermute | solution.py:33
  16.9 11.7 %copy-start = (f32[16,4096]{1,0:T(8,128)S(1)}, f32[16,4096]{1,0:T(8,128)}, u32[]{:S(2)}) copy-start(f32[16,4096]{1,0:T(8,128)} %param.5) | copy-start | bytes 786436
  29.0 22.9 %collective-permute-start.2 = (f32[16,8192]{1,0:T(8,128)S(1)}, f32[16,8192]{1,0:T(8,128)S(1)}, u32[]{:S(2)}, u32[]{:S(2)}) collective-permute-start(f32[16,8192]{1,0:T(8,128)S(1)} %get-tuple-element.23), channel_id=1, source_target_pairs={{0,1},{1,2},{2,3},{3,4},{4,5},{5,6},{6,7},{7,8},{8,9},{9,10},{10,1... | collective-permute-start | bytes 1572872 | tf_op jit(solution)/shard_map/ppermute | solution.py:24
  34.2 17.7 %collective-permute-start.3 = (f32[16,8192]{1,0:T(8,128)S(1)}, f32[16,8192]{1,0:T(8,128)S(1)}, u32[]{:S(2)}, u32[]{:S(2)}) collective-permute-start(f32[16,8192]{1,0:T(8,128)S(1)} %get-tuple-element.23), channel_id=1, source_target_pairs={{1,0},{2,1},{3,2},{4,3},{5,4},{6,5},{7,6},{8,7},{9,8},{10,9},{11,1... | collective-permute-start | bytes 1572872 | tf_op jit(solution)/shard_map/ppermute | solution.py:25
  36.1 15.7 %all-to-all-start = ((f32[16,2,16]{2,1,0:T(2,128)}), f32[16,2,16]{2,1,0:T(2,128)S(1)}, u32[]{:S(2)}, u32[]{:S(2)}) async-start(f32[16,2,16]{2,1,0:T(2,128)} %broadcast_in_dim.10), calls=%async_computation | async-start | bytes 32768 | tf_op jit(solution)/shard_map/all_to_all | solution.py:108
  52.9 6.9 %copy-start.3 = (s32[1,160]{1,0:T(1,128)S(1)}, s32[1,160]{1,0:T(1,128)}, u32[]{:S(2)}) copy-start(s32[1,160]{1,0:T(1,128)} %param.7) | copy-start | bytes 1924
  59.7 1.0 copy-start.1
  71.5 16.3 %collective-permute-start.4 = (f32[16,8192]{1,0:T(8,128)}, f32[16,8192]{1,0:T(8,128)S(1)}, u32[]{:S(2)}, u32[]{:S(2)}) collective-permute-start(f32[16,8192]{1,0:T(8,128)} %get-tuple-element.26), channel_id=1, source_target_pairs={{0,1},{1,2},{2,3},{3,4},{4,5},{5,6},{6,7},{7,8},{8,9},{9,10},{10,1... | collective-permute-start | bytes 1572872 | tf_op jit(solution)/shard_map/ppermute | solution.py:33
  73.2 14.6 %collective-permute-start.5 = (f32[16,8192]{1,0:T(8,128)S(1)}, f32[16,8192]{1,0:T(8,128)}, u32[]{:S(2)}, u32[]{:S(2)}) collective-permute-start(f32[16,8192]{1,0:T(8,128)S(1)} %get-tuple-element.27), channel_id=1, source_target_pairs={{1,0},{2,1},{3,2},{4,3},{5,4},{6,5},{7,6},{8,7},{9,8},{10,9},{11,1... | collective-permute-start | bytes 1572872 | tf_op jit(solution)/shard_map/ppermute | solution.py:33
  89.1 17.3 %collective-permute-start.6 = (f32[16,8192]{1,0:T(8,128)S(1)}, f32[16,8192]{1,0:T(8,128)S(1)}, u32[]{:S(2)}, u32[]{:S(2)}) collective-permute-start(f32[16,8192]{1,0:T(8,128)S(1)} %get-tuple-element.17), channel_id=1, source_target_pairs={{0,1},{1,2},{2,3},{3,4},{4,5},{5,6},{6,7},{7,8},{8,9},{9,10},{10,1... | collective-permute-start | bytes 1572872 | tf_op jit(solution)/shard_map/ppermute | solution.py:24
  90.9 15.6 %collective-permute-start.7 = (f32[16,8192]{1,0:T(8,128)S(1)}, f32[16,8192]{1,0:T(8,128)}, u32[]{:S(2)}, u32[]{:S(2)}) collective-permute-start(f32[16,8192]{1,0:T(8,128)S(1)} %get-tuple-element.17), channel_id=1, source_target_pairs={{1,0},{2,1},{3,2},{4,3},{5,4},{6,5},{7,6},{8,7},{9,8},{10,9},{11,1... | collective-permute-start | bytes 1572872 | tf_op jit(solution)/shard_map/ppermute | solution.py:25
  128.0 17.1 %collective-permute-start.8 = (f32[16,8192]{1,0:T(8,128)}, f32[16,8192]{1,0:T(8,128)}, u32[]{:S(2)}, u32[]{:S(2)}) collective-permute-start(f32[16,8192]{1,0:T(8,128)} %get-tuple-element.24), channel_id=1, source_target_pairs={{0,1},{1,2},{2,3},{3,4},{4,5},{5,6},{6,7},{7,8},{8,9},{9,10},{10,1... | collective-permute-start | bytes 1572872 | tf_op jit(solution)/shard_map/ppermute | solution.py:33
  130.5 14.6 %collective-permute-start.9 = (f32[16,8192]{1,0:T(8,128)S(1)}, f32[16,8192]{1,0:T(8,128)}, u32[]{:S(2)}, u32[]{:S(2)}) collective-permute-start(f32[16,8192]{1,0:T(8,128)S(1)} %get-tuple-element.25), channel_id=1, source_target_pairs={{1,0},{2,1},{3,2},{4,3},{5,4},{6,5},{7,6},{8,7},{9,8},{10,9},{11,1... | collective-permute-start | bytes 1572872 | tf_op jit(solution)/shard_map/ppermute | solution.py:33

commit v8 on v7

--- a/solution.py
+++ b/solution.py
@@ -33,26 +33,36 @@
     return lax.ppermute(shard, axis, pairs)
 
 
-def transpose_blocks(tile_stack, anchor):
+def transpose_blocks(tile_stack, anchor, first, count, into=None):
     slots, edge, _ = tile_stack.shape
-    step = 32 if slots % 32 == 0 else 1
+    step = 16 if count % 16 == 0 and first % 16 == 0 else 1
+    offset = first // step
 
-    def body(anchor_ref, x_ref, o_ref):
+    def body(anchor_ref, x_ref, *refs):
+        o_ref = refs[-1]
         for i in range(step):
             o_ref[i] = x_ref[i].T
 
-    nbytes = 2 * tile_stack.size * tile_stack.dtype.itemsize
+    in_specs = [
+        pl.BlockSpec(memory_space=pltpu.SMEM),
+        pl.BlockSpec((step, edge, edge), lambda k: (k + offset, 0, 0)),
+    ]
+    operands = [anchor, tile_stack]
+    aliases = {}
+    if into is not None:
+        in_specs.append(pl.BlockSpec(memory_space=pl.ANY))
+        operands.append(into)
+        aliases = {2: 0}
+    nbytes = 2 * count * edge * edge * tile_stack.dtype.itemsize
     return pl.pallas_call(
         body,
-        grid=(slots // step,),
-        in_specs=[
-            pl.BlockSpec(memory_space=pltpu.SMEM),
-            pl.BlockSpec((step, edge, edge), lambda k: (k, 0, 0)),
-        ],
-        out_specs=pl.BlockSpec((step, edge, edge), lambda k: (k, 0, 0)),
+        grid=(count // step,),
+        in_specs=in_specs,
+        out_specs=pl.BlockSpec((step, edge, edge), lambda k: (k + offset, 0, 0)),
         out_shape=jax.ShapeDtypeStruct(tile_stack.shape, tile_stack.dtype),
+        input_output_aliases=aliases,
         cost_estimate=pl.CostEstimate(flops=0, transcendentals=0, bytes_accessed=nbytes),
-    )(anchor, tile_stack)
+    )(*operands)
 
 
 def forward_local(window, tile_stack, rows_idx, cols_idx, live_slot):
@@ -124,10 +134,13 @@
     def backward(field):
         return transpose_apply(field, tile_stack, rows_idx, cols_idx, live_slot)[0]
 
-    start_raw, tile_stack_t = transpose_apply(
+    slots = tile_stack.shape[0]
+    half = slots // 2
+    start_raw, first_half = transpose_apply(
         observed, tile_stack, rows_idx, cols_idx, live_slot,
-        beside=lambda anchor: transpose_blocks(tile_stack, anchor),
+        beside=lambda anchor: transpose_blocks(tile_stack, anchor, 0, half),
     )
+    tile_stack_t = transpose_blocks(tile_stack, start_raw[:1, :1], half, slots - half, into=first_half)
 
     def forward(vector):
         return forward_apply(vector, tile_stack_t, rows_idx, cols_idx, live_slot)

time: 160 us -> 160 us (level)
  waiting for transfers between devices: 6.5 us -> 0.03 us
  starting transfers between devices: 29.1 us -> 34.6 us
  Pallas kernels: 11.7 us -> 15.7 us
  blocking collectives: 51.5 us -> 48.7 us
    all_to_all x1, waiting for transfers between devices: 6.48 us -> 0.01 us  [all_sum(): gathered = lax.all_to_all(spread, axes, 0, 0, tiled=True)]
    ppermute x2, starting transfers between devices: 6.88 us -> 11.1 us  [with_halo(): before = lax.ppermute(last, axis, up)]
    ppermute x6, starting transfers between devices: 10.4 us -> 14.6 us  [from_behind(): return lax.ppermute(shard, axis, pairs)]
    pallas_call x1 -> x2, Pallas kernels: 11.7 us -> 15.7 us  [transpose_blocks(): pl.pallas_call(body, grid=(count // step,), in_specs=in_specs, out_specs=...]
    all_to_all x1, starting transfers between devices: 9.21 us -> 6.25 us  [all_sum(): gathered = lax.all_to_all(spread, axes, 0, 0, tiled=True)]
    all_to_all x4, blocking collectives: 51.5 us -> 48.7 us  [all_sum(): gathered = lax.all_to_all(spread, axes, 0, 0, tiled=True)]
  transfers between devices with their start and end apart: 11 -> 11, of which waited for: 1 -> 0; matrix products, arithmetic and copies ran while one was open for 1% -> 1% of each run, Pallas kernels for 7% -> 10%
where the time goes in v8:
time: 160 us; the launch traced here: 159 us
  blocking collectives  48.7 us (30%)
  matrix products  38.7 us (24%)
  starting transfers between devices  34.6 us (22%)
  Pallas kernels  15.7 us (10%)
  local copies, waits for them, and re-layouts  12.7 us (8%)
  other arithmetic  7.25 us (5%)
  between operations  1.69 us (1%)
    all_to_all x4, blocking collectives, all_sum(): gathered = lax.all_to_all(spread, axes, 0, 0, tiled=True)  48.7 us
    dot_general x3, matrix products, transpose_local(): jnp.einsum('ski,kij->ksj', pieces, tile_stack, precision=PRODUCT_PRECISION)  20.5 us
    pallas_call x2, Pallas kernels, transpose_blocks(): pl.pallas_call(body, grid=(count // step,), in_specs=in_specs, out_specs=...  15.7 us
    ppermute x6, starting transfers between devices, from_behind(): return lax.ppermute(shard, axis, pairs)  14.6 us
    dot_general x2, matrix products, forward_local(): jnp.einsum('skj,kji->ksi', pieces, tile_stack, precision=PRODUCT_PRECISION)  13.9 us
    ppermute x2, starting transfers between devices, with_halo(): before = lax.ppermute(last, axis, up)  11.1 us
    all_to_all x1, starting transfers between devices, all_sum(): gathered = lax.all_to_all(spread, axes, 0, 0, tiled=True)  6.25 us
    reduce_sum x6, other arithmetic, squares(): return jnp.sum(field * field, axis=1)  3.77 us
  transfers between devices with their start and end apart: 11, of which 0 were waited for; matrix products, arithmetic and copies ran while one was open for 1% of the time, Pallas kernels for 10%

profile of v8, /device:TPU:0, one launch (start us, length us, event | category | flops | bytes accessed | tf_op | source)
XLA Modules:
  0.0 159.4 jit_solution(9924748805194227934)
XLA Ops:
  0.6 1.0 copy_bitcast_fusion.7
  1.6 0.7 compare_select_fusion.1
  3.0 0.8 gather_fusion
  3.8 6.8 %convolution_multiply_fusion.4 = f32[160,16,128]{2,1,0:T(8,128)S(1)} fusion(f32[160,16,128]{2,1,0:T(8,128)S(1)} %gather_fusion, f32[160]{0:T(256)S(1)} %compare_convert_fusion, f32[1,160,128,128]{3,2,1,0:T(8,128)} %param.6), kind=kOutput, calls=%fused_computation.16 | convolution fusion | flops 251985920 | bytes 13107840 | tf_op jit(solution)/shard_map/ski,kij->ksj/dot_general | solution.py:85
  10.7 1.0 fusion.13
  11.7 0.9 copy.82
  12.7 1.3 collective-permute-start.1
  14.0 3.1 %collective-permute-start = (f32[16,8192]{1,0:T(8,128)S(1)}, f32[16,8192]{1,0:T(8,128)S(1)}, u32[]{:S(2)}, u32[]{:S(2)}) collective-permute-start(f32[16,8192]{1,0:T(8,128)S(1)} %get-tuple-element.28), channel_id=1, source_target_pairs={{0,1},{1,2},{2,3},{3,4},{4,5},{5,6},{6,7},{7,8},{8,9},{9,10},{10,1... | collective-permute-start | bytes 1572872 | tf_op jit(solution)/shard_map/ppermute | solution.py:33
  17.1 0.5 slice.64.anchor_ref
  17.6 7.9 %shard_map.68.refs_0_ = f32[160,128,128]{2,1,0:T(8,128)} custom-call(f32[1,1]{1,0:T(1,128)} %slice.64.anchor_ref, f32[160,128,128]{2,1,0:T(8,128)} %bitcast.119), custom_call_target="tpu_custom_call" | custom-call | bytes 10485760 | tf_op jit(solution)/shard_map/pallas_call | solution.py:57
  25.9 1.3 collective-permute-start.3
  27.2 7.2 %collective-permute-start.2 = (f32[16,8192]{1,0:T(8,128)S(1)}, f32[16,8192]{1,0:T(8,128)S(1)}, u32[]{:S(2)}, u32[]{:S(2)}) collective-permute-start(f32[16,8192]{1,0:T(8,128)S(1)} %get-tuple-element.23), channel_id=1, source_target_pairs={{0,1},{1,2},{2,3},{3,4},{4,5},{5,6},{6,7},{7,8},{8,9},{9,10},{10,1... | collective-permute-start | bytes 1572872 | tf_op jit(solution)/shard_map/ppermute | solution.py:24
  34.4 0.6 broadcast_in_dim.10
  35.0 6.2 %all-to-all-start = ((f32[16,2,16]{2,1,0:T(2,128)}), f32[16,2,16]{2,1,0:T(2,128)S(1)}, u32[]{:S(2)}, u32[]{:S(2)}) async-start(f32[16,2,16]{2,1,0:T(2,128)} %broadcast_in_dim.10), calls=%async_computation | async-start | bytes 32768 | tf_op jit(solution)/shard_map/all_to_all | solution.py:118
  41.3 0.5 slice.67.anchor_ref
  41.8 7.8 %shard_map.69 = f32[160,128,128]{2,1,0:T(8,128)} custom-call(f32[1,1]{1,0:T(1,128)} %slice.67.anchor_ref, f32[160,128,128]{2,1,0:T(8,128)} %bitcast.120, f32[160,128,128]{2,1,0:T(8,128)} %shard_map.68.refs_0_), custom_call_target="tpu_custom_call", output_to_operand_aliasing={{}: (2, {})} | custom-call | bytes 10485760 | tf_op jit(solution)/shard_map/pallas_call | solution.py:57
  49.9 0.8 gather_fusion.1
  50.7 6.8 %convolution_multiply_fusion.3 = f32[160,16,128]{2,1,0:T(8,128)S(1)} fusion(f32[160,128,128]{2,1,0:T(8,128)} %shard_map.69, f32[160,16,128]{2,1,0:T(8,128)S(1)} %gather_fusion.1, f32[160]{0:T(256)S(1)} %compare_convert_fusion), kind=kOutput, calls=%fused_computation.15 | convolution fusion | flops 251985920 | bytes 13107840 | tf_op jit(solution)/shard_map/skj,kji->ksi/dot_general | solution.py:73
  57.6 0.7 fusion.11
  58.5 0.3 multiply_reduce_fusion.4
  58.9 0.8 gather_fusion.2
  59.7 6.8 %convolution_multiply_fusion.2 = f32[160,16,128]{2,1,0:T(8,128)S(1)} fusion(f32[160,16,128]{2,1,0:T(8,128)S(1)} %gather_fusion.2, f32[160]{0:T(256)S(1)} %compare_convert_fusion, f32[1,160,128,128]{3,2,1,0:T(8,128)} %param.6), kind=kOutput, calls=%fused_computation.14 | convolution fusion | flops 251985920 | bytes 13107840 | tf_op jit(solution)/shard_map/ski,kij->ksj/dot_general | solution.py:85
  66.5 1.0 fusion.9
  67.5 0.9 copy.81
  68.5 0.9 fusion.44
  69.3 1.3 collective-permute-start.5
  70.6 3.9 %collective-permute-start.4 = (f32[16,8192]{1,0:T(8,128)S(1)}, f32[16,8192]{1,0:T(8,128)}, u32[]{:S(2)}, u32[]{:S(2)}) collective-permute-start(f32[16,8192]{1,0:T(8,128)S(1)} %get-tuple-element.26), channel_id=1, source_target_pairs={{0,1},{1,2},{2,3},{3,4},{4,5},{5,6},{6,7},{7,8},{8,9},{9,10},{10,1... | collective-permute-start | bytes 1572872 | tf_op jit(solution)/shard_map/ppermute | solution.py:33
  74.5 12.4 %all_to_all.29 = f32[16,1,16]{2,1,0:T(1,128)S(1)} all-to-all(f32[16,1,16]{2,1,0:T(1,128)S(1)} %broadcast_in_dim.11), channel_id=1, replica_groups=mesh['group'=2,'row'=8,'col'=2] {'row','col'}, dimensions={0} | all-to-all | bytes 2048 | tf_op jit(solution)/shard_map/all_to_all | solution.py:118
  86.9 1.3 multiply_reduce_fusion.1
  88.2 1.3 collective-permute-start.7
  89.5 3.9 %collective-permute-start.6 = (f32[16,8192]{1,0:T(8,128)S(1)}, f32[16,8192]{1,0:T(8,128)}, u32[]{:S(2)}, u32[]{:S(2)}) collective-permute-start(f32[16,8192]{1,0:T(8,128)S(1)} %get-tuple-element.17), channel_id=1, source_target_pairs={{0,1},{1,2},{2,3},{3,4},{4,5},{5,6},{6,7},{7,8},{8,9},{9,10},{10,1... | collective-permute-start | bytes 1572872 | tf_op jit(solution)/shard_map/ppermute | solution.py:24
  93.4 12.5 %all_to_all.30 = f32[16,1,16]{2,1,0:T(1,128)S(1)} all-to-all(f32[16,1,16]{2,1,0:T(1,128)S(1)} %broadcast_in_dim.12), channel_id=1, replica_groups=mesh['group'=2,'row'=8,'col'=2] {'row','col'}, dimensions={0} | all-to-all | bytes 2048 | tf_op jit(solution)/shard_map/all_to_all | solution.py:118
  106.0 1.2 copy_bitcast_fusion.3
  107.1 1.9 %gather_fusion.3 = f32[160,16,128]{2,1,0:T(8,128)} fusion(f32[16,192,128]{2,0,1:T(8,128)S(1)} %copy_bitcast_fusion.3, s32[1024]{0:T(1024)S(1)} %pad_clamp_fusion), kind=kCustom, calls=%fused_computation.3 | custom fusion | bytes 2622080 | tf_op jit(solution)/shard_map/gather | solution.py:71
  109.1 7.1 %convolution_multiply_fusion.1 = f32[160,16,128]{2,1,0:T(8,128)S(1)} fusion(f32[160,128,128]{2,1,0:T(8,128)} %shard_map.69, f32[160,16,128]{2,1,0:T(8,128)} %gather_fusion.3, f32[160]{0:T(256)S(1)} %compare_convert_fusion), kind=kOutput, calls=%fused_computation.13 | convolution fusion | flops 251985920 | bytes 13107840 | tf_op jit(solution)/shard_map/skj,kji->ksi/dot_general | solution.py:73
  116.1 0.7 fusion.7
  116.8 0.3 multiply_reduce_fusion.3
  117.1 0.8 gather_fusion.4
  117.9 6.8 %convolution_multiply_fusion = f32[160,16,128]{2,1,0:T(8,128)S(1)} fusion(f32[160,16,128]{2,1,0:T(8,128)S(1)} %gather_fusion.4, f32[160]{0:T(256)S(1)} %compare_convert_fusion, f32[1,160,128,128]{3,2,1,0:T(8,128)} %param.6), kind=kOutput, calls=%fused_computation.12 | convolution fusion | flops 251985920 | bytes 13107840 | tf_op jit(solution)/shard_map/ski,kij->ksj/dot_general | solution.py:85
  124.8 1.0 fusion.5
  125.8 0.9 copy.80
  126.7 0.9 fusion.43
  127.6 1.3 collective-permute-start.9
  128.9 3.9 %collective-permute-start.8 = (f32[16,8192]{1,0:T(8,128)S(1)}, f32[16,8192]{1,0:T(8,128)}, u32[]{:S(2)}, u32[]{:S(2)}) collective-permute-start(f32[16,8192]{1,0:T(8,128)S(1)} %get-tuple-element.24), channel_id=1, source_target_pairs={{0,1},{1,2},{2,3},{3,4},{4,5},{5,6},{6,7},{7,8},{8,9},{9,10},{10,1... | collective-permute-start | bytes 1572872 | tf_op jit(solution)/shard_map/ppermute | solution.py:33
  132.7 12.3 %all_to_all.31 = f32[16,1,16]{2,1,0:T(1,128)S(1)} all-to-all(f32[16,1,16]{2,1,0:T(1,128)S(1)} %broadcast_in_dim.13), channel_id=1, replica_groups=mesh['group'=2,'row'=8,'col'=2] {'row','col'}, dimensions={0} | all-to-all | bytes 2048 | tf_op jit(solution)/shard_map/all_to_all | solution.py:118
  145.1 1.5 multiply_reduce_fusion
  146.6 11.5 %all_to_all.32 = f32[16,1,16]{2,1,0:T(1,128)S(1)} all-to-all(f32[16,1,16]{2,1,0:T(1,128)S(1)} %broadcast_in_dim.14), channel_id=1, replica_groups=mesh['group'=2,'row'=8,'col'=2] {'row','col'}, dimensions={0} | all-to-all | bytes 2048 | tf_op jit(solution)/shard_map/all_to_all | solution.py:118
  158.2 1.2 multiply_subtract_fusion
  (48 shorter events, 1.2 us)
Async XLA Ops:
  3.8 6.9 %copy-start.2 = (s32[1,160]{1,0:T(1,128)S(1)}, s32[1,160]{1,0:T(1,128)}, u32[]{:S(2)}) copy-start(s32[1,160]{1,0:T(1,128)} %param.8) | copy-start | bytes 1924
  12.7 12.9 %collective-permute-start.1 = (f32[16,8192]{1,0:T(8,128)S(1)}, f32[16,8192]{1,0:T(8,128)S(1)}, u32[]{:S(2)}, u32[]{:S(2)}) collective-permute-start(f32[16,8192]{1,0:T(8,128)S(1)} %get-tuple-element.29), channel_id=1, source_target_pairs={{1,0},{2,1},{3,2},{4,3},{5,4},{6,5},{7,6},{8,7},{9,8},{10,9},{11,1... | collective-permute-start | bytes 1572872 | tf_op jit(solution)/shard_map/ppermute | solution.py:33
  14.0 11.6 %collective-permute-start = (f32[16,8192]{1,0:T(8,128)S(1)}, f32[16,8192]{1,0:T(8,128)S(1)}, u32[]{:S(2)}, u32[]{:S(2)}) collective-permute-start(f32[16,8192]{1,0:T(8,128)S(1)} %get-tuple-element.28), channel_id=1, source_target_pairs={{0,1},{1,2},{2,3},{3,4},{4,5},{5,6},{6,7},{7,8},{8,9},{9,10},{10,1... | collective-permute-start | bytes 1572872 | tf_op jit(solution)/shard_map/ppermute | solution.py:33
  17.6 7.9 %copy-start = (f32[16,4096]{1,0:T(8,128)S(1)}, f32[16,4096]{1,0:T(8,128)}, u32[]{:S(2)}) copy-start(f32[16,4096]{1,0:T(8,128)} %param.5) | copy-start | bytes 786436
  25.9 23.9 %collective-permute-start.3 = (f32[16,8192]{1,0:T(8,128)S(1)}, f32[16,8192]{1,0:T(8,128)S(1)}, u32[]{:S(2)}, u32[]{:S(2)}) collective-permute-start(f32[16,8192]{1,0:T(8,128)S(1)} %get-tuple-element.23), channel_id=1, source_target_pairs={{1,0},{2,1},{3,2},{4,3},{5,4},{6,5},{7,6},{8,7},{9,8},{10,9},{11,1... | collective-permute-start | bytes 1572872 | tf_op jit(solution)/shard_map/ppermute | solution.py:25
  27.2 22.6 %collective-permute-start.2 = (f32[16,8192]{1,0:T(8,128)S(1)}, f32[16,8192]{1,0:T(8,128)S(1)}, u32[]{:S(2)}, u32[]{:S(2)}) collective-permute-start(f32[16,8192]{1,0:T(8,128)S(1)} %get-tuple-element.23), channel_id=1, source_target_pairs={{0,1},{1,2},{2,3},{3,4},{4,5},{5,6},{6,7},{7,8},{8,9},{9,10},{10,1... | collective-permute-start | bytes 1572872 | tf_op jit(solution)/shard_map/ppermute | solution.py:24
  35.0 14.6 %all-to-all-start = ((f32[16,2,16]{2,1,0:T(2,128)}), f32[16,2,16]{2,1,0:T(2,128)S(1)}, u32[]{:S(2)}, u32[]{:S(2)}) async-start(f32[16,2,16]{2,1,0:T(2,128)} %broadcast_in_dim.10), calls=%async_computation | async-start | bytes 32768 | tf_op jit(solution)/shard_map/all_to_all | solution.py:118
  50.7 6.9 %copy-start.3 = (s32[1,160]{1,0:T(1,128)S(1)}, s32[1,160]{1,0:T(1,128)}, u32[]{:S(2)}) copy-start(s32[1,160]{1,0:T(1,128)} %param.7) | copy-start | bytes 1924
  57.6 1.0 copy-start.1
  69.3 17.6 %collective-permute-start.5 = (f32[16,8192]{1,0:T(8,128)}, f32[16,8192]{1,0:T(8,128)S(1)}, u32[]{:S(2)}, u32[]{:S(2)}) collective-permute-start(f32[16,8192]{1,0:T(8,128)} %get-tuple-element.27), channel_id=1, source_target_pairs={{1,0},{2,1},{3,2},{4,3},{5,4},{6,5},{7,6},{8,7},{9,8},{10,9},{11,1... | collective-permute-start | bytes 1572872 | tf_op jit(solution)/shard_map/ppermute | solution.py:33
  70.6 16.3 %collective-permute-start.4 = (f32[16,8192]{1,0:T(8,128)S(1)}, f32[16,8192]{1,0:T(8,128)}, u32[]{:S(2)}, u32[]{:S(2)}) collective-permute-start(f32[16,8192]{1,0:T(8,128)S(1)} %get-tuple-element.26), channel_id=1, source_target_pairs={{0,1},{1,2},{2,3},{3,4},{4,5},{5,6},{6,7},{7,8},{8,9},{9,10},{10,1... | collective-permute-start | bytes 1572872 | tf_op jit(solution)/shard_map/ppermute | solution.py:33
  88.2 17.7 %collective-permute-start.7 = (f32[16,8192]{1,0:T(8,128)S(1)}, f32[16,8192]{1,0:T(8,128)S(1)}, u32[]{:S(2)}, u32[]{:S(2)}) collective-permute-start(f32[16,8192]{1,0:T(8,128)S(1)} %get-tuple-element.17), channel_id=1, source_target_pairs={{1,0},{2,1},{3,2},{4,3},{5,4},{6,5},{7,6},{8,7},{9,8},{10,9},{11,1... | collective-permute-start | bytes 1572872 | tf_op jit(solution)/shard_map/ppermute | solution.py:25
  89.5 16.4 %collective-permute-start.6 = (f32[16,8192]{1,0:T(8,128)S(1)}, f32[16,8192]{1,0:T(8,128)}, u32[]{:S(2)}, u32[]{:S(2)}) collective-permute-start(f32[16,8192]{1,0:T(8,128)S(1)} %get-tuple-element.17), channel_id=1, source_target_pairs={{0,1},{1,2},{2,3},{3,4},{4,5},{5,6},{6,7},{7,8},{8,9},{9,10},{10,1... | collective-permute-start | bytes 1572872 | tf_op jit(solution)/shard_map/ppermute | solution.py:24
  127.6 17.5 %collective-permute-start.9 = (f32[16,8192]{1,0:T(8,128)}, f32[16,8192]{1,0:T(8,128)}, u32[]{:S(2)}, u32[]{:S(2)}) collective-permute-start(f32[16,8192]{1,0:T(8,128)} %get-tuple-element.25), channel_id=1, source_target_pairs={{1,0},{2,1},{3,2},{4,3},{5,4},{6,5},{7,6},{8,7},{9,8},{10,9},{11,1... | collective-permute-start | bytes 1572872 | tf_op jit(solution)/shard_map/ppermute | solution.py:33
  128.9 16.2 %collective-permute-start.8 = (f32[16,8192]{1,0:T(8,128)S(1)}, f32[16,8192]{1,0:T(8,128)}, u32[]{:S(2)}, u32[]{:S(2)}) collective-permute-start(f32[16,8192]{1,0:T(8,128)S(1)} %get-tuple-element.24), channel_id=1, source_target_pairs={{0,1},{1,2},{2,3},{3,4},{4,5},{5,6},{6,7},{7,8},{8,9},{9,10},{10,1... | collective-permute-start | bytes 1572872 | tf_op jit(solution)/shard_map/ppermute | solution.py:33

commit v9 on v7

--- a/solution.py
+++ b/solution.py
@@ -55,46 +55,42 @@
     )(anchor, tile_stack)
 
 
-def forward_local(window, tile_stack, rows_idx, cols_idx, live_slot):
-    scenario_rows = window.shape[0]
-    tile_edge = tile_stack.shape[1]
-    pieces = window.reshape(scenario_rows, 3 * COL_BLOCKS, tile_edge)[:, cols_idx, :]
+def forward_local(window, tile_stack_t, rows_idx, cols_idx, live_slot):
+    pieces = window[cols_idx]
     products = (
-        jnp.einsum("skj,kji->ksi", pieces, tile_stack, precision=PRODUCT_PRECISION) * live_slot[:, None, None]
+        jnp.einsum("ksj,kji->ksi", pieces, tile_stack_t, precision=PRODUCT_PRECISION)
+        * live_slot[:, None, None]
     )
     onehot = (rows_idx[:, None] == jnp.arange(ROW_BLOCKS)[None, :]).astype(jnp.float32)
-    summed = jnp.einsum("kr,ksi->sri", onehot, products, precision=PRODUCT_PRECISION)
-    return summed.reshape(scenario_rows, ROW_BLOCKS * tile_edge)
+    return jnp.einsum("kr,ksi->rsi", onehot, products, precision=PRODUCT_PRECISION)
 
 
 def transpose_local(field, tile_stack, rows_idx, cols_idx, live_slot):
-    scenario_rows = field.shape[0]
-    tile_edge = tile_stack.shape[1]
-    pieces = field.reshape(scenario_rows, ROW_BLOCKS, tile_edge)[:, rows_idx, :]
+    pieces = field[rows_idx]
     products = (
-        jnp.einsum("ski,kij->ksj", pieces, tile_stack, precision=PRODUCT_PRECISION) * live_slot[:, None, None]
+        jnp.einsum("ksi,kij->ksj", pieces, tile_stack, precision=PRODUCT_PRECISION)
+        * live_slot[:, None, None]
     )
     onehot = (cols_idx[:, None] == jnp.arange(3 * COL_BLOCKS)[None, :]).astype(jnp.float32)
-    summed = jnp.einsum("kc,ksj->scj", onehot, products, precision=PRODUCT_PRECISION)
-    return summed.reshape(scenario_rows, 3 * COL_BLOCKS * tile_edge)
+    return jnp.einsum("kc,ksj->csj", onehot, products, precision=PRODUCT_PRECISION)
 
 
-def forward_apply(vector, tile_stack, rows_idx, cols_idx, live_slot):
-    window = with_halo(vector, ((("row", "col"), 1),), vector.shape[1])
-    return forward_local(window, tile_stack, rows_idx, cols_idx, live_slot)
+def forward_apply(vector, tile_stack_t, rows_idx, cols_idx, live_slot):
+    window = with_halo(vector, ((("row", "col"), 0),), vector.shape[0])
+    return forward_local(window, tile_stack_t, rows_idx, cols_idx, live_slot)
 
 
 def transpose_apply(field, tile_stack, rows_idx, cols_idx, live_slot, beside=None):
     partial_sums = transpose_local(field, tile_stack, rows_idx, cols_idx, live_slot)
-    band_width = partial_sums.shape[1] // 3
-    lower = partial_sums[:, :band_width]
-    middle = partial_sums[:, band_width : 2 * band_width]
-    upper = partial_sums[:, 2 * band_width :]
+    band = partial_sums.shape[0] // 3
+    lower = partial_sums[:band]
+    middle = partial_sums[band : 2 * band]
+    upper = partial_sums[2 * band :]
     from_below = from_behind(upper, ("row", "col"), 1)
     from_above = from_behind(lower, ("row", "col"), -1)
     extra = None
     if beside is not None:
-        extra = beside(middle[:1, :1])
+        extra = beside(middle[:1, :1, 0])
         middle, extra = lax.optimization_barrier((middle, extra))
     result = middle + from_below + from_above
     return result, extra
@@ -110,7 +106,11 @@
 
 
 def squares(field):
-    return jnp.sum(field * field, axis=1)
+    return jnp.sum(field * field, axis=(0, 2))
+
+
+def per_row(values):
+    return values[None, :, None]
 
 
 def per_device(observed, blocks, block_rows, block_cols, counts):
@@ -120,6 +120,9 @@
     slot_ids = jnp.arange(tile_stack.shape[0])
     live_slot = (slot_ids < counts[0]).astype(jnp.float32)
     axes = ("row", "col")
+    scenarios, rows_here = observed.shape
+    edge = tile_stack.shape[1]
+    observed = jnp.swapaxes(observed.reshape(scenarios, rows_here // edge, edge), 0, 1)
 
     def backward(field):
         return transpose_apply(field, tile_stack, rows_idx, cols_idx, live_slot)[0]
@@ -136,10 +139,10 @@
     row_norm = jnp.sqrt(totals[0] + 1e-06)
     col_norm = jnp.sqrt(totals[1] / (row_norm * row_norm) + 1e-06)
     scale = row_norm * col_norm
-    left_vec = observed / row_norm[:, None]
-    right_vec = start_raw / scale[:, None]
+    left_vec = observed / per_row(row_norm)
+    right_vec = start_raw / per_row(scale)
     left_prod = forward(start_raw)
-    left_raw = left_prod / scale[:, None] - col_norm[:, None] * left_vec
+    left_raw = left_prod / per_row(scale) - per_row(col_norm) * left_vec
     dir_now = right_vec
     solution = jnp.zeros_like(dir_now)
     phi_bar = row_norm
@@ -147,14 +150,14 @@
     for iteration in range(ITERATIONS):
         right_prod = backward(left_raw)
         row_norm = jnp.sqrt(all_sum(squares(left_raw), axes) + 1e-06)
-        left_vec = left_raw / row_norm[:, None]
-        right_raw = right_prod / row_norm[:, None] - row_norm[:, None] * right_vec
+        left_vec = left_raw / per_row(row_norm)
+        right_raw = right_prod / per_row(row_norm) - per_row(row_norm) * right_vec
         if iteration + 1 < ITERATIONS:
             left_prod = forward(right_raw)
         col_norm = jnp.sqrt(all_sum(squares(right_raw), axes) + 1e-06)
-        right_vec = right_raw / col_norm[:, None]
+        right_vec = right_raw / per_row(col_norm)
         if iteration + 1 < ITERATIONS:
-            left_raw = left_prod / col_norm[:, None] - col_norm[:, None] * left_vec
+            left_raw = left_prod / per_row(col_norm) - per_row(col_norm) * left_vec
         diag_new = jnp.sqrt(diag_bar * diag_bar + row_norm * row_norm)
         rot_cosine = diag_bar / diag_new
         rot_sine = row_norm / diag_new
@@ -162,9 +165,13 @@
         diag_bar = -rot_cosine * col_norm
         phi_now = rot_cosine * phi_bar
         phi_bar = rot_sine * phi_bar
-        solution = solution + (phi_now / diag_new)[:, None] * dir_now
-        dir_now = right_vec - (off_diag / diag_new)[:, None] * dir_now
-    return (solution, dir_now)
+        solution = solution + per_row(phi_now / diag_new) * dir_now
+        dir_now = right_vec - per_row(off_diag / diag_new) * dir_now
+
+    def rows_major(field):
+        return jnp.swapaxes(field, 0, 1).reshape(scenarios, -1)
+
+    return (rows_major(solution), rows_major(dir_now))
 
 
 def solution(mesh):

time: 160 us -> 161 us (level)
  local copies, waits for them, and re-layouts: 12.2 us -> 15.2 us
  other arithmetic: 7.25 us -> 4.75 us
    concatenate x0 -> x2, local copies, waits for them, and re-layouts: none -> 1.83 us  [with_halo(): shard = jnp.concatenate([before, shard, after], axis=dim)]
    reduce_sum x6 -> x4, other arithmetic: 3.77 us -> 3.29 us  [squares(): return jnp.sum(field * field, axis=(0, 2))]
where the time goes in v9:
time: 161 us; the launch traced here: 160 us
  blocking collectives  52.3 us (32%)
  matrix products  39.3 us (24%)
  starting transfers between devices  28.3 us (18%)
  local copies, waits for them, and re-layouts  15.2 us (9%)
  Pallas kernels  11.7 us (7%)
  waiting for transfers between devices  6.5 us (4%)
  other arithmetic  4.75 us (3%)
  between operations  1.7 us (1%)
    all_to_all x4, blocking collectives, all_sum(): gathered = lax.all_to_all(spread, axes, 0, 0, tiled=True)  52.3 us
    dot_general x3, matrix products, transpose_local(): jnp.einsum('ksi,kij->ksj', pieces, tile_stack, precision=PRODUCT_PRECISION)  20.5 us
    dot_general x2, matrix products, forward_local(): jnp.einsum('ksj,kji->ksi', pieces, tile_stack_t, precision=PRODUCT_PRECIS...  14.1 us
    pallas_call x1, Pallas kernels, transpose_blocks(): pl.pallas_call(body, grid=(slots // step,), in_specs=[pl.BlockSpec(memory...  11.7 us
    ppermute x6, starting transfers between devices, from_behind(): return lax.ppermute(shard, axis, pairs)  9.66 us
    all_to_all x1, starting transfers between devices, all_sum(): gathered = lax.all_to_all(spread, axes, 0, 0, tiled=True)  9.22 us
    ppermute x2, starting transfers between devices, with_halo(): before = lax.ppermute(last, axis, up)  6.89 us
    all_to_all x1, waiting for transfers between devices, all_sum(): gathered = lax.all_to_all(spread, axes, 0, 0, tiled=True)  6.48 us
  transfers between devices with their start and end apart: 11, of which 1 were waited for; matrix products, arithmetic and copies ran while one was open for 1% of the time, Pallas kernels for 7%

profile of v9, /device:TPU:0, one launch (start us, length us, event | category | flops | bytes accessed | tf_op | source)
XLA Modules:
  0.0 159.8 jit_solution(4806040177930572600)
XLA Ops:
  0.6 1.0 copy.45
  1.8 0.7 compare_select_fusion.1
  3.2 0.8 gather_fusion
  4.0 6.8 %convolution_multiply_fusion.4 = f32[160,16,128]{2,1,0:T(8,128)S(1)} fusion(f32[160,16,128]{2,1,0:T(8,128)S(1)} %gather_fusion, f32[160]{0:T(256)S(1)} %compare_convert_fusion, f32[1,160,128,128]{3,2,1,0:T(8,128)} %param.6), kind=kOutput, calls=%fused_computation.11 | convolution fusion | flops 251985920 | bytes 13107840 | tf_op jit(solution)/shard_map/ksi,kij->ksj/dot_general | solution.py:71
  10.9 1.0 fusion.8
  12.0 2.4 %collective-permute-start = (f32[64,16,128]{2,0,1:T(8,128)S(1)}, f32[64,16,128]{2,0,1:T(8,128)S(1)}, u32[]{:S(2)}, u32[]{:S(2)}) collective-permute-start(f32[64,16,128]{2,0,1:T(8,128)S(1)} %get-tuple-element.24), channel_id=1, source_target_pairs={{0,1},{1,2},{2,3},{3,4},{4,5},{5,6},{6,7},{7,8},{8,9},{9,10},{10,1... | collective-permute-start | bytes 1572872 | tf_op jit(solution)/shard_map/ppermute | solution.py:33
  14.4 1.3 collective-permute-start.1
  15.7 0.5 slice.60
  16.2 11.7 %shard_map.68 = f32[160,128,128]{2,1,0:T(8,128)} custom-call(f32[1,1]{1,0:T(1,128)} %bitcast.8.anchor_ref, f32[160,128,128]{2,1,0:T(8,128)} %bitcast.77), custom_call_target="tpu_custom_call" | custom-call | bytes 20971520 | tf_op jit(solution)/shard_map/pallas_call | solution.py:45
  27.9 0.2 multiply_reduce_fusion.5
  28.1 0.2 multiply_reduce_fusion.2
  28.3 5.2 %collective-permute-start.2 = (f32[64,16,128]{2,0,1:T(8,128)S(1)}, f32[64,16,128]{2,0,1:T(8,128)S(1)}, u32[]{:S(2)}, u32[]{:S(2)}) collective-permute-start(f32[64,16,128]{2,0,1:T(8,128)S(1)} %get-tuple-element.19), channel_id=1, source_target_pairs={{0,1},{1,2},{2,3},{3,4},{4,5},{5,6},{6,7},{7,8},{8,9},{9,10},{10,1... | collective-permute-start | bytes 1572872 | tf_op jit(solution)/shard_map/ppermute | solution.py:24
  33.5 1.3 collective-permute-start.3
  34.8 0.6 broadcast_in_dim.10
  35.4 9.2 %all-to-all-start = ((f32[16,2,16]{2,1,0:T(2,128)}), f32[16,2,16]{2,1,0:T(2,128)S(1)}, u32[]{:S(2)}, u32[]{:S(2)}) async-start(f32[16,2,16]{2,1,0:T(2,128)} %broadcast_in_dim.10), calls=%async_computation | async-start | bytes 32768 | tf_op jit(solution)/shard_map/all_to_all | solution.py:104
  44.7 6.5 %all-to-all-done = f32[16,2,16]{2,1,0:T(2,128)S(1)} async-done(((f32[16,2,16]{2,1,0:T(2,128)}), f32[16,2,16]{2,1,0:T(2,128)S(1)}, u32[]{:S(2)}, u32[]{:S(2)}) %all-to-all-start) | async-done | bytes 2080 | tf_op jit(solution)/shard_map/all_to_all | solution.py:104
  51.4 0.9 copy.29
  52.3 1.9 %gather_fusion.1 = f32[160,16,128]{2,1,0:T(8,128)} fusion(f32[192,16,128]{2,1,0:T(8,128)S(1)} %copy.29, s32[1024]{0:T(1024)S(1)} %pad_clamp_fusion), kind=kCustom, calls=%fused_computation.1 | custom fusion | bytes 2622080 | tf_op jit(solution)/shard_map/gather | solution.py:59
  54.2 7.1 %convolution_multiply_fusion.3 = f32[160,16,128]{2,1,0:T(8,128)S(1)} fusion(f32[160,16,128]{2,1,0:T(8,128)} %gather_fusion.1, f32[160,128,128]{2,1,0:T(8,128)} %shard_map.68, f32[160]{0:T(256)S(1)} %compare_convert_fusion), kind=kOutput, calls=%fused_computation.10 | convolution fusion | flops 251985920 | bytes 13107840 | tf_op jit(solution)/shard_map/ksj,kji->ksi/dot_general | solution.py:61
  61.3 0.8 multiply_reduce_fusion.4
  62.1 0.2 copy.32
  62.3 0.8 gather_fusion.2
  63.1 6.8 %convolution_multiply_fusion.2 = f32[160,16,128]{2,1,0:T(8,128)S(1)} fusion(f32[160,16,128]{2,1,0:T(8,128)S(1)} %gather_fusion.2, f32[160]{0:T(256)S(1)} %compare_convert_fusion, f32[1,160,128,128]{3,2,1,0:T(8,128)} %param.6), kind=kOutput, calls=%fused_computation.9 | convolution fusion | flops 251985920 | bytes 13107840 | tf_op jit(solution)/shard_map/ksi,kij->ksj/dot_general | solution.py:71
  69.9 1.0 fusion.4
  70.9 0.9 fusion.47
  71.8 1.7 %collective-permute-start.4 = (f32[64,16,128]{2,0,1:T(8,128)}, f32[64,16,128]{2,0,1:T(8,128)S(1)}, u32[]{:S(2)}, u32[]{:S(2)}) collective-permute-start(f32[64,16,128]{2,0,1:T(8,128)} %get-tuple-element.22), channel_id=1, source_target_pairs={{0,1},{1,2},{2,3},{3,4},{4,5},{5,6},{6,7},{7,8},{8,9},{9,10},{10,1... | collective-permute-start | bytes 1572872 | tf_op jit(solution)/shard_map/ppermute | solution.py:33
  73.5 1.3 collective-permute-start.5
  74.8 13.3 %all_to_all.29 = f32[16,1,16]{2,1,0:T(1,128)S(1)} all-to-all(f32[16,1,16]{2,1,0:T(1,128)S(1)} %broadcast_in_dim.11), channel_id=1, replica_groups=mesh['group'=2,'row'=8,'col'=2] {'row','col'}, dimensions={0} | all-to-all | bytes 2048 | tf_op jit(solution)/shard_map/all_to_all | solution.py:104
  88.1 1.4 multiply_reduce_fusion.1
  89.5 1.7 %collective-permute-start.6 = (f32[64,16,128]{2,0,1:T(8,128)S(1)}, f32[64,16,128]{2,0,1:T(8,128)S(1)}, u32[]{:S(2)}, u32[]{:S(2)}) collective-permute-start(f32[64,16,128]{2,0,1:T(8,128)S(1)} %get-tuple-element.15), channel_id=1, source_target_pairs={{0,1},{1,2},{2,3},{3,4},{4,5},{5,6},{6,7},{7,8},{8,9},{9,10},{10,1... | collective-permute-start | bytes 1572872 | tf_op jit(solution)/shard_map/ppermute | solution.py:24
  91.2 1.3 collective-permute-start.7
  92.5 14.2 %all_to_all.30 = f32[16,1,16]{2,1,0:T(1,128)S(1)} all-to-all(f32[16,1,16]{2,1,0:T(1,128)S(1)} %broadcast_in_dim.12), channel_id=1, replica_groups=mesh['group'=2,'row'=8,'col'=2] {'row','col'}, dimensions={0} | all-to-all | bytes 2048 | tf_op jit(solution)/shard_map/all_to_all | solution.py:104
  106.9 0.9 copy.35
  107.9 1.9 %gather_fusion.3 = f32[160,16,128]{2,1,0:T(8,128)} fusion(f32[192,16,128]{2,1,0:T(8,128)S(1)} %copy.35, s32[1024]{0:T(1024)S(1)} %pad_clamp_fusion), kind=kCustom, calls=%fused_computation.3 | custom fusion | bytes 2622080 | tf_op jit(solution)/shard_map/gather | solution.py:59
  109.8 7.1 %convolution_multiply_fusion.1 = f32[160,16,128]{2,1,0:T(8,128)S(1)} fusion(f32[160,16,128]{2,1,0:T(8,128)} %gather_fusion.3, f32[160,128,128]{2,1,0:T(8,128)} %shard_map.68, f32[160]{0:T(256)S(1)} %compare_convert_fusion), kind=kOutput, calls=%fused_computation.8 | convolution fusion | flops 251985920 | bytes 13107840 | tf_op jit(solution)/shard_map/ksj,kji->ksi/dot_general | solution.py:61
  116.8 0.8 multiply_reduce_fusion.3
  117.8 0.8 gather_fusion.4
  118.6 6.8 %convolution_multiply_fusion = f32[160,16,128]{2,1,0:T(8,128)S(1)} fusion(f32[160,16,128]{2,1,0:T(8,128)S(1)} %gather_fusion.4, f32[160]{0:T(256)S(1)} %compare_convert_fusion, f32[1,160,128,128]{3,2,1,0:T(8,128)} %param.6), kind=kOutput, calls=%fused_computation.7 | convolution fusion | flops 251985920 | bytes 13107840 | tf_op jit(solution)/shard_map/ksi,kij->ksj/dot_general | solution.py:71
  125.5 1.0 fusion
  126.5 1.0 fusion.46
  127.5 1.7 %collective-permute-start.8 = (f32[64,16,128]{2,0,1:T(8,128)}, f32[64,16,128]{2,0,1:T(8,128)S(1)}, u32[]{:S(2)}, u32[]{:S(2)}) collective-permute-start(f32[64,16,128]{2,0,1:T(8,128)} %get-tuple-element.20), channel_id=1, source_target_pairs={{0,1},{1,2},{2,3},{3,4},{4,5},{5,6},{6,7},{7,8},{8,9},{9,10},{10,1... | collective-permute-start | bytes 1572872 | tf_op jit(solution)/shard_map/ppermute | solution.py:33
  129.3 1.3 collective-permute-start.9
  130.6 14.0 %all_to_all.31 = f32[16,1,16]{2,1,0:T(1,128)S(1)} all-to-all(f32[16,1,16]{2,1,0:T(1,128)S(1)} %broadcast_in_dim.13), channel_id=1, replica_groups=mesh['group'=2,'row'=8,'col'=2] {'row','col'}, dimensions={0} | all-to-all | bytes 2048 | tf_op jit(solution)/shard_map/all_to_all | solution.py:104
  144.7 0.8 copy-done
  145.4 1.5 multiply_reduce_fusion
  147.0 10.8 %all_to_all.32 = f32[16,1,16]{2,1,0:T(1,128)S(1)} all-to-all(f32[16,1,16]{2,1,0:T(1,128)S(1)} %broadcast_in_dim.14), channel_id=1, replica_groups=mesh['group'=2,'row'=8,'col'=2] {'row','col'}, dimensions={0} | all-to-all | bytes 2048 | tf_op jit(solution)/shard_map/all_to_all | solution.py:104
  157.9 0.3 multiply_subtract_fusion
  158.2 1.6 copy_bitcast_fusion
  (43 shorter events, 1.0 us)
Async XLA Ops:
  4.0 6.9 %copy-start.1 = (s32[1,160]{1,0:T(1,128)S(1)}, s32[1,160]{1,0:T(1,128)}, u32[]{:S(2)}) copy-start(s32[1,160]{1,0:T(1,128)} %param.8) | copy-start | bytes 1924
  12.0 16.1 %collective-permute-start = (f32[64,16,128]{2,0,1:T(8,128)S(1)}, f32[64,16,128]{2,0,1:T(8,128)S(1)}, u32[]{:S(2)}, u32[]{:S(2)}) collective-permute-start(f32[64,16,128]{2,0,1:T(8,128)S(1)} %get-tuple-element.24), channel_id=1, source_target_pairs={{0,1},{1,2},{2,3},{3,4},{4,5},{5,6},{6,7},{7,8},{8,9},{9,10},{10,1... | collective-permute-start | bytes 1572872 | tf_op jit(solution)/shard_map/ppermute | solution.py:33
  14.4 13.7 %collective-permute-start.1 = (f32[64,16,128]{2,0,1:T(8,128)S(1)}, f32[64,16,128]{2,0,1:T(8,128)S(1)}, u32[]{:S(2)}, u32[]{:S(2)}) collective-permute-start(f32[64,16,128]{2,0,1:T(8,128)S(1)} %get-tuple-element.25), channel_id=1, source_target_pairs={{1,0},{2,1},{3,2},{4,3},{5,4},{6,5},{7,6},{8,7},{9,8},{10,9},{11,1... | collective-permute-start | bytes 1572872 | tf_op jit(solution)/shard_map/ppermute | solution.py:33
  28.3 22.9 %collective-permute-start.2 = (f32[64,16,128]{2,0,1:T(8,128)S(1)}, f32[64,16,128]{2,0,1:T(8,128)S(1)}, u32[]{:S(2)}, u32[]{:S(2)}) collective-permute-start(f32[64,16,128]{2,0,1:T(8,128)S(1)} %get-tuple-element.19), channel_id=1, source_target_pairs={{0,1},{1,2},{2,3},{3,4},{4,5},{5,6},{6,7},{7,8},{8,9},{9,10},{10,1... | collective-permute-start | bytes 1572872 | tf_op jit(solution)/shard_map/ppermute | solution.py:24
  33.5 17.7 %collective-permute-start.3 = (f32[64,16,128]{2,0,1:T(8,128)S(1)}, f32[64,16,128]{2,0,1:T(8,128)S(1)}, u32[]{:S(2)}, u32[]{:S(2)}) collective-permute-start(f32[64,16,128]{2,0,1:T(8,128)S(1)} %get-tuple-element.19), channel_id=1, source_target_pairs={{1,0},{2,1},{3,2},{4,3},{5,4},{6,5},{7,6},{8,7},{9,8},{10,9},{11,1... | collective-permute-start | bytes 1572872 | tf_op jit(solution)/shard_map/ppermute | solution.py:25
  35.4 15.7 %all-to-all-start = ((f32[16,2,16]{2,1,0:T(2,128)}), f32[16,2,16]{2,1,0:T(2,128)S(1)}, u32[]{:S(2)}, u32[]{:S(2)}) async-start(f32[16,2,16]{2,1,0:T(2,128)} %broadcast_in_dim.10), calls=%async_computation | async-start | bytes 32768 | tf_op jit(solution)/shard_map/all_to_all | solution.py:104
  54.2 7.1 %copy-start.2 = (s32[1,160]{1,0:T(1,128)S(1)}, s32[1,160]{1,0:T(1,128)}, u32[]{:S(2)}) copy-start(s32[1,160]{1,0:T(1,128)} %param.7) | copy-start | bytes 1924
  71.8 16.3 %collective-permute-start.4 = (f32[64,16,128]{2,0,1:T(8,128)}, f32[64,16,128]{2,0,1:T(8,128)S(1)}, u32[]{:S(2)}, u32[]{:S(2)}) collective-permute-start(f32[64,16,128]{2,0,1:T(8,128)} %get-tuple-element.22), channel_id=1, source_target_pairs={{0,1},{1,2},{2,3},{3,4},{4,5},{5,6},{6,7},{7,8},{8,9},{9,10},{10,1... | collective-permute-start | bytes 1572872 | tf_op jit(solution)/shard_map/ppermute | solution.py:33
  73.5 14.6 %collective-permute-start.5 = (f32[64,16,128]{2,0,1:T(8,128)S(1)}, f32[64,16,128]{2,0,1:T(8,128)}, u32[]{:S(2)}, u32[]{:S(2)}) collective-permute-start(f32[64,16,128]{2,0,1:T(8,128)S(1)} %get-tuple-element.23), channel_id=1, source_target_pairs={{1,0},{2,1},{3,2},{4,3},{5,4},{6,5},{7,6},{8,7},{9,8},{10,9},{11,1... | collective-permute-start | bytes 1572872 | tf_op jit(solution)/shard_map/ppermute | solution.py:33
  89.5 17.3 %collective-permute-start.6 = (f32[64,16,128]{2,0,1:T(8,128)S(1)}, f32[64,16,128]{2,0,1:T(8,128)S(1)}, u32[]{:S(2)}, u32[]{:S(2)}) collective-permute-start(f32[64,16,128]{2,0,1:T(8,128)S(1)} %get-tuple-element.15), channel_id=1, source_target_pairs={{0,1},{1,2},{2,3},{3,4},{4,5},{5,6},{6,7},{7,8},{8,9},{9,10},{10,1... | collective-permute-start | bytes 1572872 | tf_op jit(solution)/shard_map/ppermute | solution.py:24
  91.2 15.6 %collective-permute-start.7 = (f32[64,16,128]{2,0,1:T(8,128)S(1)}, f32[64,16,128]{2,0,1:T(8,128)S(1)}, u32[]{:S(2)}, u32[]{:S(2)}) collective-permute-start(f32[64,16,128]{2,0,1:T(8,128)S(1)} %get-tuple-element.15), channel_id=1, source_target_pairs={{1,0},{2,1},{3,2},{4,3},{5,4},{6,5},{7,6},{8,7},{9,8},{10,9},{11,1... | collective-permute-start | bytes 1572872 | tf_op jit(solution)/shard_map/ppermute | solution.py:25
  127.5 17.1 %collective-permute-start.8 = (f32[64,16,128]{2,0,1:T(8,128)}, f32[64,16,128]{2,0,1:T(8,128)S(1)}, u32[]{:S(2)}, u32[]{:S(2)}) collective-permute-start(f32[64,16,128]{2,0,1:T(8,128)} %get-tuple-element.20), channel_id=1, source_target_pairs={{0,1},{1,2},{2,3},{3,4},{4,5},{5,6},{6,7},{7,8},{8,9},{9,10},{10,1... | collective-permute-start | bytes 1572872 | tf_op jit(solution)/shard_map/ppermute | solution.py:33
  129.3 16.2 %collective-permute-start.9 = (f32[64,16,128]{2,0,1:T(8,128)}, f32[64,16,128]{2,0,1:T(8,128)}, u32[]{:S(2)}, u32[]{:S(2)}) collective-permute-start(f32[64,16,128]{2,0,1:T(8,128)} %get-tuple-element.21), channel_id=1, source_target_pairs={{1,0},{2,1},{3,2},{4,3},{5,4},{6,5},{7,6},{8,7},{9,8},{10,9},{11,1... | collective-permute-start | bytes 1572872 | tf_op jit(solution)/shard_map/ppermute | solution.py:33
  144.6 0.8 copy-start

commit v10 on v7

--- a/solution.py
+++ b/solution.py
@@ -35,7 +35,7 @@
 
 def transpose_blocks(tile_stack, anchor):
     slots, edge, _ = tile_stack.shape
-    step = 32 if slots % 32 == 0 else 1
+    step = 80 if slots % 80 == 0 else (32 if slots % 32 == 0 else 1)
 
     def body(anchor_ref, x_ref, o_ref):
         for i in range(step):

time: 160 us -> 156 us (0.975)
  Pallas kernels: 11.7 us -> 8.59 us
    pallas_call x1, Pallas kernels: 11.7 us -> 8.59 us  [transpose_blocks(): pl.pallas_call(body, grid=(slots // step,), in_specs=[pl.BlockSpec(memory...]
  transfers between devices with their start and end apart: 11 -> 11, of which waited for: 1 -> 1; matrix products, arithmetic and copies ran while one was open for 1% -> 1% of each run, Pallas kernels for 7% -> 6%
where the time goes in v10:
time: 156 us
  blocking collectives  51.5 us (33%)
  matrix products  38.7 us (25%)
  starting transfers between devices  29.1 us (19%)
  local copies, waits for them, and re-layouts  12.2 us (8%)
  Pallas kernels  8.59 us (6%)
  other arithmetic  7.25 us (5%)
  waiting for transfers between devices  6.5 us (4%)
  between operations  1.72 us (1%)
    all_to_all x4, blocking collectives, all_sum(): gathered = lax.all_to_all(spread, axes, 0, 0, tiled=True)  51.5 us
    dot_general x3, matrix products, transpose_local(): jnp.einsum('ski,kij->ksj', pieces, tile_stack, precision=PRODUCT_PRECISION)  20.5 us
    dot_general x2, matrix products, forward_local(): jnp.einsum('skj,kji->ksi', pieces, tile_stack, precision=PRODUCT_PRECISION)  13.9 us
    ppermute x6, starting transfers between devices, from_behind(): return lax.ppermute(shard, axis, pairs)  10.4 us
    all_to_all x1, starting transfers between devices, all_sum(): gathered = lax.all_to_all(spread, axes, 0, 0, tiled=True)  8.69 us
    pallas_call x1, Pallas kernels, transpose_blocks(): pl.pallas_call(body, grid=(slots // step,), in_specs=[pl.BlockSpec(memory...  8.59 us
    ppermute x2, starting transfers between devices, with_halo(): before = lax.ppermute(last, axis, up)  7.4 us
    all_to_all x1, waiting for transfers between devices, all_sum(): gathered = lax.all_to_all(spread, axes, 0, 0, tiled=True)  6.48 us
  transfers between devices with their start and end apart: 11, of which 1 were waited for; matrix products, arithmetic and copies ran while one was open for 1% of the time, Pallas kernels for 6%

profile of v10, /device:TPU:0, one launch (start us, length us, event | category | flops | bytes accessed | tf_op | source)
XLA Modules:
  0.0 155.7 jit_solution(63328569522769771)
XLA Ops:
  1.3 0.7 compare_select_fusion.1
  2.0 1.0 copy_bitcast_fusion.7
  3.0 0.8 gather_fusion
  3.8 6.8 %convolution_multiply_fusion.4 = f32[160,16,128]{2,1,0:T(8,128)S(1)} fusion(f32[160,16,128]{2,1,0:T(8,128)S(1)} %gather_fusion, f32[160]{0:T(256)S(1)} %compare_convert_fusion, f32[1,160,128,128]{3,2,1,0:T(8,128)} %param.6), kind=kOutput, calls=%fused_computation.16 | convolution fusion | flops 251985920 | bytes 13107840 | tf_op jit(solution)/shard_map/ski,kij->ksj/dot_general | solution.py:75
  10.7 1.0 fusion.13
  11.7 0.9 copy.81
  12.7 2.4 %collective-permute-start = (f32[16,8192]{1,0:T(8,128)S(1)}, f32[16,8192]{1,0:T(8,128)S(1)}, u32[]{:S(2)}, u32[]{:S(2)}) collective-permute-start(f32[16,8192]{1,0:T(8,128)S(1)} %get-tuple-element.28), channel_id=1, source_target_pairs={{0,1},{1,2},{2,3},{3,4},{4,5},{5,6},{6,7},{7,8},{8,9},{9,10},{10,1... | collective-permute-start | bytes 1572872 | tf_op jit(solution)/shard_map/ppermute | solution.py:33
  15.1 1.3 collective-permute-start.1
  16.4 0.5 slice.60.anchor_ref
  16.9 8.6 %shard_map.68 = f32[160,128,128]{2,1,0:T(8,128)} custom-call(f32[1,1]{1,0:T(1,128)} %slice.60.anchor_ref, f32[160,128,128]{2,1,0:T(8,128)} %bitcast.119), custom_call_target="tpu_custom_call" | custom-call | bytes 20971520 | tf_op jit(solution)/shard_map/pallas_call | solution.py:45
  25.9 5.7 %collective-permute-start.2 = (f32[16,8192]{1,0:T(8,128)S(1)}, f32[16,8192]{1,0:T(8,128)S(1)}, u32[]{:S(2)}, u32[]{:S(2)}) collective-permute-start(f32[16,8192]{1,0:T(8,128)S(1)} %get-tuple-element.23), channel_id=1, source_target_pairs={{0,1},{1,2},{2,3},{3,4},{4,5},{5,6},{6,7},{7,8},{8,9},{9,10},{10,1... | collective-permute-start | bytes 1572872 | tf_op jit(solution)/shard_map/ppermute | solution.py:24
  31.6 1.3 collective-permute-start.3
  32.9 0.6 broadcast_in_dim.10
  33.5 8.7 %all-to-all-start = ((f32[16,2,16]{2,1,0:T(2,128)}), f32[16,2,16]{2,1,0:T(2,128)S(1)}, u32[]{:S(2)}, u32[]{:S(2)}) async-start(f32[16,2,16]{2,1,0:T(2,128)} %broadcast_in_dim.10), calls=%async_computation | async-start | bytes 32768 | tf_op jit(solution)/shard_map/all_to_all | solution.py:108
  42.2 6.5 %all-to-all-done = f32[16,2,16]{2,1,0:T(2,128)S(1)} async-done(((f32[16,2,16]{2,1,0:T(2,128)}), f32[16,2,16]{2,1,0:T(2,128)S(1)}, u32[]{:S(2)}, u32[]{:S(2)}) %all-to-all-start) | async-done | bytes 2080 | tf_op jit(solution)/shard_map/all_to_all | solution.py:108
  48.9 0.8 gather_fusion.1
  49.7 6.8 %convolution_multiply_fusion.3 = f32[160,16,128]{2,1,0:T(8,128)S(1)} fusion(f32[160,128,128]{2,1,0:T(8,128)} %shard_map.68, f32[160,16,128]{2,1,0:T(8,128)S(1)} %gather_fusion.1, f32[160]{0:T(256)S(1)} %compare_convert_fusion), kind=kOutput, calls=%fused_computation.15 | convolution fusion | flops 251985920 | bytes 13107840 | tf_op jit(solution)/shard_map/skj,kji->ksi/dot_general | solution.py:63
  56.6 0.7 fusion.11
  57.3 0.3 copy-done.1
  57.6 0.3 multiply_reduce_fusion.4
  57.9 0.8 gather_fusion.2
  58.7 6.8 %convolution_multiply_fusion.2 = f32[160,16,128]{2,1,0:T(8,128)S(1)} fusion(f32[160,16,128]{2,1,0:T(8,128)S(1)} %gather_fusion.2, f32[160]{0:T(256)S(1)} %compare_convert_fusion, f32[1,160,128,128]{3,2,1,0:T(8,128)} %param.6), kind=kOutput, calls=%fused_computation.14 | convolution fusion | flops 251985920 | bytes 13107840 | tf_op jit(solution)/shard_map/ski,kij->ksj/dot_general | solution.py:75
  65.6 1.0 fusion.9
  66.6 0.9 copy.80
  67.5 0.9 fusion.44
  68.3 1.7 %collective-permute-start.4 = (f32[16,8192]{1,0:T(8,128)}, f32[16,8192]{1,0:T(8,128)S(1)}, u32[]{:S(2)}, u32[]{:S(2)}) collective-permute-start(f32[16,8192]{1,0:T(8,128)} %get-tuple-element.26), channel_id=1, source_target_pairs={{0,1},{1,2},{2,3},{3,4},{4,5},{5,6},{6,7},{7,8},{8,9},{9,10},{10,1... | collective-permute-start | bytes 1572872 | tf_op jit(solution)/shard_map/ppermute | solution.py:33
  70.0 1.3 collective-permute-start.5
  71.3 13.3 %all_to_all.29 = f32[16,1,16]{2,1,0:T(1,128)S(1)} all-to-all(f32[16,1,16]{2,1,0:T(1,128)S(1)} %broadcast_in_dim.11), channel_id=1, replica_groups=mesh['group'=2,'row'=8,'col'=2] {'row','col'}, dimensions={0} | all-to-all | bytes 2048 | tf_op jit(solution)/shard_map/all_to_all | solution.py:108
  84.6 1.3 multiply_reduce_fusion.1
  86.0 1.7 %collective-permute-start.6 = (f32[16,8192]{1,0:T(8,128)S(1)}, f32[16,8192]{1,0:T(8,128)S(1)}, u32[]{:S(2)}, u32[]{:S(2)}) collective-permute-start(f32[16,8192]{1,0:T(8,128)S(1)} %get-tuple-element.17), channel_id=1, source_target_pairs={{0,1},{1,2},{2,3},{3,4},{4,5},{5,6},{6,7},{7,8},{8,9},{9,10},{10,1... | collective-permute-start | bytes 1572872 | tf_op jit(solution)/shard_map/ppermute | solution.py:24
  87.7 1.3 collective-permute-start.7
  89.0 14.2 %all_to_all.30 = f32[16,1,16]{2,1,0:T(1,128)S(1)} all-to-all(f32[16,1,16]{2,1,0:T(1,128)S(1)} %broadcast_in_dim.12), channel_id=1, replica_groups=mesh['group'=2,'row'=8,'col'=2] {'row','col'}, dimensions={0} | all-to-all | bytes 2048 | tf_op jit(solution)/shard_map/all_to_all | solution.py:108
  103.3 1.2 copy_bitcast_fusion.3
  104.5 1.9 %gather_fusion.3 = f32[160,16,128]{2,1,0:T(8,128)} fusion(f32[16,192,128]{2,0,1:T(8,128)S(1)} %copy_bitcast_fusion.3, s32[1024]{0:T(1024)S(1)} %pad_clamp_fusion), kind=kCustom, calls=%fused_computation.3 | custom fusion | bytes 2622080 | tf_op jit(solution)/shard_map/gather | solution.py:61
  106.4 7.1 %convolution_multiply_fusion.1 = f32[160,16,128]{2,1,0:T(8,128)S(1)} fusion(f32[160,128,128]{2,1,0:T(8,128)} %shard_map.68, f32[160,16,128]{2,1,0:T(8,128)} %gather_fusion.3, f32[160]{0:T(256)S(1)} %compare_convert_fusion), kind=kOutput, calls=%fused_computation.13 | convolution fusion | flops 251985920 | bytes 13107840 | tf_op jit(solution)/shard_map/skj,kji->ksi/dot_general | solution.py:63
  113.4 0.7 fusion.7
  114.1 0.3 multiply_reduce_fusion.3
  114.4 0.8 gather_fusion.4
  115.3 6.8 %convolution_multiply_fusion = f32[160,16,128]{2,1,0:T(8,128)S(1)} fusion(f32[160,16,128]{2,1,0:T(8,128)S(1)} %gather_fusion.4, f32[160]{0:T(256)S(1)} %compare_convert_fusion, f32[1,160,128,128]{3,2,1,0:T(8,128)} %param.6), kind=kOutput, calls=%fused_computation.12 | convolution fusion | flops 251985920 | bytes 13107840 | tf_op jit(solution)/shard_map/ski,kij->ksj/dot_general | solution.py:75
  122.1 1.0 fusion.5
  123.1 0.9 copy.79
  124.0 0.9 fusion.43
  124.9 2.5 %collective-permute-start.8 = (f32[16,8192]{1,0:T(8,128)}, f32[16,8192]{1,0:T(8,128)}, u32[]{:S(2)}, u32[]{:S(2)}) collective-permute-start(f32[16,8192]{1,0:T(8,128)} %get-tuple-element.24), channel_id=1, source_target_pairs={{0,1},{1,2},{2,3},{3,4},{4,5},{5,6},{6,7},{7,8},{8,9},{9,10},{10,1... | collective-permute-start | bytes 1572872 | tf_op jit(solution)/shard_map/ppermute | solution.py:33
  127.4 1.3 collective-permute-start.9
  128.7 13.3 %all_to_all.31 = f32[16,1,16]{2,1,0:T(1,128)S(1)} all-to-all(f32[16,1,16]{2,1,0:T(1,128)S(1)} %broadcast_in_dim.13), channel_id=1, replica_groups=mesh['group'=2,'row'=8,'col'=2] {'row','col'}, dimensions={0} | all-to-all | bytes 2048 | tf_op jit(solution)/shard_map/all_to_all | solution.py:108
  142.0 1.5 multiply_reduce_fusion
  143.5 10.8 %all_to_all.32 = f32[16,1,16]{2,1,0:T(1,128)S(1)} all-to-all(f32[16,1,16]{2,1,0:T(1,128)S(1)} %broadcast_in_dim.14), channel_id=1, replica_groups=mesh['group'=2,'row'=8,'col'=2] {'row','col'}, dimensions={0} | all-to-all | bytes 2048 | tf_op jit(solution)/shard_map/all_to_all | solution.py:108
  154.4 1.2 multiply_subtract_fusion
  (46 shorter events, 1.0 us)
Async XLA Ops:
  3.8 6.9 %copy-start.2 = (s32[1,160]{1,0:T(1,128)S(1)}, s32[1,160]{1,0:T(1,128)}, u32[]{:S(2)}) copy-start(s32[1,160]{1,0:T(1,128)} %param.8) | copy-start | bytes 1924
  12.7 13.0 %collective-permute-start = (f32[16,8192]{1,0:T(8,128)S(1)}, f32[16,8192]{1,0:T(8,128)S(1)}, u32[]{:S(2)}, u32[]{:S(2)}) collective-permute-start(f32[16,8192]{1,0:T(8,128)S(1)} %get-tuple-element.28), channel_id=1, source_target_pairs={{0,1},{1,2},{2,3},{3,4},{4,5},{5,6},{6,7},{7,8},{8,9},{9,10},{10,1... | collective-permute-start | bytes 1572872 | tf_op jit(solution)/shard_map/ppermute | solution.py:33
  15.1 10.6 %collective-permute-start.1 = (f32[16,8192]{1,0:T(8,128)S(1)}, f32[16,8192]{1,0:T(8,128)S(1)}, u32[]{:S(2)}, u32[]{:S(2)}) collective-permute-start(f32[16,8192]{1,0:T(8,128)S(1)} %get-tuple-element.29), channel_id=1, source_target_pairs={{1,0},{2,1},{3,2},{4,3},{5,4},{6,5},{7,6},{8,7},{9,8},{10,9},{11,1... | collective-permute-start | bytes 1572872 | tf_op jit(solution)/shard_map/ppermute | solution.py:33
  16.9 8.6 %copy-start = (f32[16,4096]{1,0:T(8,128)S(1)}, f32[16,4096]{1,0:T(8,128)}, u32[]{:S(2)}) copy-start(f32[16,4096]{1,0:T(8,128)} %param.5) | copy-start | bytes 786436
  25.9 22.9 %collective-permute-start.2 = (f32[16,8192]{1,0:T(8,128)S(1)}, f32[16,8192]{1,0:T(8,128)S(1)}, u32[]{:S(2)}, u32[]{:S(2)}) collective-permute-start(f32[16,8192]{1,0:T(8,128)S(1)} %get-tuple-element.23), channel_id=1, source_target_pairs={{0,1},{1,2},{2,3},{3,4},{4,5},{5,6},{6,7},{7,8},{8,9},{9,10},{10,1... | collective-permute-start | bytes 1572872 | tf_op jit(solution)/shard_map/ppermute | solution.py:24
  31.6 17.2 %collective-permute-start.3 = (f32[16,8192]{1,0:T(8,128)S(1)}, f32[16,8192]{1,0:T(8,128)S(1)}, u32[]{:S(2)}, u32[]{:S(2)}) collective-permute-start(f32[16,8192]{1,0:T(8,128)S(1)} %get-tuple-element.23), channel_id=1, source_target_pairs={{1,0},{2,1},{3,2},{4,3},{5,4},{6,5},{7,6},{8,7},{9,8},{10,9},{11,1... | collective-permute-start | bytes 1572872 | tf_op jit(solution)/shard_map/ppermute | solution.py:25
  33.5 15.2 %all-to-all-start = ((f32[16,2,16]{2,1,0:T(2,128)}), f32[16,2,16]{2,1,0:T(2,128)S(1)}, u32[]{:S(2)}, u32[]{:S(2)}) async-start(f32[16,2,16]{2,1,0:T(2,128)} %broadcast_in_dim.10), calls=%async_computation | async-start | bytes 32768 | tf_op jit(solution)/shard_map/all_to_all | solution.py:108
  49.7 6.9 %copy-start.3 = (s32[1,160]{1,0:T(1,128)S(1)}, s32[1,160]{1,0:T(1,128)}, u32[]{:S(2)}) copy-start(s32[1,160]{1,0:T(1,128)} %param.7) | copy-start | bytes 1924
  56.6 1.0 copy-start.1
  68.3 16.3 %collective-permute-start.4 = (f32[16,8192]{1,0:T(8,128)}, f32[16,8192]{1,0:T(8,128)S(1)}, u32[]{:S(2)}, u32[]{:S(2)}) collective-permute-start(f32[16,8192]{1,0:T(8,128)} %get-tuple-element.26), channel_id=1, source_target_pairs={{0,1},{1,2},{2,3},{3,4},{4,5},{5,6},{6,7},{7,8},{8,9},{9,10},{10,1... | collective-permute-start | bytes 1572872 | tf_op jit(solution)/shard_map/ppermute | solution.py:33
  70.0 14.6 %collective-permute-start.5 = (f32[16,8192]{1,0:T(8,128)S(1)}, f32[16,8192]{1,0:T(8,128)}, u32[]{:S(2)}, u32[]{:S(2)}) collective-permute-start(f32[16,8192]{1,0:T(8,128)S(1)} %get-tuple-element.27), channel_id=1, source_target_pairs={{1,0},{2,1},{3,2},{4,3},{5,4},{6,5},{7,6},{8,7},{9,8},{10,9},{11,1... | collective-permute-start | bytes 1572872 | tf_op jit(solution)/shard_map/ppermute | solution.py:33
  86.0 17.3 %collective-permute-start.6 = (f32[16,8192]{1,0:T(8,128)S(1)}, f32[16,8192]{1,0:T(8,128)S(1)}, u32[]{:S(2)}, u32[]{:S(2)}) collective-permute-start(f32[16,8192]{1,0:T(8,128)S(1)} %get-tuple-element.17), channel_id=1, source_target_pairs={{0,1},{1,2},{2,3},{3,4},{4,5},{5,6},{6,7},{7,8},{8,9},{9,10},{10,1... | collective-permute-start | bytes 1572872 | tf_op jit(solution)/shard_map/ppermute | solution.py:24
  87.7 15.6 %collective-permute-start.7 = (f32[16,8192]{1,0:T(8,128)S(1)}, f32[16,8192]{1,0:T(8,128)}, u32[]{:S(2)}, u32[]{:S(2)}) collective-permute-start(f32[16,8192]{1,0:T(8,128)S(1)} %get-tuple-element.17), channel_id=1, source_target_pairs={{1,0},{2,1},{3,2},{4,3},{5,4},{6,5},{7,6},{8,7},{9,8},{10,9},{11,1... | collective-permute-start | bytes 1572872 | tf_op jit(solution)/shard_map/ppermute | solution.py:25
  124.9 17.1 %collective-permute-start.8 = (f32[16,8192]{1,0:T(8,128)}, f32[16,8192]{1,0:T(8,128)}, u32[]{:S(2)}, u32[]{:S(2)}) collective-permute-start(f32[16,8192]{1,0:T(8,128)} %get-tuple-element.24), channel_id=1, source_target_pairs={{0,1},{1,2},{2,3},{3,4},{4,5},{5,6},{6,7},{7,8},{8,9},{9,10},{10,1... | collective-permute-start | bytes 1572872 | tf_op jit(solution)/shard_map/ppermute | solution.py:33
  127.4 14.6 %collective-permute-start.9 = (f32[16,8192]{1,0:T(8,128)S(1)}, f32[16,8192]{1,0:T(8,128)}, u32[]{:S(2)}, u32[]{:S(2)}) collective-permute-start(f32[16,8192]{1,0:T(8,128)S(1)} %get-tuple-element.25), channel_id=1, source_target_pairs={{1,0},{2,1},{3,2},{4,3},{5,4},{6,5},{7,6},{8,7},{9,8},{10,9},{11,1... | collective-permute-start | bytes 1572872 | tf_op jit(solution)/shard_map/ppermute | solution.py:33

commit v11 on v10

--- a/solution.py
+++ b/solution.py
@@ -129,8 +129,11 @@
         beside=lambda anchor: transpose_blocks(tile_stack, anchor),
     )
 
-    def forward(vector):
-        return forward_apply(vector, tile_stack_t, rows_idx, cols_idx, live_slot)
+    def halo(vector):
+        return with_halo(vector, ((axes, 1),), vector.shape[1])
+
+    def forward_window(window):
+        return forward_local(window, tile_stack_t, rows_idx, cols_idx, live_slot)
 
     totals = all_sum(jnp.stack([squares(observed), squares(start_raw)]), axes)
     row_norm = jnp.sqrt(totals[0] + 1e-06)
@@ -138,7 +141,9 @@
     scale = row_norm * col_norm
     left_vec = observed / row_norm[:, None]
     right_vec = start_raw / scale[:, None]
-    left_prod = forward(start_raw)
+    start_window = halo(start_raw)
+    left_prod = forward_window(start_window)
+    right_window = start_window / scale[:, None]
     left_raw = left_prod / scale[:, None] - col_norm[:, None] * left_vec
     dir_now = right_vec
     solution = jnp.zeros_like(dir_now)
@@ -150,11 +155,13 @@
         left_vec = left_raw / row_norm[:, None]
         right_raw = right_prod / row_norm[:, None] - row_norm[:, None] * right_vec
         if iteration + 1 < ITERATIONS:
-            left_prod = forward(right_raw)
+            raw_window = halo(right_prod) / row_norm[:, None] - row_norm[:, None] * right_window
+            left_prod = forward_window(raw_window)
         col_norm = jnp.sqrt(all_sum(squares(right_raw), axes) + 1e-06)
         right_vec = right_raw / col_norm[:, None]
         if iteration + 1 < ITERATIONS:
             left_raw = left_prod / col_norm[:, None] - col_norm[:, None] * left_vec
+            right_window = raw_window / col_norm[:, None]
         diag_new = jnp.sqrt(diag_bar * diag_bar + row_norm * row_norm)
         rot_cosine = diag_bar / diag_new
         rot_sine = row_norm / diag_new

time: 156 us -> 160 us (1.026)
  blocking collectives: 51.5 us -> 23.8 us
  starting transfers between devices: 29.1 us -> 41.2 us
  waiting for transfers between devices: 6.5 us -> 17.6 us
  local copies, waits for them, and re-layouts: 12.2 us -> 19.7 us
    all_to_all x4 -> x2, blocking collectives: 51.5 us -> 23.8 us  [all_sum(): gathered = lax.all_to_all(spread, axes, 0, 0, tiled=True)]
    all_to_all x1 -> x3, waiting for transfers between devices: 6.48 us -> 17.6 us  [all_sum(): gathered = lax.all_to_all(spread, axes, 0, 0, tiled=True)]
    all_to_all x1 -> x3, starting transfers between devices: 8.69 us -> 19.5 us  [all_sum(): gathered = lax.all_to_all(spread, axes, 0, 0, tiled=True)]
    unnamed x11 -> x23, local copies, waits for them, and re-layouts: 3.03 us -> 6.35 us
    concatenate x0 -> x6, local copies, waits for them, and re-layouts: none -> 2.6 us  [with_halo(): shard = jnp.concatenate([before, shard, after], axis=dim)]
  transfers between devices with their start and end apart: 11 -> 13, of which waited for: 1 -> 3; matrix products, arithmetic and copies ran while one was open for 1% -> 3% of each run, Pallas kernels for 6% -> 5%
where the time goes in v11:
time: 160 us; the launch traced here: 159 us
  starting transfers between devices  41.2 us (26%)
  matrix products  38.7 us (24%)
  blocking collectives  23.8 us (15%)
  local copies, waits for them, and re-layouts  19.7 us (12%)
  waiting for transfers between devices  17.6 us (11%)
  Pallas kernels  8.57 us (5%)
  other arithmetic  7.9 us (5%)
  between operations  1.8 us (1%)
    all_to_all x2, blocking collectives, all_sum(): gathered = lax.all_to_all(spread, axes, 0, 0, tiled=True)  23.8 us
    dot_general x3, matrix products, transpose_local(): jnp.einsum('ski,kij->ksj', pieces, tile_stack, precision=PRODUCT_PRECISION)  20.5 us
    all_to_all x3, starting transfers between devices, all_sum(): gathered = lax.all_to_all(spread, axes, 0, 0, tiled=True)  19.5 us
    all_to_all x3, waiting for transfers between devices, all_sum(): gathered = lax.all_to_all(spread, axes, 0, 0, tiled=True)  17.6 us
    dot_general x2, matrix products, forward_local(): jnp.einsum('skj,kji->ksi', pieces, tile_stack, precision=PRODUCT_PRECISION)  13.9 us
    ppermute x6, starting transfers between devices, from_behind(): return lax.ppermute(shard, axis, pairs)  10.4 us
    ppermute x2, starting transfers between devices, with_halo(): before = lax.ppermute(last, axis, up)  8.75 us
    pallas_call x1, Pallas kernels, transpose_blocks(): pl.pallas_call(body, grid=(slots // step,), in_specs=[pl.BlockSpec(memory...  8.57 us
  transfers between devices with their start and end apart: 13, of which 3 were waited for; matrix products, arithmetic and copies ran while one was open for 3% of the time, Pallas kernels for 5%

profile of v11, /device:TPU:0, one launch (start us, length us, event | category | flops | bytes accessed | tf_op | source)
XLA Modules:
  0.0 159.3 jit_solution(16405161853859157743)
XLA Ops:
  2.0 1.0 copy_bitcast_fusion.12
  3.0 0.8 gather_fusion
  3.8 6.8 %convolution_multiply_fusion.4 = f32[160,16,128]{2,1,0:T(8,128)S(1)} fusion(f32[160,16,128]{2,1,0:T(8,128)S(1)} %gather_fusion, f32[160]{0:T(256)S(1)} %compare_convert_fusion, f32[1,160,128,128]{3,2,1,0:T(8,128)} %param.6), kind=kOutput, calls=%fused_computation.18 | convolution fusion | flops 251985920 | bytes 13107840 | tf_op jit(solution)/shard_map/ski,kij->ksj/dot_general | solution.py:75
  10.7 1.0 fusion.15
  11.7 0.9 copy.111
  12.7 2.4 %collective-permute-start = (f32[16,8192]{1,0:T(8,128)S(1)}, f32[16,8192]{1,0:T(8,128)S(1)}, u32[]{:S(2)}, u32[]{:S(2)}) collective-permute-start(f32[16,8192]{1,0:T(8,128)S(1)} %get-tuple-element.28), channel_id=1, source_target_pairs={{0,1},{1,2},{2,3},{3,4},{4,5},{5,6},{6,7},{7,8},{8,9},{9,10},{10,1... | collective-permute-start | bytes 1572872 | tf_op jit(solution)/shard_map/ppermute | solution.py:33
  15.1 1.3 collective-permute-start.1
  16.9 8.6 %shard_map.68 = f32[160,128,128]{2,1,0:T(8,128)} custom-call(f32[1,1]{1,0:T(1,128)} %slice.60.anchor_ref, f32[160,128,128]{2,1,0:T(8,128)} %bitcast.144), custom_call_target="tpu_custom_call" | custom-call | bytes 20971520 | tf_op jit(solution)/shard_map/pallas_call | solution.py:45
  25.9 5.7 %collective-permute-start.2 = (f32[16,8192]{1,0:T(8,128)S(1)}, f32[16,8192]{1,0:T(8,128)S(1)}, u32[]{:S(2)}, u32[]{:S(2)}) collective-permute-start(f32[16,8192]{1,0:T(8,128)S(1)} %get-tuple-element.23), channel_id=1, source_target_pairs={{0,1},{1,2},{2,3},{3,4},{4,5},{5,6},{6,7},{7,8},{8,9},{9,10},{10,1... | collective-permute-start | bytes 1572872 | tf_op jit(solution)/shard_map/ppermute | solution.py:24
  31.6 1.3 collective-permute-start.3
  33.5 8.7 %all-to-all-start = ((f32[16,2,16]{2,1,0:T(2,128)}), f32[16,2,16]{2,1,0:T(2,128)S(1)}, u32[]{:S(2)}, u32[]{:S(2)}) async-start(f32[16,2,16]{2,1,0:T(2,128)} %broadcast_in_dim.10), calls=%async_computation | async-start | bytes 32768 | tf_op jit(solution)/shard_map/all_to_all | solution.py:108
  42.2 6.5 %all-to-all-done = f32[16,2,16]{2,1,0:T(2,128)S(1)} async-done(((f32[16,2,16]{2,1,0:T(2,128)}), f32[16,2,16]{2,1,0:T(2,128)S(1)}, u32[]{:S(2)}, u32[]{:S(2)}) %all-to-all-start) | async-done | bytes 2080 | tf_op jit(solution)/shard_map/all_to_all | solution.py:108
  48.8 0.8 copy-done.3
  49.6 0.8 copy-done.5
  50.5 0.8 gather_fusion.1
  51.3 6.8 %convolution_multiply_fusion.3 = f32[160,16,128]{2,1,0:T(8,128)S(1)} fusion(f32[160,128,128]{2,1,0:T(8,128)} %shard_map.68, f32[160,16,128]{2,1,0:T(8,128)S(1)} %gather_fusion.1, f32[160]{0:T(256)S(1)} %compare_convert_fusion), kind=kOutput, calls=%fused_computation.17 | convolution fusion | flops 251985920 | bytes 13107840 | tf_op jit(solution)/shard_map/skj,kji->ksi/dot_general | solution.py:63
  59.5 0.8 gather_fusion.2
  60.3 6.8 %convolution_multiply_fusion.2 = f32[160,16,128]{2,1,0:T(8,128)S(1)} fusion(f32[160,16,128]{2,1,0:T(8,128)S(1)} %gather_fusion.2, f32[160]{0:T(256)S(1)} %compare_convert_fusion, f32[1,160,128,128]{3,2,1,0:T(8,128)} %param.6), kind=kOutput, calls=%fused_computation.16 | convolution fusion | flops 251985920 | bytes 13107840 | tf_op jit(solution)/shard_map/ski,kij->ksj/dot_general | solution.py:75
  67.2 1.0 fusion.11
  68.2 0.9 copy.110
  69.1 1.0 fusion.44
  70.1 2.5 %collective-permute-start.4 = (f32[16,8192]{1,0:T(8,128)}, f32[16,8192]{1,0:T(8,128)}, u32[]{:S(2)}, u32[]{:S(2)}) collective-permute-start(f32[16,8192]{1,0:T(8,128)} %get-tuple-element.26), channel_id=1, source_target_pairs={{0,1},{1,2},{2,3},{3,4},{4,5},{5,6},{6,7},{7,8},{8,9},{9,10},{10,1... | collective-permute-start | bytes 1572872 | tf_op jit(solution)/shard_map/ppermute | solution.py:33
  72.6 1.3 collective-permute-start.5
  74.5 6.3 %all-to-all-start.1 = ((f32[16,1,16]{2,1,0:T(1,128)}), f32[16,1,16]{2,1,0:T(1,128)S(1)}, u32[]{:S(2)}, u32[]{:S(2)}) async-start(f32[16,1,16]{2,1,0:T(1,128)} %broadcast_in_dim.11), calls=%async_computation.1 | async-start | bytes 16384 | tf_op jit(solution)/shard_map/all_to_all | solution.py:108
  80.8 0.8 copy_bitcast_fusion.4
  81.7 5.6 %all-to-all-done.1 = f32[16,1,16]{2,1,0:T(1,128)S(1)} async-done(((f32[16,1,16]{2,1,0:T(1,128)}), f32[16,1,16]{2,1,0:T(1,128)S(1)}, u32[]{:S(2)}, u32[]{:S(2)}) %all-to-all-start.1) | async-done | bytes 1056 | tf_op jit(solution)/shard_map/all_to_all | solution.py:108
  87.3 1.6 multiply_reduce_fusion.1
  88.8 1.3 collective-permute-start.7
  90.1 0.8 copy_bitcast_fusion.6
  91.0 3.1 %collective-permute-start.6 = (f32[16,8192]{1,0:T(8,128)S(1)}, f32[16,8192]{1,0:T(8,128)S(1)}, u32[]{:S(2)}, u32[]{:S(2)}) collective-permute-start(f32[16,8192]{1,0:T(8,128)S(1)} %get-tuple-element.17), channel_id=1, source_target_pairs={{0,1},{1,2},{2,3},{3,4},{4,5},{5,6},{6,7},{7,8},{8,9},{9,10},{10,1... | collective-permute-start | bytes 1572872 | tf_op jit(solution)/shard_map/ppermute | solution.py:24
  94.6 4.5 %all-to-all-start.2 = ((f32[16,1,16]{2,1,0:T(1,128)}), f32[16,1,16]{2,1,0:T(1,128)S(1)}, u32[]{:S(2)}, u32[]{:S(2)}) async-start(f32[16,1,16]{2,1,0:T(1,128)} %broadcast_in_dim.12), calls=%async_computation.2 | async-start | bytes 16384 | tf_op jit(solution)/shard_map/all_to_all | solution.py:108
  99.2 0.8 copy_bitcast_fusion.8
  100.0 5.5 %all-to-all-done.2 = f32[16,1,16]{2,1,0:T(1,128)S(1)} async-done(((f32[16,1,16]{2,1,0:T(1,128)}), f32[16,1,16]{2,1,0:T(1,128)S(1)}, u32[]{:S(2)}, u32[]{:S(2)}) %all-to-all-start.2) | async-done | bytes 1056 | tf_op jit(solution)/shard_map/all_to_all | solution.py:108
  105.7 0.9 copy-done.2
  106.6 1.5 fusion
  108.1 1.9 %gather_fusion.3 = f32[160,16,128]{2,1,0:T(8,128)} fusion(f32[16,192,128]{2,0,1:T(8,128)S(1)} %fusion, s32[1024]{0:T(1024)S(1)} %pad_clamp_fusion), kind=kCustom, calls=%fused_computation.3 | custom fusion | bytes 2622080 | tf_op jit(solution)/shard_map/gather | solution.py:61
  110.0 7.1 %convolution_multiply_fusion.1 = f32[160,16,128]{2,1,0:T(8,128)S(1)} fusion(f32[160,128,128]{2,1,0:T(8,128)} %shard_map.68, f32[160,16,128]{2,1,0:T(8,128)} %gather_fusion.3, f32[160]{0:T(256)S(1)} %compare_convert_fusion), kind=kOutput, calls=%fused_computation.15 | convolution fusion | flops 251985920 | bytes 13107840 | tf_op jit(solution)/shard_map/skj,kji->ksi/dot_general | solution.py:63
  118.0 0.8 gather_fusion.4
  118.9 6.8 %convolution_multiply_fusion = f32[160,16,128]{2,1,0:T(8,128)S(1)} fusion(f32[160,16,128]{2,1,0:T(8,128)S(1)} %gather_fusion.4, f32[160]{0:T(256)S(1)} %compare_convert_fusion, f32[1,160,128,128]{3,2,1,0:T(8,128)} %param.6), kind=kOutput, calls=%fused_computation.14 | convolution fusion | flops 251985920 | bytes 13107840 | tf_op jit(solution)/shard_map/ski,kij->ksj/dot_general | solution.py:75
  125.7 1.0 fusion.7
  126.7 0.9 copy.109
  127.6 1.0 fusion.43
  128.7 1.7 %collective-permute-start.8 = (f32[16,8192]{1,0:T(8,128)}, f32[16,8192]{1,0:T(8,128)S(1)}, u32[]{:S(2)}, u32[]{:S(2)}) collective-permute-start(f32[16,8192]{1,0:T(8,128)} %get-tuple-element.24), channel_id=1, source_target_pairs={{0,1},{1,2},{2,3},{3,4},{4,5},{5,6},{6,7},{7,8},{8,9},{9,10},{10,1... | collective-permute-start | bytes 1572872 | tf_op jit(solution)/shard_map/ppermute | solution.py:33
  130.4 1.3 collective-permute-start.9
  131.7 13.0 %all_to_all.29 = f32[16,1,16]{2,1,0:T(1,128)S(1)} all-to-all(f32[16,1,16]{2,1,0:T(1,128)S(1)} %broadcast_in_dim.13), channel_id=1, replica_groups=mesh['group'=2,'row'=8,'col'=2] {'row','col'}, dimensions={0} | all-to-all | bytes 2048 | tf_op jit(solution)/shard_map/all_to_all | solution.py:108
  145.6 1.6 multiply_reduce_fusion
  147.1 10.8 %all_to_all.30 = f32[16,1,16]{2,1,0:T(1,128)S(1)} all-to-all(f32[16,1,16]{2,1,0:T(1,128)S(1)} %broadcast_in_dim.14), channel_id=1, replica_groups=mesh['group'=2,'row'=8,'col'=2] {'row','col'}, dimensions={0} | all-to-all | bytes 2048 | tf_op jit(solution)/shard_map/all_to_all | solution.py:108
  158.1 1.3 multiply_subtract_fusion
  (66 shorter events, 7.0 us)
Async XLA Ops:
  3.8 6.9 %copy-start.8 = (s32[1,160]{1,0:T(1,128)S(1)}, s32[1,160]{1,0:T(1,128)}, u32[]{:S(2)}) copy-start(s32[1,160]{1,0:T(1,128)} %param.8) | copy-start | bytes 1924
  12.7 12.9 %collective-permute-start = (f32[16,8192]{1,0:T(8,128)S(1)}, f32[16,8192]{1,0:T(8,128)S(1)}, u32[]{:S(2)}, u32[]{:S(2)}) collective-permute-start(f32[16,8192]{1,0:T(8,128)S(1)} %get-tuple-element.28), channel_id=1, source_target_pairs={{0,1},{1,2},{2,3},{3,4},{4,5},{5,6},{6,7},{7,8},{8,9},{9,10},{10,1... | collective-permute-start | bytes 1572872 | tf_op jit(solution)/shard_map/ppermute | solution.py:33
  15.1 10.6 %collective-permute-start.1 = (f32[16,8192]{1,0:T(8,128)S(1)}, f32[16,8192]{1,0:T(8,128)S(1)}, u32[]{:S(2)}, u32[]{:S(2)}) collective-permute-start(f32[16,8192]{1,0:T(8,128)S(1)} %get-tuple-element.29), channel_id=1, source_target_pairs={{1,0},{2,1},{3,2},{4,3},{5,4},{6,5},{7,6},{8,7},{9,8},{10,9},{11,1... | collective-permute-start | bytes 1572872 | tf_op jit(solution)/shard_map/ppermute | solution.py:33
  16.9 8.6 %copy-start = (f32[16,4096]{1,0:T(8,128)S(1)}, f32[16,4096]{1,0:T(8,128)}, u32[]{:S(2)}) copy-start(f32[16,4096]{1,0:T(8,128)} %param.5) | copy-start | bytes 786436
  25.9 22.9 %collective-permute-start.2 = (f32[16,8192]{1,0:T(8,128)S(1)}, f32[16,8192]{1,0:T(8,128)S(1)}, u32[]{:S(2)}, u32[]{:S(2)}) collective-permute-start(f32[16,8192]{1,0:T(8,128)S(1)} %get-tuple-element.23), channel_id=1, source_target_pairs={{0,1},{1,2},{2,3},{3,4},{4,5},{5,6},{6,7},{7,8},{8,9},{9,10},{10,1... | collective-permute-start | bytes 1572872 | tf_op jit(solution)/shard_map/ppermute | solution.py:24
  31.6 17.2 %collective-permute-start.3 = (f32[16,8192]{1,0:T(8,128)S(1)}, f32[16,8192]{1,0:T(8,128)S(1)}, u32[]{:S(2)}, u32[]{:S(2)}) collective-permute-start(f32[16,8192]{1,0:T(8,128)S(1)} %get-tuple-element.23), channel_id=1, source_target_pairs={{1,0},{2,1},{3,2},{4,3},{5,4},{6,5},{7,6},{8,7},{9,8},{10,9},{11,1... | collective-permute-start | bytes 1572872 | tf_op jit(solution)/shard_map/ppermute | solution.py:25
  33.5 15.2 %all-to-all-start = ((f32[16,2,16]{2,1,0:T(2,128)}), f32[16,2,16]{2,1,0:T(2,128)S(1)}, u32[]{:S(2)}, u32[]{:S(2)}) async-start(f32[16,2,16]{2,1,0:T(2,128)} %broadcast_in_dim.10), calls=%async_computation | async-start | bytes 32768 | tf_op jit(solution)/shard_map/all_to_all | solution.py:108
  48.7 0.8 copy-start.3
  49.6 0.8 copy-start.5
  51.3 6.9 %copy-start.9 = (s32[1,160]{1,0:T(1,128)S(1)}, s32[1,160]{1,0:T(1,128)}, u32[]{:S(2)}) copy-start(s32[1,160]{1,0:T(1,128)} %param.7) | copy-start | bytes 1924
  58.2 1.0 copy-start.1
  69.1 11.7 %copy-start.6 = (f32[16,8192]{1,0:T(8,128)S(1)}, f32[16,8192]{1,0:T(8,128)}, u32[]{:S(2)}) copy-start(f32[16,8192]{1,0:T(8,128)} %copy-done.5) | copy-start | bytes 1572868
  70.1 17.1 %collective-permute-start.4 = (f32[16,8192]{1,0:T(8,128)}, f32[16,8192]{1,0:T(8,128)}, u32[]{:S(2)}, u32[]{:S(2)}) collective-permute-start(f32[16,8192]{1,0:T(8,128)} %get-tuple-element.26), channel_id=1, source_target_pairs={{0,1},{1,2},{2,3},{3,4},{4,5},{5,6},{6,7},{7,8},{8,9},{9,10},{10,1... | collective-permute-start | bytes 1572872 | tf_op jit(solution)/shard_map/ppermute | solution.py:33
  72.6 14.7 %collective-permute-start.5 = (f32[16,8192]{1,0:T(8,128)}, f32[16,8192]{1,0:T(8,128)}, u32[]{:S(2)}, u32[]{:S(2)}) collective-permute-start(f32[16,8192]{1,0:T(8,128)} %get-tuple-element.27), channel_id=1, source_target_pairs={{1,0},{2,1},{3,2},{4,3},{5,4},{6,5},{7,6},{8,7},{9,8},{10,9},{11,1... | collective-permute-start | bytes 1572872 | tf_op jit(solution)/shard_map/ppermute | solution.py:33
  74.5 12.7 %all-to-all-start.1 = ((f32[16,1,16]{2,1,0:T(1,128)}), f32[16,1,16]{2,1,0:T(1,128)S(1)}, u32[]{:S(2)}, u32[]{:S(2)}) async-start(f32[16,1,16]{2,1,0:T(1,128)} %broadcast_in_dim.11), calls=%async_computation.1 | async-start | bytes 16384 | tf_op jit(solution)/shard_map/all_to_all | solution.py:108
  87.3 2.9 %copy-start.4 = (f32[16,8192]{1,0:T(8,128)S(1)}, f32[16,8192]{1,0:T(8,128)}, u32[]{:S(2)}) copy-start(f32[16,8192]{1,0:T(8,128)} %copy-done.3) | copy-start | bytes 1572868
  88.8 16.7 %collective-permute-start.7 = (f32[16,8192]{1,0:T(8,128)S(1)}, f32[16,8192]{1,0:T(8,128)S(1)}, u32[]{:S(2)}, u32[]{:S(2)}) collective-permute-start(f32[16,8192]{1,0:T(8,128)S(1)} %get-tuple-element.17), channel_id=1, source_target_pairs={{1,0},{2,1},{3,2},{4,3},{5,4},{6,5},{7,6},{8,7},{9,8},{10,9},{11,1... | collective-permute-start | bytes 1572872 | tf_op jit(solution)/shard_map/ppermute | solution.py:25
  91.0 14.7 %collective-permute-start.6 = (f32[16,8192]{1,0:T(8,128)S(1)}, f32[16,8192]{1,0:T(8,128)S(1)}, u32[]{:S(2)}, u32[]{:S(2)}) collective-permute-start(f32[16,8192]{1,0:T(8,128)S(1)} %get-tuple-element.17), channel_id=1, source_target_pairs={{0,1},{1,2},{2,3},{3,4},{4,5},{5,6},{6,7},{7,8},{8,9},{9,10},{10,1... | collective-permute-start | bytes 1572872 | tf_op jit(solution)/shard_map/ppermute | solution.py:24
  94.6 10.9 %all-to-all-start.2 = ((f32[16,1,16]{2,1,0:T(1,128)}), f32[16,1,16]{2,1,0:T(1,128)S(1)}, u32[]{:S(2)}, u32[]{:S(2)}) async-start(f32[16,1,16]{2,1,0:T(1,128)} %broadcast_in_dim.12), calls=%async_computation.2 | async-start | bytes 16384 | tf_op jit(solution)/shard_map/all_to_all | solution.py:108
  105.6 1.0 copy-start.2
  128.7 16.1 %collective-permute-start.8 = (f32[16,8192]{1,0:T(8,128)}, f32[16,8192]{1,0:T(8,128)S(1)}, u32[]{:S(2)}, u32[]{:S(2)}) collective-permute-start(f32[16,8192]{1,0:T(8,128)} %get-tuple-element.24), channel_id=1, source_target_pairs={{0,1},{1,2},{2,3},{3,4},{4,5},{5,6},{6,7},{7,8},{8,9},{9,10},{10,1... | collective-permute-start | bytes 1572872 | tf_op jit(solution)/shard_map/ppermute | solution.py:33
  130.4 15.1 %collective-permute-start.9 = (f32[16,8192]{1,0:T(8,128)}, f32[16,8192]{1,0:T(8,128)}, u32[]{:S(2)}, u32[]{:S(2)}) collective-permute-start(f32[16,8192]{1,0:T(8,128)} %get-tuple-element.25), channel_id=1, source_target_pairs={{1,0},{2,1},{3,2},{4,3},{5,4},{6,5},{7,6},{8,7},{9,8},{10,9},{11,1... | collective-permute-start | bytes 1572872 | tf_op jit(solution)/shard_map/ppermute | solution.py:33
  144.8 0.8 copy-start.7

commit v12 on v10

--- a/solution.py
+++ b/solution.py
@@ -62,8 +62,8 @@
     products = (
         jnp.einsum("skj,kji->ksi", pieces, tile_stack, precision=PRODUCT_PRECISION) * live_slot[:, None, None]
     )
-    onehot = (rows_idx[:, None] == jnp.arange(ROW_BLOCKS)[None, :]).astype(jnp.float32)
-    summed = jnp.einsum("kr,ksi->sri", onehot, products, precision=PRODUCT_PRECISION)
+    summed = jnp.zeros((scenario_rows, ROW_BLOCKS, tile_edge), jnp.float32)
+    summed = summed.at[:, rows_idx, :].add(jnp.swapaxes(products, 0, 1), mode="promise_in_bounds")
     return summed.reshape(scenario_rows, ROW_BLOCKS * tile_edge)
 
 
@@ -74,8 +74,8 @@
     products = (
         jnp.einsum("ski,kij->ksj", pieces, tile_stack, precision=PRODUCT_PRECISION) * live_slot[:, None, None]
     )
-    onehot = (cols_idx[:, None] == jnp.arange(3 * COL_BLOCKS)[None, :]).astype(jnp.float32)
-    summed = jnp.einsum("kc,ksj->scj", onehot, products, precision=PRODUCT_PRECISION)
+    summed = jnp.zeros((scenario_rows, 3 * COL_BLOCKS, tile_edge), jnp.float32)
+    summed = summed.at[:, cols_idx, :].add(jnp.swapaxes(products, 0, 1), mode="promise_in_bounds")
     return summed.reshape(scenario_rows, 3 * COL_BLOCKS * tile_edge)
 
 

time: 156 us -> 191 us (1.22)
  other arithmetic: 7.25 us -> 46.1 us
  matrix products: 38.7 us -> 35.1 us
    scatter-add x0 -> x5, other arithmetic: none -> 38.4 us  [the longest x3 25.7 us: transpose_local(): summed.at[:, cols_idx, :]]
    dot_general x5 -> x0, matrix products: 4.3 us -> none  [the longest x3 2.97 us: transpose_local(): jnp.einsum('kc,ksj->scj', onehot, products, precision=PRODUCT_PRECISION)]
  transfers between devices with their start and end apart: 11 -> 11, of which waited for: 1 -> 1; matrix products, arithmetic and copies ran while one was open for 1% -> 1% of each run, Pallas kernels for 6% -> 5%
where the time goes in v12:
time: 191 us; the launch traced here: 190 us
  blocking collectives  51.8 us (27%)
  other arithmetic  46.1 us (24%)
  matrix products  35.1 us (18%)
  starting transfers between devices  28.4 us (15%)
  local copies, waits for them, and re-layouts  11.3 us (6%)
  Pallas kernels  8.59 us (4%)
  waiting for transfers between devices  6.5 us (3%)
    all_to_all x4, blocking collectives, all_sum(): gathered = lax.all_to_all(spread, axes, 0, 0, tiled=True)  51.8 us
    scatter-add x3, other arithmetic, transpose_local(): summed.at[:, cols_idx, :]  25.7 us
    dot_general x3, matrix products, transpose_local(): jnp.einsum('ski,kij->ksj', pieces, tile_stack, precision=PRODUCT_PRECISION)  21.3 us
    dot_general x2, matrix products, forward_local(): jnp.einsum('skj,kji->ksi', pieces, tile_stack, precision=PRODUCT_PRECISION)  13.8 us
    scatter-add x2, other arithmetic, forward_local(): summed.at[:, rows_idx, :]  12.8 us
    ppermute x6, starting transfers between devices, from_behind(): return lax.ppermute(shard, axis, pairs)  9.72 us
    all_to_all x1, starting transfers between devices, all_sum(): gathered = lax.all_to_all(spread, axes, 0, 0, tiled=True)  8.69 us
    pallas_call x1, Pallas kernels, transpose_blocks(): pl.pallas_call(body, grid=(slots // step,), in_specs=[pl.BlockSpec(memory...  8.59 us
  transfers between devices with their start and end apart: 11, of which 1 were waited for; matrix products, arithmetic and copies ran while one was open for 1% of the time, Pallas kernels for 5%

profile of v12, /device:TPU:0, one launch (start us, length us, event | category | flops | bytes accessed | tf_op | source)
XLA Modules:
  0.0 189.6 jit_solution(10744883230754353465)
XLA Ops:
  0.6 0.7 compare_select_fusion
  1.3 1.0 copy_bitcast_fusion.7
  3.0 0.7 compare_select_fusion.1
  3.6 0.8 gather_fusion
  4.5 6.8 %convolution_multiply_fusion.4 = f32[160,16,128]{2,1,0:T(8,128)S(1)} fusion(f32[160,16,128]{2,1,0:T(8,128)S(1)} %gather_fusion, f32[160]{0:T(256)S(1)} %compare_convert_fusion, f32[1,160,128,128]{3,2,1,0:T(8,128)} %param.6), kind=kOutput, calls=%fused_computation.21 | convolution fusion | flops 251985920 | bytes 13107840 | tf_op jit(solution)/shard_map/ski,kij->ksj/dot_general | solution.py:75
  11.4 6.3 %scatter_fusion = f32[16,192,128]{2,0,1:T(8,128)S(1)} fusion(f32[16,192,128]{2,0,1:T(8,128)S(1)} %broadcast.164.clone, s32[160]{0:T(256)S(1)} %bitcast.115, f32[160,16,128]{2,1,0:T(8,128)S(1)} %convolution_multiply_fusion.4), kind=kCustom, calls=%fused_computation.5 | custom fusion | flops 327680 | bytes 3932800 | tf_op jit(solution)/shard_map/scatter-add | solution.py:78
  18.0 2.4 %collective-permute-start = (f32[16,8192]{1,0:T(8,128)S(1)}, f32[16,8192]{1,0:T(8,128)S(1)}, u32[]{:S(2)}, u32[]{:S(2)}) collective-permute-start(f32[16,8192]{1,0:T(8,128)S(1)} %get-tuple-element.28), channel_id=1, source_target_pairs={{0,1},{1,2},{2,3},{3,4},{4,5},{5,6},{6,7},{7,8},{8,9},{9,10},{10,1... | collective-permute-start | bytes 1572872 | tf_op jit(solution)/shard_map/ppermute | solution.py:33
  20.4 1.3 collective-permute-start.1
  21.7 0.5 slice.60.anchor_ref
  22.2 8.6 %shard_map.68 = f32[160,128,128]{2,1,0:T(8,128)} custom-call(f32[1,1]{1,0:T(1,128)} %slice.60.anchor_ref, f32[160,128,128]{2,1,0:T(8,128)} %bitcast.110), custom_call_target="tpu_custom_call" | custom-call | bytes 20971520 | tf_op jit(solution)/shard_map/pallas_call | solution.py:45
  30.8 0.1 multiply_reduce_fusion.5
  30.9 0.2 multiply_reduce_fusion.2
  31.1 5.7 %collective-permute-start.2 = (f32[16,8192]{1,0:T(8,128)S(1)}, f32[16,8192]{1,0:T(8,128)S(1)}, u32[]{:S(2)}, u32[]{:S(2)}) collective-permute-start(f32[16,8192]{1,0:T(8,128)S(1)} %get-tuple-element.23), channel_id=1, source_target_pairs={{0,1},{1,2},{2,3},{3,4},{4,5},{5,6},{6,7},{7,8},{8,9},{9,10},{10,1... | collective-permute-start | bytes 1572872 | tf_op jit(solution)/shard_map/ppermute | solution.py:24
  36.8 1.3 collective-permute-start.3
  38.2 0.6 broadcast_in_dim.10
  38.8 8.7 %all-to-all-start = ((f32[16,2,16]{2,1,0:T(2,128)}), f32[16,2,16]{2,1,0:T(2,128)S(1)}, u32[]{:S(2)}, u32[]{:S(2)}) async-start(f32[16,2,16]{2,1,0:T(2,128)} %broadcast_in_dim.10), calls=%async_computation | async-start | bytes 32768 | tf_op jit(solution)/shard_map/all_to_all | solution.py:108
  47.5 6.5 %all-to-all-done = f32[16,2,16]{2,1,0:T(2,128)S(1)} async-done(((f32[16,2,16]{2,1,0:T(2,128)}), f32[16,2,16]{2,1,0:T(2,128)S(1)}, u32[]{:S(2)}, u32[]{:S(2)}) %all-to-all-start) | async-done | bytes 2080 | tf_op jit(solution)/shard_map/all_to_all | solution.py:108
  54.2 0.8 gather_fusion.1
  55.0 6.8 %convolution_multiply_fusion.3 = f32[160,16,128]{2,1,0:T(8,128)S(1)} fusion(f32[160,128,128]{2,1,0:T(8,128)} %shard_map.68, f32[160,16,128]{2,1,0:T(8,128)S(1)} %gather_fusion.1, f32[160]{0:T(256)S(1)} %compare_convert_fusion), kind=kOutput, calls=%fused_computation.20 | convolution fusion | flops 251985920 | bytes 13107840 | tf_op jit(solution)/shard_map/skj,kji->ksi/dot_general | solution.py:63
  61.9 6.4 %scatter_fusion.1 = f32[16,32,128]{2,0,1:T(8,128)S(1)} fusion(f32[16,32,128]{2,0,1:T(8,128)S(1)} %broadcast.170.clone, s32[160]{0:T(256)S(1)} %bitcast.120, f32[160,16,128]{2,1,0:T(8,128)S(1)} %convolution_multiply_fusion.3), kind=kCustom, calls=%fused_computation.6 | custom fusion | flops 327680 | bytes 3932800 | tf_op jit(solution)/shard_map/scatter-add | solution.py:66
  68.3 0.2 multiply_reduce_fusion.4
  68.5 0.7 copy-done.4
  69.2 0.8 gather_fusion.2
  70.1 6.8 %convolution_multiply_fusion.2 = f32[160,16,128]{2,1,0:T(8,128)S(1)} fusion(f32[160,16,128]{2,1,0:T(8,128)S(1)} %gather_fusion.2, f32[160]{0:T(256)S(1)} %compare_convert_fusion, f32[1,160,128,128]{3,2,1,0:T(8,128)} %param.6), kind=kOutput, calls=%fused_computation.19 | convolution fusion | flops 251985920 | bytes 13107840 | tf_op jit(solution)/shard_map/ski,kij->ksj/dot_general | solution.py:75
  77.0 6.3 %scatter_fusion.2 = f32[16,192,128]{2,0,1:T(8,128)S(1)} fusion(f32[16,192,128]{2,0,1:T(8,128)S(1)} %broadcast.164.clone.1, s32[160]{0:T(256)S(1)} %bitcast.117, f32[160,16,128]{2,1,0:T(8,128)S(1)} %convolution_multiply_fusion.2), kind=kCustom, calls=%fused_computation.7 | custom fusion | flops 327680 | bytes 3932800 | tf_op jit(solution)/shard_map/scatter-add | solution.py:78
  83.5 1.1 copy-done
  84.7 1.7 collective-permute-start.4
  86.4 1.3 collective-permute-start.5
  87.7 13.2 %all_to_all.29 = f32[16,1,16]{2,1,0:T(1,128)S(1)} all-to-all(f32[16,1,16]{2,1,0:T(1,128)S(1)} %broadcast_in_dim.11), channel_id=1, replica_groups=mesh['group'=2,'row'=8,'col'=2] {'row','col'}, dimensions={0} | all-to-all | bytes 2048 | tf_op jit(solution)/shard_map/all_to_all | solution.py:108
  101.0 1.3 multiply_reduce_fusion.1
  102.3 1.7 collective-permute-start.6
  104.1 1.3 collective-permute-start.7
  105.4 14.0 %all_to_all.30 = f32[16,1,16]{2,1,0:T(1,128)S(1)} all-to-all(f32[16,1,16]{2,1,0:T(1,128)S(1)} %broadcast_in_dim.12), channel_id=1, replica_groups=mesh['group'=2,'row'=8,'col'=2] {'row','col'}, dimensions={0} | all-to-all | bytes 2048 | tf_op jit(solution)/shard_map/all_to_all | solution.py:108
  119.5 1.2 copy_bitcast_fusion.3
  120.6 1.9 %gather_fusion.3 = f32[160,16,128]{2,1,0:T(8,128)} fusion(f32[16,192,128]{2,0,1:T(8,128)S(1)} %copy_bitcast_fusion.3, s32[1024]{0:T(1024)S(1)} %pad_clamp_fusion), kind=kCustom, calls=%fused_computation.3 | custom fusion | bytes 2622080 | tf_op jit(solution)/shard_map/gather | solution.py:61
  122.5 7.0 %convolution_multiply_fusion.1 = f32[160,16,128]{2,1,0:T(8,128)S(1)} fusion(f32[160,128,128]{2,1,0:T(8,128)} %shard_map.68, f32[160,16,128]{2,1,0:T(8,128)} %gather_fusion.3, f32[160]{0:T(256)S(1)} %compare_convert_fusion), kind=kOutput, calls=%fused_computation.18 | convolution fusion | flops 251985920 | bytes 13107840 | tf_op jit(solution)/shard_map/skj,kji->ksi/dot_general | solution.py:63
  129.6 6.4 %scatter_fusion.3 = f32[16,32,128]{2,0,1:T(8,128)S(1)} fusion(f32[16,32,128]{2,0,1:T(8,128)S(1)} %broadcast.170, s32[160]{0:T(256)S(1)} %bitcast.121, f32[160,16,128]{2,1,0:T(8,128)S(1)} %convolution_multiply_fusion.1), kind=kCustom, calls=%fused_computation.8 | custom fusion | flops 327680 | bytes 3932800 | tf_op jit(solution)/shard_map/scatter-add | solution.py:66
  136.0 0.2 multiply_reduce_fusion.3
  136.3 0.8 gather_fusion.4
  137.1 7.7 %convolution_multiply_fusion = f32[160,16,128]{2,1,0:T(8,128)} fusion(f32[160,16,128]{2,1,0:T(8,128)S(1)} %gather_fusion.4, f32[160]{0:T(256)S(1)} %compare_convert_fusion, f32[1,160,128,128]{3,2,1,0:T(8,128)} %param.6), kind=kOutput, calls=%fused_computation.17 | convolution fusion | flops 251985920 | bytes 13107840 | tf_op jit(solution)/shard_map/ski,kij->ksj/dot_general | solution.py:75
  144.9 13.0 %scatter_fusion.4 = f32[16,192,128]{2,0,1:T(8,128)S(1)} fusion(f32[16,192,128]{2,0,1:T(8,128)S(1)} %broadcast.164, s32[160]{0:T(256)S(1)} %bitcast.118, f32[160,16,128]{2,1,0:T(8,128)} %convolution_multiply_fusion), kind=kCustom, calls=%fused_computation.9 | custom fusion | flops 327680 | bytes 3932800 | tf_op jit(solution)/shard_map/scatter-add | solution.py:78
  158.0 1.1 copy-done.1
  159.2 1.7 collective-permute-start.8
  161.0 1.3 collective-permute-start.9
  162.3 14.0 %all_to_all.31 = f32[16,1,16]{2,1,0:T(1,128)S(1)} all-to-all(f32[16,1,16]{2,1,0:T(1,128)S(1)} %broadcast_in_dim.13), channel_id=1, replica_groups=mesh['group'=2,'row'=8,'col'=2] {'row','col'}, dimensions={0} | all-to-all | bytes 2048 | tf_op jit(solution)/shard_map/all_to_all | solution.py:108
  176.3 1.3 multiply_reduce_fusion
  177.7 10.6 %all_to_all.32 = f32[16,1,16]{2,1,0:T(1,128)S(1)} all-to-all(f32[16,1,16]{2,1,0:T(1,128)S(1)} %broadcast_in_dim.14), channel_id=1, replica_groups=mesh['group'=2,'row'=8,'col'=2] {'row','col'}, dimensions={0} | all-to-all | bytes 2048 | tf_op jit(solution)/shard_map/all_to_all | solution.py:108
  188.4 1.2 multiply_subtract_fusion
  (55 shorter events, 1.4 us)
Async XLA Ops:
  18.0 12.9 %collective-permute-start = (f32[16,8192]{1,0:T(8,128)S(1)}, f32[16,8192]{1,0:T(8,128)S(1)}, u32[]{:S(2)}, u32[]{:S(2)}) collective-permute-start(f32[16,8192]{1,0:T(8,128)S(1)} %get-tuple-element.28), channel_id=1, source_target_pairs={{0,1},{1,2},{2,3},{3,4},{4,5},{5,6},{6,7},{7,8},{8,9},{9,10},{10,1... | collective-permute-start | bytes 1572872 | tf_op jit(solution)/shard_map/ppermute | solution.py:33
  20.4 10.6 %collective-permute-start.1 = (f32[16,8192]{1,0:T(8,128)S(1)}, f32[16,8192]{1,0:T(8,128)S(1)}, u32[]{:S(2)}, u32[]{:S(2)}) collective-permute-start(f32[16,8192]{1,0:T(8,128)S(1)} %get-tuple-element.29), channel_id=1, source_target_pairs={{1,0},{2,1},{3,2},{4,3},{5,4},{6,5},{7,6},{8,7},{9,8},{10,9},{11,1... | collective-permute-start | bytes 1572872 | tf_op jit(solution)/shard_map/ppermute | solution.py:33
  22.2 8.6 %copy-start.2 = (f32[16,4096]{1,0:T(8,128)S(1)}, f32[16,4096]{1,0:T(8,128)}, u32[]{:S(2)}) copy-start(f32[16,4096]{1,0:T(8,128)} %param.5) | copy-start | bytes 786436
  31.1 22.9 %collective-permute-start.2 = (f32[16,8192]{1,0:T(8,128)S(1)}, f32[16,8192]{1,0:T(8,128)S(1)}, u32[]{:S(2)}, u32[]{:S(2)}) collective-permute-start(f32[16,8192]{1,0:T(8,128)S(1)} %get-tuple-element.23), channel_id=1, source_target_pairs={{0,1},{1,2},{2,3},{3,4},{4,5},{5,6},{6,7},{7,8},{8,9},{9,10},{10,1... | collective-permute-start | bytes 1572872 | tf_op jit(solution)/shard_map/ppermute | solution.py:24
  36.8 17.2 %collective-permute-start.3 = (f32[16,8192]{1,0:T(8,128)S(1)}, f32[16,8192]{1,0:T(8,128)S(1)}, u32[]{:S(2)}, u32[]{:S(2)}) collective-permute-start(f32[16,8192]{1,0:T(8,128)S(1)} %get-tuple-element.23), channel_id=1, source_target_pairs={{1,0},{2,1},{3,2},{4,3},{5,4},{6,5},{7,6},{8,7},{9,8},{10,9},{11,1... | collective-permute-start | bytes 1572872 | tf_op jit(solution)/shard_map/ppermute | solution.py:25
  38.8 15.2 %all-to-all-start = ((f32[16,2,16]{2,1,0:T(2,128)}), f32[16,2,16]{2,1,0:T(2,128)S(1)}, u32[]{:S(2)}, u32[]{:S(2)}) async-start(f32[16,2,16]{2,1,0:T(2,128)} %broadcast_in_dim.10), calls=%async_computation | async-start | bytes 32768 | tf_op jit(solution)/shard_map/all_to_all | solution.py:108
  61.8 6.4 %copy-start.3 = (f32[16,4096]{1,0:T(8,128)S(1)}, f32[16,4096]{1,0:T(8,128)}, u32[]{:S(2)}) copy-start(f32[16,4096]{1,0:T(8,128)} %param.5) | copy-start | bytes 786436
  68.5 0.7 copy-start.4
  83.5 1.1 copy-start
  84.7 16.3 %collective-permute-start.4 = (f32[16,8192]{1,0:T(8,128)S(1)}, f32[16,8192]{1,0:T(8,128)S(1)}, u32[]{:S(2)}, u32[]{:S(2)}) collective-permute-start(f32[16,8192]{1,0:T(8,128)S(1)} %get-tuple-element.26), channel_id=1, source_target_pairs={{0,1},{1,2},{2,3},{3,4},{4,5},{5,6},{6,7},{7,8},{8,9},{9,10},{10,1... | collective-permute-start | bytes 1572872 | tf_op jit(solution)/shard_map/ppermute | solution.py:33
  86.4 14.6 %collective-permute-start.5 = (f32[16,8192]{1,0:T(8,128)S(1)}, f32[16,8192]{1,0:T(8,128)S(1)}, u32[]{:S(2)}, u32[]{:S(2)}) collective-permute-start(f32[16,8192]{1,0:T(8,128)S(1)} %get-tuple-element.27), channel_id=1, source_target_pairs={{1,0},{2,1},{3,2},{4,3},{5,4},{6,5},{7,6},{8,7},{9,8},{10,9},{11,1... | collective-permute-start | bytes 1572872 | tf_op jit(solution)/shard_map/ppermute | solution.py:33
  102.3 17.1 %collective-permute-start.6 = (f32[16,8192]{1,0:T(8,128)S(1)}, f32[16,8192]{1,0:T(8,128)S(1)}, u32[]{:S(2)}, u32[]{:S(2)}) collective-permute-start(f32[16,8192]{1,0:T(8,128)S(1)} %get-tuple-element.17), channel_id=1, source_target_pairs={{0,1},{1,2},{2,3},{3,4},{4,5},{5,6},{6,7},{7,8},{8,9},{9,10},{10,1... | collective-permute-start | bytes 1572872 | tf_op jit(solution)/shard_map/ppermute | solution.py:24
  104.1 15.4 %collective-permute-start.7 = (f32[16,8192]{1,0:T(8,128)S(1)}, f32[16,8192]{1,0:T(8,128)}, u32[]{:S(2)}, u32[]{:S(2)}) collective-permute-start(f32[16,8192]{1,0:T(8,128)S(1)} %get-tuple-element.17), channel_id=1, source_target_pairs={{1,0},{2,1},{3,2},{4,3},{5,4},{6,5},{7,6},{8,7},{9,8},{10,9},{11,1... | collective-permute-start | bytes 1572872 | tf_op jit(solution)/shard_map/ppermute | solution.py:25
  129.6 6.4 %copy-start.5 = (f32[16,4096]{1,0:T(8,128)S(1)}, f32[16,4096]{1,0:T(8,128)}, u32[]{:S(2)}) copy-start(f32[16,4096]{1,0:T(8,128)} %copy-done.4) | copy-start | bytes 786436
  158.0 1.2 copy-start.1
  159.2 17.1 %collective-permute-start.8 = (f32[16,8192]{1,0:T(8,128)S(1)}, f32[16,8192]{1,0:T(8,128)S(1)}, u32[]{:S(2)}, u32[]{:S(2)}) collective-permute-start(f32[16,8192]{1,0:T(8,128)S(1)} %get-tuple-element.24), channel_id=1, source_target_pairs={{0,1},{1,2},{2,3},{3,4},{4,5},{5,6},{6,7},{7,8},{8,9},{9,10},{10,1... | collective-permute-start | bytes 1572872 | tf_op jit(solution)/shard_map/ppermute | solution.py:33
  161.0 15.4 %collective-permute-start.9 = (f32[16,8192]{1,0:T(8,128)S(1)}, f32[16,8192]{1,0:T(8,128)S(1)}, u32[]{:S(2)}, u32[]{:S(2)}) collective-permute-start(f32[16,8192]{1,0:T(8,128)S(1)} %get-tuple-element.25), channel_id=1, source_target_pairs={{1,0},{2,1},{3,2},{4,3},{5,4},{6,5},{7,6},{8,7},{9,8},{10,9},{11,1... | collective-permute-start | bytes 1572872 | tf_op jit(solution)/shard_map/ppermute | solution.py:33

commit v13 on v10

--- a/solution.py
+++ b/solution.py
@@ -60,9 +60,9 @@
     tile_edge = tile_stack.shape[1]
     pieces = window.reshape(scenario_rows, 3 * COL_BLOCKS, tile_edge)[:, cols_idx, :]
     products = (
-        jnp.einsum("skj,kji->ksi", pieces, tile_stack, precision=PRODUCT_PRECISION) * live_slot[:, None, None]
+        jnp.einsum("skj,kji->ksi", pieces, tile_stack, precision=PRODUCT_PRECISION)
     )
-    onehot = (rows_idx[:, None] == jnp.arange(ROW_BLOCKS)[None, :]).astype(jnp.float32)
+    onehot = (rows_idx[:, None] == jnp.arange(ROW_BLOCKS)[None, :]).astype(jnp.float32) * live_slot[:, None]
     summed = jnp.einsum("kr,ksi->sri", onehot, products, precision=PRODUCT_PRECISION)
     return summed.reshape(scenario_rows, ROW_BLOCKS * tile_edge)
 
@@ -72,9 +72,9 @@
     tile_edge = tile_stack.shape[1]
     pieces = field.reshape(scenario_rows, ROW_BLOCKS, tile_edge)[:, rows_idx, :]
     products = (
-        jnp.einsum("ski,kij->ksj", pieces, tile_stack, precision=PRODUCT_PRECISION) * live_slot[:, None, None]
+        jnp.einsum("ski,kij->ksj", pieces, tile_stack, precision=PRODUCT_PRECISION)
     )
-    onehot = (cols_idx[:, None] == jnp.arange(3 * COL_BLOCKS)[None, :]).astype(jnp.float32)
+    onehot = (cols_idx[:, None] == jnp.arange(3 * COL_BLOCKS)[None, :]).astype(jnp.float32) * live_slot[:, None]
     summed = jnp.einsum("kc,ksj->scj", onehot, products, precision=PRODUCT_PRECISION)
     return summed.reshape(scenario_rows, 3 * COL_BLOCKS * tile_edge)
 

time: 156 us -> 157 us (level)
  no operation moved by 1% of the time
where the time goes in v13:
time: 157 us; the launch traced here: 156 us
  blocking collectives  51.5 us (33%)
  matrix products  39.2 us (25%)
  starting transfers between devices  29.1 us (19%)
  local copies, waits for them, and re-layouts  12.1 us (8%)
  Pallas kernels  8.59 us (5%)
  other arithmetic  7.25 us (5%)
  waiting for transfers between devices  6.5 us (4%)
  between operations  1.69 us (1%)
    all_to_all x4, blocking collectives, all_sum(): gathered = lax.all_to_all(spread, axes, 0, 0, tiled=True)  51.5 us
    dot_general x3, matrix products, transpose_local(): jnp.einsum('ski,kij->ksj', pieces, tile_stack, precision=PRODUCT_PRECISION)  20.3 us
    dot_general x2, matrix products, forward_local(): jnp.einsum('skj,kji->ksi', pieces, tile_stack, precision=PRODUCT_PRECISION)  13.8 us
    ppermute x6, starting transfers between devices, from_behind(): return lax.ppermute(shard, axis, pairs)  10.4 us
    all_to_all x1, starting transfers between devices, all_sum(): gathered = lax.all_to_all(spread, axes, 0, 0, tiled=True)  8.69 us
    pallas_call x1, Pallas kernels, transpose_blocks(): pl.pallas_call(body, grid=(slots // step,), in_specs=[pl.BlockSpec(memory...  8.59 us
    ppermute x2, starting transfers between devices, with_halo(): before = lax.ppermute(last, axis, up)  7.4 us
    all_to_all x1, waiting for transfers between devices, all_sum(): gathered = lax.all_to_all(spread, axes, 0, 0, tiled=True)  6.48 us
  transfers between devices with their start and end apart: 11, of which 1 were waited for; matrix products, arithmetic and copies ran while one was open for 1% of the time, Pallas kernels for 6%

profile of v13, /device:TPU:0, one launch (start us, length us, event | category | flops | bytes accessed | tf_op | source)
XLA Modules:
  0.0 156.0 jit_solution(18152274361635964576)
XLA Ops:
  1.3 0.7 compare_select_fusion.1
  2.0 1.0 copy_bitcast_fusion.7
  3.0 0.8 gather_fusion
  3.8 6.8 %fusion.8 = f32[160,16,128]{2,1,0:T(8,128)S(1)} fusion(f32[160,16,128]{2,1,0:T(8,128)S(1)} %gather_fusion, f32[1,160,128,128]{3,2,1,0:T(8,128)} %param.6), kind=kOutput, calls=%fused_computation.20 | convolution fusion | flops 251658240 | bytes 13107200 | tf_op jit(solution)/shard_map/ski,kij->ksj/dot_general | solution.py:75
  10.6 1.2 fusion.18
  11.8 0.9 copy.81
  12.8 2.4 %collective-permute-start = (f32[16,8192]{1,0:T(8,128)S(1)}, f32[16,8192]{1,0:T(8,128)S(1)}, u32[]{:S(2)}, u32[]{:S(2)}) collective-permute-start(f32[16,8192]{1,0:T(8,128)S(1)} %get-tuple-element.28), channel_id=1, source_target_pairs={{0,1},{1,2},{2,3},{3,4},{4,5},{5,6},{6,7},{7,8},{8,9},{9,10},{10,1... | collective-permute-start | bytes 1572872 | tf_op jit(solution)/shard_map/ppermute | solution.py:33
  15.2 1.3 collective-permute-start.1
  16.5 0.5 slice.60.anchor_ref
  17.0 8.6 %shard_map.68 = f32[160,128,128]{2,1,0:T(8,128)} custom-call(f32[1,1]{1,0:T(1,128)} %slice.60.anchor_ref, f32[160,128,128]{2,1,0:T(8,128)} %bitcast.122), custom_call_target="tpu_custom_call" | custom-call | bytes 20971520 | tf_op jit(solution)/shard_map/pallas_call | solution.py:45
  25.8 0.2 multiply_reduce_fusion.2
  26.0 5.7 %collective-permute-start.2 = (f32[16,8192]{1,0:T(8,128)S(1)}, f32[16,8192]{1,0:T(8,128)S(1)}, u32[]{:S(2)}, u32[]{:S(2)}) collective-permute-start(f32[16,8192]{1,0:T(8,128)S(1)} %get-tuple-element.23), channel_id=1, source_target_pairs={{0,1},{1,2},{2,3},{3,4},{4,5},{5,6},{6,7},{7,8},{8,9},{9,10},{10,1... | collective-permute-start | bytes 1572872 | tf_op jit(solution)/shard_map/ppermute | solution.py:24
  31.7 1.3 collective-permute-start.3
  33.0 0.6 broadcast_in_dim.10
  33.6 8.7 %all-to-all-start = ((f32[16,2,16]{2,1,0:T(2,128)}), f32[16,2,16]{2,1,0:T(2,128)S(1)}, u32[]{:S(2)}, u32[]{:S(2)}) async-start(f32[16,2,16]{2,1,0:T(2,128)} %broadcast_in_dim.10), calls=%async_computation | async-start | bytes 32768 | tf_op jit(solution)/shard_map/all_to_all | solution.py:108
  42.3 6.5 %all-to-all-done = f32[16,2,16]{2,1,0:T(2,128)S(1)} async-done(((f32[16,2,16]{2,1,0:T(2,128)}), f32[16,2,16]{2,1,0:T(2,128)S(1)}, u32[]{:S(2)}, u32[]{:S(2)}) %all-to-all-start) | async-done | bytes 2080 | tf_op jit(solution)/shard_map/all_to_all | solution.py:108
  49.0 0.8 gather_fusion.1
  49.9 6.8 %fusion.6 = f32[160,16,128]{2,1,0:T(8,128)S(1)} fusion(f32[160,128,128]{2,1,0:T(8,128)} %shard_map.68, f32[160,16,128]{2,1,0:T(8,128)S(1)} %gather_fusion.1), kind=kOutput, calls=%fused_computation.18 | convolution fusion | flops 251658240 | bytes 13107200 | tf_op jit(solution)/shard_map/skj,kji->ksi/dot_general | solution.py:63
  56.7 0.8 fusion.16
  57.6 0.3 multiply_reduce_fusion.4
  57.9 0.8 gather_fusion.2
  58.7 6.8 %fusion.4 = f32[160,16,128]{2,1,0:T(8,128)S(1)} fusion(f32[160,16,128]{2,1,0:T(8,128)S(1)} %gather_fusion.2, f32[1,160,128,128]{3,2,1,0:T(8,128)} %param.6), kind=kOutput, calls=%fused_computation.16 | convolution fusion | flops 251658240 | bytes 13107200 | tf_op jit(solution)/shard_map/ski,kij->ksj/dot_general | solution.py:75
  65.5 1.2 fusion.14
  66.7 0.9 copy.80
  67.7 0.9 fusion.67
  68.5 1.7 %collective-permute-start.4 = (f32[16,8192]{1,0:T(8,128)}, f32[16,8192]{1,0:T(8,128)S(1)}, u32[]{:S(2)}, u32[]{:S(2)}) collective-permute-start(f32[16,8192]{1,0:T(8,128)} %get-tuple-element.26), channel_id=1, source_target_pairs={{0,1},{1,2},{2,3},{3,4},{4,5},{5,6},{6,7},{7,8},{8,9},{9,10},{10,1... | collective-permute-start | bytes 1572872 | tf_op jit(solution)/shard_map/ppermute | solution.py:33
  70.2 1.3 collective-permute-start.5
  71.5 13.3 %all_to_all.29 = f32[16,1,16]{2,1,0:T(1,128)S(1)} all-to-all(f32[16,1,16]{2,1,0:T(1,128)S(1)} %broadcast_in_dim.11), channel_id=1, replica_groups=mesh['group'=2,'row'=8,'col'=2] {'row','col'}, dimensions={0} | all-to-all | bytes 2048 | tf_op jit(solution)/shard_map/all_to_all | solution.py:108
  84.8 1.3 multiply_reduce_fusion.1
  86.2 1.7 %collective-permute-start.6 = (f32[16,8192]{1,0:T(8,128)S(1)}, f32[16,8192]{1,0:T(8,128)S(1)}, u32[]{:S(2)}, u32[]{:S(2)}) collective-permute-start(f32[16,8192]{1,0:T(8,128)S(1)} %get-tuple-element.17), channel_id=1, source_target_pairs={{0,1},{1,2},{2,3},{3,4},{4,5},{5,6},{6,7},{7,8},{8,9},{9,10},{10,1... | collective-permute-start | bytes 1572872 | tf_op jit(solution)/shard_map/ppermute | solution.py:24
  87.9 1.3 collective-permute-start.7
  89.2 14.2 %all_to_all.30 = f32[16,1,16]{2,1,0:T(1,128)S(1)} all-to-all(f32[16,1,16]{2,1,0:T(1,128)S(1)} %broadcast_in_dim.12), channel_id=1, replica_groups=mesh['group'=2,'row'=8,'col'=2] {'row','col'}, dimensions={0} | all-to-all | bytes 2048 | tf_op jit(solution)/shard_map/all_to_all | solution.py:108
  103.5 1.2 copy_bitcast_fusion.3
  104.6 1.9 %gather_fusion.3 = f32[160,16,128]{2,1,0:T(8,128)} fusion(f32[16,192,128]{2,0,1:T(8,128)S(1)} %copy_bitcast_fusion.3, s32[1024]{0:T(1024)S(1)} %pad_clamp_fusion), kind=kCustom, calls=%fused_computation.3 | custom fusion | bytes 2622080 | tf_op jit(solution)/shard_map/gather | solution.py:61
  106.6 7.0 %fusion.2 = f32[160,16,128]{2,1,0:T(8,128)S(1)} fusion(f32[160,128,128]{2,1,0:T(8,128)} %shard_map.68, f32[160,16,128]{2,1,0:T(8,128)} %gather_fusion.3), kind=kOutput, calls=%fused_computation.14 | convolution fusion | flops 251658240 | bytes 13107200 | tf_op jit(solution)/shard_map/skj,kji->ksi/dot_general | solution.py:63
  113.5 0.8 fusion.12
  114.3 0.3 multiply_reduce_fusion.3
  114.6 0.8 gather_fusion.4
  115.5 6.8 %fusion = f32[160,16,128]{2,1,0:T(8,128)S(1)} fusion(f32[160,16,128]{2,1,0:T(8,128)S(1)} %gather_fusion.4, f32[1,160,128,128]{3,2,1,0:T(8,128)} %param.6), kind=kOutput, calls=%fused_computation.12 | convolution fusion | flops 251658240 | bytes 13107200 | tf_op jit(solution)/shard_map/ski,kij->ksj/dot_general | solution.py:75
  122.2 1.2 fusion.10
  123.4 0.9 copy.79
  124.4 0.9 fusion.66
  125.2 2.5 %collective-permute-start.8 = (f32[16,8192]{1,0:T(8,128)}, f32[16,8192]{1,0:T(8,128)}, u32[]{:S(2)}, u32[]{:S(2)}) collective-permute-start(f32[16,8192]{1,0:T(8,128)} %get-tuple-element.24), channel_id=1, source_target_pairs={{0,1},{1,2},{2,3},{3,4},{4,5},{5,6},{6,7},{7,8},{8,9},{9,10},{10,1... | collective-permute-start | bytes 1572872 | tf_op jit(solution)/shard_map/ppermute | solution.py:33
  127.7 1.3 collective-permute-start.9
  129.0 13.3 %all_to_all.31 = f32[16,1,16]{2,1,0:T(1,128)S(1)} all-to-all(f32[16,1,16]{2,1,0:T(1,128)S(1)} %broadcast_in_dim.13), channel_id=1, replica_groups=mesh['group'=2,'row'=8,'col'=2] {'row','col'}, dimensions={0} | all-to-all | bytes 2048 | tf_op jit(solution)/shard_map/all_to_all | solution.py:108
  142.3 1.5 multiply_reduce_fusion
  143.8 10.8 %all_to_all.32 = f32[16,1,16]{2,1,0:T(1,128)S(1)} all-to-all(f32[16,1,16]{2,1,0:T(1,128)S(1)} %broadcast_in_dim.14), channel_id=1, replica_groups=mesh['group'=2,'row'=8,'col'=2] {'row','col'}, dimensions={0} | all-to-all | bytes 2048 | tf_op jit(solution)/shard_map/all_to_all | solution.py:108
  154.8 1.2 multiply_subtract_fusion
  (46 shorter events, 0.9 us)
Async XLA Ops:
  3.8 6.8 %copy-start.2 = (s32[1,160]{1,0:T(1,128)S(1)}, s32[1,160]{1,0:T(1,128)}, u32[]{:S(2)}) copy-start(s32[1,160]{1,0:T(1,128)} %param.8) | copy-start | bytes 1924
  12.8 12.9 %collective-permute-start = (f32[16,8192]{1,0:T(8,128)S(1)}, f32[16,8192]{1,0:T(8,128)S(1)}, u32[]{:S(2)}, u32[]{:S(2)}) collective-permute-start(f32[16,8192]{1,0:T(8,128)S(1)} %get-tuple-element.28), channel_id=1, source_target_pairs={{0,1},{1,2},{2,3},{3,4},{4,5},{5,6},{6,7},{7,8},{8,9},{9,10},{10,1... | collective-permute-start | bytes 1572872 | tf_op jit(solution)/shard_map/ppermute | solution.py:33
  15.2 10.6 %collective-permute-start.1 = (f32[16,8192]{1,0:T(8,128)S(1)}, f32[16,8192]{1,0:T(8,128)S(1)}, u32[]{:S(2)}, u32[]{:S(2)}) collective-permute-start(f32[16,8192]{1,0:T(8,128)S(1)} %get-tuple-element.29), channel_id=1, source_target_pairs={{1,0},{2,1},{3,2},{4,3},{5,4},{6,5},{7,6},{8,7},{9,8},{10,9},{11,1... | collective-permute-start | bytes 1572872 | tf_op jit(solution)/shard_map/ppermute | solution.py:33
  17.0 8.6 %copy-start = (f32[16,4096]{1,0:T(8,128)S(1)}, f32[16,4096]{1,0:T(8,128)}, u32[]{:S(2)}) copy-start(f32[16,4096]{1,0:T(8,128)} %param.5) | copy-start | bytes 786436
  26.0 22.9 %collective-permute-start.2 = (f32[16,8192]{1,0:T(8,128)S(1)}, f32[16,8192]{1,0:T(8,128)S(1)}, u32[]{:S(2)}, u32[]{:S(2)}) collective-permute-start(f32[16,8192]{1,0:T(8,128)S(1)} %get-tuple-element.23), channel_id=1, source_target_pairs={{0,1},{1,2},{2,3},{3,4},{4,5},{5,6},{6,7},{7,8},{8,9},{9,10},{10,1... | collective-permute-start | bytes 1572872 | tf_op jit(solution)/shard_map/ppermute | solution.py:24
  31.7 17.2 %collective-permute-start.3 = (f32[16,8192]{1,0:T(8,128)S(1)}, f32[16,8192]{1,0:T(8,128)S(1)}, u32[]{:S(2)}, u32[]{:S(2)}) collective-permute-start(f32[16,8192]{1,0:T(8,128)S(1)} %get-tuple-element.23), channel_id=1, source_target_pairs={{1,0},{2,1},{3,2},{4,3},{5,4},{6,5},{7,6},{8,7},{9,8},{10,9},{11,1... | collective-permute-start | bytes 1572872 | tf_op jit(solution)/shard_map/ppermute | solution.py:25
  33.6 15.2 %all-to-all-start = ((f32[16,2,16]{2,1,0:T(2,128)}), f32[16,2,16]{2,1,0:T(2,128)S(1)}, u32[]{:S(2)}, u32[]{:S(2)}) async-start(f32[16,2,16]{2,1,0:T(2,128)} %broadcast_in_dim.10), calls=%async_computation | async-start | bytes 32768 | tf_op jit(solution)/shard_map/all_to_all | solution.py:108
  49.9 6.8 %copy-start.3 = (s32[1,160]{1,0:T(1,128)S(1)}, s32[1,160]{1,0:T(1,128)}, u32[]{:S(2)}) copy-start(s32[1,160]{1,0:T(1,128)} %param.7) | copy-start | bytes 1924
  56.6 1.0 copy-start.1
  68.5 16.3 %collective-permute-start.4 = (f32[16,8192]{1,0:T(8,128)}, f32[16,8192]{1,0:T(8,128)S(1)}, u32[]{:S(2)}, u32[]{:S(2)}) collective-permute-start(f32[16,8192]{1,0:T(8,128)} %get-tuple-element.26), channel_id=1, source_target_pairs={{0,1},{1,2},{2,3},{3,4},{4,5},{5,6},{6,7},{7,8},{8,9},{9,10},{10,1... | collective-permute-start | bytes 1572872 | tf_op jit(solution)/shard_map/ppermute | solution.py:33
  70.2 14.6 %collective-permute-start.5 = (f32[16,8192]{1,0:T(8,128)S(1)}, f32[16,8192]{1,0:T(8,128)}, u32[]{:S(2)}, u32[]{:S(2)}) collective-permute-start(f32[16,8192]{1,0:T(8,128)S(1)} %get-tuple-element.27), channel_id=1, source_target_pairs={{1,0},{2,1},{3,2},{4,3},{5,4},{6,5},{7,6},{8,7},{9,8},{10,9},{11,1... | collective-permute-start | bytes 1572872 | tf_op jit(solution)/shard_map/ppermute | solution.py:33
  86.2 17.3 %collective-permute-start.6 = (f32[16,8192]{1,0:T(8,128)S(1)}, f32[16,8192]{1,0:T(8,128)S(1)}, u32[]{:S(2)}, u32[]{:S(2)}) collective-permute-start(f32[16,8192]{1,0:T(8,128)S(1)} %get-tuple-element.17), channel_id=1, source_target_pairs={{0,1},{1,2},{2,3},{3,4},{4,5},{5,6},{6,7},{7,8},{8,9},{9,10},{10,1... | collective-permute-start | bytes 1572872 | tf_op jit(solution)/shard_map/ppermute | solution.py:24
  87.9 15.6 %collective-permute-start.7 = (f32[16,8192]{1,0:T(8,128)S(1)}, f32[16,8192]{1,0:T(8,128)}, u32[]{:S(2)}, u32[]{:S(2)}) collective-permute-start(f32[16,8192]{1,0:T(8,128)S(1)} %get-tuple-element.17), channel_id=1, source_target_pairs={{1,0},{2,1},{3,2},{4,3},{5,4},{6,5},{7,6},{8,7},{9,8},{10,9},{11,1... | collective-permute-start | bytes 1572872 | tf_op jit(solution)/shard_map/ppermute | solution.py:25
  125.2 17.1 %collective-permute-start.8 = (f32[16,8192]{1,0:T(8,128)}, f32[16,8192]{1,0:T(8,128)}, u32[]{:S(2)}, u32[]{:S(2)}) collective-permute-start(f32[16,8192]{1,0:T(8,128)} %get-tuple-element.24), channel_id=1, source_target_pairs={{0,1},{1,2},{2,3},{3,4},{4,5},{5,6},{6,7},{7,8},{8,9},{9,10},{10,1... | collective-permute-start | bytes 1572872 | tf_op jit(solution)/shard_map/ppermute | solution.py:33
  127.7 14.6 %collective-permute-start.9 = (f32[16,8192]{1,0:T(8,128)S(1)}, f32[16,8192]{1,0:T(8,128)}, u32[]{:S(2)}, u32[]{:S(2)}) collective-permute-start(f32[16,8192]{1,0:T(8,128)S(1)} %get-tuple-element.25), channel_id=1, source_target_pairs={{1,0},{2,1},{3,2},{4,3},{5,4},{6,5},{7,6},{8,7},{9,8},{10,9},{11,1... | collective-permute-start | bytes 1572872 | tf_op jit(solution)/shard_map/ppermute | solution.py:33

commit v14 on v10

--- a/solution.py
+++ b/solution.py
@@ -74,9 +74,13 @@
     products = (
         jnp.einsum("ski,kij->ksj", pieces, tile_stack, precision=PRODUCT_PRECISION) * live_slot[:, None, None]
     )
-    onehot = (cols_idx[:, None] == jnp.arange(3 * COL_BLOCKS)[None, :]).astype(jnp.float32)
-    summed = jnp.einsum("kc,ksj->scj", onehot, products, precision=PRODUCT_PRECISION)
-    return summed.reshape(scenario_rows, 3 * COL_BLOCKS * tile_edge)
+    bands = []
+    for band in range(3):
+        targets = band * COL_BLOCKS + jnp.arange(COL_BLOCKS)
+        onehot = (cols_idx[:, None] == targets[None, :]).astype(jnp.float32)
+        summed = jnp.einsum("kc,ksj->scj", onehot, products, precision=PRODUCT_PRECISION)
+        bands.append(summed.reshape(scenario_rows, COL_BLOCKS * tile_edge))
+    return bands
 
 
 def forward_apply(vector, tile_stack, rows_idx, cols_idx, live_slot):
@@ -86,10 +90,7 @@
 
 def transpose_apply(field, tile_stack, rows_idx, cols_idx, live_slot, beside=None):
     partial_sums = transpose_local(field, tile_stack, rows_idx, cols_idx, live_slot)
-    band_width = partial_sums.shape[1] // 3
-    lower = partial_sums[:, :band_width]
-    middle = partial_sums[:, band_width : 2 * band_width]
-    upper = partial_sums[:, 2 * band_width :]
+    lower, middle, upper = partial_sums
     from_below = from_behind(upper, ("row", "col"), 1)
     from_above = from_behind(lower, ("row", "col"), -1)
     extra = None

time: 156 us -> 158 us (1.013)
  blocking collectives: 51.5 us -> 22.2 us
  starting transfers between devices: 29.1 us -> 43.2 us
  waiting for transfers between devices: 6.5 us -> 17.7 us
  matrix products: 38.7 us -> 42.3 us
    all_to_all x4 -> x2, blocking collectives: 51.5 us -> 22.2 us  [all_sum(): gathered = lax.all_to_all(spread, axes, 0, 0, tiled=True)]
    all_to_all x1 -> x3, starting transfers between devices: 8.69 us -> 22.5 us  [all_sum(): gathered = lax.all_to_all(spread, axes, 0, 0, tiled=True)]
    all_to_all x1 -> x3, waiting for transfers between devices: 6.48 us -> 17.7 us  [all_sum(): gathered = lax.all_to_all(spread, axes, 0, 0, tiled=True)]
    dot_general x3 -> x9, matrix products: 2.97 us -> 6.49 us  [transpose_local(): jnp.einsum('kc,ksj->scj', onehot, products, precision=PRODUCT_PRECISION)]
    slice x3 -> x0, local copies, waits for them, and re-layouts: 1.83 us -> none  [transpose_apply(): upper = partial_sums[:, 2 * band_width:]]
    unnamed x11 -> x15, local copies, waits for them, and re-layouts: 3.03 us -> 4.02 us
  transfers between devices with their start and end apart: 11 -> 13, of which waited for: 1 -> 3; matrix products, arithmetic and copies ran while one was open for 1% -> 5% of each run, Pallas kernels for 6% -> 5%
where the time goes in v14:
time: 158 us; the launch traced here: 157 us
  starting transfers between devices  43.2 us (27%)
  matrix products  42.3 us (27%)
  blocking collectives  22.2 us (14%)
  waiting for transfers between devices  17.7 us (11%)
  local copies, waits for them, and re-layouts  13.7 us (9%)
  Pallas kernels  8.59 us (5%)
  other arithmetic  7.79 us (5%)
  between operations  1.77 us (1%)
    all_to_all x3, starting transfers between devices, all_sum(): gathered = lax.all_to_all(spread, axes, 0, 0, tiled=True)  22.5 us
    all_to_all x2, blocking collectives, all_sum(): gathered = lax.all_to_all(spread, axes, 0, 0, tiled=True)  22.2 us
    dot_general x3, matrix products, transpose_local(): jnp.einsum('ski,kij->ksj', pieces, tile_stack, precision=PRODUCT_PRECISION)  20.6 us
    all_to_all x3, waiting for transfers between devices, all_sum(): gathered = lax.all_to_all(spread, axes, 0, 0, tiled=True)  17.7 us
    dot_general x2, matrix products, forward_local(): jnp.einsum('skj,kji->ksi', pieces, tile_stack, precision=PRODUCT_PRECISION)  13.8 us
    ppermute x6, starting transfers between devices, from_behind(): return lax.ppermute(shard, axis, pairs)  11.2 us
    pallas_call x1, Pallas kernels, transpose_blocks(): pl.pallas_call(body, grid=(slots // step,), in_specs=[pl.BlockSpec(memory...  8.59 us
    ppermute x2, starting transfers between devices, with_halo(): before = lax.ppermute(last, axis, up)  6.88 us
  transfers between devices with their start and end apart: 13, of which 3 were waited for; matrix products, arithmetic and copies ran while one was open for 5% of the time, Pallas kernels for 5%

profile of v14, /device:TPU:0, one launch (start us, length us, event | category | flops | bytes accessed | tf_op | source)
XLA Modules:
  0.0 157.2 jit_solution(4760968388168535516)
XLA Ops:
  1.3 0.7 compare_select_fusion.1
  2.0 1.0 copy_bitcast_fusion.11
  3.0 0.8 gather_fusion
  3.8 6.8 %convolution_multiply_fusion.4 = f32[160,16,128]{2,1,0:T(8,128)S(1)} fusion(f32[160,16,128]{2,1,0:T(8,128)S(1)} %gather_fusion, f32[160]{0:T(256)S(1)} %compare_convert_fusion, f32[1,160,128,128]{3,2,1,0:T(8,128)} %param.6), kind=kOutput, calls=%fused_computation.13 | convolution fusion | flops 251985920 | bytes 13107840 | tf_op jit(solution)/shard_map/ski,kij->ksj/dot_general | solution.py:75
  10.6 0.7 fusion.23
  11.7 2.4 %collective-permute-start = (f32[16,8192]{1,0:T(8,128)S(1)}, f32[16,8192]{1,0:T(8,128)S(1)}, u32[]{:S(2)}, u32[]{:S(2)}) collective-permute-start(f32[16,8192]{1,0:T(8,128)S(1)} %bitcast.191), channel_id=1, source_target_pairs={{0,1},{1,2},{2,3},{3,4},{4,5},{5,6},{6,7},{7,8},{8,9},{9,10},{10,1... | collective-permute-start | bytes 1572872 | tf_op jit(solution)/shard_map/ppermute | solution.py:33
  14.1 0.7 fusion.21
  15.1 1.3 collective-permute-start.1
  16.4 0.7 fusion.25
  18.0 8.6 %shard_map.68 = f32[160,128,128]{2,1,0:T(8,128)} custom-call(f32[1,1]{1,0:T(1,128)} %slice.22.anchor_ref, f32[160,128,128]{2,1,0:T(8,128)} %bitcast.175), custom_call_target="tpu_custom_call" | custom-call | bytes 20971520 | tf_op jit(solution)/shard_map/pallas_call | solution.py:45
  27.0 5.2 %collective-permute-start.2 = (f32[16,8192]{1,0:T(8,128)S(1)}, f32[16,8192]{1,0:T(8,128)S(1)}, u32[]{:S(2)}, u32[]{:S(2)}) collective-permute-start(f32[16,8192]{1,0:T(8,128)S(1)} %get-tuple-element.23), channel_id=1, source_target_pairs={{0,1},{1,2},{2,3},{3,4},{4,5},{5,6},{6,7},{7,8},{8,9},{9,10},{10,1... | collective-permute-start | bytes 1572872 | tf_op jit(solution)/shard_map/ppermute | solution.py:24
  32.1 1.3 collective-permute-start.3
  34.1 9.2 %all-to-all-start = ((f32[16,2,16]{2,1,0:T(2,128)}), f32[16,2,16]{2,1,0:T(2,128)S(1)}, u32[]{:S(2)}, u32[]{:S(2)}) async-start(f32[16,2,16]{2,1,0:T(2,128)} %broadcast_in_dim.10), calls=%async_computation | async-start | bytes 32768 | tf_op jit(solution)/shard_map/all_to_all | solution.py:109
  43.3 6.5 %all-to-all-done = f32[16,2,16]{2,1,0:T(2,128)S(1)} async-done(((f32[16,2,16]{2,1,0:T(2,128)}), f32[16,2,16]{2,1,0:T(2,128)S(1)}, u32[]{:S(2)}, u32[]{:S(2)}) %all-to-all-start) | async-done | bytes 2080 | tf_op jit(solution)/shard_map/all_to_all | solution.py:109
  50.0 0.8 gather_fusion.1
  50.8 6.8 %convolution_multiply_fusion.3 = f32[160,16,128]{2,1,0:T(8,128)S(1)} fusion(f32[160,128,128]{2,1,0:T(8,128)} %shard_map.68, f32[160,16,128]{2,1,0:T(8,128)S(1)} %gather_fusion.1, f32[160]{0:T(256)S(1)} %compare_convert_fusion), kind=kOutput, calls=%fused_computation.12 | convolution fusion | flops 251985920 | bytes 13107840 | tf_op jit(solution)/shard_map/skj,kji->ksi/dot_general | solution.py:63
  57.7 0.7 fusion.7
  58.9 0.8 gather_fusion.2
  59.7 6.8 %convolution_multiply_fusion.2 = f32[160,16,128]{2,1,0:T(8,128)S(1)} fusion(f32[160,16,128]{2,1,0:T(8,128)S(1)} %gather_fusion.2, f32[160]{0:T(256)S(1)} %compare_convert_fusion, f32[1,160,128,128]{3,2,1,0:T(8,128)} %param.6), kind=kOutput, calls=%fused_computation.11 | convolution fusion | flops 251985920 | bytes 13107840 | tf_op jit(solution)/shard_map/ski,kij->ksj/dot_general | solution.py:75
  66.6 0.7 fusion.17
  67.3 0.7 fusion.15
  68.0 1.1 copy.148
  69.1 2.5 %collective-permute-start.4 = (f32[16,8192]{1,0:T(8,128)}, f32[16,8192]{1,0:T(8,128)}, u32[]{:S(2)}, u32[]{:S(2)}) collective-permute-start(f32[16,8192]{1,0:T(8,128)} %bitcast.170), channel_id=1, source_target_pairs={{0,1},{1,2},{2,3},{3,4},{4,5},{5,6},{6,7},{7,8},{8,9},{9,10},{10,1... | collective-permute-start | bytes 1572872 | tf_op jit(solution)/shard_map/ppermute | solution.py:33
  71.9 1.3 collective-permute-start.5
  73.8 6.3 %all-to-all-start.1 = ((f32[16,1,16]{2,1,0:T(1,128)}), f32[16,1,16]{2,1,0:T(1,128)S(1)}, u32[]{:S(2)}, u32[]{:S(2)}) async-start(f32[16,1,16]{2,1,0:T(1,128)} %broadcast_in_dim.11), calls=%async_computation.1 | async-start | bytes 16384 | tf_op jit(solution)/shard_map/all_to_all | solution.py:109
  80.1 0.7 fusion.19
  80.8 5.6 %all-to-all-done.1 = f32[16,1,16]{2,1,0:T(1,128)S(1)} async-done(((f32[16,1,16]{2,1,0:T(1,128)}), f32[16,1,16]{2,1,0:T(1,128)S(1)}, u32[]{:S(2)}, u32[]{:S(2)}) %all-to-all-start.1) | async-done | bytes 1056 | tf_op jit(solution)/shard_map/all_to_all | solution.py:109
  86.5 1.7 %multiply_reduce_fusion.1 = (f32[16]{0:T(128)S(1)}, f32[16,8192]{1,0:T(8,128)S(1)}) fusion(f32[16,8192]{1,0:T(8,128)S(1)} %get-tuple-element.23, f32[16]{0:T(128)S(1)} %get-tuple-element.20, f32[16]{0:T(128)S(1)} %add_sqrt_fusion.3, f32[16,8192]{1,0:T(8,128)} %collective-permute-done.5, f32[16,8192]{1,0:T(8,128)} %collective-permute-done.4, ...), kind=kLoop, calls=%fused_computation.60 | loop fusion | flops 1048560 | bytes 2621632 | tf_op jit(solution)/shard_map/reduce_sum | solution.py:114
  88.1 1.7 %collective-permute-start.6 = (f32[16,8192]{1,0:T(8,128)S(1)}, f32[16,8192]{1,0:T(8,128)S(1)}, u32[]{:S(2)}, u32[]{:S(2)}) collective-permute-start(f32[16,8192]{1,0:T(8,128)S(1)} %get-tuple-element.17), channel_id=1, source_target_pairs={{0,1},{1,2},{2,3},{3,4},{4,5},{5,6},{6,7},{7,8},{8,9},{9,10},{10,1... | collective-permute-start | bytes 1572872 | tf_op jit(solution)/shard_map/ppermute | solution.py:24
  89.9 1.3 collective-permute-start.7
  91.2 13.2 %all_to_all.29 = f32[16,1,16]{2,1,0:T(1,128)S(1)} all-to-all(f32[16,1,16]{2,1,0:T(1,128)S(1)} %broadcast_in_dim.12), channel_id=1, replica_groups=mesh['group'=2,'row'=8,'col'=2] {'row','col'}, dimensions={0} | all-to-all | bytes 2048 | tf_op jit(solution)/shard_map/all_to_all | solution.py:109
  104.4 1.2 copy_bitcast_fusion
  105.6 1.9 %gather_fusion.3 = f32[160,16,128]{2,1,0:T(8,128)} fusion(f32[16,192,128]{2,0,1:T(8,128)S(1)} %copy_bitcast_fusion, s32[1024]{0:T(1024)S(1)} %pad_clamp_fusion), kind=kCustom, calls=%fused_computation.3 | custom fusion | bytes 2622080 | tf_op jit(solution)/shard_map/gather | solution.py:61
  107.5 7.0 %convolution_multiply_fusion.1 = f32[160,16,128]{2,1,0:T(8,128)S(1)} fusion(f32[160,128,128]{2,1,0:T(8,128)} %shard_map.68, f32[160,16,128]{2,1,0:T(8,128)} %gather_fusion.3, f32[160]{0:T(256)S(1)} %compare_convert_fusion), kind=kOutput, calls=%fused_computation.10 | convolution fusion | flops 251985920 | bytes 13107840 | tf_op jit(solution)/shard_map/skj,kji->ksi/dot_general | solution.py:63
  114.5 0.7 fusion.5
  115.5 1.9 %gather_fusion.4 = f32[160,16,128]{2,1,0:T(8,128)} fusion(f32[16,32,128]{2,0,1:T(8,128)S(1)} %copy_bitcast_fusion.9, s32[1024]{0:T(1024)S(1)} %pad_clamp_fusion.1), kind=kCustom, calls=%fused_computation.4 | custom fusion | bytes 2622080 | tf_op jit(solution)/shard_map/gather | solution.py:73
  117.4 7.0 %convolution_multiply_fusion = f32[160,16,128]{2,1,0:T(8,128)S(1)} fusion(f32[160,16,128]{2,1,0:T(8,128)} %gather_fusion.4, f32[160]{0:T(256)S(1)} %compare_convert_fusion, f32[1,160,128,128]{3,2,1,0:T(8,128)} %param.6), kind=kOutput, calls=%fused_computation.9 | convolution fusion | flops 251985920 | bytes 13107840 | tf_op jit(solution)/shard_map/ski,kij->ksj/dot_general | solution.py:75
  124.4 0.7 fusion.11
  125.2 0.7 fusion.9
  126.2 2.5 %collective-permute-start.8 = (f32[16,8192]{1,0:T(8,128)S(1)}, f32[16,8192]{1,0:T(8,128)}, u32[]{:S(2)}, u32[]{:S(2)}) collective-permute-start(f32[16,8192]{1,0:T(8,128)S(1)} %bitcast.189), channel_id=1, source_target_pairs={{0,1},{1,2},{2,3},{3,4},{4,5},{5,6},{6,7},{7,8},{8,9},{9,10},{10,1... | collective-permute-start | bytes 1572872 | tf_op jit(solution)/shard_map/ppermute | solution.py:33
  128.7 1.1 copy.145
  129.8 1.3 collective-permute-start.9
  131.7 7.0 %all-to-all-start.3 = ((f32[16,1,16]{2,1,0:T(1,128)}), f32[16,1,16]{2,1,0:T(1,128)S(1)}, u32[]{:S(2)}, u32[]{:S(2)}) async-start(f32[16,1,16]{2,1,0:T(1,128)} %broadcast_in_dim.13), calls=%async_computation.3 | async-start | bytes 16384 | tf_op jit(solution)/shard_map/all_to_all | solution.py:109
  138.8 0.7 fusion.13
  139.5 5.6 %all-to-all-done.3 = f32[16,1,16]{2,1,0:T(1,128)S(1)} async-done(((f32[16,1,16]{2,1,0:T(1,128)}), f32[16,1,16]{2,1,0:T(1,128)S(1)}, u32[]{:S(2)}, u32[]{:S(2)}) %all-to-all-start.3) | async-done | bytes 1056 | tf_op jit(solution)/shard_map/all_to_all | solution.py:109
  145.1 1.7 %multiply_reduce_fusion = (f32[16]{0:T(128)S(1)}, f32[16,8192]{1,0:T(8,128)S(1)}) fusion(f32[16,8192]{1,0:T(8,128)S(1)} %get-tuple-element.17, f32[16]{0:T(128)S(1)} %add_sqrt_fusion.2, f32[16]{0:T(128)S(1)} %add_sqrt_fusion.1, f32[16,8192]{1,0:T(8,128)} %collective-permute-done.9, f32[16,8192]{1,0:T(8,128)} %collective-permute-done.8, ...), kind=kLoop, calls=%fused_computation.57 | loop fusion | flops 1048560 | bytes 2621632 | tf_op jit(solution)/shard_map/reduce_sum | solution.py:114
  146.8 9.0 %all_to_all.30 = f32[16,1,16]{2,1,0:T(1,128)S(1)} all-to-all(f32[16,1,16]{2,1,0:T(1,128)S(1)} %broadcast_in_dim.14), channel_id=1, replica_groups=mesh['group'=2,'row'=8,'col'=2] {'row','col'}, dimensions={0} | all-to-all | bytes 2048 | tf_op jit(solution)/shard_map/all_to_all | solution.py:109
  155.9 1.2 multiply_subtract_fusion
  (57 shorter events, 5.6 us)
Async XLA Ops:
  3.8 6.8 %copy-start.2 = (s32[1,160]{1,0:T(1,128)S(1)}, s32[1,160]{1,0:T(1,128)}, u32[]{:S(2)}) copy-start(s32[1,160]{1,0:T(1,128)} %param.8) | copy-start | bytes 1924
  11.7 15.1 %collective-permute-start = (f32[16,8192]{1,0:T(8,128)S(1)}, f32[16,8192]{1,0:T(8,128)S(1)}, u32[]{:S(2)}, u32[]{:S(2)}) collective-permute-start(f32[16,8192]{1,0:T(8,128)S(1)} %bitcast.191), channel_id=1, source_target_pairs={{0,1},{1,2},{2,3},{3,4},{4,5},{5,6},{6,7},{7,8},{8,9},{9,10},{10,1... | collective-permute-start | bytes 1572872 | tf_op jit(solution)/shard_map/ppermute | solution.py:33
  15.1 11.6 %collective-permute-start.1 = (f32[16,8192]{1,0:T(8,128)S(1)}, f32[16,8192]{1,0:T(8,128)S(1)}, u32[]{:S(2)}, u32[]{:S(2)}) collective-permute-start(f32[16,8192]{1,0:T(8,128)S(1)} %bitcast.192), channel_id=1, source_target_pairs={{1,0},{2,1},{3,2},{4,3},{5,4},{6,5},{7,6},{8,7},{9,8},{10,9},{11,1... | collective-permute-start | bytes 1572872 | tf_op jit(solution)/shard_map/ppermute | solution.py:33
  18.0 8.6 %copy-start = (f32[16,4096]{1,0:T(8,128)S(1)}, f32[16,4096]{1,0:T(8,128)}, u32[]{:S(2)}) copy-start(f32[16,4096]{1,0:T(8,128)} %param.5) | copy-start | bytes 786436
  27.0 22.9 %collective-permute-start.2 = (f32[16,8192]{1,0:T(8,128)S(1)}, f32[16,8192]{1,0:T(8,128)S(1)}, u32[]{:S(2)}, u32[]{:S(2)}) collective-permute-start(f32[16,8192]{1,0:T(8,128)S(1)} %get-tuple-element.23), channel_id=1, source_target_pairs={{0,1},{1,2},{2,3},{3,4},{4,5},{5,6},{6,7},{7,8},{8,9},{9,10},{10,1... | collective-permute-start | bytes 1572872 | tf_op jit(solution)/shard_map/ppermute | solution.py:24
  32.1 17.7 %collective-permute-start.3 = (f32[16,8192]{1,0:T(8,128)S(1)}, f32[16,8192]{1,0:T(8,128)S(1)}, u32[]{:S(2)}, u32[]{:S(2)}) collective-permute-start(f32[16,8192]{1,0:T(8,128)S(1)} %get-tuple-element.23), channel_id=1, source_target_pairs={{1,0},{2,1},{3,2},{4,3},{5,4},{6,5},{7,6},{8,7},{9,8},{10,9},{11,1... | collective-permute-start | bytes 1572872 | tf_op jit(solution)/shard_map/ppermute | solution.py:25
  34.1 15.7 %all-to-all-start = ((f32[16,2,16]{2,1,0:T(2,128)}), f32[16,2,16]{2,1,0:T(2,128)S(1)}, u32[]{:S(2)}, u32[]{:S(2)}) async-start(f32[16,2,16]{2,1,0:T(2,128)} %broadcast_in_dim.10), calls=%async_computation | async-start | bytes 32768 | tf_op jit(solution)/shard_map/all_to_all | solution.py:109
  50.8 6.8 %copy-start.3 = (s32[1,160]{1,0:T(1,128)S(1)}, s32[1,160]{1,0:T(1,128)}, u32[]{:S(2)}) copy-start(s32[1,160]{1,0:T(1,128)} %param.7) | copy-start | bytes 1924
  57.6 1.0 copy-start.1
  69.1 17.3 %collective-permute-start.4 = (f32[16,8192]{1,0:T(8,128)}, f32[16,8192]{1,0:T(8,128)}, u32[]{:S(2)}, u32[]{:S(2)}) collective-permute-start(f32[16,8192]{1,0:T(8,128)} %bitcast.170), channel_id=1, source_target_pairs={{0,1},{1,2},{2,3},{3,4},{4,5},{5,6},{6,7},{7,8},{8,9},{9,10},{10,1... | collective-permute-start | bytes 1572872 | tf_op jit(solution)/shard_map/ppermute | solution.py:33
  71.9 14.6 %collective-permute-start.5 = (f32[16,8192]{1,0:T(8,128)S(1)}, f32[16,8192]{1,0:T(8,128)}, u32[]{:S(2)}, u32[]{:S(2)}) collective-permute-start(f32[16,8192]{1,0:T(8,128)S(1)} %bitcast.190), channel_id=1, source_target_pairs={{1,0},{2,1},{3,2},{4,3},{5,4},{6,5},{7,6},{8,7},{9,8},{10,9},{11,1... | collective-permute-start | bytes 1572872 | tf_op jit(solution)/shard_map/ppermute | solution.py:33
  73.8 12.6 %all-to-all-start.1 = ((f32[16,1,16]{2,1,0:T(1,128)}), f32[16,1,16]{2,1,0:T(1,128)S(1)}, u32[]{:S(2)}, u32[]{:S(2)}) async-start(f32[16,1,16]{2,1,0:T(1,128)} %broadcast_in_dim.11), calls=%async_computation.1 | async-start | bytes 16384 | tf_op jit(solution)/shard_map/all_to_all | solution.py:109
  88.1 16.3 %collective-permute-start.6 = (f32[16,8192]{1,0:T(8,128)S(1)}, f32[16,8192]{1,0:T(8,128)S(1)}, u32[]{:S(2)}, u32[]{:S(2)}) collective-permute-start(f32[16,8192]{1,0:T(8,128)S(1)} %get-tuple-element.17), channel_id=1, source_target_pairs={{0,1},{1,2},{2,3},{3,4},{4,5},{5,6},{6,7},{7,8},{8,9},{9,10},{10,1... | collective-permute-start | bytes 1572872 | tf_op jit(solution)/shard_map/ppermute | solution.py:24
  89.9 14.6 %collective-permute-start.7 = (f32[16,8192]{1,0:T(8,128)S(1)}, f32[16,8192]{1,0:T(8,128)}, u32[]{:S(2)}, u32[]{:S(2)}) collective-permute-start(f32[16,8192]{1,0:T(8,128)S(1)} %get-tuple-element.17), channel_id=1, source_target_pairs={{1,0},{2,1},{3,2},{4,3},{5,4},{6,5},{7,6},{8,7},{9,8},{10,9},{11,1... | collective-permute-start | bytes 1572872 | tf_op jit(solution)/shard_map/ppermute | solution.py:25
  126.2 18.9 %collective-permute-start.8 = (f32[16,8192]{1,0:T(8,128)S(1)}, f32[16,8192]{1,0:T(8,128)}, u32[]{:S(2)}, u32[]{:S(2)}) collective-permute-start(f32[16,8192]{1,0:T(8,128)S(1)} %bitcast.189), channel_id=1, source_target_pairs={{0,1},{1,2},{2,3},{3,4},{4,5},{5,6},{6,7},{7,8},{8,9},{9,10},{10,1... | collective-permute-start | bytes 1572872 | tf_op jit(solution)/shard_map/ppermute | solution.py:33
  129.8 15.3 %collective-permute-start.9 = (f32[16,8192]{1,0:T(8,128)}, f32[16,8192]{1,0:T(8,128)}, u32[]{:S(2)}, u32[]{:S(2)}) collective-permute-start(f32[16,8192]{1,0:T(8,128)} %bitcast.167), channel_id=1, source_target_pairs={{1,0},{2,1},{3,2},{4,3},{5,4},{6,5},{7,6},{8,7},{9,8},{10,9},{11,1... | collective-permute-start | bytes 1572872 | tf_op jit(solution)/shard_map/ppermute | solution.py:33
  131.7 13.4 %all-to-all-start.3 = ((f32[16,1,16]{2,1,0:T(1,128)}), f32[16,1,16]{2,1,0:T(1,128)S(1)}, u32[]{:S(2)}, u32[]{:S(2)}) async-start(f32[16,1,16]{2,1,0:T(1,128)} %broadcast_in_dim.13), calls=%async_computation.3 | async-start | bytes 16384 | tf_op jit(solution)/shard_map/all_to_all | solution.py:109

commit v15 on v10

--- a/solution.py
+++ b/solution.py
@@ -133,6 +133,7 @@
         return forward_apply(vector, tile_stack_t, rows_idx, cols_idx, live_slot)
 
     totals = all_sum(jnp.stack([squares(observed), squares(start_raw)]), axes)
+    start_raw, totals = lax.optimization_barrier((start_raw, totals))
     row_norm = jnp.sqrt(totals[0] + 1e-06)
     col_norm = jnp.sqrt(totals[1] / (row_norm * row_norm) + 1e-06)
     scale = row_norm * col_norm

time: 156 us -> 164 us (1.051)
  starting transfers between devices: 29.1 us -> 36.3 us
  blocking collectives: 51.5 us -> 48.1 us
  waiting for transfers between devices: 6.5 us -> 9.06 us
    ppermute x6, starting transfers between devices: 10.4 us -> 19.1 us  [from_behind(): return lax.ppermute(shard, axis, pairs)]
    all_to_all x4, blocking collectives: 51.5 us -> 48.1 us  [all_sum(): gathered = lax.all_to_all(spread, axes, 0, 0, tiled=True)]
    ppermute x2, starting transfers between devices: 7.4 us -> 4.46 us  [with_halo(): before = lax.ppermute(last, axis, up)]
    ppermute x2, waiting for transfers between devices: 0.01 us -> 2.55 us  [with_halo(): after = lax.ppermute(leading, axis, down)]
    unnamed x11 -> x13, local copies, waits for them, and re-layouts: 3.03 us -> 3.81 us
  transfers between devices with their start and end apart: 11 -> 11, of which waited for: 1 -> 2; matrix products, arithmetic and copies ran while one was open for 1% -> 0% of each run, Pallas kernels for 6% -> 5%
where the time goes in v15:
time: 164 us; the launch traced here: 163 us
  blocking collectives  48.1 us (29%)
  matrix products  38.8 us (24%)
  starting transfers between devices  36.3 us (22%)
  local copies, waits for them, and re-layouts  13.2 us (8%)
  waiting for transfers between devices  9.06 us (6%)
  Pallas kernels  8.59 us (5%)
  other arithmetic  7.25 us (4%)
  between operations  1.72 us (1%)
    all_to_all x4, blocking collectives, all_sum(): gathered = lax.all_to_all(spread, axes, 0, 0, tiled=True)  48.1 us
    dot_general x3, matrix products, transpose_local(): jnp.einsum('ski,kij->ksj', pieces, tile_stack, precision=PRODUCT_PRECISION)  20.5 us
    ppermute x6, starting transfers between devices, from_behind(): return lax.ppermute(shard, axis, pairs)  19.1 us
    dot_general x2, matrix products, forward_local(): jnp.einsum('skj,kji->ksi', pieces, tile_stack, precision=PRODUCT_PRECISION)  13.9 us
    all_to_all x1, starting transfers between devices, all_sum(): gathered = lax.all_to_all(spread, axes, 0, 0, tiled=True)  9.91 us
    pallas_call x1, Pallas kernels, transpose_blocks(): pl.pallas_call(body, grid=(slots // step,), in_specs=[pl.BlockSpec(memory...  8.59 us
    all_to_all x1, waiting for transfers between devices, all_sum(): gathered = lax.all_to_all(spread, axes, 0, 0, tiled=True)  6.48 us
    ppermute x2, starting transfers between devices, with_halo(): before = lax.ppermute(last, axis, up)  4.46 us
  transfers between devices with their start and end apart: 11, of which 2 were waited for; matrix products, arithmetic and copies ran while one was open for 0% of the time, Pallas kernels for 5%

profile of v15, /device:TPU:0, one launch (start us, length us, event | category | flops | bytes accessed | tf_op | source)
XLA Modules:
  0.0 162.9 jit_solution(4509183019002612304)
XLA Ops:
  1.3 0.7 compare_select_fusion.1
  2.0 1.0 copy_bitcast_fusion.7
  3.0 0.8 gather_fusion
  3.8 6.8 %convolution_multiply_fusion.4 = f32[160,16,128]{2,1,0:T(8,128)S(1)} fusion(f32[160,16,128]{2,1,0:T(8,128)S(1)} %gather_fusion, f32[160]{0:T(256)S(1)} %compare_convert_fusion, f32[1,160,128,128]{3,2,1,0:T(8,128)} %param.6), kind=kOutput, calls=%fused_computation.16 | convolution fusion | flops 251985920 | bytes 13107840 | tf_op jit(solution)/shard_map/ski,kij->ksj/dot_general | solution.py:75
  10.7 1.0 fusion.13
  11.7 0.9 copy.79
  12.7 2.4 %collective-permute-start = (f32[16,8192]{1,0:T(8,128)S(1)}, f32[16,8192]{1,0:T(8,128)S(1)}, u32[]{:S(2)}, u32[]{:S(2)}) collective-permute-start(f32[16,8192]{1,0:T(8,128)S(1)} %get-tuple-element.32), channel_id=1, source_target_pairs={{0,1},{1,2},{2,3},{3,4},{4,5},{5,6},{6,7},{7,8},{8,9},{9,10},{10,1... | collective-permute-start | bytes 1572872 | tf_op jit(solution)/shard_map/ppermute | solution.py:33
  15.1 1.3 collective-permute-start.1
  16.4 0.5 slice.60.anchor_ref
  16.9 8.6 %shard_map.68 = f32[160,128,128]{2,1,0:T(8,128)} custom-call(f32[1,1]{1,0:T(1,128)} %slice.60.anchor_ref, f32[160,128,128]{2,1,0:T(8,128)} %bitcast.119), custom_call_target="tpu_custom_call" | custom-call | bytes 20971520 | tf_op jit(solution)/shard_map/pallas_call | solution.py:45
  25.9 0.6 broadcast_in_dim.10
  26.5 9.9 %all-to-all-start = ((f32[16,2,16]{2,1,0:T(2,128)}), f32[16,2,16]{2,1,0:T(2,128)S(1)}, u32[]{:S(2)}, u32[]{:S(2)}) async-start(f32[16,2,16]{2,1,0:T(2,128)} %broadcast_in_dim.10), calls=%async_computation | async-start | bytes 32768 | tf_op jit(solution)/shard_map/all_to_all | solution.py:108
  36.4 6.5 %all-to-all-done = f32[16,2,16]{2,1,0:T(2,128)S(1)} async-done(((f32[16,2,16]{2,1,0:T(2,128)}), f32[16,2,16]{2,1,0:T(2,128)S(1)}, u32[]{:S(2)}, u32[]{:S(2)}) %all-to-all-start) | async-done | bytes 2080 | tf_op jit(solution)/shard_map/all_to_all | solution.py:108
  42.9 1.7 %collective-permute-start.2 = (f32[16,8192]{1,0:T(8,128)S(1)}, f32[16,8192]{1,0:T(8,128)S(1)}, u32[]{:S(2)}, u32[]{:S(2)}) collective-permute-start(f32[16,8192]{1,0:T(8,128)S(1)} %get-tuple-element.8), channel_id=1, source_target_pairs={{0,1},{1,2},{2,3},{3,4},{4,5},{5,6},{6,7},{7,8},{8,9},{9,10},{10,1... | collective-permute-start | bytes 1572872 | tf_op jit(solution)/shard_map/ppermute | solution.py:24
  44.6 1.5 collective-permute-start.3
  46.2 2.6 %collective-permute-done.3 = f32[16,8192]{1,0:T(8,128)S(1)} collective-permute-done((f32[16,8192]{1,0:T(8,128)S(1)}, f32[16,8192]{1,0:T(8,128)S(1)}, u32[]{:S(2)}, u32[]{:S(2)}) %collective-permute-start.3) | collective-permute-done | bytes 524320 | tf_op jit(solution)/shard_map/ppermute | solution.py:25
  48.8 0.8 gather_fusion.1
  49.7 6.8 %convolution_multiply_fusion.3 = f32[160,16,128]{2,1,0:T(8,128)S(1)} fusion(f32[160,128,128]{2,1,0:T(8,128)} %shard_map.68, f32[160,16,128]{2,1,0:T(8,128)S(1)} %gather_fusion.1, f32[160]{0:T(256)S(1)} %compare_convert_fusion), kind=kOutput, calls=%fused_computation.15 | convolution fusion | flops 251985920 | bytes 13107840 | tf_op jit(solution)/shard_map/skj,kji->ksi/dot_general | solution.py:63
  56.6 0.7 fusion.11
  57.8 0.8 gather_fusion.2
  58.6 6.8 %convolution_multiply_fusion.2 = f32[160,16,128]{2,1,0:T(8,128)S(1)} fusion(f32[160,16,128]{2,1,0:T(8,128)S(1)} %gather_fusion.2, f32[160]{0:T(256)S(1)} %compare_convert_fusion, f32[1,160,128,128]{3,2,1,0:T(8,128)} %param.6), kind=kOutput, calls=%fused_computation.14 | convolution fusion | flops 251985920 | bytes 13107840 | tf_op jit(solution)/shard_map/ski,kij->ksj/dot_general | solution.py:75
  65.5 1.0 fusion.9
  66.5 0.9 copy.78
  67.4 0.9 fusion.44
  68.3 10.3 %collective-permute-start.4 = (f32[16,8192]{1,0:T(8,128)}, f32[16,8192]{1,0:T(8,128)S(1)}, u32[]{:S(2)}, u32[]{:S(2)}) collective-permute-start(f32[16,8192]{1,0:T(8,128)} %get-tuple-element.30), channel_id=1, source_target_pairs={{0,1},{1,2},{2,3},{3,4},{4,5},{5,6},{6,7},{7,8},{8,9},{9,10},{10,1... | collective-permute-start | bytes 1572872 | tf_op jit(solution)/shard_map/ppermute | solution.py:33
  78.6 1.3 collective-permute-start.5
  80.0 12.4 %all_to_all.29 = f32[16,1,16]{2,1,0:T(1,128)S(1)} all-to-all(f32[16,1,16]{2,1,0:T(1,128)S(1)} %broadcast_in_dim.11), channel_id=1, replica_groups=mesh['group'=2,'row'=8,'col'=2] {'row','col'}, dimensions={0} | all-to-all | bytes 2048 | tf_op jit(solution)/shard_map/all_to_all | solution.py:108
  92.4 1.3 multiply_reduce_fusion.1
  93.7 2.8 %collective-permute-start.6 = (f32[16,8192]{1,0:T(8,128)S(1)}, f32[16,8192]{1,0:T(8,128)S(1)}, u32[]{:S(2)}, u32[]{:S(2)}) collective-permute-start(f32[16,8192]{1,0:T(8,128)S(1)} %get-tuple-element.21), channel_id=1, source_target_pairs={{0,1},{1,2},{2,3},{3,4},{4,5},{5,6},{6,7},{7,8},{8,9},{9,10},{10,1... | collective-permute-start | bytes 1572872 | tf_op jit(solution)/shard_map/ppermute | solution.py:24
  96.5 1.3 collective-permute-start.7
  97.8 12.3 %all_to_all.30 = f32[16,1,16]{2,1,0:T(1,128)S(1)} all-to-all(f32[16,1,16]{2,1,0:T(1,128)S(1)} %broadcast_in_dim.12), channel_id=1, replica_groups=mesh['group'=2,'row'=8,'col'=2] {'row','col'}, dimensions={0} | all-to-all | bytes 2048 | tf_op jit(solution)/shard_map/all_to_all | solution.py:108
  110.2 1.2 copy_bitcast_fusion.3
  111.4 1.9 %gather_fusion.3 = f32[160,16,128]{2,1,0:T(8,128)} fusion(f32[16,192,128]{2,0,1:T(8,128)S(1)} %copy_bitcast_fusion.3, s32[1024]{0:T(1024)S(1)} %pad_clamp_fusion), kind=kCustom, calls=%fused_computation.3 | custom fusion | bytes 2622080 | tf_op jit(solution)/shard_map/gather | solution.py:61
  113.3 7.1 %convolution_multiply_fusion.1 = f32[160,16,128]{2,1,0:T(8,128)S(1)} fusion(f32[160,128,128]{2,1,0:T(8,128)} %shard_map.68, f32[160,16,128]{2,1,0:T(8,128)} %gather_fusion.3, f32[160]{0:T(256)S(1)} %compare_convert_fusion), kind=kOutput, calls=%fused_computation.13 | convolution fusion | flops 251985920 | bytes 13107840 | tf_op jit(solution)/shard_map/skj,kji->ksi/dot_general | solution.py:63
  120.3 0.7 fusion.7
  121.0 0.3 multiply_reduce_fusion.3
  121.3 0.8 gather_fusion.4
  122.2 6.8 %convolution_multiply_fusion = f32[160,16,128]{2,1,0:T(8,128)S(1)} fusion(f32[160,16,128]{2,1,0:T(8,128)S(1)} %gather_fusion.4, f32[160]{0:T(256)S(1)} %compare_convert_fusion, f32[1,160,128,128]{3,2,1,0:T(8,128)} %param.6), kind=kOutput, calls=%fused_computation.12 | convolution fusion | flops 251985920 | bytes 13107840 | tf_op jit(solution)/shard_map/ski,kij->ksj/dot_general | solution.py:75
  129.0 1.0 fusion.5
  130.0 0.9 copy.77
  131.0 1.0 fusion.43
  132.0 2.5 %collective-permute-start.8 = (f32[16,8192]{1,0:T(8,128)}, f32[16,8192]{1,0:T(8,128)S(1)}, u32[]{:S(2)}, u32[]{:S(2)}) collective-permute-start(f32[16,8192]{1,0:T(8,128)} %get-tuple-element.28), channel_id=1, source_target_pairs={{0,1},{1,2},{2,3},{3,4},{4,5},{5,6},{6,7},{7,8},{8,9},{9,10},{10,1... | collective-permute-start | bytes 1572872 | tf_op jit(solution)/shard_map/ppermute | solution.py:33
  134.5 1.3 collective-permute-start.9
  135.9 12.6 %all_to_all.31 = f32[16,1,16]{2,1,0:T(1,128)S(1)} all-to-all(f32[16,1,16]{2,1,0:T(1,128)S(1)} %broadcast_in_dim.13), channel_id=1, replica_groups=mesh['group'=2,'row'=8,'col'=2] {'row','col'}, dimensions={0} | all-to-all | bytes 2048 | tf_op jit(solution)/shard_map/all_to_all | solution.py:108
  148.5 0.8 copy-done.2
  149.3 1.5 multiply_reduce_fusion
  150.8 10.8 %all_to_all.32 = f32[16,1,16]{2,1,0:T(1,128)S(1)} all-to-all(f32[16,1,16]{2,1,0:T(1,128)S(1)} %broadcast_in_dim.14), channel_id=1, replica_groups=mesh['group'=2,'row'=8,'col'=2] {'row','col'}, dimensions={0} | all-to-all | bytes 2048 | tf_op jit(solution)/shard_map/all_to_all | solution.py:108
  161.7 1.2 multiply_subtract_fusion
  (48 shorter events, 1.5 us)
Async XLA Ops:
  3.8 6.9 %copy-start.3 = (s32[1,160]{1,0:T(1,128)S(1)}, s32[1,160]{1,0:T(1,128)}, u32[]{:S(2)}) copy-start(s32[1,160]{1,0:T(1,128)} %param.8) | copy-start | bytes 1924
  12.7 12.9 %collective-permute-start = (f32[16,8192]{1,0:T(8,128)S(1)}, f32[16,8192]{1,0:T(8,128)S(1)}, u32[]{:S(2)}, u32[]{:S(2)}) collective-permute-start(f32[16,8192]{1,0:T(8,128)S(1)} %get-tuple-element.32), channel_id=1, source_target_pairs={{0,1},{1,2},{2,3},{3,4},{4,5},{5,6},{6,7},{7,8},{8,9},{9,10},{10,1... | collective-permute-start | bytes 1572872 | tf_op jit(solution)/shard_map/ppermute | solution.py:33
  15.1 10.6 %collective-permute-start.1 = (f32[16,8192]{1,0:T(8,128)S(1)}, f32[16,8192]{1,0:T(8,128)S(1)}, u32[]{:S(2)}, u32[]{:S(2)}) collective-permute-start(f32[16,8192]{1,0:T(8,128)S(1)} %get-tuple-element.33), channel_id=1, source_target_pairs={{1,0},{2,1},{3,2},{4,3},{5,4},{6,5},{7,6},{8,7},{9,8},{10,9},{11,1... | collective-permute-start | bytes 1572872 | tf_op jit(solution)/shard_map/ppermute | solution.py:33
  16.9 8.6 %copy-start = (f32[16,4096]{1,0:T(8,128)S(1)}, f32[16,4096]{1,0:T(8,128)}, u32[]{:S(2)}) copy-start(f32[16,4096]{1,0:T(8,128)} %param.5) | copy-start | bytes 786436
  26.5 16.4 %all-to-all-start = ((f32[16,2,16]{2,1,0:T(2,128)}), f32[16,2,16]{2,1,0:T(2,128)S(1)}, u32[]{:S(2)}, u32[]{:S(2)}) async-start(f32[16,2,16]{2,1,0:T(2,128)} %broadcast_in_dim.10), calls=%async_computation | async-start | bytes 32768 | tf_op jit(solution)/shard_map/all_to_all | solution.py:108
  42.9 3.2 %collective-permute-start.2 = (f32[16,8192]{1,0:T(8,128)S(1)}, f32[16,8192]{1,0:T(8,128)S(1)}, u32[]{:S(2)}, u32[]{:S(2)}) collective-permute-start(f32[16,8192]{1,0:T(8,128)S(1)} %get-tuple-element.8), channel_id=1, source_target_pairs={{0,1},{1,2},{2,3},{3,4},{4,5},{5,6},{6,7},{7,8},{8,9},{9,10},{10,1... | collective-permute-start | bytes 1572872 | tf_op jit(solution)/shard_map/ppermute | solution.py:24
  44.6 4.1 %collective-permute-start.3 = (f32[16,8192]{1,0:T(8,128)S(1)}, f32[16,8192]{1,0:T(8,128)S(1)}, u32[]{:S(2)}, u32[]{:S(2)}) collective-permute-start(f32[16,8192]{1,0:T(8,128)S(1)} %get-tuple-element.8), channel_id=1, source_target_pairs={{1,0},{2,1},{3,2},{4,3},{5,4},{6,5},{7,6},{8,7},{9,8},{10,9},{11,1... | collective-permute-start | bytes 1572872 | tf_op jit(solution)/shard_map/ppermute | solution.py:25
  49.7 6.9 %copy-start.4 = (s32[1,160]{1,0:T(1,128)S(1)}, s32[1,160]{1,0:T(1,128)}, u32[]{:S(2)}) copy-start(s32[1,160]{1,0:T(1,128)} %param.7) | copy-start | bytes 1924
  56.5 1.0 copy-start.1
  68.3 24.1 %collective-permute-start.4 = (f32[16,8192]{1,0:T(8,128)}, f32[16,8192]{1,0:T(8,128)S(1)}, u32[]{:S(2)}, u32[]{:S(2)}) collective-permute-start(f32[16,8192]{1,0:T(8,128)} %get-tuple-element.30), channel_id=1, source_target_pairs={{0,1},{1,2},{2,3},{3,4},{4,5},{5,6},{6,7},{7,8},{8,9},{9,10},{10,1... | collective-permute-start | bytes 1572872 | tf_op jit(solution)/shard_map/ppermute | solution.py:33
  78.6 13.8 %collective-permute-start.5 = (f32[16,8192]{1,0:T(8,128)S(1)}, f32[16,8192]{1,0:T(8,128)}, u32[]{:S(2)}, u32[]{:S(2)}) collective-permute-start(f32[16,8192]{1,0:T(8,128)S(1)} %get-tuple-element.31), channel_id=1, source_target_pairs={{1,0},{2,1},{3,2},{4,3},{5,4},{6,5},{7,6},{8,7},{9,8},{10,9},{11,1... | collective-permute-start | bytes 1572872 | tf_op jit(solution)/shard_map/ppermute | solution.py:33
  93.7 16.5 %collective-permute-start.6 = (f32[16,8192]{1,0:T(8,128)S(1)}, f32[16,8192]{1,0:T(8,128)S(1)}, u32[]{:S(2)}, u32[]{:S(2)}) collective-permute-start(f32[16,8192]{1,0:T(8,128)S(1)} %get-tuple-element.21), channel_id=1, source_target_pairs={{0,1},{1,2},{2,3},{3,4},{4,5},{5,6},{6,7},{7,8},{8,9},{9,10},{10,1... | collective-permute-start | bytes 1572872 | tf_op jit(solution)/shard_map/ppermute | solution.py:24
  96.5 13.7 %collective-permute-start.7 = (f32[16,8192]{1,0:T(8,128)S(1)}, f32[16,8192]{1,0:T(8,128)}, u32[]{:S(2)}, u32[]{:S(2)}) collective-permute-start(f32[16,8192]{1,0:T(8,128)S(1)} %get-tuple-element.21), channel_id=1, source_target_pairs={{1,0},{2,1},{3,2},{4,3},{5,4},{6,5},{7,6},{8,7},{9,8},{10,9},{11,1... | collective-permute-start | bytes 1572872 | tf_op jit(solution)/shard_map/ppermute | solution.py:25
  132.0 16.5 %collective-permute-start.8 = (f32[16,8192]{1,0:T(8,128)}, f32[16,8192]{1,0:T(8,128)S(1)}, u32[]{:S(2)}, u32[]{:S(2)}) collective-permute-start(f32[16,8192]{1,0:T(8,128)} %get-tuple-element.28), channel_id=1, source_target_pairs={{0,1},{1,2},{2,3},{3,4},{4,5},{5,6},{6,7},{7,8},{8,9},{9,10},{10,1... | collective-permute-start | bytes 1572872 | tf_op jit(solution)/shard_map/ppermute | solution.py:33
  134.5 14.7 %collective-permute-start.9 = (f32[16,8192]{1,0:T(8,128)}, f32[16,8192]{1,0:T(8,128)}, u32[]{:S(2)}, u32[]{:S(2)}) collective-permute-start(f32[16,8192]{1,0:T(8,128)} %get-tuple-element.29), channel_id=1, source_target_pairs={{1,0},{2,1},{3,2},{4,3},{5,4},{6,5},{7,6},{8,7},{9,8},{10,9},{11,1... | collective-permute-start | bytes 1572872 | tf_op jit(solution)/shard_map/ppermute | solution.py:33
  148.5 0.8 copy-start.2

commit v16 on v8

--- a/solution.py
+++ b/solution.py
@@ -35,7 +35,7 @@
 
 def transpose_blocks(tile_stack, anchor, first, count, into=None):
     slots, edge, _ = tile_stack.shape
-    step = 16 if count % 16 == 0 and first % 16 == 0 else 1
+    step = count if first % count == 0 else 1
     offset = first // step
 
     def body(anchor_ref, x_ref, *refs):

time: 160 us -> 159 us (level)
  Pallas kernels: 15.7 us -> 13.8 us
    pallas_call x2, Pallas kernels: 15.7 us -> 13.8 us  [transpose_blocks(): pl.pallas_call(body, grid=(count // step,), in_specs=in_specs, out_specs=...]
  transfers between devices with their start and end apart: 11 -> 11, of which waited for: 0 -> 0; matrix products, arithmetic and copies ran while one was open for 1% -> 1% of each run, Pallas kernels for 10% -> 9%
where the time goes in v16:
time: 159 us; the launch traced here: 158 us
  blocking collectives  48.7 us (31%)
  matrix products  38.7 us (24%)
  starting transfers between devices  35.6 us (22%)
  Pallas kernels  13.8 us (9%)
  local copies, waits for them, and re-layouts  12.7 us (8%)
  other arithmetic  7.25 us (5%)
  between operations  1.69 us (1%)
    all_to_all x4, blocking collectives, all_sum(): gathered = lax.all_to_all(spread, axes, 0, 0, tiled=True)  48.7 us
    dot_general x3, matrix products, transpose_local(): jnp.einsum('ski,kij->ksj', pieces, tile_stack, precision=PRODUCT_PRECISION)  20.5 us
    ppermute x6, starting transfers between devices, from_behind(): return lax.ppermute(shard, axis, pairs)  14.6 us
    dot_general x2, matrix products, forward_local(): jnp.einsum('skj,kji->ksi', pieces, tile_stack, precision=PRODUCT_PRECISION)  13.9 us
    pallas_call x2, Pallas kernels, transpose_blocks(): pl.pallas_call(body, grid=(count // step,), in_specs=in_specs, out_specs=...  13.8 us
    ppermute x2, starting transfers between devices, with_halo(): before = lax.ppermute(last, axis, up)  12.1 us
    all_to_all x1, starting transfers between devices, all_sum(): gathered = lax.all_to_all(spread, axes, 0, 0, tiled=True)  6.25 us
    reduce_sum x6, other arithmetic, squares(): return jnp.sum(field * field, axis=1)  3.77 us
  transfers between devices with their start and end apart: 11, of which 0 were waited for; matrix products, arithmetic and copies ran while one was open for 1% of the time, Pallas kernels for 9%

profile of v16, /device:TPU:0, one launch (start us, length us, event | category | flops | bytes accessed | tf_op | source)
XLA Modules:
  0.0 158.5 jit_solution(6030115367863035863)
XLA Ops:
  0.6 1.0 copy_bitcast_fusion.7
  1.6 0.7 compare_select_fusion.1
  3.0 0.8 gather_fusion
  3.8 6.8 %convolution_multiply_fusion.4 = f32[160,16,128]{2,1,0:T(8,128)S(1)} fusion(f32[160,16,128]{2,1,0:T(8,128)S(1)} %gather_fusion, f32[160]{0:T(256)S(1)} %compare_convert_fusion, f32[1,160,128,128]{3,2,1,0:T(8,128)} %param.6), kind=kOutput, calls=%fused_computation.16 | convolution fusion | flops 251985920 | bytes 13107840 | tf_op jit(solution)/shard_map/ski,kij->ksj/dot_general | solution.py:85
  10.7 1.0 fusion.13
  11.7 0.9 copy.82
  12.7 1.3 collective-permute-start.1
  14.0 3.1 %collective-permute-start = (f32[16,8192]{1,0:T(8,128)S(1)}, f32[16,8192]{1,0:T(8,128)S(1)}, u32[]{:S(2)}, u32[]{:S(2)}) collective-permute-start(f32[16,8192]{1,0:T(8,128)S(1)} %get-tuple-element.28), channel_id=1, source_target_pairs={{0,1},{1,2},{2,3},{3,4},{4,5},{5,6},{6,7},{7,8},{8,9},{9,10},{10,1... | collective-permute-start | bytes 1572872 | tf_op jit(solution)/shard_map/ppermute | solution.py:33
  17.1 0.5 slice.64.anchor_ref
  17.6 6.9 %shard_map.68.refs_0_ = f32[160,128,128]{2,1,0:T(8,128)} custom-call(f32[1,1]{1,0:T(1,128)} %slice.64.anchor_ref, f32[160,128,128]{2,1,0:T(8,128)} %bitcast.119), custom_call_target="tpu_custom_call" | custom-call | bytes 10485760 | tf_op jit(solution)/shard_map/pallas_call | solution.py:57
  24.9 1.3 collective-permute-start.3
  26.2 8.2 %collective-permute-start.2 = (f32[16,8192]{1,0:T(8,128)S(1)}, f32[16,8192]{1,0:T(8,128)S(1)}, u32[]{:S(2)}, u32[]{:S(2)}) collective-permute-start(f32[16,8192]{1,0:T(8,128)S(1)} %get-tuple-element.23), channel_id=1, source_target_pairs={{0,1},{1,2},{2,3},{3,4},{4,5},{5,6},{6,7},{7,8},{8,9},{9,10},{10,1... | collective-permute-start | bytes 1572872 | tf_op jit(solution)/shard_map/ppermute | solution.py:24
  34.4 0.6 broadcast_in_dim.10
  35.0 6.2 %all-to-all-start = ((f32[16,2,16]{2,1,0:T(2,128)}), f32[16,2,16]{2,1,0:T(2,128)S(1)}, u32[]{:S(2)}, u32[]{:S(2)}) async-start(f32[16,2,16]{2,1,0:T(2,128)} %broadcast_in_dim.10), calls=%async_computation | async-start | bytes 32768 | tf_op jit(solution)/shard_map/all_to_all | solution.py:118
  41.3 0.5 slice.67.anchor_ref
  41.8 6.9 %shard_map.69 = f32[160,128,128]{2,1,0:T(8,128)} custom-call(f32[1,1]{1,0:T(1,128)} %slice.67.anchor_ref, f32[160,128,128]{2,1,0:T(8,128)} %bitcast.120, f32[160,128,128]{2,1,0:T(8,128)} %shard_map.68.refs_0_), custom_call_target="tpu_custom_call", output_to_operand_aliasing={{}: (2, {})} | custom-call | bytes 10485760 | tf_op jit(solution)/shard_map/pallas_call | solution.py:57
  48.9 0.8 gather_fusion.1
  49.8 6.8 %convolution_multiply_fusion.3 = f32[160,16,128]{2,1,0:T(8,128)S(1)} fusion(f32[160,128,128]{2,1,0:T(8,128)} %shard_map.69, f32[160,16,128]{2,1,0:T(8,128)S(1)} %gather_fusion.1, f32[160]{0:T(256)S(1)} %compare_convert_fusion), kind=kOutput, calls=%fused_computation.15 | convolution fusion | flops 251985920 | bytes 13107840 | tf_op jit(solution)/shard_map/skj,kji->ksi/dot_general | solution.py:73
  56.6 0.7 fusion.11
  57.6 0.3 multiply_reduce_fusion.4
  57.9 0.8 gather_fusion.2
  58.7 6.8 %convolution_multiply_fusion.2 = f32[160,16,128]{2,1,0:T(8,128)S(1)} fusion(f32[160,16,128]{2,1,0:T(8,128)S(1)} %gather_fusion.2, f32[160]{0:T(256)S(1)} %compare_convert_fusion, f32[1,160,128,128]{3,2,1,0:T(8,128)} %param.6), kind=kOutput, calls=%fused_computation.14 | convolution fusion | flops 251985920 | bytes 13107840 | tf_op jit(solution)/shard_map/ski,kij->ksj/dot_general | solution.py:85
  65.6 1.0 fusion.9
  66.6 0.9 copy.81
  67.5 0.9 fusion.44
  68.4 1.3 collective-permute-start.5
  69.7 3.9 %collective-permute-start.4 = (f32[16,8192]{1,0:T(8,128)S(1)}, f32[16,8192]{1,0:T(8,128)}, u32[]{:S(2)}, u32[]{:S(2)}) collective-permute-start(f32[16,8192]{1,0:T(8,128)S(1)} %get-tuple-element.26), channel_id=1, source_target_pairs={{0,1},{1,2},{2,3},{3,4},{4,5},{5,6},{6,7},{7,8},{8,9},{9,10},{10,1... | collective-permute-start | bytes 1572872 | tf_op jit(solution)/shard_map/ppermute | solution.py:33
  73.5 12.4 %all_to_all.29 = f32[16,1,16]{2,1,0:T(1,128)S(1)} all-to-all(f32[16,1,16]{2,1,0:T(1,128)S(1)} %broadcast_in_dim.11), channel_id=1, replica_groups=mesh['group'=2,'row'=8,'col'=2] {'row','col'}, dimensions={0} | all-to-all | bytes 2048 | tf_op jit(solution)/shard_map/all_to_all | solution.py:118
  86.0 1.3 multiply_reduce_fusion.1
  87.3 1.3 collective-permute-start.7
  88.6 3.9 %collective-permute-start.6 = (f32[16,8192]{1,0:T(8,128)S(1)}, f32[16,8192]{1,0:T(8,128)}, u32[]{:S(2)}, u32[]{:S(2)}) collective-permute-start(f32[16,8192]{1,0:T(8,128)S(1)} %get-tuple-element.17), channel_id=1, source_target_pairs={{0,1},{1,2},{2,3},{3,4},{4,5},{5,6},{6,7},{7,8},{8,9},{9,10},{10,1... | collective-permute-start | bytes 1572872 | tf_op jit(solution)/shard_map/ppermute | solution.py:24
  92.5 12.5 %all_to_all.30 = f32[16,1,16]{2,1,0:T(1,128)S(1)} all-to-all(f32[16,1,16]{2,1,0:T(1,128)S(1)} %broadcast_in_dim.12), channel_id=1, replica_groups=mesh['group'=2,'row'=8,'col'=2] {'row','col'}, dimensions={0} | all-to-all | bytes 2048 | tf_op jit(solution)/shard_map/all_to_all | solution.py:118
  105.0 1.2 copy_bitcast_fusion.3
  106.2 1.9 %gather_fusion.3 = f32[160,16,128]{2,1,0:T(8,128)} fusion(f32[16,192,128]{2,0,1:T(8,128)S(1)} %copy_bitcast_fusion.3, s32[1024]{0:T(1024)S(1)} %pad_clamp_fusion), kind=kCustom, calls=%fused_computation.3 | custom fusion | bytes 2622080 | tf_op jit(solution)/shard_map/gather | solution.py:71
  108.1 7.1 %convolution_multiply_fusion.1 = f32[160,16,128]{2,1,0:T(8,128)S(1)} fusion(f32[160,128,128]{2,1,0:T(8,128)} %shard_map.69, f32[160,16,128]{2,1,0:T(8,128)} %gather_fusion.3, f32[160]{0:T(256)S(1)} %compare_convert_fusion), kind=kOutput, calls=%fused_computation.13 | convolution fusion | flops 251985920 | bytes 13107840 | tf_op jit(solution)/shard_map/skj,kji->ksi/dot_general | solution.py:73
  115.2 0.7 fusion.7
  115.8 0.3 multiply_reduce_fusion.3
  116.1 0.8 gather_fusion.4
  117.0 6.8 %convolution_multiply_fusion = f32[160,16,128]{2,1,0:T(8,128)S(1)} fusion(f32[160,16,128]{2,1,0:T(8,128)S(1)} %gather_fusion.4, f32[160]{0:T(256)S(1)} %compare_convert_fusion, f32[1,160,128,128]{3,2,1,0:T(8,128)} %param.6), kind=kOutput, calls=%fused_computation.12 | convolution fusion | flops 251985920 | bytes 13107840 | tf_op jit(solution)/shard_map/ski,kij->ksj/dot_general | solution.py:85
  123.8 1.0 fusion.5
  124.8 0.9 copy.80
  125.8 0.9 fusion.43
  126.6 1.3 collective-permute-start.9
  127.9 3.9 %collective-permute-start.8 = (f32[16,8192]{1,0:T(8,128)S(1)}, f32[16,8192]{1,0:T(8,128)}, u32[]{:S(2)}, u32[]{:S(2)}) collective-permute-start(f32[16,8192]{1,0:T(8,128)S(1)} %get-tuple-element.24), channel_id=1, source_target_pairs={{0,1},{1,2},{2,3},{3,4},{4,5},{5,6},{6,7},{7,8},{8,9},{9,10},{10,1... | collective-permute-start | bytes 1572872 | tf_op jit(solution)/shard_map/ppermute | solution.py:33
  131.8 12.3 %all_to_all.31 = f32[16,1,16]{2,1,0:T(1,128)S(1)} all-to-all(f32[16,1,16]{2,1,0:T(1,128)S(1)} %broadcast_in_dim.13), channel_id=1, replica_groups=mesh['group'=2,'row'=8,'col'=2] {'row','col'}, dimensions={0} | all-to-all | bytes 2048 | tf_op jit(solution)/shard_map/all_to_all | solution.py:118
  144.1 1.5 multiply_reduce_fusion
  145.6 11.5 %all_to_all.32 = f32[16,1,16]{2,1,0:T(1,128)S(1)} all-to-all(f32[16,1,16]{2,1,0:T(1,128)S(1)} %broadcast_in_dim.14), channel_id=1, replica_groups=mesh['group'=2,'row'=8,'col'=2] {'row','col'}, dimensions={0} | all-to-all | bytes 2048 | tf_op jit(solution)/shard_map/all_to_all | solution.py:118
  157.3 1.2 multiply_subtract_fusion
  (48 shorter events, 1.2 us)
Async XLA Ops:
  3.8 6.9 %copy-start.2 = (s32[1,160]{1,0:T(1,128)S(1)}, s32[1,160]{1,0:T(1,128)}, u32[]{:S(2)}) copy-start(s32[1,160]{1,0:T(1,128)} %param.8) | copy-start | bytes 1924
  12.7 11.9 %collective-permute-start.1 = (f32[16,8192]{1,0:T(8,128)S(1)}, f32[16,8192]{1,0:T(8,128)S(1)}, u32[]{:S(2)}, u32[]{:S(2)}) collective-permute-start(f32[16,8192]{1,0:T(8,128)S(1)} %get-tuple-element.29), channel_id=1, source_target_pairs={{1,0},{2,1},{3,2},{4,3},{5,4},{6,5},{7,6},{8,7},{9,8},{10,9},{11,1... | collective-permute-start | bytes 1572872 | tf_op jit(solution)/shard_map/ppermute | solution.py:33
  14.0 10.7 %collective-permute-start = (f32[16,8192]{1,0:T(8,128)S(1)}, f32[16,8192]{1,0:T(8,128)S(1)}, u32[]{:S(2)}, u32[]{:S(2)}) collective-permute-start(f32[16,8192]{1,0:T(8,128)S(1)} %get-tuple-element.28), channel_id=1, source_target_pairs={{0,1},{1,2},{2,3},{3,4},{4,5},{5,6},{6,7},{7,8},{8,9},{9,10},{10,1... | collective-permute-start | bytes 1572872 | tf_op jit(solution)/shard_map/ppermute | solution.py:33
  17.6 6.9 %copy-start = (f32[16,4096]{1,0:T(8,128)S(1)}, f32[16,4096]{1,0:T(8,128)}, u32[]{:S(2)}) copy-start(f32[16,4096]{1,0:T(8,128)} %param.5) | copy-start | bytes 786436
  24.9 23.9 %collective-permute-start.3 = (f32[16,8192]{1,0:T(8,128)S(1)}, f32[16,8192]{1,0:T(8,128)S(1)}, u32[]{:S(2)}, u32[]{:S(2)}) collective-permute-start(f32[16,8192]{1,0:T(8,128)S(1)} %get-tuple-element.23), channel_id=1, source_target_pairs={{1,0},{2,1},{3,2},{4,3},{5,4},{6,5},{7,6},{8,7},{9,8},{10,9},{11,1... | collective-permute-start | bytes 1572872 | tf_op jit(solution)/shard_map/ppermute | solution.py:25
  26.2 22.6 %collective-permute-start.2 = (f32[16,8192]{1,0:T(8,128)S(1)}, f32[16,8192]{1,0:T(8,128)S(1)}, u32[]{:S(2)}, u32[]{:S(2)}) collective-permute-start(f32[16,8192]{1,0:T(8,128)S(1)} %get-tuple-element.23), channel_id=1, source_target_pairs={{0,1},{1,2},{2,3},{3,4},{4,5},{5,6},{6,7},{7,8},{8,9},{9,10},{10,1... | collective-permute-start | bytes 1572872 | tf_op jit(solution)/shard_map/ppermute | solution.py:24
  35.0 13.7 %all-to-all-start = ((f32[16,2,16]{2,1,0:T(2,128)}), f32[16,2,16]{2,1,0:T(2,128)S(1)}, u32[]{:S(2)}, u32[]{:S(2)}) async-start(f32[16,2,16]{2,1,0:T(2,128)} %broadcast_in_dim.10), calls=%async_computation | async-start | bytes 32768 | tf_op jit(solution)/shard_map/all_to_all | solution.py:118
  49.8 6.9 %copy-start.3 = (s32[1,160]{1,0:T(1,128)S(1)}, s32[1,160]{1,0:T(1,128)}, u32[]{:S(2)}) copy-start(s32[1,160]{1,0:T(1,128)} %param.7) | copy-start | bytes 1924
  56.6 1.0 copy-start.1
  68.4 17.6 %collective-permute-start.5 = (f32[16,8192]{1,0:T(8,128)}, f32[16,8192]{1,0:T(8,128)S(1)}, u32[]{:S(2)}, u32[]{:S(2)}) collective-permute-start(f32[16,8192]{1,0:T(8,128)} %get-tuple-element.27), channel_id=1, source_target_pairs={{1,0},{2,1},{3,2},{4,3},{5,4},{6,5},{7,6},{8,7},{9,8},{10,9},{11,1... | collective-permute-start | bytes 1572872 | tf_op jit(solution)/shard_map/ppermute | solution.py:33
  69.7 16.3 %collective-permute-start.4 = (f32[16,8192]{1,0:T(8,128)S(1)}, f32[16,8192]{1,0:T(8,128)}, u32[]{:S(2)}, u32[]{:S(2)}) collective-permute-start(f32[16,8192]{1,0:T(8,128)S(1)} %get-tuple-element.26), channel_id=1, source_target_pairs={{0,1},{1,2},{2,3},{3,4},{4,5},{5,6},{6,7},{7,8},{8,9},{9,10},{10,1... | collective-permute-start | bytes 1572872 | tf_op jit(solution)/shard_map/ppermute | solution.py:33
  87.3 17.7 %collective-permute-start.7 = (f32[16,8192]{1,0:T(8,128)S(1)}, f32[16,8192]{1,0:T(8,128)S(1)}, u32[]{:S(2)}, u32[]{:S(2)}) collective-permute-start(f32[16,8192]{1,0:T(8,128)S(1)} %get-tuple-element.17), channel_id=1, source_target_pairs={{1,0},{2,1},{3,2},{4,3},{5,4},{6,5},{7,6},{8,7},{9,8},{10,9},{11,1... | collective-permute-start | bytes 1572872 | tf_op jit(solution)/shard_map/ppermute | solution.py:25
  88.6 16.4 %collective-permute-start.6 = (f32[16,8192]{1,0:T(8,128)S(1)}, f32[16,8192]{1,0:T(8,128)}, u32[]{:S(2)}, u32[]{:S(2)}) collective-permute-start(f32[16,8192]{1,0:T(8,128)S(1)} %get-tuple-element.17), channel_id=1, source_target_pairs={{0,1},{1,2},{2,3},{3,4},{4,5},{5,6},{6,7},{7,8},{8,9},{9,10},{10,1... | collective-permute-start | bytes 1572872 | tf_op jit(solution)/shard_map/ppermute | solution.py:24
  126.6 17.5 %collective-permute-start.9 = (f32[16,8192]{1,0:T(8,128)}, f32[16,8192]{1,0:T(8,128)}, u32[]{:S(2)}, u32[]{:S(2)}) collective-permute-start(f32[16,8192]{1,0:T(8,128)} %get-tuple-element.25), channel_id=1, source_target_pairs={{1,0},{2,1},{3,2},{4,3},{5,4},{6,5},{7,6},{8,7},{9,8},{10,9},{11,1... | collective-permute-start | bytes 1572872 | tf_op jit(solution)/shard_map/ppermute | solution.py:33
  127.9 16.2 %collective-permute-start.8 = (f32[16,8192]{1,0:T(8,128)S(1)}, f32[16,8192]{1,0:T(8,128)}, u32[]{:S(2)}, u32[]{:S(2)}) collective-permute-start(f32[16,8192]{1,0:T(8,128)S(1)} %get-tuple-element.24), channel_id=1, source_target_pairs={{0,1},{1,2},{2,3},{3,4},{4,5},{5,6},{6,7},{7,8},{8,9},{9,10},{10,1... | collective-permute-start | bytes 1572872 | tf_op jit(solution)/shard_map/ppermute | solution.py:33

commit v17 on v10

--- a/solution.py
+++ b/solution.py
@@ -107,6 +107,24 @@
     spread = jnp.broadcast_to(values[None], (peers,) + values.shape)
     gathered = lax.all_to_all(spread, axes, 0, 0, tiled=True)
     return jnp.sum(gathered, axis=0)
+
+
+def xor_sum(values, axes):
+    peers = 1
+    for axis in axes:
+        peers *= lax.axis_size(axis)
+    if peers & (peers - 1):
+        return all_sum(values, axes)
+    shift = 1
+    while shift < peers:
+        width = 4 if shift * 4 <= peers else 2
+        parts = [values] + [
+            lax.ppermute(values, axes, [(i, i ^ (k * shift)) for i in range(peers)])
+            for k in range(1, width)
+        ]
+        values = (parts[0] + parts[1]) + (parts[2] + parts[3]) if width == 4 else parts[0] + parts[1]
+        shift *= width
+    return values
 
 
 def squares(field):
@@ -151,7 +169,8 @@
         right_raw = right_prod / row_norm[:, None] - row_norm[:, None] * right_vec
         if iteration + 1 < ITERATIONS:
             left_prod = forward(right_raw)
-        col_norm = jnp.sqrt(all_sum(squares(right_raw), axes) + 1e-06)
+        reduce = all_sum if iteration + 1 < ITERATIONS else xor_sum
+        col_norm = jnp.sqrt(reduce(squares(right_raw), axes) + 1e-06)
         right_vec = right_raw / col_norm[:, None]
         if iteration + 1 < ITERATIONS:
             left_raw = left_prod / col_norm[:, None] - col_norm[:, None] * left_vec

time: 156 us -> 158 us (1.013)
  blocking collectives: 51.5 us -> 41.5 us
  waiting for transfers between devices: 6.5 us -> 13 us
  starting transfers between devices: 29.1 us -> 34.7 us
    all_to_all x4 -> x3, blocking collectives: 51.5 us -> 41.5 us  [all_sum(): gathered = lax.all_to_all(spread, axes, 0, 0, tiled=True)]
    ppermute x0 -> x6, waiting for transfers between devices: none -> 6.53 us  [xor_sum(): lax.ppermute(values, axes, [(i, i ^ k * shift) for i in range(peers)])]
    ppermute x0 -> x6, starting transfers between devices: none -> 6.32 us  [xor_sum(): lax.ppermute(values, axes, [(i, i ^ k * shift) for i in range(peers)])]
  transfers between devices with their start and end apart: 11 -> 17, of which waited for: 1 -> 5; matrix products, arithmetic and copies ran while one was open for 1% -> 1% of each run, Pallas kernels for 6% -> 5%
where the time goes in v17:
time: 158 us
  blocking collectives  41.5 us (26%)
  matrix products  38.7 us (24%)
  starting transfers between devices  34.7 us (22%)
  waiting for transfers between devices  13 us (8%)
  local copies, waits for them, and re-layouts  12.4 us (8%)
  Pallas kernels  8.57 us (5%)
  other arithmetic  7.07 us (4%)
  between operations  1.74 us (1%)
    all_to_all x3, blocking collectives, all_sum(): gathered = lax.all_to_all(spread, axes, 0, 0, tiled=True)  41.5 us
    dot_general x3, matrix products, transpose_local(): jnp.einsum('ski,kij->ksj', pieces, tile_stack, precision=PRODUCT_PRECISION)  20.5 us
    dot_general x2, matrix products, forward_local(): jnp.einsum('skj,kji->ksi', pieces, tile_stack, precision=PRODUCT_PRECISION)  13.9 us
    ppermute x6, starting transfers between devices, from_behind(): return lax.ppermute(shard, axis, pairs)  9.66 us
    all_to_all x1, starting transfers between devices, all_sum(): gathered = lax.all_to_all(spread, axes, 0, 0, tiled=True)  8.68 us
    pallas_call x1, Pallas kernels, transpose_blocks(): pl.pallas_call(body, grid=(slots // step,), in_specs=[pl.BlockSpec(memory...  8.57 us
    ppermute x2, starting transfers between devices, with_halo(): before = lax.ppermute(last, axis, up)  7.41 us
    ppermute x6, waiting for transfers between devices, xor_sum(): lax.ppermute(values, axes, [(i, i ^ k * shift) for i in range(peers)])  6.53 us
  transfers between devices with their start and end apart: 17, of which 5 were waited for; matrix products, arithmetic and copies ran while one was open for 1% of the time, Pallas kernels for 5%

profile of v17, /device:TPU:0, one launch (start us, length us, event | category | flops | bytes accessed | tf_op | source)
XLA Modules:
  0.0 157.7 jit_solution(4717813760513374263)
XLA Ops:
  1.3 0.7 compare_select_fusion.1
  2.0 1.0 copy_bitcast_fusion.7
  3.0 0.8 gather_fusion
  3.8 6.8 %convolution_multiply_fusion.4 = f32[160,16,128]{2,1,0:T(8,128)S(1)} fusion(f32[160,16,128]{2,1,0:T(8,128)S(1)} %gather_fusion, f32[160]{0:T(256)S(1)} %compare_convert_fusion, f32[1,160,128,128]{3,2,1,0:T(8,128)} %param.6), kind=kOutput, calls=%fused_computation.16 | convolution fusion | flops 251985920 | bytes 13107840 | tf_op jit(solution)/shard_map/ski,kij->ksj/dot_general | solution.py:75
  10.7 1.0 fusion.13
  11.7 0.9 copy.80
  12.7 2.4 %collective-permute-start = (f32[16,8192]{1,0:T(8,128)S(1)}, f32[16,8192]{1,0:T(8,128)S(1)}, u32[]{:S(2)}, u32[]{:S(2)}) collective-permute-start(f32[16,8192]{1,0:T(8,128)S(1)} %get-tuple-element.29), channel_id=1, source_target_pairs={{0,1},{1,2},{2,3},{3,4},{4,5},{5,6},{6,7},{7,8},{8,9},{9,10},{10,1... | collective-permute-start | bytes 1572872 | tf_op jit(solution)/shard_map/ppermute | solution.py:33
  15.1 1.3 collective-permute-start.1
  16.9 8.6 %shard_map.68 = f32[160,128,128]{2,1,0:T(8,128)} custom-call(f32[1,1]{1,0:T(1,128)} %slice.60.anchor_ref, f32[160,128,128]{2,1,0:T(8,128)} %bitcast.118), custom_call_target="tpu_custom_call" | custom-call | bytes 20971520 | tf_op jit(solution)/shard_map/pallas_call | solution.py:45
  25.9 5.7 %collective-permute-start.2 = (f32[16,8192]{1,0:T(8,128)S(1)}, f32[16,8192]{1,0:T(8,128)S(1)}, u32[]{:S(2)}, u32[]{:S(2)}) collective-permute-start(f32[16,8192]{1,0:T(8,128)S(1)} %get-tuple-element.24), channel_id=1, source_target_pairs={{0,1},{1,2},{2,3},{3,4},{4,5},{5,6},{6,7},{7,8},{8,9},{9,10},{10,1... | collective-permute-start | bytes 1572872 | tf_op jit(solution)/shard_map/ppermute | solution.py:24
  31.6 1.3 collective-permute-start.3
  33.5 8.7 %all-to-all-start = ((f32[16,2,16]{2,1,0:T(2,128)}), f32[16,2,16]{2,1,0:T(2,128)S(1)}, u32[]{:S(2)}, u32[]{:S(2)}) async-start(f32[16,2,16]{2,1,0:T(2,128)} %broadcast_in_dim.8), calls=%async_computation | async-start | bytes 32768 | tf_op jit(solution)/shard_map/all_to_all | solution.py:108
  42.2 6.5 %all-to-all-done = f32[16,2,16]{2,1,0:T(2,128)S(1)} async-done(((f32[16,2,16]{2,1,0:T(2,128)}), f32[16,2,16]{2,1,0:T(2,128)S(1)}, u32[]{:S(2)}, u32[]{:S(2)}) %all-to-all-start) | async-done | bytes 2080 | tf_op jit(solution)/shard_map/all_to_all | solution.py:108
  48.9 0.8 gather_fusion.1
  49.7 6.8 %convolution_multiply_fusion.3 = f32[160,16,128]{2,1,0:T(8,128)S(1)} fusion(f32[160,128,128]{2,1,0:T(8,128)} %shard_map.68, f32[160,16,128]{2,1,0:T(8,128)S(1)} %gather_fusion.1, f32[160]{0:T(256)S(1)} %compare_convert_fusion), kind=kOutput, calls=%fused_computation.15 | convolution fusion | flops 251985920 | bytes 13107840 | tf_op jit(solution)/shard_map/skj,kji->ksi/dot_general | solution.py:63
  57.9 0.8 gather_fusion.2
  58.7 6.8 %convolution_multiply_fusion.2 = f32[160,16,128]{2,1,0:T(8,128)S(1)} fusion(f32[160,16,128]{2,1,0:T(8,128)S(1)} %gather_fusion.2, f32[160]{0:T(256)S(1)} %compare_convert_fusion, f32[1,160,128,128]{3,2,1,0:T(8,128)} %param.6), kind=kOutput, calls=%fused_computation.14 | convolution fusion | flops 251985920 | bytes 13107840 | tf_op jit(solution)/shard_map/ski,kij->ksj/dot_general | solution.py:75
  65.5 1.0 fusion.9
  66.5 0.9 copy.79
  67.5 0.9 fusion.44
  68.3 1.7 %collective-permute-start.4 = (f32[16,8192]{1,0:T(8,128)}, f32[16,8192]{1,0:T(8,128)S(1)}, u32[]{:S(2)}, u32[]{:S(2)}) collective-permute-start(f32[16,8192]{1,0:T(8,128)} %get-tuple-element.27), channel_id=1, source_target_pairs={{0,1},{1,2},{2,3},{3,4},{4,5},{5,6},{6,7},{7,8},{8,9},{9,10},{10,1... | collective-permute-start | bytes 1572872 | tf_op jit(solution)/shard_map/ppermute | solution.py:33
  70.0 1.3 collective-permute-start.5
  71.3 13.3 %all_to_all.23 = f32[16,1,16]{2,1,0:T(1,128)S(1)} all-to-all(f32[16,1,16]{2,1,0:T(1,128)S(1)} %broadcast_in_dim.9), channel_id=1, replica_groups=mesh['group'=2,'row'=8,'col'=2] {'row','col'}, dimensions={0} | all-to-all | bytes 2048 | tf_op jit(solution)/shard_map/all_to_all | solution.py:108
  84.6 1.3 multiply_reduce_fusion.1
  86.0 1.7 %collective-permute-start.6 = (f32[16,8192]{1,0:T(8,128)S(1)}, f32[16,8192]{1,0:T(8,128)S(1)}, u32[]{:S(2)}, u32[]{:S(2)}) collective-permute-start(f32[16,8192]{1,0:T(8,128)S(1)} %get-tuple-element.18), channel_id=1, source_target_pairs={{0,1},{1,2},{2,3},{3,4},{4,5},{5,6},{6,7},{7,8},{8,9},{9,10},{10,1... | collective-permute-start | bytes 1572872 | tf_op jit(solution)/shard_map/ppermute | solution.py:24
  87.7 1.3 collective-permute-start.7
  89.0 14.2 %all_to_all.24 = f32[16,1,16]{2,1,0:T(1,128)S(1)} all-to-all(f32[16,1,16]{2,1,0:T(1,128)S(1)} %broadcast_in_dim.10), channel_id=1, replica_groups=mesh['group'=2,'row'=8,'col'=2] {'row','col'}, dimensions={0} | all-to-all | bytes 2048 | tf_op jit(solution)/shard_map/all_to_all | solution.py:108
  103.3 1.2 copy_bitcast_fusion.3
  104.5 1.9 %gather_fusion.3 = f32[160,16,128]{2,1,0:T(8,128)} fusion(f32[16,192,128]{2,0,1:T(8,128)S(1)} %copy_bitcast_fusion.3, s32[1024]{0:T(1024)S(1)} %pad_clamp_fusion), kind=kCustom, calls=%fused_computation.3 | custom fusion | bytes 2622080 | tf_op jit(solution)/shard_map/gather | solution.py:61
  106.4 7.1 %convolution_multiply_fusion.1 = f32[160,16,128]{2,1,0:T(8,128)S(1)} fusion(f32[160,128,128]{2,1,0:T(8,128)} %shard_map.68, f32[160,16,128]{2,1,0:T(8,128)} %gather_fusion.3, f32[160]{0:T(256)S(1)} %compare_convert_fusion), kind=kOutput, calls=%fused_computation.13 | convolution fusion | flops 251985920 | bytes 13107840 | tf_op jit(solution)/shard_map/skj,kji->ksi/dot_general | solution.py:63
  114.4 0.8 gather_fusion.4
  115.2 6.8 %convolution_multiply_fusion = f32[160,16,128]{2,1,0:T(8,128)S(1)} fusion(f32[160,16,128]{2,1,0:T(8,128)S(1)} %gather_fusion.4, f32[160]{0:T(256)S(1)} %compare_convert_fusion, f32[1,160,128,128]{3,2,1,0:T(8,128)} %param.6), kind=kOutput, calls=%fused_computation.12 | convolution fusion | flops 251985920 | bytes 13107840 | tf_op jit(solution)/shard_map/ski,kij->ksj/dot_general | solution.py:75
  122.1 1.0 fusion.5
  123.1 0.9 copy.78
  124.0 1.0 fusion.43
  125.1 1.7 %collective-permute-start.8 = (f32[16,8192]{1,0:T(8,128)}, f32[16,8192]{1,0:T(8,128)S(1)}, u32[]{:S(2)}, u32[]{:S(2)}) collective-permute-start(f32[16,8192]{1,0:T(8,128)} %get-tuple-element.25), channel_id=1, source_target_pairs={{0,1},{1,2},{2,3},{3,4},{4,5},{5,6},{6,7},{7,8},{8,9},{9,10},{10,1... | collective-permute-start | bytes 1572872 | tf_op jit(solution)/shard_map/ppermute | solution.py:33
  126.8 1.3 collective-permute-start.9
  128.1 14.0 %all_to_all.25 = f32[16,1,16]{2,1,0:T(1,128)S(1)} all-to-all(f32[16,1,16]{2,1,0:T(1,128)S(1)} %broadcast_in_dim.11), channel_id=1, replica_groups=mesh['group'=2,'row'=8,'col'=2] {'row','col'}, dimensions={0} | all-to-all | bytes 2048 | tf_op jit(solution)/shard_map/all_to_all | solution.py:108
  142.2 1.3 multiply_reduce_fusion
  143.6 1.3 collective-permute-start.11
  145.4 1.7 %collective-permute-done.11 = f32[16]{0:T(128)S(1)} collective-permute-done((f32[16]{0:T(128)S(1)}, f32[16]{0:T(128)S(1)}, u32[]{:S(2)}, u32[]{:S(2)}) %collective-permute-start.11) | collective-permute-done | bytes 96 | tf_op jit(solution)/shard_map/ppermute | solution.py:122
  147.2 0.7 collective-permute-done.12
  147.9 0.9 collective-permute-start.13
  148.7 2.3 %collective-permute-start.14 = (f32[16]{0:T(128)S(1)}, f32[16]{0:T(128)S(1)}, u32[]{:S(2)}, u32[]{:S(2)}) collective-permute-start(f32[16]{0:T(128)S(1)} %add_add_fusion.1), channel_id=1, source_target_pairs={{0,8},{1,9},{2,10},{3,11},{4,12},{5,13},{6,14},{7,15},{8,0},{9,1},... | collective-permute-start | bytes 200 | tf_op jit(solution)/shard_map/ppermute | solution.py:122
  151.0 1.2 collective-permute-start.15
  152.3 0.9 collective-permute-done.14
  153.2 3.2 %collective-permute-done.15 = f32[16]{0:T(128)S(1)} collective-permute-done((f32[16]{0:T(128)S(1)}, f32[16]{0:T(128)S(1)}, u32[]{:S(2)}, u32[]{:S(2)}) %collective-permute-start.15) | collective-permute-done | bytes 96 | tf_op jit(solution)/shard_map/ppermute | solution.py:122
  156.5 1.2 multiply_subtract_fusion
  (56 shorter events, 4.8 us)
Async XLA Ops:
  3.8 6.9 %copy-start.2 = (s32[1,160]{1,0:T(1,128)S(1)}, s32[1,160]{1,0:T(1,128)}, u32[]{:S(2)}) copy-start(s32[1,160]{1,0:T(1,128)} %param.8) | copy-start | bytes 1924
  12.7 12.9 %collective-permute-start = (f32[16,8192]{1,0:T(8,128)S(1)}, f32[16,8192]{1,0:T(8,128)S(1)}, u32[]{:S(2)}, u32[]{:S(2)}) collective-permute-start(f32[16,8192]{1,0:T(8,128)S(1)} %get-tuple-element.29), channel_id=1, source_target_pairs={{0,1},{1,2},{2,3},{3,4},{4,5},{5,6},{6,7},{7,8},{8,9},{9,10},{10,1... | collective-permute-start | bytes 1572872 | tf_op jit(solution)/shard_map/ppermute | solution.py:33
  15.1 10.6 %collective-permute-start.1 = (f32[16,8192]{1,0:T(8,128)S(1)}, f32[16,8192]{1,0:T(8,128)S(1)}, u32[]{:S(2)}, u32[]{:S(2)}) collective-permute-start(f32[16,8192]{1,0:T(8,128)S(1)} %get-tuple-element.30), channel_id=1, source_target_pairs={{1,0},{2,1},{3,2},{4,3},{5,4},{6,5},{7,6},{8,7},{9,8},{10,9},{11,1... | collective-permute-start | bytes 1572872 | tf_op jit(solution)/shard_map/ppermute | solution.py:33
  16.9 8.6 %copy-start = (f32[16,4096]{1,0:T(8,128)S(1)}, f32[16,4096]{1,0:T(8,128)}, u32[]{:S(2)}) copy-start(f32[16,4096]{1,0:T(8,128)} %param.5) | copy-start | bytes 786436
  25.9 22.9 %collective-permute-start.2 = (f32[16,8192]{1,0:T(8,128)S(1)}, f32[16,8192]{1,0:T(8,128)S(1)}, u32[]{:S(2)}, u32[]{:S(2)}) collective-permute-start(f32[16,8192]{1,0:T(8,128)S(1)} %get-tuple-element.24), channel_id=1, source_target_pairs={{0,1},{1,2},{2,3},{3,4},{4,5},{5,6},{6,7},{7,8},{8,9},{9,10},{10,1... | collective-permute-start | bytes 1572872 | tf_op jit(solution)/shard_map/ppermute | solution.py:24
  31.6 17.2 %collective-permute-start.3 = (f32[16,8192]{1,0:T(8,128)S(1)}, f32[16,8192]{1,0:T(8,128)S(1)}, u32[]{:S(2)}, u32[]{:S(2)}) collective-permute-start(f32[16,8192]{1,0:T(8,128)S(1)} %get-tuple-element.24), channel_id=1, source_target_pairs={{1,0},{2,1},{3,2},{4,3},{5,4},{6,5},{7,6},{8,7},{9,8},{10,9},{11,1... | collective-permute-start | bytes 1572872 | tf_op jit(solution)/shard_map/ppermute | solution.py:25
  33.5 15.2 %all-to-all-start = ((f32[16,2,16]{2,1,0:T(2,128)}), f32[16,2,16]{2,1,0:T(2,128)S(1)}, u32[]{:S(2)}, u32[]{:S(2)}) async-start(f32[16,2,16]{2,1,0:T(2,128)} %broadcast_in_dim.8), calls=%async_computation | async-start | bytes 32768 | tf_op jit(solution)/shard_map/all_to_all | solution.py:108
  49.7 6.9 %copy-start.3 = (s32[1,160]{1,0:T(1,128)S(1)}, s32[1,160]{1,0:T(1,128)}, u32[]{:S(2)}) copy-start(s32[1,160]{1,0:T(1,128)} %param.7) | copy-start | bytes 1924
  56.6 1.0 copy-start.1
  68.3 16.3 %collective-permute-start.4 = (f32[16,8192]{1,0:T(8,128)}, f32[16,8192]{1,0:T(8,128)S(1)}, u32[]{:S(2)}, u32[]{:S(2)}) collective-permute-start(f32[16,8192]{1,0:T(8,128)} %get-tuple-element.27), channel_id=1, source_target_pairs={{0,1},{1,2},{2,3},{3,4},{4,5},{5,6},{6,7},{7,8},{8,9},{9,10},{10,1... | collective-permute-start | bytes 1572872 | tf_op jit(solution)/shard_map/ppermute | solution.py:33
  70.0 14.6 %collective-permute-start.5 = (f32[16,8192]{1,0:T(8,128)S(1)}, f32[16,8192]{1,0:T(8,128)}, u32[]{:S(2)}, u32[]{:S(2)}) collective-permute-start(f32[16,8192]{1,0:T(8,128)S(1)} %get-tuple-element.28), channel_id=1, source_target_pairs={{1,0},{2,1},{3,2},{4,3},{5,4},{6,5},{7,6},{8,7},{9,8},{10,9},{11,1... | collective-permute-start | bytes 1572872 | tf_op jit(solution)/shard_map/ppermute | solution.py:33
  86.0 17.3 %collective-permute-start.6 = (f32[16,8192]{1,0:T(8,128)S(1)}, f32[16,8192]{1,0:T(8,128)S(1)}, u32[]{:S(2)}, u32[]{:S(2)}) collective-permute-start(f32[16,8192]{1,0:T(8,128)S(1)} %get-tuple-element.18), channel_id=1, source_target_pairs={{0,1},{1,2},{2,3},{3,4},{4,5},{5,6},{6,7},{7,8},{8,9},{9,10},{10,1... | collective-permute-start | bytes 1572872 | tf_op jit(solution)/shard_map/ppermute | solution.py:24
  87.7 15.6 %collective-permute-start.7 = (f32[16,8192]{1,0:T(8,128)S(1)}, f32[16,8192]{1,0:T(8,128)}, u32[]{:S(2)}, u32[]{:S(2)}) collective-permute-start(f32[16,8192]{1,0:T(8,128)S(1)} %get-tuple-element.18), channel_id=1, source_target_pairs={{1,0},{2,1},{3,2},{4,3},{5,4},{6,5},{7,6},{8,7},{9,8},{10,9},{11,1... | collective-permute-start | bytes 1572872 | tf_op jit(solution)/shard_map/ppermute | solution.py:25
  125.1 17.1 %collective-permute-start.8 = (f32[16,8192]{1,0:T(8,128)}, f32[16,8192]{1,0:T(8,128)S(1)}, u32[]{:S(2)}, u32[]{:S(2)}) collective-permute-start(f32[16,8192]{1,0:T(8,128)} %get-tuple-element.25), channel_id=1, source_target_pairs={{0,1},{1,2},{2,3},{3,4},{4,5},{5,6},{6,7},{7,8},{8,9},{9,10},{10,1... | collective-permute-start | bytes 1572872 | tf_op jit(solution)/shard_map/ppermute | solution.py:33
  126.8 15.4 %collective-permute-start.9 = (f32[16,8192]{1,0:T(8,128)}, f32[16,8192]{1,0:T(8,128)}, u32[]{:S(2)}, u32[]{:S(2)}) collective-permute-start(f32[16,8192]{1,0:T(8,128)} %get-tuple-element.26), channel_id=1, source_target_pairs={{1,0},{2,1},{3,2},{4,3},{5,4},{6,5},{7,6},{8,7},{9,8},{10,9},{11,1... | collective-permute-start | bytes 1572872 | tf_op jit(solution)/shard_map/ppermute | solution.py:33
  143.5 1.9 %collective-permute-start.10 = (f32[16]{0:T(128)S(1)}, f32[16]{0:T(128)S(1)}, u32[]{:S(2)}, u32[]{:S(2)}) collective-permute-start(f32[16]{0:T(128)S(1)} %get-tuple-element.9), channel_id=1, source_target_pairs={{0,1},{1,0},{2,3},{3,2},{4,5},{5,4},{6,7},{7,6},{8,9},{9,8},{10,11... | collective-permute-start | bytes 200 | tf_op jit(solution)/shard_map/ppermute | solution.py:122
  143.6 3.6 %collective-permute-start.11 = (f32[16]{0:T(128)S(1)}, f32[16]{0:T(128)S(1)}, u32[]{:S(2)}, u32[]{:S(2)}) collective-permute-start(f32[16]{0:T(128)S(1)} %get-tuple-element.9), channel_id=1, source_target_pairs={{0,2},{1,3},{2,0},{3,1},{4,6},{5,7},{6,4},{7,5},{8,10},{9,11},{10,... | collective-permute-start | bytes 200 | tf_op jit(solution)/shard_map/ppermute | solution.py:122
  144.9 3.0 %collective-permute-start.12 = (f32[16]{0:T(128)S(1)}, f32[16]{0:T(128)S(1)}, u32[]{:S(2)}, u32[]{:S(2)}) collective-permute-start(f32[16]{0:T(128)S(1)} %get-tuple-element.9), channel_id=1, source_target_pairs={{0,3},{1,2},{2,1},{3,0},{4,7},{5,6},{6,5},{7,4},{8,11},{9,10},{10,... | collective-permute-start | bytes 200 | tf_op jit(solution)/shard_map/ppermute | solution.py:122
  147.9 4.4 %collective-permute-start.13 = (f32[16]{0:T(128)S(1)}, f32[16]{0:T(128)S(1)}, u32[]{:S(2)}, u32[]{:S(2)}) collective-permute-start(f32[16]{0:T(128)S(1)} %add_add_fusion.1), channel_id=1, source_target_pairs={{0,4},{1,5},{2,6},{3,7},{4,0},{5,1},{6,2},{7,3},{8,12},{9,13},{10,... | collective-permute-start | bytes 200 | tf_op jit(solution)/shard_map/ppermute | solution.py:122
  148.7 4.4 %collective-permute-start.14 = (f32[16]{0:T(128)S(1)}, f32[16]{0:T(128)S(1)}, u32[]{:S(2)}, u32[]{:S(2)}) collective-permute-start(f32[16]{0:T(128)S(1)} %add_add_fusion.1), channel_id=1, source_target_pairs={{0,8},{1,9},{2,10},{3,11},{4,12},{5,13},{6,14},{7,15},{8,0},{9,1},... | collective-permute-start | bytes 200 | tf_op jit(solution)/shard_map/ppermute | solution.py:122
  151.0 5.3 %collective-permute-start.15 = (f32[16]{0:T(128)S(1)}, f32[16]{0:T(128)S(1)}, u32[]{:S(2)}, u32[]{:S(2)}) collective-permute-start(f32[16]{0:T(128)S(1)} %add_add_fusion.1), channel_id=1, source_target_pairs={{0,12},{1,13},{2,14},{3,15},{4,8},{5,9},{6,10},{7,11},{8,4},{9,5},... | collective-permute-start | bytes 200 | tf_op jit(solution)/shard_map/ppermute | solution.py:122
